TPU v7x, 32 devices: a whole 2x2x4 slice. The times are simulated.
32 devices in a mesh: survey: 2 (over y), xb: 4 (over z), yb: 2 (over x), tx: 2 (over core).
Axes of the slice: x: 2, y: 2, z: 4, core: 2. Of those that a mesh axis runs over, the one named last changes fastest.
Arguments:
- primaries: bfloat16 [64, 2, 3, 32, 16, 256], P(('survey', 'tx'), None, None, None, 'xb', 'yb'), parts along dimension 0, may hold values from -6 to 6
- conductivity: float32 [6, 32, 16, 256], P('survey', 'tx', 'xb', 'yb'), parts along dimension 0, may hold values from 0.3 to 3
- group_of: int32 [64], P('survey'), parts along dimension 0, may hold values from 0 to 1, as said below
- sign_of: int32 [64], P('survey'), parts along dimension 0, may hold values from -1 to 1, as said below
Outputs:
- secondary: float32 [4, 2, 3, 32, 16, 256], P(('survey', 'tx'), None, None, None, 'xb', 'yb'), parts along dimension 0
There are 2 independent parts, one for each index of `survey`. A program takes and returns all parts, laid end to end along the dimension named above; each array names one. Nothing has to cross between parts.
Inputs may be any that keep to these rules, and one draw needn't show every extreme that they name: `group_of`: every supershot is joined by exactly 16 transmitters. `sign_of`: each weight is -1 or +1, never 0.
All inputs are finite; a program needn't handle non-finite values.
Results may differ from a plain program's by a relative error of at most 0.0003.
Values may be sent and summed in bfloat16 or wider, within the bound.
No kernel may reach another device: no remote copies, remote signals or barrier semaphores. Data moves between devices by JAX's collectives and lax.ppermute only.
A program may use at most 64 MiB of HBM per device.

v0:
```python
import jax
import jax.numpy as jnp
from jax import lax
from jax.sharding import PartitionSpec as P

NS_DEV = 1
SWEEPS = 2


K_FREQ = 2.0
RELAX = 0.6


def from_behind(block, axis, distance):
    devices = range(lax.axis_size(axis))
    route = [(i - distance, i) for i in devices if i - distance in devices]
    return lax.ppermute(block, axis, route)


def with_halo(cells, sides, width):
    for axis, dim in sides:
        count = lax.axis_size(axis)
        ends = count - 1
        head = lax.slice_in_dim(cells, 0, width, axis=dim)
        tail = lax.slice_in_dim(cells, cells.shape[dim] - width, cells.shape[dim], axis=dim)
        cells = jnp.concatenate(
            [
                lax.ppermute(tail, axis, [(i, (i + 1) % count) for i in range(ends)]),
                cells,
                lax.ppermute(head, axis, [((i + 1) % count, i) for i in range(ends)]),
            ],
            axis=dim,
        )
    return cells


def inner(f):
    return f[..., :-1, :-1, :-1]


def fwd_z(f):
    return f[..., 1:, :-1, :-1] - inner(f)


def fwd_x(f):
    return f[..., :-1, 1:, :-1] - inner(f)


def fwd_y(f):
    return f[..., :-1, :-1, 1:] - inner(f)


def back_z(g):
    return g[..., 1:, 1:, 1:] - g[..., :-1, 1:, 1:]


def back_x(g):
    return g[..., 1:, 1:, 1:] - g[..., 1:, :-1, 1:]


def back_y(g):
    return g[..., 1:, 1:, 1:] - g[..., 1:, 1:, :-1]


def curl_curl(padded):
    e_x = padded[..., 0, :, :, :]
    e_y = padded[..., 1, :, :, :]
    e_z = padded[..., 2, :, :, :]
    h_x = fwd_y(e_z) - fwd_z(e_y)
    h_y = fwd_z(e_x) - fwd_x(e_z)
    h_z = fwd_x(e_y) - fwd_y(e_x)
    c_x = back_y(h_z) - back_z(h_y)
    c_y = back_z(h_x) - back_x(h_z)
    c_z = back_x(h_y) - back_y(h_x)
    return jnp.stack([c_x, c_y, c_z], axis=-4)


def apply_operator(field, padded, kappa):
    curled = curl_curl(padded)
    real_part = curled[..., 0, :, :, :, :] - kappa * field[..., 1, :, :, :, :]
    imag_part = curled[..., 1, :, :, :, :] + kappa * field[..., 0, :, :, :, :]
    return jnp.stack([real_part, imag_part], axis=-5)


def jacobi(resid, kappa):
    denom = 16.0 + kappa * kappa
    real_part = (4.0 * resid[..., 0, :, :, :, :] + kappa * resid[..., 1, :, :, :, :]) / denom
    imag_part = (4.0 * resid[..., 1, :, :, :, :] - kappa * resid[..., 0, :, :, :, :]) / denom
    return jnp.stack([real_part, imag_part], axis=-5)


def source_term(shot, delta):
    return jnp.stack([delta * shot[..., 1, :, :, :, :], -delta * shot[..., 0, :, :, :, :]], axis=-5)


def y_extend(field):
    face_shape = field.shape[:-1] + (1,)
    leading = field.shape[0]
    last_layer = field[..., -1:].reshape(leading, -1)
    first_layer = field[..., :1].reshape(leading, -1)
    from_low = from_behind(last_layer, "yb", 1)
    from_high = from_behind(first_layer, "yb", -1)
    return jnp.concatenate(
        [from_low.reshape(face_shape), field, from_high.reshape(face_shape)], axis=5
    )


def x_extend(field):
    return with_halo(field, (("xb", 4),), 1)


def extend_field(field):
    wider = x_extend(y_extend(field))
    return jnp.pad(wider, [(0, 0), (0, 0), (0, 0), (1, 1), (0, 0), (0, 0)])


def encode_weights(group_part, sign_part, rows):
    picked = group_part[None, :] == rows[:, None]
    return jnp.where(picked, sign_part[None, :], 0).astype(jnp.float32).astype(jnp.bfloat16)


def body(primaries, conductivity, group_of, sign_of):
    nt_local = primaries.shape[0]
    depth = primaries.shape[3]
    width_x = primaries.shape[4]
    width_y = primaries.shape[5]
    tx_index = lax.axis_index("tx")
    flat = primaries.reshape(nt_local, -1)
    own_groups = lax.dynamic_slice_in_dim(group_of, tx_index * nt_local, nt_local, 0)
    own_signs = lax.dynamic_slice_in_dim(sign_of, tx_index * nt_local, nt_local, 0)
    rows = jnp.arange(NS_DEV * lax.axis_size("tx"), dtype=jnp.int32)
    weights = encode_weights(own_groups, own_signs, rows)
    shots = lax.psum_scatter(
        jnp.dot(weights, flat, preferred_element_type=jnp.float32),
        "tx",
        scatter_dimension=0,
        tiled=True,
    )
    shots = shots.reshape(NS_DEV, 2, 3, depth, width_x, width_y)
    sigma_all = lax.all_gather(conductivity, "tx", axis=1, tiled=True)
    kappa = K_FREQ * sigma_all
    delta = K_FREQ * (sigma_all - 1.0)
    rhs = source_term(shots, delta)
    field = jacobi(rhs, kappa)
    for sweep in range(SWEEPS):
        padded = extend_field(field)
        resid = rhs - apply_operator(field, padded, kappa)
        field = field + RELAX * jacobi(resid, kappa)
    return field


def solution(mesh):
    in_specs = (
        P(("survey", "tx"), None, None, None, "xb", "yb"),
        P("survey", "tx", "xb", "yb"),
        P("survey"),
        P("survey"),
    )
    out_specs = P(("survey", "tx"), None, None, None, "xb", "yb")
    return jax.shard_map(body, mesh=mesh, in_specs=in_specs, out_specs=out_specs, check_vma=False)
```

profile of v0, /device:TPU:0, one launch (start us, length us, event | category | flops | bytes accessed | tf_op | source)
XLA Modules:
  0.0 101.2 jit_solution(11120184185977460906)
XLA Ops:
  8.0 3.8 %reshape.374 = bf16[16,98304]{1,0:T(8,128)(2,1)S(1)} reshape(bf16[16,2,3,32,4,128]{5,4,3,2,1,0:T(4,128)(2,1)} %param.4) | data formatting | bytes 6291456 | tf_op jit(solution)/shard_map/reshape | solution.py:128
  11.8 1.5 %fusion.42 = f32[2,98304]{1,0:T(2,128)} fusion(bf16[16,98304]{1,0:T(8,128)(2,1)S(1)} %reshape.374, s32[16]{0:T(128)S(1)} %dynamic_slice.7, s32[16]{0:T(128)S(1)} %dynamic_slice.6), kind=kOutput, calls=%fused_computation.125 | convolution fusion | flops 6291584 | bytes 3932288 | tf_op jit(solution)/shard_map/dot_general | solution.py:134
  13.9 2.1 %all_gather.3 = f32[3,32,4,128]{3,2,1,0:T(4,128)S(1)} all-gather(f32[3,16,4,128]{3,2,1,0:T(4,128)S(1)} %copy-done), channel_id=1, replica_groups=mesh['survey'=2,'xb'=4,'yb'=2,'tx'=2] {'tx'}, dimensions={1}, use_global_device_ids=true | all-gather | bytes 294912 | tf_op jit(solution)/shard_map/all_gather | solution.py:140
  16.0 19.2 %all-reduce.5.cloned.1.call-done = f32[2,98304]{1,0:T(2,128)} async-done(((f32[2,98304]{1,0:T(2,128)}), f32[2,98304]{1,0:T(2,128)}) %all-reduce.5.cloned.1.call-update) | async-done | bytes 786448
  35.2 2.1 %constant_dynamic-slice_fusion = f32[1,98304]{1,0:T(1,128)S(1)} fusion(f32[2,98304]{1,0:T(2,128)} %all-reduce.5.cloned.1.call-done, u32[]{:T(128)} %bitcast.41), kind=kLoop, calls=%fused_computation.126 | loop fusion | bytes 786436
  39.2 3.7 %collective-permute-start = (f32[1,768]{1,0:T(1,128)S(1)}, f32[1,768]{1,0:T(1,128)S(1)}, u32[]{:S(2)}, u32[]{:S(2)}) collective-permute-start(f32[1,768]{1,0:T(1,128)S(1)} %reshape.376), channel_id=1, source_target_pairs={{0,2},{1,3},{4,6},{5,7},{8,10},{9,11},{12,14},{13,15},{16,18},{17,... | collective-permute-start | bytes 9224 | tf_op jit(solution)/shard_map/ppermute | solution.py:17
  44.2 1.3 %collective-permute-start.1 = (f32[1,768]{1,0:T(1,128)S(1)}, f32[1,768]{1,0:T(1,128)S(1)}, u32[]{:S(2)}, u32[]{:S(2)}) collective-permute-start(f32[1,768]{1,0:T(1,128)S(1)} %reshape.378), channel_id=1, source_target_pairs={{2,0},{3,1},{6,4},{7,5},{10,8},{11,9},{14,12},{15,13},{18,16},{19,... | collective-permute-start | bytes 9224 | tf_op jit(solution)/shard_map/ppermute | solution.py:17
  45.7 4.0 %collective-permute-done.1 = f32[1,768]{1,0:T(1,128)S(1)} collective-permute-done((f32[1,768]{1,0:T(1,128)S(1)}, f32[1,768]{1,0:T(1,128)S(1)}, u32[]{:S(2)}, u32[]{:S(2)}) %collective-permute-start.1) | collective-permute-done | bytes 3104 | tf_op jit(solution)/shard_map/ppermute | solution.py:17
  49.9 1.3 %copy.26 = f32[1,2,3,32,4,1]{5,4,3,1,2,0:T(4,128)S(1)} copy(f32[1,2,3,32,4,1]{4,3,2,1,5,0:T(8,128)S(1)} %reshape.379) | data formatting | bytes 6144 | tf_op jit(solution)/shard_map/reshape | solution.py:104
  51.1 1.3 %copy.25 = f32[1,2,3,32,4,1]{5,4,3,1,2,0:T(4,128)S(1)} copy(f32[1,2,3,32,4,1]{4,3,2,1,5,0:T(8,128)S(1)} %reshape.377) | data formatting | bytes 6144 | tf_op jit(solution)/shard_map/reshape | solution.py:104
  52.4 1.3 %pad_maximum_fusion.10 = (f32[1,2,3,32,1,130]{5,4,3,1,2,0:T(1,128)S(1)}, f32[1,2,3,32,1,130]{5,4,3,1,2,0:T(1,128)S(1)}) fusion(f32[1,2,3,32,4,1]{5,4,3,1,2,0:T(4,128)S(1)} %copy.26, f32[1,2,3,32,4,1]{5,4,3,1,2,0:T(4,128)S(1)} %copy.25, f32[1,1,3,32,4,128]{5,4,3,1,2,0:T(4,128)S(1)} %bitcast.150, f32[1,1,3,32,4,128]{5,4,3,1,2,0:T(4,128)S(1)} %bitcast.156), kind=kLoop, calls=%fused_computation.80 | loop fusion | flops 149760 | bytes 599040 | tf_op jit(solution)/shard_map/slice | solution.py:25
  53.7 3.4 %collective-permute-start.2 = (f32[1,2,3,32,1,130]{5,4,3,1,2,0:T(1,128)S(1)}, f32[1,2,3,32,1,130]{5,4,3,1,2,0:T(1,128)S(1)}, u32[]{:S(2)}, u32[]{:S(2)}) collective-permute-start(f32[1,2,3,32,1,130]{5,4,3,1,2,0:T(1,128)S(1)} %get-tuple-element.15), channel_id=1, source_target_pairs={{0,4},{4,8},{8,12},{1,5},{5,9},{9,13},{2,6},{6,10},{10,14},{3,7},{... | collective-permute-start | bytes 299528 | tf_op jit(solution)/shard_map/ppermute | solution.py:28
  57.1 1.3 %collective-permute-start.3 = (f32[1,2,3,32,1,130]{5,4,3,1,2,0:T(1,128)S(1)}, f32[1,2,3,32,1,130]{5,4,3,1,2,0:T(1,128)S(1)}, u32[]{:S(2)}, u32[]{:S(2)}) collective-permute-start(f32[1,2,3,32,1,130]{5,4,3,1,2,0:T(1,128)S(1)} %get-tuple-element.16), channel_id=1, source_target_pairs={{4,0},{8,4},{12,8},{5,1},{9,5},{13,9},{6,2},{10,6},{14,10},{7,3},{... | collective-permute-start | bytes 299528 | tf_op jit(solution)/shard_map/ppermute | solution.py:30
  58.4 1.9 %collective-permute-done.2 = f32[1,2,3,32,1,130]{5,4,3,1,2,0:T(1,128)S(1)} collective-permute-done((f32[1,2,3,32,1,130]{5,4,3,1,2,0:T(1,128)S(1)}, f32[1,2,3,32,1,130]{5,4,3,1,2,0:T(1,128)S(1)}, u32[]{:S(2)}, u32[]{:S(2)}) %collective-permute-start.2) | collective-permute-done | bytes 99872 | tf_op jit(solution)/shard_map/ppermute | solution.py:28
  60.3 4.4 %collective-permute-done.3 = f32[1,2,3,32,1,130]{5,4,3,1,2,0:T(1,128)S(1)} collective-permute-done((f32[1,2,3,32,1,130]{5,4,3,1,2,0:T(1,128)S(1)}, f32[1,2,3,32,1,130]{5,4,3,1,2,0:T(1,128)S(1)}, u32[]{:S(2)}, u32[]{:S(2)}) %collective-permute-start.3) | collective-permute-done | bytes 99872 | tf_op jit(solution)/shard_map/ppermute | solution.py:30
  68.4 1.3 %collective-permute-start.5 = (f32[1,768]{1,0:T(1,128)S(1)}, f32[1,768]{1,0:T(1,128)S(1)}, u32[]{:S(2)}, u32[]{:S(2)}) collective-permute-start(f32[1,768]{1,0:T(1,128)S(1)} %reshape.382), channel_id=1, source_target_pairs={{2,0},{3,1},{6,4},{7,5},{10,8},{11,9},{14,12},{15,13},{18,16},{19,... | collective-permute-start | bytes 9224 | tf_op jit(solution)/shard_map/ppermute | solution.py:17
  69.7 4.7 %collective-permute-start.4 = (f32[1,768]{1,0:T(1,128)S(1)}, f32[1,768]{1,0:T(1,128)S(1)}, u32[]{:S(2)}, u32[]{:S(2)}) collective-permute-start(f32[1,768]{1,0:T(1,128)S(1)} %reshape.380), channel_id=1, source_target_pairs={{0,2},{1,3},{4,6},{5,7},{8,10},{9,11},{12,14},{13,15},{16,18},{17,... | collective-permute-start | bytes 9224 | tf_op jit(solution)/shard_map/ppermute | solution.py:17
  75.8 1.3 %copy.32 = f32[1,2,3,32,4,1]{5,4,3,1,2,0:T(4,128)S(1)} copy(f32[1,2,3,32,4,1]{4,3,2,1,5,0:T(8,128)S(1)} %reshape.383) | data formatting | bytes 6144 | tf_op jit(solution)/shard_map/reshape | solution.py:104
  77.1 1.3 %copy.30 = f32[1,2,3,32,4,1]{5,4,3,1,2,0:T(4,128)S(1)} copy(f32[1,2,3,32,4,1]{4,3,2,1,5,0:T(8,128)S(1)} %reshape.381) | data formatting | bytes 6144 | tf_op jit(solution)/shard_map/reshape | solution.py:104
  78.4 1.3 %pad_maximum_fusion.6 = (f32[1,2,3,32,1,130]{5,4,3,1,2,0:T(1,128)S(1)}, f32[1,2,3,32,1,130]{5,4,3,1,2,0:T(1,128)S(1)}) fusion(f32[1,2,3,32,4,1]{5,4,3,1,2,0:T(4,128)S(1)} %copy.32, f32[1,2,3,32,4,1]{5,4,3,1,2,0:T(4,128)S(1)} %copy.30, f32[1,1,3,32,4,128]{5,4,3,2,1,0:T(4,128)S(1)} %get-tuple-element.22, f32[1,1,3,32,4,128]{5,4,3,2,1,0:T(4,128)S(1)} %get-tuple-element.21, ...), kind=kLoop, calls=%fused_computation.68 | loop fusion | flops 394752 | bytes 992256 | tf_op jit(solution)/shard_map/slice | solution.py:25
  79.7 3.4 %collective-permute-start.6 = (f32[1,2,3,32,1,130]{5,4,3,1,2,0:T(1,128)S(1)}, f32[1,2,3,32,1,130]{5,4,3,1,2,0:T(1,128)S(1)}, u32[]{:S(2)}, u32[]{:S(2)}) collective-permute-start(f32[1,2,3,32,1,130]{5,4,3,1,2,0:T(1,128)S(1)} %get-tuple-element.13), channel_id=1, source_target_pairs={{0,4},{4,8},{8,12},{1,5},{5,9},{9,13},{2,6},{6,10},{10,14},{3,7},{... | collective-permute-start | bytes 299528 | tf_op jit(solution)/shard_map/ppermute | solution.py:28
  83.1 1.3 %collective-permute-start.7 = (f32[1,2,3,32,1,130]{5,4,3,1,2,0:T(1,128)S(1)}, f32[1,2,3,32,1,130]{5,4,3,1,2,0:T(1,128)S(1)}, u32[]{:S(2)}, u32[]{:S(2)}) collective-permute-start(f32[1,2,3,32,1,130]{5,4,3,1,2,0:T(1,128)S(1)} %get-tuple-element.14), channel_id=1, source_target_pairs={{4,0},{8,4},{12,8},{5,1},{9,5},{13,9},{6,2},{10,6},{14,10},{7,3},{... | collective-permute-start | bytes 299528 | tf_op jit(solution)/shard_map/ppermute | solution.py:30
  84.4 1.9 %collective-permute-done.6 = f32[1,2,3,32,1,130]{5,4,3,1,2,0:T(1,128)S(1)} collective-permute-done((f32[1,2,3,32,1,130]{5,4,3,1,2,0:T(1,128)S(1)}, f32[1,2,3,32,1,130]{5,4,3,1,2,0:T(1,128)S(1)}, u32[]{:S(2)}, u32[]{:S(2)}) %collective-permute-start.6) | collective-permute-done | bytes 99872 | tf_op jit(solution)/shard_map/ppermute | solution.py:28
  86.2 4.4 %collective-permute-done.7 = f32[1,2,3,32,1,130]{5,4,3,1,2,0:T(1,128)S(1)} collective-permute-done((f32[1,2,3,32,1,130]{5,4,3,1,2,0:T(1,128)S(1)}, f32[1,2,3,32,1,130]{5,4,3,1,2,0:T(1,128)S(1)}, u32[]{:S(2)}, u32[]{:S(2)}) %collective-permute-start.7) | collective-permute-done | bytes 99872 | tf_op jit(solution)/shard_map/ppermute | solution.py:30
  (48 shorter events, 14.2 us)
Async XLA Ops:
  6.5 28.7 %all-reduce.5.cloned.1.call-start = ((), (), s32[]{:S(2)}) async-start(), calls=%async_computation | async-start | bytes 1572864
  11.8 1.5 %copy-start.1 = (u32[32]{0:T(128)S(1)}, u32[32]{0:T(128)}, u32[]{:S(2)}) copy-start(u32[32]{0:T(128)} %constant.30) | copy-start | bytes 388
  11.8 2.1 %copy-start = (f32[3,16,4,128]{3,2,1,0:T(4,128)S(1)}, f32[3,16,4,128]{3,2,1,0:T(4,128)}, u32[]{:S(2)}) copy-start(f32[3,16,4,128]{3,2,1,0:T(4,128)} %param.5) | copy-start | bytes 294916
  39.2 6.3 %collective-permute-start = (f32[1,768]{1,0:T(1,128)S(1)}, f32[1,768]{1,0:T(1,128)S(1)}, u32[]{:S(2)}, u32[]{:S(2)}) collective-permute-start(f32[1,768]{1,0:T(1,128)S(1)} %reshape.376), channel_id=1, source_target_pairs={{0,2},{1,3},{4,6},{5,7},{8,10},{9,11},{12,14},{13,15},{16,18},{17,... | collective-permute-start | bytes 9224 | tf_op jit(solution)/shard_map/ppermute | solution.py:17
  44.2 5.5 %collective-permute-start.1 = (f32[1,768]{1,0:T(1,128)S(1)}, f32[1,768]{1,0:T(1,128)S(1)}, u32[]{:S(2)}, u32[]{:S(2)}) collective-permute-start(f32[1,768]{1,0:T(1,128)S(1)} %reshape.378), channel_id=1, source_target_pairs={{2,0},{3,1},{6,4},{7,5},{10,8},{11,9},{14,12},{15,13},{18,16},{19,... | collective-permute-start | bytes 9224 | tf_op jit(solution)/shard_map/ppermute | solution.py:17
  53.7 6.6 %collective-permute-start.2 = (f32[1,2,3,32,1,130]{5,4,3,1,2,0:T(1,128)S(1)}, f32[1,2,3,32,1,130]{5,4,3,1,2,0:T(1,128)S(1)}, u32[]{:S(2)}, u32[]{:S(2)}) collective-permute-start(f32[1,2,3,32,1,130]{5,4,3,1,2,0:T(1,128)S(1)} %get-tuple-element.15), channel_id=1, source_target_pairs={{0,4},{4,8},{8,12},{1,5},{5,9},{9,13},{2,6},{6,10},{10,14},{3,7},{... | collective-permute-start | bytes 299528 | tf_op jit(solution)/shard_map/ppermute | solution.py:28
  57.1 7.6 %collective-permute-start.3 = (f32[1,2,3,32,1,130]{5,4,3,1,2,0:T(1,128)S(1)}, f32[1,2,3,32,1,130]{5,4,3,1,2,0:T(1,128)S(1)}, u32[]{:S(2)}, u32[]{:S(2)}) collective-permute-start(f32[1,2,3,32,1,130]{5,4,3,1,2,0:T(1,128)S(1)} %get-tuple-element.16), channel_id=1, source_target_pairs={{4,0},{8,4},{12,8},{5,1},{9,5},{13,9},{6,2},{10,6},{14,10},{7,3},{... | collective-permute-start | bytes 299528 | tf_op jit(solution)/shard_map/ppermute | solution.py:30
  68.4 7.3 %collective-permute-start.5 = (f32[1,768]{1,0:T(1,128)S(1)}, f32[1,768]{1,0:T(1,128)S(1)}, u32[]{:S(2)}, u32[]{:S(2)}) collective-permute-start(f32[1,768]{1,0:T(1,128)S(1)} %reshape.382), channel_id=1, source_target_pairs={{2,0},{3,1},{6,4},{7,5},{10,8},{11,9},{14,12},{15,13},{18,16},{19,... | collective-permute-start | bytes 9224 | tf_op jit(solution)/shard_map/ppermute | solution.py:17
  69.7 5.9 %collective-permute-start.4 = (f32[1,768]{1,0:T(1,128)S(1)}, f32[1,768]{1,0:T(1,128)S(1)}, u32[]{:S(2)}, u32[]{:S(2)}) collective-permute-start(f32[1,768]{1,0:T(1,128)S(1)} %reshape.380), channel_id=1, source_target_pairs={{0,2},{1,3},{4,6},{5,7},{8,10},{9,11},{12,14},{13,15},{16,18},{17,... | collective-permute-start | bytes 9224 | tf_op jit(solution)/shard_map/ppermute | solution.py:17
  79.7 6.6 %collective-permute-start.6 = (f32[1,2,3,32,1,130]{5,4,3,1,2,0:T(1,128)S(1)}, f32[1,2,3,32,1,130]{5,4,3,1,2,0:T(1,128)S(1)}, u32[]{:S(2)}, u32[]{:S(2)}) collective-permute-start(f32[1,2,3,32,1,130]{5,4,3,1,2,0:T(1,128)S(1)} %get-tuple-element.13), channel_id=1, source_target_pairs={{0,4},{4,8},{8,12},{1,5},{5,9},{9,13},{2,6},{6,10},{10,14},{3,7},{... | collective-permute-start | bytes 299528 | tf_op jit(solution)/shard_map/ppermute | solution.py:28
  83.1 7.6 %collective-permute-start.7 = (f32[1,2,3,32,1,130]{5,4,3,1,2,0:T(1,128)S(1)}, f32[1,2,3,32,1,130]{5,4,3,1,2,0:T(1,128)S(1)}, u32[]{:S(2)}, u32[]{:S(2)}) collective-permute-start(f32[1,2,3,32,1,130]{5,4,3,1,2,0:T(1,128)S(1)} %get-tuple-element.14), channel_id=1, source_target_pairs={{4,0},{8,4},{12,8},{5,1},{9,5},{13,9},{6,2},{10,6},{14,10},{7,3},{... | collective-permute-start | bytes 299528 | tf_op jit(solution)/shard_map/ppermute | solution.py:30
Sparse Core Ops, SparseCore 0:
  13.5 21.6 all-reduce.4
where the time goes:
time: 101 us
  waiting for transfers between devices  36.8 us (36%)
  starting transfers between devices  20.4 us (20%)
  local copies, waits for them, and re-layouts  17.6 us (17%)
  between operations  13.7 us (14%)
  other arithmetic  9.19 us (9%)
  blocking collectives  2.07 us (2%)
  matrix products  1.49 us (1%)
    unnamed x2, waiting for transfers between devices  19.2 us
    ppermute x4, starting transfers between devices, from_behind(): return lax.ppermute(block, axis, route)  11 us
    ppermute x2, waiting for transfers between devices, with_halo(): lax.ppermute(head, axis, [((i + 1) % count, i) for i in range(ends)])  8.81 us
    ppermute x2, starting transfers between devices, with_halo(): lax.ppermute(tail, axis, [(i, (i + 1) % count) for i in range(ends)])  6.79 us
    ppermute x4, waiting for transfers between devices, from_behind(): return lax.ppermute(block, axis, route)  5.06 us
    reshape x1, local copies, waits for them, and re-layouts, body(): flat = primaries.reshape(nt_local, -1)  3.79 us
    ppermute x2, waiting for transfers between devices, with_halo(): lax.ppermute(tail, axis, [(i, (i + 1) % count) for i in range(ends)])  3.72 us
    reshape x4, local copies, waits for them, and re-layouts, y_extend(): from_high.reshape(face_shape)  2.78 us
  transfers between devices with their start and end apart: 9, of which 7 were waited for; matrix products, arithmetic and copies ran while one was open for 2% of the time, Pallas kernels for 0%

commit v1 on v0

v1 whole, which is shorter than its diff:
```python
import jax
import jax.numpy as jnp
from jax import lax
from jax.sharding import PartitionSpec as P

NS_DEV = 1
SWEEPS = 2


K_FREQ = 2.0
RELAX = 0.6


def inner(f):
    return f[..., :-1, :-1, :-1]


def fwd_z(f):
    return f[..., 1:, :-1, :-1] - inner(f)


def fwd_x(f):
    return f[..., :-1, 1:, :-1] - inner(f)


def fwd_y(f):
    return f[..., :-1, :-1, 1:] - inner(f)


def back_z(g):
    return g[..., 1:, 1:, 1:] - g[..., :-1, 1:, 1:]


def back_x(g):
    return g[..., 1:, 1:, 1:] - g[..., 1:, :-1, 1:]


def back_y(g):
    return g[..., 1:, 1:, 1:] - g[..., 1:, 1:, :-1]


def curl_curl(padded):
    e_x = padded[..., 0, :, :, :]
    e_y = padded[..., 1, :, :, :]
    e_z = padded[..., 2, :, :, :]
    h_x = fwd_y(e_z) - fwd_z(e_y)
    h_y = fwd_z(e_x) - fwd_x(e_z)
    h_z = fwd_x(e_y) - fwd_y(e_x)
    c_x = back_y(h_z) - back_z(h_y)
    c_y = back_z(h_x) - back_x(h_z)
    c_z = back_x(h_y) - back_y(h_x)
    return jnp.stack([c_x, c_y, c_z], axis=-4)


def jacobi(resid, kappa):
    denom = 16.0 + kappa * kappa
    real_part = (4.0 * resid[..., 0, :, :, :, :] + kappa * resid[..., 1, :, :, :, :]) / denom
    imag_part = (4.0 * resid[..., 1, :, :, :, :] - kappa * resid[..., 0, :, :, :, :]) / denom
    return jnp.stack([real_part, imag_part], axis=-5)


def source_term(shot, delta):
    return jnp.stack([delta * shot[..., 1, :, :, :, :], -delta * shot[..., 0, :, :, :, :]], axis=-5)


def shrink(f, ring):
    return f[..., ring:f.shape[-2] - ring, ring:f.shape[-1] - ring]


def pad_z(f):
    return jnp.pad(f, [(0, 0)] * (f.ndim - 3) + [(1, 1), (0, 0), (0, 0)])


def halo(cells, axis, dim, width):
    count = lax.axis_size(axis)
    size = cells.shape[dim]
    head = lax.slice_in_dim(cells, 0, width, axis=dim)
    tail = lax.slice_in_dim(cells, size - width, size, axis=dim)
    from_low = lax.ppermute(tail, axis, [(i, i + 1) for i in range(count - 1)])
    from_high = lax.ppermute(head, axis, [(i + 1, i) for i in range(count - 1)])
    return jnp.concatenate([from_low, cells, from_high], axis=dim)


def encode_weights(group_part, sign_part, rows):
    picked = group_part[None, :] == rows[:, None]
    return jnp.where(picked, sign_part[None, :], 0).astype(jnp.float32).astype(jnp.bfloat16)


def body(primaries, conductivity, group_of, sign_of):
    nt_local = primaries.shape[0]
    depth = primaries.shape[3]
    width_x = primaries.shape[4]
    width_y = primaries.shape[5]
    n_tx = lax.axis_size("tx")
    tx_index = lax.axis_index("tx")
    other = (tx_index + 1) % n_tx
    own_groups = lax.dynamic_slice_in_dim(group_of, tx_index * nt_local, nt_local, 0)
    own_signs = lax.dynamic_slice_in_dim(sign_of, tx_index * nt_local, nt_local, 0)
    rows = jnp.stack([other, tx_index]).astype(jnp.int32)
    weights = encode_weights(own_groups, own_signs, rows)
    partial = lax.dot_general(
        weights, primaries, (((1,), (0,)), ((), ())), preferred_element_type=jnp.float32
    )
    send = jnp.concatenate([partial[0].reshape(-1), conductivity.reshape(-1)])
    got = lax.ppermute(send, "tx", [(i, (i + 1) % n_tx) for i in range(n_tx)])
    shot_cells = partial[1].size
    shot = partial[1] + got[:shot_cells].reshape(partial[1].shape)
    sigma_other = got[shot_cells:].reshape(conductivity.shape)
    low_first = tx_index == 0
    sigma_all = jnp.where(
        low_first,
        jnp.concatenate([conductivity, sigma_other], axis=1),
        jnp.concatenate([sigma_other, conductivity], axis=1),
    )

    planes = jnp.concatenate([shot.reshape(-1, depth, width_x, width_y), sigma_all], axis=0)
    planes = halo(planes, "yb", 3, SWEEPS)
    planes = halo(planes, "xb", 2, SWEEPS)
    ext_x = width_x + 2 * SWEEPS
    ext_y = width_y + 2 * SWEEPS
    n_shot = shot.shape[0] * shot.shape[1]
    shot_ext = planes[:n_shot].reshape(shot.shape[:2] + (depth, ext_x, ext_y))
    sigma_ext = planes[n_shot:]

    gx = lax.axis_index("xb") * width_x - SWEEPS + lax.broadcasted_iota(jnp.int32, (ext_x, ext_y), 0)
    gy = lax.axis_index("yb") * width_y - SWEEPS + lax.broadcasted_iota(jnp.int32, (ext_x, ext_y), 1)
    inside = (gx >= 0) & (gx < width_x * lax.axis_size("xb")) & (gy >= 0) & (gy < width_y * lax.axis_size("yb"))

    kappa = K_FREQ * sigma_ext
    delta = K_FREQ * (sigma_ext - 1.0)
    rhs = source_term(shot_ext, delta)
    field = jacobi(rhs, kappa)
    for sweep in range(SWEEPS):
        curled = curl_curl(pad_z(field))
        field = shrink(field, 1)
        kappa = shrink(kappa, 1)
        rhs = shrink(rhs, 1)
        inside = shrink(inside, 1)
        real_part = curled[..., 0, :, :, :, :] - kappa * field[..., 1, :, :, :, :]
        imag_part = curled[..., 1, :, :, :, :] + kappa * field[..., 0, :, :, :, :]
        applied = jnp.stack([real_part, imag_part], axis=-5)
        field = field + RELAX * jacobi(rhs - applied, kappa)
        if sweep < SWEEPS - 1:
            field = jnp.where(inside, field, 0.0)
    return field[None]


def solution(mesh):
    in_specs = (
        P(("survey", "tx"), None, None, None, "xb", "yb"),
        P("survey", "tx", "xb", "yb"),
        P("survey"),
        P("survey"),
    )
    out_specs = P(("survey", "tx"), None, None, None, "xb", "yb")
    return jax.shard_map(body, mesh=mesh, in_specs=in_specs, out_specs=out_specs, check_vma=False)
```

time: 101 us -> 64.2 us (0.64)
  waiting for transfers between devices: 36.8 us -> 17.2 us
  between operations: 13.7 us -> 0.19 us
  other arithmetic: 9.19 us -> 16 us
  starting transfers between devices: 20.4 us -> 13.9 us
  local copies, waits for them, and re-layouts: 17.6 us -> 14.4 us
  blocking collectives: 2.07 us -> 0 us
    unnamed x2 -> x0, waiting for transfers between devices: 19.2 us -> none
    reshape x13 -> x0, local copies, waits for them, and re-layouts: 9.81 us -> none  [the longest x1 3.79 us: body(): flat = primaries.reshape(nt_local, -1)]
    ppermute x8 -> x5, starting transfers between devices: 20.4 us -> 13.9 us  [the longest x2 10.6 us: halo(): from_low = lax.ppermute(tail, axis, [(i, i + 1) for i in range(count - 1)])]
    slice x3 -> x9, local copies, waits for them, and re-layouts: 3.19 us -> 7.98 us  [the longest x2 2.53 us: halo(): tail = lax.slice_in_dim(cells, size - width, size, axis=dim)]
    concatenate x2 -> x4, other arithmetic: 1.82 us -> 5.87 us  [the longest x2 3.55 us: halo(): return jnp.concatenate([from_low, cells, from_high], axis=dim)]
    ppermute x0 -> x2, local copies, waits for them, and re-layouts: none -> 3.78 us  [the longest x1 1.89 us: halo(): from_low = lax.ppermute(tail, axis, [(i, i + 1) for i in range(count - 1)])]
    slice x2 -> x0, other arithmetic: 2.58 us -> none  [with_halo(): lax.slice_in_dim(cells, cells.shape[dim] - width, cells.shape[dim], axis=...]
    all_gather x1 -> x0, blocking collectives: 2.07 us -> none  [body(): sigma_all = lax.all_gather(conductivity, 'tx', axis=1, tiled=True)]
  transfers between devices with their start and end apart: 9 -> 5, of which waited for: 7 -> 4; matrix products, arithmetic and copies ran while one was open for 2% -> 3% of each run, Pallas kernels for 0% -> 0%
where the time goes in v1:
time: 64.2 us; the launch traced here: 63.6 us
  waiting for transfers between devices  17.2 us (27%)
  other arithmetic  16 us (25%)
  local copies, waits for them, and re-layouts  14.4 us (22%)
  starting transfers between devices  13.9 us (22%)
  matrix products  1.93 us (3%)
    ppermute x2, waiting for transfers between devices, halo(): from_low = lax.ppermute(tail, axis, [(i, i + 1) for i in range(count - 1)])  11.2 us
    ppermute x2, starting transfers between devices, halo(): from_low = lax.ppermute(tail, axis, [(i, i + 1) for i in range(count - 1)])  10.6 us
    ppermute x2, waiting for transfers between devices, halo(): from_high = lax.ppermute(head, axis, [(i + 1, i) for i in range(count - 1)])  4.15 us
    concatenate x2, other arithmetic, halo(): return jnp.concatenate([from_low, cells, from_high], axis=dim)  3.55 us
    ppermute x2, starting transfers between devices, halo(): from_high = lax.ppermute(head, axis, [(i + 1, i) for i in range(count - 1)])  2.75 us
    slice x2, local copies, waits for them, and re-layouts, halo(): tail = lax.slice_in_dim(cells, size - width, size, axis=dim)  2.53 us
    slice x2, local copies, waits for them, and re-layouts, body(): shot = partial[1] + got[:shot_cells].reshape(partial[1].shape)  2.38 us
    slice x1, local copies, waits for them, and re-layouts, halo(): head = lax.slice_in_dim(cells, 0, width, axis=dim)  1.95 us
  transfers between devices with their start and end apart: 5, of which 4 were waited for; matrix products, arithmetic and copies ran while one was open for 3% of the time, Pallas kernels for 0%

profile of v1, /device:TPU:0, one launch (start us, length us, event | category | flops | bytes accessed | tf_op | source)
XLA Modules:
  0.0 63.6 jit_solution(15779771790645101090)
XLA Ops:
  0.0 0.9 %dynamic_slice.6 = s32[16]{0:T(128)S(1)} dynamic-slice(s32[32]{0:T(128)} %param.6, s32[]{:T(128)S(6)} %select_n.27), dynamic_slice_sizes={16} | dynamic-slice | bytes 132 | tf_op jit(solution)/shard_map/dynamic_slice | solution.py:97
  1.9 1.9 %fusion = f32[2,2,3,32,4,128]{5,0,4,3,2,1:T(2,128)S(1)} fusion(bf16[16,2,3,32,4,128]{5,4,3,2,1,0:T(4,128)(2,1)S(1)} %copy-done, s32[16]{0:T(128)S(1)} %dynamic_slice.7, s32[16]{0:T(128)S(1)} %dynamic_slice.6, s32[2]{0:T(128)S(1)} %pad_add_fusion), kind=kOutput, calls=%fused_computation | convolution fusion | flops 6291584 | bytes 3932296 | tf_op jit(solution)/shard_map/dot_general | solution.py:101
  3.8 1.4 %fusion.60 = (f32[1,2,3,32,4,128]{5,0,4,3,2,1:T(1,128)}, f32[1,2,3,32,4,128]{5,0,4,3,2,1:T(1,128)S(1)}) fusion(f32[2,2,3,32,4,128]{5,0,4,3,2,1:T(2,128)S(1)} %fusion), kind=kLoop, calls=%fused_computation.134 | loop fusion | bytes 1572864 | tf_op jit(solution)/shard_map/slice | solution.py:107
  6.5 1.8 %collective-permute-done = f32[122880]{0:T(1024)} collective-permute-done((f32[122880]{0:T(1024)}, f32[122880]{0:T(1024)}, u32[]{:S(2)}, u32[]{:S(2)}) %collective-permute-start) | collective-permute-done | bytes 491552 | tf_op jit(solution)/shard_map/ppermute | solution.py:105
  8.3 1.0 %slice.333 = f32[98304]{0:T(1024)S(1)} slice(f32[122880]{0:T(1024)} %collective-permute-done), slice={[0:98304]} | slice | bytes 786432 | tf_op jit(solution)/shard_map/slice | solution.py:107
  9.4 1.1 %add.82 = f32[6,32,4,128]{3,2,1,0:T(4,128)S(1)} add(f32[6,32,4,128]{3,2,1,0:T(4,128)} %bitcast.145, f32[6,32,4,128]{3,2,1,0:T(4,128)S(1)} %bitcast.144) | non-fusion elementwise | flops 98304 | bytes 1179648 | tf_op jit(solution)/shard_map/add | solution.py:107
  10.5 0.9 %slice.334 = f32[24576]{0:T(1024)S(1)} slice(f32[122880]{0:T(1024)} %collective-permute-done), slice={[98304:122880]} | slice | bytes 196608 | tf_op jit(solution)/shard_map/slice | solution.py:108
  11.4 1.0 %maximum_select_fusion = f32[3,32,4,128]{3,2,1,0:T(4,128)S(1)} fusion(f32[3,16,4,128]{3,2,1,0:T(4,128)S(1)} %bitcast.147, f32[3,16,4,128]{3,2,1,0:T(4,128)} %param.5, pred[]{:T(512)S(6)} %eq.21), kind=kLoop, calls=%fused_computation.98 | loop fusion | flops 147456 | bytes 393217 | tf_op jit(solution)/shard_map/jit(_where)/select_n | solution.py:110
  13.1 1.5 %slice_maximum_fusion = (f32[9,32,4,2]{3,2,1,0:T(4,128)}, f32[9,32,4,2]{3,2,1,0:T(4,128)}) fusion(f32[3,32,4,128]{3,2,1,0:T(4,128)S(1)} %maximum_select_fusion, f32[6,32,4,128]{3,2,1,0:T(4,128)S(1)} %add.82), kind=kLoop, calls=%fused_computation.42 | loop fusion | flops 4608 | bytes 608256 | tf_op jit(solution)/shard_map/concatenate | solution.py:116
  14.6 2.0 %copy.24 = f32[9,32,4,2]{1,2,3,0:T(4,128)} copy(f32[9,32,4,2]{3,2,1,0:T(4,128)} %get-tuple-element.28) | data formatting | bytes 18432 | tf_op jit(solution)/shard_map/slice | solution.py:78
  16.6 1.9 %copy.25 = f32[9,32,4,2]{1,2,3,0:T(4,128)} copy(f32[9,32,4,2]{3,2,1,0:T(4,128)} %get-tuple-element.29) | data formatting | bytes 18432 | tf_op jit(solution)/shard_map/slice | solution.py:77
  18.5 1.3 %collective-permute-start.2 = (f32[9,32,4,2]{1,2,3,0:T(4,128)}, f32[9,32,4,2]{1,2,3,0:T(4,128)}, u32[]{:S(2)}, u32[]{:S(2)}) collective-permute-start(f32[9,32,4,2]{1,2,3,0:T(4,128)} %copy.25), channel_id=1, source_target_pairs={{2,0},{3,1},{6,4},{7,5},{10,8},{11,9},{14,12},{15,13},{18,16},{19,... | collective-permute-start | bytes 27656 | tf_op jit(solution)/shard_map/ppermute | solution.py:80
  19.8 6.0 %collective-permute-start.1 = (f32[9,32,4,2]{1,2,3,0:T(4,128)}, f32[9,32,4,2]{1,2,3,0:T(4,128)}, u32[]{:S(2)}, u32[]{:S(2)}) collective-permute-start(f32[9,32,4,2]{1,2,3,0:T(4,128)} %copy.24), channel_id=1, source_target_pairs={{0,2},{1,3},{4,6},{5,7},{8,10},{9,11},{12,14},{13,15},{16,18},{17,... | collective-permute-start | bytes 27656 | tf_op jit(solution)/shard_map/ppermute | solution.py:79
  25.8 1.2 %collective-permute-done.1 = f32[9,32,4,2]{1,2,3,0:T(4,128)} collective-permute-done((f32[9,32,4,2]{1,2,3,0:T(4,128)}, f32[9,32,4,2]{1,2,3,0:T(4,128)}, u32[]{:S(2)}, u32[]{:S(2)}) %collective-permute-start.1) | collective-permute-done | bytes 9248 | tf_op jit(solution)/shard_map/ppermute | solution.py:79
  27.1 1.9 %copy.26 = f32[9,32,4,2]{3,2,1,0:T(4,128)} copy(f32[9,32,4,2]{1,2,3,0:T(4,128)} %collective-permute-done.1) | data formatting | bytes 18432 | tf_op jit(solution)/shard_map/ppermute | solution.py:79
  29.0 1.9 %copy.27 = f32[9,32,4,2]{3,2,1,0:T(4,128)} copy(f32[9,32,4,2]{1,2,3,0:T(4,128)} %collective-permute-done.2) | data formatting | bytes 18432 | tf_op jit(solution)/shard_map/ppermute | solution.py:80
  30.9 2.3 %pad_maximum_fusion.3 = f32[9,32,4,132]{3,2,1,0:T(4,128)S(1)} fusion(f32[9,32,4,2]{3,2,1,0:T(4,128)} %copy.27, f32[3,32,4,128]{3,2,1,0:T(4,128)} %copy-done.3, f32[6,32,4,128]{3,2,1,0:T(4,128)S(1)} %add.82, f32[9,32,4,2]{3,2,1,0:T(4,128)} %copy.26), kind=kLoop, calls=%fused_computation.18 | loop fusion | flops 456192 | bytes 1216512 | tf_op jit(solution)/shard_map/concatenate | solution.py:81
  33.8 4.7 %collective-permute-start.3 = (f32[9,32,2,132]{3,2,1,0:T(2,128)S(1)}, f32[9,32,2,132]{3,2,1,0:T(2,128)S(1)}, u32[]{:S(2)}, u32[]{:S(2)}) collective-permute-start(f32[9,32,2,132]{3,2,1,0:T(2,128)S(1)} %get-tuple-element.24), channel_id=1, source_target_pairs={{0,4},{4,8},{8,12},{1,5},{5,9},{9,13},{2,6},{6,10},{10,14},{3,7},{... | collective-permute-start | bytes 912392 | tf_op jit(solution)/shard_map/ppermute | solution.py:79
  38.4 1.5 %collective-permute-start.4 = (f32[9,32,2,132]{3,2,1,0:T(2,128)S(1)}, f32[9,32,2,132]{3,2,1,0:T(2,128)S(1)}, u32[]{:S(2)}, u32[]{:S(2)}) collective-permute-start(f32[9,32,2,132]{3,2,1,0:T(2,128)S(1)} %get-tuple-element.25), channel_id=1, source_target_pairs={{4,0},{8,4},{12,8},{5,1},{9,5},{13,9},{6,2},{10,6},{14,10},{7,3},{... | collective-permute-start | bytes 912392 | tf_op jit(solution)/shard_map/ppermute | solution.py:80
  40.2 10.0 %collective-permute-done.3 = f32[9,32,2,132]{3,2,1,0:T(2,128)S(1)} collective-permute-done((f32[9,32,2,132]{3,2,1,0:T(2,128)S(1)}, f32[9,32,2,132]{3,2,1,0:T(2,128)S(1)}, u32[]{:S(2)}, u32[]{:S(2)}) %collective-permute-start.3) | collective-permute-done | bytes 304160 | tf_op jit(solution)/shard_map/ppermute | solution.py:79
  50.1 4.1 %collective-permute-done.4 = f32[9,32,2,132]{3,2,1,0:T(2,128)S(1)} collective-permute-done((f32[9,32,2,132]{3,2,1,0:T(2,128)S(1)}, f32[9,32,2,132]{3,2,1,0:T(2,128)S(1)}, u32[]{:S(2)}, u32[]{:S(2)}) %collective-permute-start.4) | collective-permute-done | bytes 304160 | tf_op jit(solution)/shard_map/ppermute | solution.py:80
  54.3 1.3 %pad_maximum_fusion = f32[9,32,8,132]{3,2,1,0:T(8,128)S(1)} fusion(f32[9,32,2,132]{3,2,1,0:T(2,128)S(1)} %collective-permute-done.4, f32[9,32,4,2]{3,2,1,0:T(4,128)S(1)} %copy-done.2, f32[3,32,4,128]{3,2,1,0:T(4,128)S(1)} %copy-done.4, f32[6,32,4,128]{3,2,1,0:T(4,128)S(1)} %add.82, f32[9,32,4,2]{3,2,1,0:T(4,128)S(1)} %copy-done.1, ...), kind=kLoop, calls=%fused_computation.2 | loop fusion | flops 1520640 | bytes 2433024 | tf_op jit(solution)/shard_map/concatenate | solution.py:81
  56.7 1.0 %fusion.28 = (f32[2,1,32,6,130]{4,3,2,0,1:T(8,128)S(1)}, f32[2,1,32,6,130]{4,3,2,0,1:T(8,128)S(1)}, f32[2,1,32,6,130]{4,3,2,0,1:T(8,128)S(1)}) fusion(f32[2,33,7,131]{3,2,1,0:T(8,128)S(1)} %get-tuple-element.35, f32[2,33,7,131]{3,2,1,0:T(8,128)S(1)} %get-tuple-element.33, f32[2,33,7,131]{3,2,1,0:T(8,128)S(1)} %get-tuple-element.34), kind=kLoop, calls=%fused_computation.77 | loop fusion | flops 449280 | bytes 2396160 | tf_op jit(solution)/shard_map/stack | solution.py:52
  62.6 1.0 %fusion.30 = f32[1,2,3,32,4,128]{5,4,3,2,1,0:T(4,128)} fusion(f32[2,3,32,6,130]{4,3,2,1,0:T(8,128)S(1)} %fusion.4, f32[1,3,32,4,128]{4,3,2,1,0:T(4,128)S(1)} %get-tuple-element.23, f32[1,3,32,4,128]{4,3,2,1,0:T(4,128)S(1)} %get-tuple-element.22), kind=kLoop, calls=%fused_computation.83 | loop fusion | flops 294912 | bytes 1179648 | tf_op jit(solution)/shard_map/broadcast_in_dim | solution.py:145
  (40 shorter events, 9.8 us)
Async XLA Ops:
  0.0 1.9 %copy-start = (bf16[16,2,3,32,4,128]{5,4,3,2,1,0:T(4,128)(2,1)S(1)}, bf16[16,2,3,32,4,128]{5,4,3,2,1,0:T(4,128)(2,1)}, u32[]{:S(2)}) copy-start(bf16[16,2,3,32,4,128]{5,4,3,2,1,0:T(4,128)(2,1)} %param.4) | copy-start | bytes 9437188
  3.8 1.4 %copy-start.5 = (f32[3,16,4,128]{3,2,1,0:T(4,128)S(1)}, f32[3,16,4,128]{3,2,1,0:T(4,128)}, u32[]{:S(2)}) copy-start(f32[3,16,4,128]{3,2,1,0:T(4,128)} %param.5) | copy-start | bytes 294916
  6.0 2.3 %collective-permute-start = (f32[122880]{0:T(1024)}, f32[122880]{0:T(1024)}, u32[]{:S(2)}, u32[]{:S(2)}) collective-permute-start(f32[122880]{0:T(1024)} %pad_maximum_fusion.5), channel_id=1, source_target_pairs={{0,1},{1,0},{2,3},{3,2},{4,5},{5,4},{6,7},{7,6},{8,9},{9,8},{10,11... | collective-permute-start | bytes 1474568 | tf_op jit(solution)/shard_map/ppermute | solution.py:105
  12.4 0.7 %copy-start.3 = (f32[3,32,4,128]{3,2,1,0:T(4,128)}, f32[3,32,4,128]{3,2,1,0:T(4,128)S(1)}, u32[]{:S(2)}) copy-start(f32[3,32,4,128]{3,2,1,0:T(4,128)S(1)} %maximum_select_fusion) | copy-start | bytes 589828
  18.5 10.5 %collective-permute-start.2 = (f32[9,32,4,2]{1,2,3,0:T(4,128)}, f32[9,32,4,2]{1,2,3,0:T(4,128)}, u32[]{:S(2)}, u32[]{:S(2)}) collective-permute-start(f32[9,32,4,2]{1,2,3,0:T(4,128)} %copy.25), channel_id=1, source_target_pairs={{2,0},{3,1},{6,4},{7,5},{10,8},{11,9},{14,12},{15,13},{18,16},{19,... | collective-permute-start | bytes 27656 | tf_op jit(solution)/shard_map/ppermute | solution.py:80
  19.8 7.3 %collective-permute-start.1 = (f32[9,32,4,2]{1,2,3,0:T(4,128)}, f32[9,32,4,2]{1,2,3,0:T(4,128)}, u32[]{:S(2)}, u32[]{:S(2)}) collective-permute-start(f32[9,32,4,2]{1,2,3,0:T(4,128)} %copy.24), channel_id=1, source_target_pairs={{0,2},{1,3},{4,6},{5,7},{8,10},{9,11},{12,14},{13,15},{16,18},{17,... | collective-permute-start | bytes 27656 | tf_op jit(solution)/shard_map/ppermute | solution.py:79
  33.2 21.1 %copy-start.1 = (f32[9,32,4,2]{3,2,1,0:T(4,128)S(1)}, f32[9,32,4,2]{3,2,1,0:T(4,128)}, u32[]{:S(2)}) copy-start(f32[9,32,4,2]{3,2,1,0:T(4,128)} %copy.26) | copy-start | bytes 27652
  33.2 21.1 %copy-start.2 = (f32[9,32,4,2]{3,2,1,0:T(4,128)S(1)}, f32[9,32,4,2]{3,2,1,0:T(4,128)}, u32[]{:S(2)}) copy-start(f32[9,32,4,2]{3,2,1,0:T(4,128)} %copy.27) | copy-start | bytes 27652
  33.2 21.1 %copy-start.4 = (f32[3,32,4,128]{3,2,1,0:T(4,128)S(1)}, f32[3,32,4,128]{3,2,1,0:T(4,128)}, u32[]{:S(2)}) copy-start(f32[3,32,4,128]{3,2,1,0:T(4,128)} %copy-done.3) | copy-start | bytes 589828
  33.8 16.4 %collective-permute-start.3 = (f32[9,32,2,132]{3,2,1,0:T(2,128)S(1)}, f32[9,32,2,132]{3,2,1,0:T(2,128)S(1)}, u32[]{:S(2)}, u32[]{:S(2)}) collective-permute-start(f32[9,32,2,132]{3,2,1,0:T(2,128)S(1)} %get-tuple-element.24), channel_id=1, source_target_pairs={{0,4},{4,8},{8,12},{1,5},{5,9},{9,13},{2,6},{6,10},{10,14},{3,7},{... | collective-permute-start | bytes 912392 | tf_op jit(solution)/shard_map/ppermute | solution.py:79
  38.4 15.8 %collective-permute-start.4 = (f32[9,32,2,132]{3,2,1,0:T(2,128)S(1)}, f32[9,32,2,132]{3,2,1,0:T(2,128)S(1)}, u32[]{:S(2)}, u32[]{:S(2)}) collective-permute-start(f32[9,32,2,132]{3,2,1,0:T(2,128)S(1)} %get-tuple-element.25), channel_id=1, source_target_pairs={{4,0},{8,4},{12,8},{5,1},{9,5},{13,9},{6,2},{10,6},{14,10},{7,3},{... | collective-permute-start | bytes 912392 | tf_op jit(solution)/shard_map/ppermute | solution.py:80

commit v2 on v1

--- a/solution.py
+++ b/solution.py
@@ -94,18 +94,22 @@
     n_tx = lax.axis_size("tx")
     tx_index = lax.axis_index("tx")
     other = (tx_index + 1) % n_tx
-    own_groups = lax.dynamic_slice_in_dim(group_of, tx_index * nt_local, nt_local, 0)
-    own_signs = lax.dynamic_slice_in_dim(sign_of, tx_index * nt_local, nt_local, 0)
+    mine = lax.broadcasted_iota(jnp.int32, (n_tx, nt_local), 0) == tx_index
+    own_groups = jnp.sum(jnp.where(mine, group_of.reshape(n_tx, nt_local), 0), axis=0)
+    own_signs = jnp.sum(jnp.where(mine, sign_of.reshape(n_tx, nt_local), 0), axis=0)
     rows = jnp.stack([other, tx_index]).astype(jnp.int32)
     weights = encode_weights(own_groups, own_signs, rows)
     partial = lax.dot_general(
         weights, primaries, (((1,), (0,)), ((), ())), preferred_element_type=jnp.float32
     )
-    send = jnp.concatenate([partial[0].reshape(-1), conductivity.reshape(-1)])
+    n_shot = partial.shape[1] * partial.shape[2]
+    shot_planes = n_shot * depth
+    partial = partial.reshape(2, shot_planes, width_x, width_y)
+    sigma_planes = conductivity.reshape(-1, width_x, width_y)
+    send = jnp.concatenate([partial[0], sigma_planes], axis=0)
     got = lax.ppermute(send, "tx", [(i, (i + 1) % n_tx) for i in range(n_tx)])
-    shot_cells = partial[1].size
-    shot = partial[1] + got[:shot_cells].reshape(partial[1].shape)
-    sigma_other = got[shot_cells:].reshape(conductivity.shape)
+    shot = partial[1] + got[:shot_planes]
+    sigma_other = got[shot_planes:].reshape(conductivity.shape)
     low_first = tx_index == 0
     sigma_all = jnp.where(
         low_first,
@@ -113,14 +117,14 @@
         jnp.concatenate([sigma_other, conductivity], axis=1),
     )
 
-    planes = jnp.concatenate([shot.reshape(-1, depth, width_x, width_y), sigma_all], axis=0)
-    planes = halo(planes, "yb", 3, SWEEPS)
-    planes = halo(planes, "xb", 2, SWEEPS)
+    planes = jnp.concatenate([shot, sigma_all.reshape(-1, width_x, width_y)], axis=0)
+    planes = halo(planes, "xb", 1, SWEEPS)
+    planes = halo(planes, "yb", 2, SWEEPS)
+    shot_shape = primaries.shape[1:3]
     ext_x = width_x + 2 * SWEEPS
     ext_y = width_y + 2 * SWEEPS
-    n_shot = shot.shape[0] * shot.shape[1]
-    shot_ext = planes[:n_shot].reshape(shot.shape[:2] + (depth, ext_x, ext_y))
-    sigma_ext = planes[n_shot:]
+    shot_ext = planes[:shot_planes].reshape(shot_shape + (depth, ext_x, ext_y))
+    sigma_ext = planes[shot_planes:].reshape(-1, depth, ext_x, ext_y)
 
     gx = lax.axis_index("xb") * width_x - SWEEPS + lax.broadcasted_iota(jnp.int32, (ext_x, ext_y), 0)
     gy = lax.axis_index("yb") * width_y - SWEEPS + lax.broadcasted_iota(jnp.int32, (ext_x, ext_y), 1)

time: 64.2 us -> 72.6 us (1.13)
  local copies, waits for them, and re-layouts: 14.4 us -> 21.5 us
  other arithmetic: 16 us -> 20.3 us
  starting transfers between devices: 13.9 us -> 11.9 us
  waiting for transfers between devices: 17.2 us -> 16.1 us
    mul x0 -> x3, local copies, waits for them, and re-layouts: none -> 7.04 us  [the longest x1 2.36 us: body(): kappa = K_FREQ * sigma_ext]
    slice x6 -> x3, local copies, waits for them, and re-layouts: 7.75 us -> 2.68 us  [the longest x1 1.42 us: body(): shot = partial[1] + got[:shot_planes]]
    ppermute x2, waiting for transfers between devices: 4.15 us -> 9.02 us  [halo(): from_high = lax.ppermute(head, axis, [(i + 1, i) for i in range(count - 1)])]
    ppermute x2, waiting for transfers between devices: 11.2 us -> 7.03 us  [halo(): from_low = lax.ppermute(tail, axis, [(i, i + 1) for i in range(count - 1)])]
    ppermute x2 -> x0, local copies, waits for them, and re-layouts: 3.78 us -> none  [the longest x1 1.89 us: halo(): from_low = lax.ppermute(tail, axis, [(i, i + 1) for i in range(count - 1)])]
    reshape x0 -> x3, local copies, waits for them, and re-layouts: none -> 3.41 us  [the longest x1 1.72 us: body(): sigma_planes = conductivity.reshape(-1, width_x, width_y)]
    unnamed x12 -> x13, local copies, waits for them, and re-layouts: 0.83 us -> 3.93 us
    squeeze x0 -> x2, local copies, waits for them, and re-layouts: none -> 3 us  [the longest x1 1.99 us: body(): send = jnp.concatenate([partial[0], sigma_planes], axis=0)]
  transfers between devices with their start and end apart: 5 -> 5, of which waited for: 4 -> 3; matrix products, arithmetic and copies ran while one was open for 3% -> 4% of each run, Pallas kernels for 0% -> 0%
where the time goes in v2:
time: 72.6 us; the launch traced here: 71.9 us
  local copies, waits for them, and re-layouts  21.5 us (30%)
  other arithmetic  20.3 us (28%)
  waiting for transfers between devices  16.1 us (22%)
  starting transfers between devices  11.9 us (16%)
  matrix products  1.93 us (3%)
    ppermute x2, waiting for transfers between devices, halo(): from_high = lax.ppermute(head, axis, [(i + 1, i) for i in range(count - 1)])  9.02 us
    ppermute x2, starting transfers between devices, halo(): from_low = lax.ppermute(tail, axis, [(i, i + 1) for i in range(count - 1)])  8.61 us
    ppermute x2, waiting for transfers between devices, halo(): from_low = lax.ppermute(tail, axis, [(i, i + 1) for i in range(count - 1)])  7.03 us
    unnamed x13, local copies, waits for them, and re-layouts  3.93 us
    ppermute x2, starting transfers between devices, halo(): from_high = lax.ppermute(head, axis, [(i + 1, i) for i in range(count - 1)])  2.75 us
    mul x1, local copies, waits for them, and re-layouts, body(): kappa = K_FREQ * sigma_ext  2.36 us
    mul x1, local copies, waits for them, and re-layouts, source_term(): delta * shot[..., 1, :, :, :, :]  2.34 us
    mul x1, local copies, waits for them, and re-layouts, source_term(): -delta * shot[..., 0, :, :, :, :]  2.34 us
  transfers between devices with their start and end apart: 5, of which 3 were waited for; matrix products, arithmetic and copies ran while one was open for 4% of the time, Pallas kernels for 0%

profile of v2, /device:TPU:0, one launch (start us, length us, event | category | flops | bytes accessed | tf_op | source)
XLA Modules:
  0.0 71.9 jit_solution(8176082262341924319)
XLA Ops:
  1.7 1.7 %copy.78 = f32[48,4,128]{0,1,2:T(4,128)} copy(f32[48,4,128]{2,1,0:T(4,128)} %bitcast.152) | data formatting | bytes 196608 | tf_op jit(solution)/shard_map/reshape | solution.py:108
  3.6 1.9 %fusion = f32[2,2,3,32,4,128]{5,0,4,3,2,1:T(2,128)S(1)} fusion(bf16[16,2,3,32,4,128]{5,4,3,2,1,0:T(4,128)(2,1)S(1)} %copy-done, s32[16]{0:T(128)S(1)} %get-tuple-element.6, s32[16]{0:T(128)S(1)} %get-tuple-element.5, s32[2]{0:T(128)S(1)} %pad_add_fusion), kind=kOutput, calls=%fused_computation | convolution fusion | flops 6291584 | bytes 3932296 | tf_op jit(solution)/shard_map/dot_general | solution.py:102
  5.5 1.4 %fusion.59 = (f32[1,2,3,32,4,128]{5,0,4,3,2,1:T(1,128)S(1)}, f32[1,2,3,32,4,128]{5,0,4,3,2,1:T(1,128)}) fusion(f32[2,2,3,32,4,128]{5,0,4,3,2,1:T(2,128)S(1)} %fusion), kind=kLoop, calls=%fused_computation.140 | loop fusion | bytes 1572864 | tf_op jit(solution)/shard_map/slice | solution.py:111
  6.9 2.0 %copy.77 = f32[192,4,128]{0,1,2:T(4,128)} copy(f32[192,4,128]{2,1,0:T(4,128)} %bitcast.150) | data formatting | bytes 786432 | tf_op jit(solution)/shard_map/squeeze | solution.py:109
  8.9 2.2 %pad_maximum_fusion.3 = f32[240,4,128]{0,1,2:T(4,128)} fusion(f32[48,4,128]{0,1,2:T(4,128)} %copy.78, f32[192,4,128]{0,1,2:T(4,128)} %copy.77), kind=kLoop, calls=%fused_computation.78 | loop fusion | flops 122880 | bytes 983040 | tf_op jit(solution)/shard_map/concatenate | solution.py:109
  11.6 1.5 %copy.81 = f32[3,16,4,128]{3,1,0,2:T(8,128)} copy(f32[3,16,4,128]{3,2,1,0:T(4,128)} %param.5) | data formatting | bytes 196608 | tf_op args[1]
  14.1 1.1 %slice.325 = f32[48,4,128]{0,1,2:T(4,128)S(1)} slice(f32[240,4,128]{0,1,2:T(4,128)} %collective-permute-done), slice={[192:240], [0:4], [0:128]} | slice | bytes 196608 | tf_op jit(solution)/shard_map/slice | solution.py:112
  15.4 1.7 %maximum_select_fusion = f32[3,32,4,128]{3,1,0,2:T(8,128)} fusion(f32[3,16,4,128]{3,1,0,2:T(8,128)S(1)} %bitcast.153, f32[3,16,4,128]{3,1,0,2:T(8,128)} %copy.81, pred[]{:T(512)S(6)} %eq.30), kind=kLoop, calls=%fused_computation.100 | loop fusion | flops 147456 | bytes 393217 | tf_op jit(solution)/shard_map/jit(_where)/select_n | solution.py:114
  17.1 1.1 %copy.83 = f32[96,4,128]{0,1,2:T(4,128)S(1)} copy(f32[96,4,128]{2,0,1:T(8,128)} %bitcast.151) | data formatting | bytes 393216 | tf_op jit(solution)/shard_map/jit(_where)/select_n | solution.py:114
  18.2 1.3 %slice_add_fusion = f32[192,4,128]{0,1,2:T(4,128)S(1)} fusion(f32[192,4,128]{0,1,2:T(4,128)} %copy.79, f32[240,4,128]{0,1,2:T(4,128)} %collective-permute-done), kind=kLoop, calls=%fused_computation.77 | loop fusion | flops 98304 | bytes 1179648 | tf_op jit(solution)/shard_map/add | solution.py:111
  20.3 1.5 %fusion.30 = (f32[288,2,128]{0,1,2:T(2,128)}, f32[288,2,128]{0,1,2:T(2,128)}) fusion(f32[192,4,128]{0,1,2:T(4,128)S(1)} %slice_add_fusion, f32[96,4,128]{0,1,2:T(4,128)S(1)} %copy.83), kind=kLoop, calls=%fused_computation.80 | loop fusion | flops 147456 | bytes 1179648 | tf_op jit(solution)/shard_map/concatenate | solution.py:120
  21.8 5.2 %collective-permute-start.1 = (f32[288,2,128]{0,1,2:T(2,128)}, f32[288,2,128]{0,1,2:T(2,128)}, u32[]{:S(2)}, u32[]{:S(2)}) collective-permute-start(f32[288,2,128]{0,1,2:T(2,128)} %get-tuple-element.28), channel_id=1, source_target_pairs={{0,4},{4,8},{8,12},{1,5},{5,9},{9,13},{2,6},{6,10},{10,14},{3,7},{... | collective-permute-start | bytes 884744 | tf_op jit(solution)/shard_map/ppermute | solution.py:79
  27.0 1.3 %collective-permute-start.2 = (f32[288,2,128]{0,1,2:T(2,128)}, f32[288,2,128]{0,1,2:T(2,128)}, u32[]{:S(2)}, u32[]{:S(2)}) collective-permute-start(f32[288,2,128]{0,1,2:T(2,128)} %get-tuple-element.29), channel_id=1, source_target_pairs={{4,0},{8,4},{12,8},{5,1},{9,5},{13,9},{6,2},{10,6},{14,10},{7,3},{... | collective-permute-start | bytes 884744 | tf_op jit(solution)/shard_map/ppermute | solution.py:80
  28.6 7.0 %collective-permute-done.1 = f32[288,2,128]{0,1,2:T(2,128)} collective-permute-done((f32[288,2,128]{0,1,2:T(2,128)}, f32[288,2,128]{0,1,2:T(2,128)}, u32[]{:S(2)}, u32[]{:S(2)}) %collective-permute-start.1) | collective-permute-done | bytes 294944 | tf_op jit(solution)/shard_map/ppermute | solution.py:79
  35.6 4.9 %collective-permute-done.2 = f32[288,2,128]{0,1,2:T(2,128)} collective-permute-done((f32[288,2,128]{0,1,2:T(2,128)}, f32[288,2,128]{0,1,2:T(2,128)}, u32[]{:S(2)}, u32[]{:S(2)}) %collective-permute-start.2) | collective-permute-done | bytes 294944 | tf_op jit(solution)/shard_map/ppermute | solution.py:80
  41.4 3.4 %collective-permute-start.3 = (f32[288,8,2]{0,1,2:T(8,128)S(1)}, f32[288,8,2]{0,1,2:T(8,128)S(1)}, u32[]{:S(2)}, u32[]{:S(2)}) collective-permute-start(f32[288,8,2]{0,1,2:T(8,128)S(1)} %get-tuple-element.24), channel_id=1, source_target_pairs={{0,2},{1,3},{4,6},{5,7},{8,10},{9,11},{12,14},{13,15},{16,18},{17,... | collective-permute-start | bytes 55304 | tf_op jit(solution)/shard_map/ppermute | solution.py:79
  44.7 1.5 %collective-permute-start.4 = (f32[288,8,2]{0,1,2:T(8,128)S(1)}, f32[288,8,2]{0,1,2:T(8,128)S(1)}, u32[]{:S(2)}, u32[]{:S(2)}) collective-permute-start(f32[288,8,2]{0,1,2:T(8,128)S(1)} %get-tuple-element.25), channel_id=1, source_target_pairs={{2,0},{3,1},{6,4},{7,5},{10,8},{11,9},{14,12},{15,13},{18,16},{19,... | collective-permute-start | bytes 55304 | tf_op jit(solution)/shard_map/ppermute | solution.py:80
  46.3 4.2 %collective-permute-done.4 = f32[288,8,2]{0,1,2:T(8,128)S(1)} collective-permute-done((f32[288,8,2]{0,1,2:T(8,128)S(1)}, f32[288,8,2]{0,1,2:T(8,128)S(1)}, u32[]{:S(2)}, u32[]{:S(2)}) %collective-permute-start.4) | collective-permute-done | bytes 18464 | tf_op jit(solution)/shard_map/ppermute | solution.py:80
  50.5 1.8 %pad_maximum_fusion.1 = f32[288,8,132]{0,1,2:T(8,128)S(1)} fusion(f32[288,8,2]{0,1,2:T(8,128)S(1)} %collective-permute-done.4, f32[288,2,128]{0,1,2:T(2,128)} %collective-permute-done.2, f32[96,4,128]{0,1,2:T(4,128)S(1)} %copy.83, f32[192,4,128]{0,1,2:T(4,128)S(1)} %copy-done.5, f32[288,2,128]{0,1,2:T(2,128)} %collective-permute-done.1, ...), kind=kLoop, calls=%fused_computation.5 | loop fusion | flops 1520640 | bytes 2433024 | tf_op jit(solution)/shard_map/concatenate | solution.py:81
  52.2 1.5 %slice_multiply_fusion.1 = (f32[96,8,132]{0,1,2:T(8,128)}, f32[96,8,132]{0,1,2:T(8,128)}, f32[96,8,132]{0,1,2:T(8,128)}) fusion(f32[288,8,132]{0,1,2:T(8,128)S(1)} %pad_maximum_fusion.1), kind=kLoop, calls=%fused_computation.63 | loop fusion | flops 608256 | bytes 2433024 | tf_op jit(solution)/shard_map/mul | solution.py:63
  53.7 2.3 %copy.84 = f32[96,8,132]{2,1,0:T(8,128)} copy(f32[96,8,132]{0,1,2:T(8,128)} %get-tuple-element.15) | data formatting | bytes 811008 | tf_op jit(solution)/shard_map/mul | solution.py:63
  56.1 2.4 %copy.85 = f32[96,8,132]{2,1,0:T(8,128)} copy(f32[96,8,132]{0,1,2:T(8,128)} %get-tuple-element.17) | data formatting | bytes 811008 | tf_op jit(solution)/shard_map/mul | solution.py:133
  58.4 2.3 %copy.86 = f32[96,8,132]{2,1,0:T(8,128)} copy(f32[96,8,132]{0,1,2:T(8,128)} %get-tuple-element.16) | data formatting | bytes 811008 | tf_op jit(solution)/shard_map/mul | solution.py:63
  60.8 1.9 %subtract_divide_fusion = (f32[1,3,32,8,132]{4,3,2,1,0:T(8,128)S(1)}, f32[1,3,32,8,132]{4,3,2,1,0:T(8,128)S(1)}) fusion(f32[1,3,32,8,132]{4,3,2,1,0:T(8,128)} %bitcast.138, f32[1,3,32,8,132]{4,3,2,1,0:T(8,128)} %bitcast.143, f32[1,3,32,8,132]{4,3,2,1,0:T(8,128)} %bitcast.146), kind=kLoop, calls=%fused_computation.35 | loop fusion | flops 1013760 | bytes 2027520 | tf_op jit(solution)/shard_map/div | solution.py:58
  (46 shorter events, 14.5 us)
Async XLA Ops:
  0.0 3.6 %copy-start = (bf16[16,2,3,32,4,128]{5,4,3,2,1,0:T(4,128)(2,1)S(1)}, bf16[16,2,3,32,4,128]{5,4,3,2,1,0:T(4,128)(2,1)}, u32[]{:S(2)}) copy-start(bf16[16,2,3,32,4,128]{5,4,3,2,1,0:T(4,128)(2,1)} %param.4) | copy-start | bytes 9437188
  11.1 3.0 %collective-permute-start = (f32[240,4,128]{0,1,2:T(4,128)}, f32[240,4,128]{0,1,2:T(4,128)}, u32[]{:S(2)}, u32[]{:S(2)}) collective-permute-start(f32[240,4,128]{0,1,2:T(4,128)} %pad_maximum_fusion.3), channel_id=1, source_target_pairs={{0,1},{1,0},{2,3},{3,2},{4,5},{5,4},{6,7},{7,6},{8,9},{9,8},{10,11... | collective-permute-start | bytes 1474568 | tf_op jit(solution)/shard_map/ppermute | solution.py:110
  19.5 0.8 %copy-start.4 = (f32[192,4,128]{0,1,2:T(4,128)}, f32[192,4,128]{0,1,2:T(4,128)S(1)}, u32[]{:S(2)}) copy-start(f32[192,4,128]{0,1,2:T(4,128)S(1)} %slice_add_fusion) | copy-start | bytes 1179652
  21.8 13.8 %collective-permute-start.1 = (f32[288,2,128]{0,1,2:T(2,128)}, f32[288,2,128]{0,1,2:T(2,128)}, u32[]{:S(2)}, u32[]{:S(2)}) collective-permute-start(f32[288,2,128]{0,1,2:T(2,128)} %get-tuple-element.28), channel_id=1, source_target_pairs={{0,4},{4,8},{8,12},{1,5},{5,9},{9,13},{2,6},{6,10},{10,14},{3,7},{... | collective-permute-start | bytes 884744 | tf_op jit(solution)/shard_map/ppermute | solution.py:79
  27.0 13.4 %collective-permute-start.2 = (f32[288,2,128]{0,1,2:T(2,128)}, f32[288,2,128]{0,1,2:T(2,128)}, u32[]{:S(2)}, u32[]{:S(2)}) collective-permute-start(f32[288,2,128]{0,1,2:T(2,128)} %get-tuple-element.29), channel_id=1, source_target_pairs={{4,0},{8,4},{12,8},{5,1},{9,5},{13,9},{6,2},{10,6},{14,10},{7,3},{... | collective-permute-start | bytes 884744 | tf_op jit(solution)/shard_map/ppermute | solution.py:80
  28.3 22.1 %copy-start.5 = (f32[192,4,128]{0,1,2:T(4,128)S(1)}, f32[192,4,128]{0,1,2:T(4,128)}, u32[]{:S(2)}) copy-start(f32[192,4,128]{0,1,2:T(4,128)} %copy-done.4) | copy-start | bytes 1179652
  41.4 5.0 %collective-permute-start.3 = (f32[288,8,2]{0,1,2:T(8,128)S(1)}, f32[288,8,2]{0,1,2:T(8,128)S(1)}, u32[]{:S(2)}, u32[]{:S(2)}) collective-permute-start(f32[288,8,2]{0,1,2:T(8,128)S(1)} %get-tuple-element.24), channel_id=1, source_target_pairs={{0,2},{1,3},{4,6},{5,7},{8,10},{9,11},{12,14},{13,15},{16,18},{17,... | collective-permute-start | bytes 55304 | tf_op jit(solution)/shard_map/ppermute | solution.py:79
  44.7 5.7 %collective-permute-start.4 = (f32[288,8,2]{0,1,2:T(8,128)S(1)}, f32[288,8,2]{0,1,2:T(8,128)S(1)}, u32[]{:S(2)}, u32[]{:S(2)}) collective-permute-start(f32[288,8,2]{0,1,2:T(8,128)S(1)} %get-tuple-element.25), channel_id=1, source_target_pairs={{2,0},{3,1},{6,4},{7,5},{10,8},{11,9},{14,12},{15,13},{18,16},{19,... | collective-permute-start | bytes 55304 | tf_op jit(solution)/shard_map/ppermute | solution.py:80
  64.4 1.1 %copy-start.1 = (f32[96,8,132]{2,1,0:T(8,128)S(1)}, f32[96,8,132]{2,1,0:T(8,128)}, u32[]{:S(2)}) copy-start(f32[96,8,132]{2,1,0:T(8,128)} %copy.85) | copy-start | bytes 1216516
  65.5 1.1 %copy-start.2 = (f32[96,8,132]{2,1,0:T(8,128)S(1)}, f32[96,8,132]{2,1,0:T(8,128)}, u32[]{:S(2)}) copy-start(f32[96,8,132]{2,1,0:T(8,128)} %copy.84) | copy-start | bytes 1216516
  65.5 1.4 %copy-start.3 = (f32[96,8,132]{2,1,0:T(8,128)S(1)}, f32[96,8,132]{2,1,0:T(8,128)}, u32[]{:S(2)}) copy-start(f32[96,8,132]{2,1,0:T(8,128)} %copy.86) | copy-start | bytes 1216516

commit v3 on v2

--- a/solution.py
+++ b/solution.py
@@ -102,28 +102,26 @@
     partial = lax.dot_general(
         weights, primaries, (((1,), (0,)), ((), ())), preferred_element_type=jnp.float32
     )
-    n_shot = partial.shape[1] * partial.shape[2]
-    shot_planes = n_shot * depth
-    partial = partial.reshape(2, shot_planes, width_x, width_y)
-    sigma_planes = conductivity.reshape(-1, width_x, width_y)
-    send = jnp.concatenate([partial[0], sigma_planes], axis=0)
-    got = lax.ppermute(send, "tx", [(i, (i + 1) % n_tx) for i in range(n_tx)])
-    shot = partial[1] + got[:shot_planes]
-    sigma_other = got[shot_planes:].reshape(conductivity.shape)
+    sigma_half = halo(conductivity, "xb", 2, SWEEPS)
+    tx_ring = [(i, (i + 1) % n_tx) for i in range(n_tx)]
+    got = lax.ppermute(partial[0], "tx", tx_ring)
+    shot = partial[1] + got
+    sigma_other = lax.ppermute(sigma_half, "tx", tx_ring)
     low_first = tx_index == 0
     sigma_all = jnp.where(
         low_first,
-        jnp.concatenate([conductivity, sigma_other], axis=1),
-        jnp.concatenate([sigma_other, conductivity], axis=1),
+        jnp.concatenate([sigma_half, sigma_other], axis=1),
+        jnp.concatenate([sigma_other, sigma_half], axis=1),
     )
-
-    planes = jnp.concatenate([shot, sigma_all.reshape(-1, width_x, width_y)], axis=0)
-    planes = halo(planes, "xb", 1, SWEEPS)
-    planes = halo(planes, "yb", 2, SWEEPS)
-    shot_shape = primaries.shape[1:3]
+    shot = halo(shot, "xb", 3, SWEEPS)
     ext_x = width_x + 2 * SWEEPS
     ext_y = width_y + 2 * SWEEPS
-    shot_ext = planes[:shot_planes].reshape(shot_shape + (depth, ext_x, ext_y))
+    shot_planes = shot.shape[0] * shot.shape[1] * depth
+    planes = jnp.concatenate(
+        [shot.reshape(-1, ext_x, width_y), sigma_all.reshape(-1, ext_x, width_y)], axis=0
+    )
+    planes = halo(planes, "yb", 2, SWEEPS)
+    shot_ext = planes[:shot_planes].reshape(shot.shape[:2] + (depth, ext_x, ext_y))
     sigma_ext = planes[shot_planes:].reshape(-1, depth, ext_x, ext_y)
 
     gx = lax.axis_index("xb") * width_x - SWEEPS + lax.broadcasted_iota(jnp.int32, (ext_x, ext_y), 0)

time: 72.6 us -> 62.7 us (0.86)
  local copies, waits for them, and re-layouts: 21.5 us -> 13.4 us
  starting transfers between devices: 11.9 us -> 18.1 us
  other arithmetic: 20.3 us -> 16.1 us
  waiting for transfers between devices: 16.1 us -> 12.3 us
    mul x3 -> x0, local copies, waits for them, and re-layouts: 7.04 us -> none  [the longest x1 2.36 us: body(): kappa = K_FREQ * sigma_ext]
    ppermute x2 -> x3, starting transfers between devices: 8.61 us -> 13.7 us  [halo(): from_low = lax.ppermute(tail, axis, [(i, i + 1) for i in range(count - 1)])]
    ppermute x0 -> x2, local copies, waits for them, and re-layouts: none -> 4.34 us  [the longest x1 2.18 us: halo(): from_low = lax.ppermute(tail, axis, [(i, i + 1) for i in range(count - 1)])]
    slice x3 -> x5, local copies, waits for them, and re-layouts: 2.68 us -> 6.96 us  [the longest x3 3.19 us: halo(): tail = lax.slice_in_dim(cells, size - width, size, axis=dim)]
    unnamed x13 -> x8, local copies, waits for them, and re-layouts: 3.93 us -> 0.06 us
    ppermute x2 -> x3, waiting for transfers between devices: 7.03 us -> 3.35 us  [halo(): from_low = lax.ppermute(tail, axis, [(i, i + 1) for i in range(count - 1)])]
    squeeze x2 -> x0, local copies, waits for them, and re-layouts: 3 us -> none  [the longest x1 1.99 us: body(): send = jnp.concatenate([partial[0], sigma_planes], axis=0)]
    concatenate x1 -> x3, other arithmetic: 1.75 us -> 4.06 us  [halo(): return jnp.concatenate([from_low, cells, from_high], axis=dim)]
  transfers between devices with their start and end apart: 5 -> 8, of which waited for: 3 -> 4; matrix products, arithmetic and copies ran while one was open for 4% -> 10% of each run, Pallas kernels for 0% -> 0%
where the time goes in v3:
time: 62.7 us; the launch traced here: 62.1 us
  starting transfers between devices  18.1 us (29%)
  other arithmetic  16.1 us (26%)
  local copies, waits for them, and re-layouts  13.4 us (21%)
  waiting for transfers between devices  12.3 us (20%)
  matrix products  1.93 us (3%)
    ppermute x3, starting transfers between devices, halo(): from_low = lax.ppermute(tail, axis, [(i, i + 1) for i in range(count - 1)])  13.7 us
    ppermute x3, waiting for transfers between devices, halo(): from_high = lax.ppermute(head, axis, [(i + 1, i) for i in range(count - 1)])  8.98 us
    concatenate x3, other arithmetic, halo(): return jnp.concatenate([from_low, cells, from_high], axis=dim)  4.06 us
    ppermute x3, starting transfers between devices, halo(): from_high = lax.ppermute(head, axis, [(i + 1, i) for i in range(count - 1)])  3.85 us
    ppermute x3, waiting for transfers between devices, halo(): from_low = lax.ppermute(tail, axis, [(i, i + 1) for i in range(count - 1)])  3.35 us
    slice x3, local copies, waits for them, and re-layouts, halo(): tail = lax.slice_in_dim(cells, size - width, size, axis=dim)  3.19 us
    slice x1, local copies, waits for them, and re-layouts, halo(): head = lax.slice_in_dim(cells, 0, width, axis=dim)  2.35 us
    ppermute x1, local copies, waits for them, and re-layouts, halo(): from_low = lax.ppermute(tail, axis, [(i, i + 1) for i in range(count - 1)])  2.18 us
  transfers between devices with their start and end apart: 8, of which 4 were waited for; matrix products, arithmetic and copies ran while one was open for 10% of the time, Pallas kernels for 0%

profile of v3, /device:TPU:0, one launch (start us, length us, event | category | flops | bytes accessed | tf_op | source)
XLA Modules:
  0.0 62.1 jit_solution(10522451726193774567)
XLA Ops:
  0.0 0.9 %reshape.140 = s32[2,16]{1,0:T(2,128)S(1)} reshape(s32[32]{0:T(128)} %param.6) | data formatting | bytes 256 | tf_op jit(solution)/shard_map/reshape | solution.py:98
  1.9 1.9 %fusion = f32[2,2,3,32,4,128]{5,0,4,3,2,1:T(2,128)S(1)} fusion(bf16[16,2,3,32,4,128]{5,4,3,2,1,0:T(4,128)(2,1)S(1)} %copy-done, s32[16]{0:T(128)S(1)} %get-tuple-element.6, s32[16]{0:T(128)S(1)} %get-tuple-element.5, s32[2]{0:T(128)S(1)} %pad_add_fusion), kind=kOutput, calls=%fused_computation | convolution fusion | flops 6291584 | bytes 3932296 | tf_op jit(solution)/shard_map/dot_general | solution.py:102
  3.8 1.4 %fusion.58 = (f32[1,2,3,32,4,128]{5,0,4,3,2,1:T(1,128)}, f32[1,2,3,32,4,128]{5,0,4,3,2,1:T(1,128)S(1)}) fusion(f32[2,2,3,32,4,128]{5,0,4,3,2,1:T(2,128)S(1)} %fusion), kind=kLoop, calls=%fused_computation.134 | loop fusion | bytes 1572864 | tf_op jit(solution)/shard_map/slice | solution.py:107
  6.4 5.1 %collective-permute-start.3 = (f32[3,16,2,128]{3,2,1,0:T(2,128)}, f32[3,16,2,128]{3,2,1,0:T(2,128)}, u32[]{:S(2)}, u32[]{:S(2)}) collective-permute-start(f32[3,16,2,128]{3,2,1,0:T(2,128)} %get-tuple-element.44), channel_id=1, source_target_pairs={{0,4},{4,8},{8,12},{1,5},{5,9},{9,13},{2,6},{6,10},{10,14},{3,7},{... | collective-permute-start | bytes 147464 | tf_op jit(solution)/shard_map/ppermute | solution.py:79
  11.5 1.3 %collective-permute-start.4 = (f32[3,16,2,128]{3,2,1,0:T(2,128)}, f32[3,16,2,128]{3,2,1,0:T(2,128)}, u32[]{:S(2)}, u32[]{:S(2)}) collective-permute-start(f32[3,16,2,128]{3,2,1,0:T(2,128)} %get-tuple-element.45), channel_id=1, source_target_pairs={{4,0},{8,4},{12,8},{5,1},{9,5},{13,9},{6,2},{10,6},{14,10},{7,3},{... | collective-permute-start | bytes 147464 | tf_op jit(solution)/shard_map/ppermute | solution.py:80
  12.9 4.9 %collective-permute-done.4 = f32[3,16,2,128]{3,2,1,0:T(2,128)} collective-permute-done((f32[3,16,2,128]{3,2,1,0:T(2,128)}, f32[3,16,2,128]{3,2,1,0:T(2,128)}, u32[]{:S(2)}, u32[]{:S(2)}) %collective-permute-start.4) | collective-permute-done | bytes 49184 | tf_op jit(solution)/shard_map/ppermute | solution.py:80
  17.8 1.0 %pad_maximum_fusion.7 = f32[3,16,8,128]{3,2,1,0:T(8,128)S(1)} fusion(f32[3,16,2,128]{3,2,1,0:T(2,128)} %collective-permute-done.4, f32[3,16,4,128]{3,2,1,0:T(4,128)} %param.5, f32[3,16,2,128]{3,2,1,0:T(2,128)} %collective-permute-done.3), kind=kLoop, calls=%fused_computation.98 | loop fusion | flops 98304 | bytes 393216 | tf_op jit(solution)/shard_map/concatenate | solution.py:81
  18.8 1.1 %add.114 = f32[2,3,32,4,128]{4,3,2,1,0:T(4,128)S(1)} add(f32[2,3,32,4,128]{4,3,2,1,0:T(4,128)S(1)} %bitcast.154, f32[2,3,32,4,128]{4,3,2,1,0:T(4,128)} %collective-permute-done) | non-fusion elementwise | flops 98304 | bytes 1179648 | tf_op jit(solution)/shard_map/add | solution.py:108
  20.1 2.9 %collective-permute-start.1 = (f32[2,3,32,2,128]{4,3,2,1,0:T(2,128)S(1)}, f32[2,3,32,2,128]{4,3,2,1,0:T(2,128)S(1)}, u32[]{:S(2)}, u32[]{:S(2)}) collective-permute-start(f32[2,3,32,2,128]{4,3,2,1,0:T(2,128)S(1)} %get-tuple-element.42), channel_id=1, source_target_pairs={{0,4},{4,8},{8,12},{1,5},{5,9},{9,13},{2,6},{6,10},{10,14},{3,7},{... | collective-permute-start | bytes 589832 | tf_op jit(solution)/shard_map/ppermute | solution.py:79
  23.0 1.3 %collective-permute-start.2 = (f32[2,3,32,2,128]{4,3,2,1,0:T(2,128)S(1)}, f32[2,3,32,2,128]{4,3,2,1,0:T(2,128)S(1)}, u32[]{:S(2)}, u32[]{:S(2)}) collective-permute-start(f32[2,3,32,2,128]{4,3,2,1,0:T(2,128)S(1)} %get-tuple-element.43), channel_id=1, source_target_pairs={{4,0},{8,4},{12,8},{5,1},{9,5},{13,9},{6,2},{10,6},{14,10},{7,3},{... | collective-permute-start | bytes 589832 | tf_op jit(solution)/shard_map/ppermute | solution.py:80
  24.5 1.0 %maximum_select_fusion = f32[3,32,8,128]{3,2,1,0:T(8,128)S(1)} fusion(f32[3,16,8,128]{3,2,1,0:T(8,128)S(1)} %collective-permute-done.5, f32[3,16,2,128]{3,2,1,0:T(2,128)} %collective-permute-done.4, f32[3,16,4,128]{3,2,1,0:T(4,128)S(1)} %copy-done.3, f32[3,16,2,128]{3,2,1,0:T(2,128)} %collective-permute-done.3, pred[]{:T(512)S(6)} %eq.30), kind=kLoop, calls=%fused_computation.83 | loop fusion | flops 688128 | bytes 786433 | tf_op jit(solution)/shard_map/jit(_where)/select_n | solution.py:111
  25.5 2.3 %collective-permute-done.1 = f32[2,3,32,2,128]{4,3,2,1,0:T(2,128)S(1)} collective-permute-done((f32[2,3,32,2,128]{4,3,2,1,0:T(2,128)S(1)}, f32[2,3,32,2,128]{4,3,2,1,0:T(2,128)S(1)}, u32[]{:S(2)}, u32[]{:S(2)}) %collective-permute-start.1) | collective-permute-done | bytes 196640 | tf_op jit(solution)/shard_map/ppermute | solution.py:79
  27.8 4.1 %collective-permute-done.2 = f32[2,3,32,2,128]{4,3,2,1,0:T(2,128)S(1)} collective-permute-done((f32[2,3,32,2,128]{4,3,2,1,0:T(2,128)S(1)}, f32[2,3,32,2,128]{4,3,2,1,0:T(2,128)S(1)}, u32[]{:S(2)}, u32[]{:S(2)}) %collective-permute-start.2) | collective-permute-done | bytes 196640 | tf_op jit(solution)/shard_map/ppermute | solution.py:80
  32.2 1.8 %slice_maximum_fusion = (f32[288,8,2]{2,1,0:T(8,128)}, f32[288,8,2]{2,1,0:T(8,128)}) fusion(f32[96,8,128]{2,1,0:T(8,128)S(1)} %bitcast.152, f32[192,8,128]{2,1,0:T(8,128)S(1)} %bitcast.150), kind=kLoop, calls=%fused_computation.19 | loop fusion | flops 9216 | bytes 1216512 | tf_op jit(solution)/shard_map/concatenate | solution.py:120
  34.0 2.4 %copy.36 = f32[288,8,2]{0,1,2:T(8,128)} copy(f32[288,8,2]{2,1,0:T(8,128)} %get-tuple-element.26) | data formatting | bytes 36864 | tf_op jit(solution)/shard_map/slice | solution.py:78
  36.3 2.4 %copy.37 = f32[288,8,2]{0,1,2:T(8,128)} copy(f32[288,8,2]{2,1,0:T(8,128)} %get-tuple-element.27) | data formatting | bytes 36864 | tf_op jit(solution)/shard_map/slice | solution.py:77
  38.7 1.3 %collective-permute-start.7 = (f32[288,8,2]{0,1,2:T(8,128)}, f32[288,8,2]{0,1,2:T(8,128)}, u32[]{:S(2)}, u32[]{:S(2)}) collective-permute-start(f32[288,8,2]{0,1,2:T(8,128)} %copy.37), channel_id=1, source_target_pairs={{2,0},{3,1},{6,4},{7,5},{10,8},{11,9},{14,12},{15,13},{18,16},{19,... | collective-permute-start | bytes 55304 | tf_op jit(solution)/shard_map/ppermute | solution.py:80
  40.0 5.8 %collective-permute-start.6 = (f32[288,8,2]{0,1,2:T(8,128)}, f32[288,8,2]{0,1,2:T(8,128)}, u32[]{:S(2)}, u32[]{:S(2)}) collective-permute-start(f32[288,8,2]{0,1,2:T(8,128)} %copy.36), channel_id=1, source_target_pairs={{0,2},{1,3},{4,6},{5,7},{8,10},{9,11},{12,14},{13,15},{16,18},{17,... | collective-permute-start | bytes 55304 | tf_op jit(solution)/shard_map/ppermute | solution.py:79
  45.8 1.0 %collective-permute-done.6 = f32[288,8,2]{0,1,2:T(8,128)} collective-permute-done((f32[288,8,2]{0,1,2:T(8,128)}, f32[288,8,2]{0,1,2:T(8,128)}, u32[]{:S(2)}, u32[]{:S(2)}) %collective-permute-start.6) | collective-permute-done | bytes 18464 | tf_op jit(solution)/shard_map/ppermute | solution.py:79
  46.8 2.2 %copy.38 = f32[288,8,2]{2,1,0:T(8,128)} copy(f32[288,8,2]{0,1,2:T(8,128)} %collective-permute-done.6) | data formatting | bytes 36864 | tf_op jit(solution)/shard_map/ppermute | solution.py:79
  49.0 2.2 %copy.39 = f32[288,8,2]{2,1,0:T(8,128)} copy(f32[288,8,2]{0,1,2:T(8,128)} %collective-permute-done.7) | data formatting | bytes 36864 | tf_op jit(solution)/shard_map/ppermute | solution.py:80
  51.2 2.8 %pad_maximum_fusion = f32[288,8,132]{2,1,0:T(8,128)S(1)} fusion(f32[288,8,2]{2,1,0:T(8,128)} %copy.39, f32[96,8,128]{2,1,0:T(8,128)S(1)} %bitcast.153, f32[192,8,128]{2,1,0:T(8,128)} %bitcast.151, f32[288,8,2]{2,1,0:T(8,128)} %copy.38), kind=kLoop, calls=%fused_computation.2 | loop fusion | flops 912384 | bytes 2433024 | tf_op jit(solution)/shard_map/concatenate | solution.py:81
  55.2 1.0 %fusion.29 = (f32[2,1,32,6,130]{4,3,2,0,1:T(8,128)S(1)}, f32[2,1,32,6,130]{4,3,2,0,1:T(8,128)S(1)}, f32[2,1,32,6,130]{4,3,2,0,1:T(8,128)S(1)}) fusion(f32[2,33,7,131]{3,2,1,0:T(8,128)S(1)} %get-tuple-element.35, f32[2,33,7,131]{3,2,1,0:T(8,128)S(1)} %get-tuple-element.33, f32[2,33,7,131]{3,2,1,0:T(8,128)S(1)} %get-tuple-element.34), kind=kLoop, calls=%fused_computation.77 | loop fusion | flops 449280 | bytes 2396160 | tf_op jit(solution)/shard_map/stack | solution.py:52
  61.1 1.0 %fusion.31 = f32[1,2,3,32,4,128]{5,4,3,2,1,0:T(4,128)} fusion(f32[2,3,32,6,130]{4,3,2,1,0:T(8,128)S(1)} %fusion.4, f32[1,3,32,4,128]{4,3,2,1,0:T(4,128)S(1)} %get-tuple-element.25, f32[1,3,32,4,128]{4,3,2,1,0:T(4,128)S(1)} %get-tuple-element.24), kind=kLoop, calls=%fused_computation.82 | loop fusion | flops 294912 | bytes 1179648 | tf_op jit(solution)/shard_map/broadcast_in_dim | solution.py:147
  (44 shorter events, 9.0 us)
Async XLA Ops:
  0.0 1.9 %copy-start = (bf16[16,2,3,32,4,128]{5,4,3,2,1,0:T(4,128)(2,1)S(1)}, bf16[16,2,3,32,4,128]{5,4,3,2,1,0:T(4,128)(2,1)}, u32[]{:S(2)}) copy-start(bf16[16,2,3,32,4,128]{5,4,3,2,1,0:T(4,128)(2,1)} %param.4) | copy-start | bytes 9437188
  3.8 1.9 %copy-start.2 = (f32[3,16,4,128]{3,2,1,0:T(4,128)S(1)}, f32[3,16,4,128]{3,2,1,0:T(4,128)}, u32[]{:S(2)}) copy-start(f32[3,16,4,128]{3,2,1,0:T(4,128)} %param.5) | copy-start | bytes 294916
  5.3 13.6 %collective-permute-start = (f32[2,3,32,4,128]{4,3,2,1,0:T(4,128)}, f32[2,3,32,4,128]{4,3,2,1,0:T(4,128)}, u32[]{:S(2)}, u32[]{:S(2)}) collective-permute-start(f32[2,3,32,4,128]{4,3,2,1,0:T(4,128)} %bitcast.5), channel_id=1, source_target_pairs={{0,1},{1,0},{2,3},{3,2},{4,5},{5,4},{6,7},{7,6},{8,9},{9,8},{10,11... | collective-permute-start | bytes 1179656 | tf_op jit(solution)/shard_map/ppermute | solution.py:107
  6.4 6.5 %collective-permute-start.3 = (f32[3,16,2,128]{3,2,1,0:T(2,128)}, f32[3,16,2,128]{3,2,1,0:T(2,128)}, u32[]{:S(2)}, u32[]{:S(2)}) collective-permute-start(f32[3,16,2,128]{3,2,1,0:T(2,128)} %get-tuple-element.44), channel_id=1, source_target_pairs={{0,4},{4,8},{8,12},{1,5},{5,9},{9,13},{2,6},{6,10},{10,14},{3,7},{... | collective-permute-start | bytes 147464 | tf_op jit(solution)/shard_map/ppermute | solution.py:79
  11.5 6.3 %collective-permute-start.4 = (f32[3,16,2,128]{3,2,1,0:T(2,128)}, f32[3,16,2,128]{3,2,1,0:T(2,128)}, u32[]{:S(2)}, u32[]{:S(2)}) collective-permute-start(f32[3,16,2,128]{3,2,1,0:T(2,128)} %get-tuple-element.45), channel_id=1, source_target_pairs={{4,0},{8,4},{12,8},{5,1},{9,5},{13,9},{6,2},{10,6},{14,10},{7,3},{... | collective-permute-start | bytes 147464 | tf_op jit(solution)/shard_map/ppermute | solution.py:80
  12.8 11.7 %copy-start.3 = (f32[3,16,4,128]{3,2,1,0:T(4,128)S(1)}, f32[3,16,4,128]{3,2,1,0:T(4,128)}, u32[]{:S(2)}) copy-start(f32[3,16,4,128]{3,2,1,0:T(4,128)} %param.5) | copy-start | bytes 294916
  18.8 5.7 %collective-permute-start.5 = (f32[3,16,8,128]{3,2,1,0:T(8,128)S(1)}, f32[3,16,8,128]{3,2,1,0:T(8,128)S(1)}, u32[]{:S(2)}, u32[]{:S(2)}) collective-permute-start(f32[3,16,8,128]{3,2,1,0:T(8,128)S(1)} %pad_maximum_fusion.7), channel_id=1, source_target_pairs={{0,1},{1,0},{2,3},{3,2},{4,5},{5,4},{6,7},{7,6},{8,9},{9,8},{10,11... | collective-permute-start | bytes 589832 | tf_op jit(solution)/shard_map/ppermute | solution.py:109
  20.1 7.7 %collective-permute-start.1 = (f32[2,3,32,2,128]{4,3,2,1,0:T(2,128)S(1)}, f32[2,3,32,2,128]{4,3,2,1,0:T(2,128)S(1)}, u32[]{:S(2)}, u32[]{:S(2)}) collective-permute-start(f32[2,3,32,2,128]{4,3,2,1,0:T(2,128)S(1)} %get-tuple-element.42), channel_id=1, source_target_pairs={{0,4},{4,8},{8,12},{1,5},{5,9},{9,13},{2,6},{6,10},{10,14},{3,7},{... | collective-permute-start | bytes 589832 | tf_op jit(solution)/shard_map/ppermute | solution.py:79
  23.0 8.9 %collective-permute-start.2 = (f32[2,3,32,2,128]{4,3,2,1,0:T(2,128)S(1)}, f32[2,3,32,2,128]{4,3,2,1,0:T(2,128)S(1)}, u32[]{:S(2)}, u32[]{:S(2)}) collective-permute-start(f32[2,3,32,2,128]{4,3,2,1,0:T(2,128)S(1)} %get-tuple-element.43), channel_id=1, source_target_pairs={{4,0},{8,4},{12,8},{5,1},{9,5},{13,9},{6,2},{10,6},{14,10},{7,3},{... | collective-permute-start | bytes 589832 | tf_op jit(solution)/shard_map/ppermute | solution.py:80
  32.2 1.8 %copy-start.1 = (f32[2,3,32,8,128]{4,3,2,1,0:T(8,128)}, f32[2,3,32,8,128]{4,3,2,1,0:T(8,128)S(1)}, u32[]{:S(2)}) copy-start(f32[2,3,32,8,128]{4,3,2,1,0:T(8,128)S(1)} %pad_maximum_fusion.4) | copy-start | bytes 2359300
  38.7 10.3 %collective-permute-start.7 = (f32[288,8,2]{0,1,2:T(8,128)}, f32[288,8,2]{0,1,2:T(8,128)}, u32[]{:S(2)}, u32[]{:S(2)}) collective-permute-start(f32[288,8,2]{0,1,2:T(8,128)} %copy.37), channel_id=1, source_target_pairs={{2,0},{3,1},{6,4},{7,5},{10,8},{11,9},{14,12},{15,13},{18,16},{19,... | collective-permute-start | bytes 55304 | tf_op jit(solution)/shard_map/ppermute | solution.py:80
  40.0 6.9 %collective-permute-start.6 = (f32[288,8,2]{0,1,2:T(8,128)}, f32[288,8,2]{0,1,2:T(8,128)}, u32[]{:S(2)}, u32[]{:S(2)}) collective-permute-start(f32[288,8,2]{0,1,2:T(8,128)} %copy.36), channel_id=1, source_target_pairs={{0,2},{1,3},{4,6},{5,7},{8,10},{9,11},{12,14},{13,15},{16,18},{17,... | collective-permute-start | bytes 55304 | tf_op jit(solution)/shard_map/ppermute | solution.py:79

commit v4 on v3

--- a/solution.py
+++ b/solution.py
@@ -76,8 +76,20 @@
     size = cells.shape[dim]
     head = lax.slice_in_dim(cells, 0, width, axis=dim)
     tail = lax.slice_in_dim(cells, size - width, size, axis=dim)
-    from_low = lax.ppermute(tail, axis, [(i, i + 1) for i in range(count - 1)])
-    from_high = lax.ppermute(head, axis, [(i + 1, i) for i in range(count - 1)])
+    even = lax.axis_index(axis) % 2 == 0
+    from_low = jnp.zeros_like(tail)
+    from_high = jnp.zeros_like(head)
+    for first in (0, 1):
+        pairs = []
+        for i in range(first, count - 1, 2):
+            pairs += [(i, i + 1), (i + 1, i)]
+        if not pairs:
+            continue
+        lower_is_even = first == 0
+        send = jnp.where(even == lower_is_even, tail, head)
+        got = lax.ppermute(send, axis, pairs)
+        from_high = jnp.where(even == lower_is_even, got, from_high)
+        from_low = jnp.where(even == lower_is_even, from_low, got)
     return jnp.concatenate([from_low, cells, from_high], axis=dim)
 
 
@@ -102,24 +114,23 @@
     partial = lax.dot_general(
         weights, primaries, (((1,), (0,)), ((), ())), preferred_element_type=jnp.float32
     )
-    sigma_half = halo(conductivity, "xb", 2, SWEEPS)
     tx_ring = [(i, (i + 1) % n_tx) for i in range(n_tx)]
     got = lax.ppermute(partial[0], "tx", tx_ring)
+    sigma_other = lax.ppermute(conductivity, "tx", tx_ring)
     shot = partial[1] + got
-    sigma_other = lax.ppermute(sigma_half, "tx", tx_ring)
     low_first = tx_index == 0
     sigma_all = jnp.where(
         low_first,
-        jnp.concatenate([sigma_half, sigma_other], axis=1),
-        jnp.concatenate([sigma_other, sigma_half], axis=1),
+        jnp.concatenate([conductivity, sigma_other], axis=1),
+        jnp.concatenate([sigma_other, conductivity], axis=1),
     )
-    shot = halo(shot, "xb", 3, SWEEPS)
     ext_x = width_x + 2 * SWEEPS
     ext_y = width_y + 2 * SWEEPS
     shot_planes = shot.shape[0] * shot.shape[1] * depth
     planes = jnp.concatenate(
-        [shot.reshape(-1, ext_x, width_y), sigma_all.reshape(-1, ext_x, width_y)], axis=0
+        [shot.reshape(-1, width_x, width_y), sigma_all.reshape(-1, width_x, width_y)], axis=0
     )
+    planes = halo(planes, "xb", 1, SWEEPS)
     planes = halo(planes, "yb", 2, SWEEPS)
     shot_ext = planes[:shot_planes].reshape(shot.shape[:2] + (depth, ext_x, ext_y))
     sigma_ext = planes[shot_planes:].reshape(-1, depth, ext_x, ext_y)

time: 62.7 us -> 57.5 us (0.917)
  the two profiles are of different devices: /device:TPU:0 before, /device:TPU:16 now
where the time goes in v4:
time: 57.5 us; the launch traced here: 57 us
  other arithmetic  19.3 us (34%)
  local copies, waits for them, and re-layouts  15.4 us (27%)
  waiting for transfers between devices  14.4 us (25%)
  starting transfers between devices  5.76 us (10%)
  matrix products  1.93 us (3%)
    ppermute x3, waiting for transfers between devices, halo(): got = lax.ppermute(send, axis, pairs)  13 us
    ppermute x3, starting transfers between devices, halo(): got = lax.ppermute(send, axis, pairs)  5.18 us
    select_n x2, other arithmetic, halo(): send = jnp.where(even == lower_is_even, tail, head)  3.54 us
    mul x1, local copies, waits for them, and re-layouts, body(): kappa = K_FREQ * sigma_ext  2.37 us
    mul x1, local copies, waits for them, and re-layouts, source_term(): delta * shot[..., 1, :, :, :, :]  2.34 us
    mul x1, local copies, waits for them, and re-layouts, source_term(): -delta * shot[..., 0, :, :, :, :]  2.33 us
    reshape x1, local copies, waits for them, and re-layouts, body(): shot.reshape(-1, width_x, width_y)  2 us
    add x1, other arithmetic, body(): shot = partial[1] + got  1.97 us
  transfers between devices with their start and end apart: 5, of which 4 were waited for; matrix products, arithmetic and copies ran while one was open for 4% of the time, Pallas kernels for 0%

profile of v4, /device:TPU:16, one launch (start us, length us, event | category | flops | bytes accessed | tf_op | source)
XLA Modules:
  0.0 57.0 jit_solution(9592553750431192285)
XLA Ops:
  0.0 0.9 %reshape.140 = s32[2,16]{1,0:T(2,128)S(1)} reshape(s32[32]{0:T(128)} %param.6) | data formatting | bytes 256 | tf_op jit(solution)/shard_map/reshape | solution.py:110
  0.9 0.8 %reshape.141 = s32[2,16]{1,0:T(2,128)S(1)} reshape(s32[32]{0:T(128)} %param.7) | data formatting | bytes 256 | tf_op jit(solution)/shard_map/reshape | solution.py:111
  1.9 1.9 %fusion = f32[2,2,3,32,4,128]{5,0,4,3,2,1:T(2,128)S(1)} fusion(bf16[16,2,3,32,4,128]{5,4,3,2,1,0:T(4,128)(2,1)S(1)} %copy-done, s32[16]{0:T(128)S(1)} %get-tuple-element.6, s32[16]{0:T(128)S(1)} %get-tuple-element.5, s32[2]{0:T(128)S(1)} %pad_add_fusion), kind=kOutput, calls=%fused_computation | convolution fusion | flops 6291584 | bytes 3932296 | tf_op jit(solution)/shard_map/dot_general | solution.py:114
  3.8 1.6 %fusion.60 = (f32[1,2,3,32,4,128]{5,0,4,3,2,1:T(1,128)}, f32[1,2,3,32,4,128]{5,0,4,3,2,1:T(1,128)}) fusion(f32[2,2,3,32,4,128]{5,0,4,3,2,1:T(2,128)S(1)} %fusion), kind=kLoop, calls=%fused_computation.144 | loop fusion | bytes 1572864 | tf_op jit(solution)/shard_map/slice | solution.py:118
  6.0 1.5 %collective-permute-done.1 = f32[3,16,4,128]{3,1,0,2:T(8,128)S(1)} collective-permute-done((f32[3,16,4,128]{3,1,0,2:T(8,128)S(1)}, f32[3,16,4,128]{3,1,0,2:T(8,128)S(1)}, u32[]{:S(2)}, u32[]{:S(2)}) %collective-permute-start.1) | collective-permute-done | bytes 98336 | tf_op jit(solution)/shard_map/ppermute | solution.py:119
  8.2 1.1 %copy.75 = f32[96,4,128]{0,1,2:T(4,128)S(1)} copy(f32[96,4,128]{2,0,1:T(8,128)} %bitcast.152) | data formatting | bytes 393216 | tf_op jit(solution)/shard_map/jit(_where)/select_n | solution.py:122
  9.2 2.0 %add.122 = f32[2,3,32,4,128]{4,3,2,1,0:T(4,128)} add(f32[2,3,32,4,128]{4,3,2,1,0:T(4,128)} %bitcast.151, f32[2,3,32,4,128]{4,3,2,1,0:T(4,128)} %collective-permute-done) | non-fusion elementwise | flops 98304 | bytes 1179648 | tf_op jit(solution)/shard_map/add | solution.py:120
  11.2 2.0 %copy.74 = f32[192,4,128]{0,1,2:T(4,128)} copy(f32[192,4,128]{2,1,0:T(4,128)} %bitcast.150) | data formatting | bytes 786432 | tf_op jit(solution)/shard_map/reshape | solution.py:131
  13.2 3.5 %broadcast_select_fusion = (f32[288,2,128]{0,1,2:T(2,128)}, f32[288,2,128]{0,1,2:T(2,128)}) fusion(pred[]{:T(512)S(6)} %eq.39, f32[96,4,128]{0,1,2:T(4,128)S(1)} %copy.75, f32[192,4,128]{0,1,2:T(4,128)} %copy.74, pred[]{:T(512)S(6)} %eq.40), kind=kLoop, calls=%fused_computation.88 | loop fusion | flops 368640 | bytes 1179650 | tf_op jit(solution)/shard_map/jit(_where)/select_n | solution.py:89
  16.7 1.6 %collective-permute-start.2 = (f32[288,2,128]{0,1,2:T(2,128)}, f32[288,2,128]{0,1,2:T(2,128)}, u32[]{:S(2)}, u32[]{:S(2)}) collective-permute-start(f32[288,2,128]{0,1,2:T(2,128)} %get-tuple-element.28), channel_id=1, source_target_pairs={{0,4},{4,0},{8,12},{12,8},{1,5},{5,1},{9,13},{13,9},{2,6},{6,2},{1... | collective-permute-start | bytes 884744 | tf_op jit(solution)/shard_map/ppermute | solution.py:90
  18.2 2.1 %collective-permute-start.3 = (f32[288,2,128]{0,1,2:T(2,128)}, f32[288,2,128]{0,1,2:T(2,128)}, u32[]{:S(2)}, u32[]{:S(2)}) collective-permute-start(f32[288,2,128]{0,1,2:T(2,128)} %get-tuple-element.29), channel_id=1, source_target_pairs={{4,8},{8,4},{5,9},{9,5},{6,10},{10,6},{7,11},{11,7},{20,24},{24,20... | collective-permute-start | bytes 884744 | tf_op jit(solution)/shard_map/ppermute | solution.py:90
  20.6 7.5 %collective-permute-done.2 = f32[288,2,128]{0,1,2:T(2,128)} collective-permute-done((f32[288,2,128]{0,1,2:T(2,128)}, f32[288,2,128]{0,1,2:T(2,128)}, u32[]{:S(2)}, u32[]{:S(2)}) %collective-permute-start.2) | collective-permute-done | bytes 294944 | tf_op jit(solution)/shard_map/ppermute | solution.py:90
  28.1 3.2 %collective-permute-done.3 = f32[288,2,128]{0,1,2:T(2,128)} collective-permute-done((f32[288,2,128]{0,1,2:T(2,128)}, f32[288,2,128]{0,1,2:T(2,128)}, u32[]{:S(2)}, u32[]{:S(2)}) %collective-permute-start.3) | collective-permute-done | bytes 294944 | tf_op jit(solution)/shard_map/ppermute | solution.py:90
  31.3 1.5 %select_select_fusion.1 = (f32[288,2,128]{0,1,2:T(2,128)S(1)}, f32[288,2,128]{0,1,2:T(2,128)S(1)}) fusion(f32[288,2,128]{0,1,2:T(2,128)} %collective-permute-done.3, f32[288,2,128]{0,1,2:T(2,128)} %collective-permute-done.2, pred[]{:T(512)S(6)} %eq.39, pred[]{:T(512)S(6)} %eq.40), kind=kLoop, calls=%fused_computation.87 | loop fusion | flops 294912 | bytes 1179650 | tf_op jit(solution)/shard_map/jit(_where)/select_n | solution.py:92
  32.9 1.5 %collective-permute-start.4 = (f32[288,8,2]{0,1,2:T(8,128)S(1)}, f32[288,8,2]{0,1,2:T(8,128)S(1)}, u32[]{:S(2)}, u32[]{:S(2)}) collective-permute-start(f32[288,8,2]{0,1,2:T(8,128)S(1)} %fusion.48), channel_id=1, source_target_pairs={{0,2},{2,0},{1,3},{3,1},{4,6},{6,4},{5,7},{7,5},{8,10},{10,8},{9,1... | collective-permute-start | bytes 55304 | tf_op jit(solution)/shard_map/ppermute | solution.py:90
  34.5 2.3 %collective-permute-done.4 = f32[288,8,2]{0,1,2:T(8,128)S(1)} collective-permute-done((f32[288,8,2]{0,1,2:T(8,128)S(1)}, f32[288,8,2]{0,1,2:T(8,128)S(1)}, u32[]{:S(2)}, u32[]{:S(2)}) %collective-permute-start.4) | collective-permute-done | bytes 18464 | tf_op jit(solution)/shard_map/ppermute | solution.py:90
  37.4 1.5 %slice_multiply_fusion.1 = (f32[96,8,132]{0,1,2:T(8,128)}, f32[96,8,132]{0,1,2:T(8,128)}, f32[96,8,132]{0,1,2:T(8,128)}) fusion(f32[288,8,132]{0,1,2:T(8,128)S(1)} %pad_maximum_fusion.1), kind=kLoop, calls=%fused_computation.63 | loop fusion | flops 608256 | bytes 2433024 | tf_op jit(solution)/shard_map/mul | solution.py:63
  38.9 2.3 %copy.76 = f32[96,8,132]{2,1,0:T(8,128)} copy(f32[96,8,132]{0,1,2:T(8,128)} %get-tuple-element.15) | data formatting | bytes 811008 | tf_op jit(solution)/shard_map/mul | solution.py:63
  41.2 2.4 %copy.77 = f32[96,8,132]{2,1,0:T(8,128)} copy(f32[96,8,132]{0,1,2:T(8,128)} %get-tuple-element.17) | data formatting | bytes 811008 | tf_op jit(solution)/shard_map/mul | solution.py:142
  43.6 2.3 %copy.78 = f32[96,8,132]{2,1,0:T(8,128)} copy(f32[96,8,132]{0,1,2:T(8,128)} %get-tuple-element.16) | data formatting | bytes 811008 | tf_op jit(solution)/shard_map/mul | solution.py:63
  45.9 1.9 %subtract_divide_fusion = (f32[1,3,32,8,132]{4,3,2,1,0:T(8,128)S(1)}, f32[1,3,32,8,132]{4,3,2,1,0:T(8,128)S(1)}) fusion(f32[1,3,32,8,132]{4,3,2,1,0:T(8,128)} %bitcast.139, f32[1,3,32,8,132]{4,3,2,1,0:T(8,128)} %bitcast.144, f32[1,3,32,8,132]{4,3,2,1,0:T(8,128)} %bitcast.147), kind=kLoop, calls=%fused_computation.35 | loop fusion | flops 1013760 | bytes 2027520 | tf_op jit(solution)/shard_map/div | solution.py:58
  48.5 1.0 %fusion.29 = (f32[2,1,32,6,130]{4,3,2,0,1:T(8,128)S(1)}, f32[2,1,32,6,130]{4,3,2,0,1:T(8,128)S(1)}, f32[2,1,32,6,130]{4,3,2,0,1:T(8,128)S(1)}) fusion(f32[2,33,7,131]{3,2,1,0:T(8,128)S(1)} %get-tuple-element.37, f32[2,33,7,131]{3,2,1,0:T(8,128)S(1)} %get-tuple-element.35, f32[2,33,7,131]{3,2,1,0:T(8,128)S(1)} %get-tuple-element.36), kind=kLoop, calls=%fused_computation.75 | loop fusion | flops 449280 | bytes 2396160 | tf_op jit(solution)/shard_map/stack | solution.py:52
  49.7 0.9 %copy-done.1 = f32[96,8,132]{2,1,0:T(8,128)S(1)} copy-done((f32[96,8,132]{2,1,0:T(8,128)S(1)}, f32[96,8,132]{2,1,0:T(8,128)}, u32[]{:S(2)}) %copy-start.1) | copy-done | bytes 405528
  55.9 1.0 %fusion.32 = f32[1,2,3,32,4,128]{5,4,3,2,1,0:T(4,128)} fusion(f32[2,3,32,6,130]{4,3,2,1,0:T(8,128)S(1)} %fusion.4, f32[1,3,32,4,128]{4,3,2,1,0:T(4,128)S(1)} %get-tuple-element.25, f32[1,3,32,4,128]{4,3,2,1,0:T(4,128)S(1)} %get-tuple-element.24), kind=kLoop, calls=%fused_computation.82 | loop fusion | flops 294912 | bytes 1179648 | tf_op jit(solution)/shard_map/broadcast_in_dim | solution.py:158
  (43 shorter events, 8.6 us)
Async XLA Ops:
  0.0 1.9 %copy-start = (bf16[16,2,3,32,4,128]{5,4,3,2,1,0:T(4,128)(2,1)S(1)}, bf16[16,2,3,32,4,128]{5,4,3,2,1,0:T(4,128)(2,1)}, u32[]{:S(2)}) copy-start(bf16[16,2,3,32,4,128]{5,4,3,2,1,0:T(4,128)(2,1)} %param.4) | copy-start | bytes 9437188
  3.8 1.6 %copy-start.5 = (f32[3,16,4,128]{3,2,1,0:T(4,128)S(1)}, f32[3,16,4,128]{3,2,1,0:T(4,128)}, u32[]{:S(2)}) copy-start(f32[3,16,4,128]{3,2,1,0:T(4,128)} %param.5) | copy-start | bytes 294916
  5.4 3.8 %collective-permute-start = (f32[2,3,32,4,128]{4,3,2,1,0:T(4,128)}, f32[2,3,32,4,128]{4,3,2,1,0:T(4,128)}, u32[]{:S(2)}, u32[]{:S(2)}) collective-permute-start(f32[2,3,32,4,128]{4,3,2,1,0:T(4,128)} %bitcast.5), channel_id=1, source_target_pairs={{0,1},{1,0},{2,3},{3,2},{4,5},{5,4},{6,7},{7,6},{8,9},{9,8},{10,11... | collective-permute-start | bytes 1179656 | tf_op jit(solution)/shard_map/ppermute | solution.py:118
  5.4 2.1 %collective-permute-start.1 = (f32[3,16,4,128]{3,1,0,2:T(8,128)S(1)}, f32[3,16,4,128]{3,1,0,2:T(8,128)S(1)}, u32[]{:S(2)}, u32[]{:S(2)}) collective-permute-start(f32[3,16,4,128]{3,1,0,2:T(8,128)S(1)} %copy.72), channel_id=1, source_target_pairs={{0,1},{1,0},{2,3},{3,2},{4,5},{5,4},{6,7},{7,6},{8,9},{9,8},{10,11... | collective-permute-start | bytes 294920 | tf_op jit(solution)/shard_map/ppermute | solution.py:119
  16.7 11.5 %collective-permute-start.2 = (f32[288,2,128]{0,1,2:T(2,128)}, f32[288,2,128]{0,1,2:T(2,128)}, u32[]{:S(2)}, u32[]{:S(2)}) collective-permute-start(f32[288,2,128]{0,1,2:T(2,128)} %get-tuple-element.28), channel_id=1, source_target_pairs={{0,4},{4,0},{8,12},{12,8},{1,5},{5,1},{9,13},{13,9},{2,6},{6,2},{1... | collective-permute-start | bytes 884744 | tf_op jit(solution)/shard_map/ppermute | solution.py:90
  18.2 13.1 %collective-permute-start.3 = (f32[288,2,128]{0,1,2:T(2,128)}, f32[288,2,128]{0,1,2:T(2,128)}, u32[]{:S(2)}, u32[]{:S(2)}) collective-permute-start(f32[288,2,128]{0,1,2:T(2,128)} %get-tuple-element.29), channel_id=1, source_target_pairs={{4,8},{8,4},{5,9},{9,5},{6,10},{10,6},{7,11},{11,7},{20,24},{24,20... | collective-permute-start | bytes 884744 | tf_op jit(solution)/shard_map/ppermute | solution.py:90
  20.4 12.4 %copy-start.4 = (f32[192,4,128]{0,1,2:T(4,128)S(1)}, f32[192,4,128]{0,1,2:T(4,128)}, u32[]{:S(2)}) copy-start(f32[192,4,128]{0,1,2:T(4,128)} %copy.74) | copy-start | bytes 1179652
  32.9 3.9 %collective-permute-start.4 = (f32[288,8,2]{0,1,2:T(8,128)S(1)}, f32[288,8,2]{0,1,2:T(8,128)S(1)}, u32[]{:S(2)}, u32[]{:S(2)}) collective-permute-start(f32[288,8,2]{0,1,2:T(8,128)S(1)} %fusion.48), channel_id=1, source_target_pairs={{0,2},{2,0},{1,3},{3,1},{4,6},{6,4},{5,7},{7,5},{8,10},{10,8},{9,1... | collective-permute-start | bytes 55304 | tf_op jit(solution)/shard_map/ppermute | solution.py:90
  49.5 1.1 %copy-start.1 = (f32[96,8,132]{2,1,0:T(8,128)S(1)}, f32[96,8,132]{2,1,0:T(8,128)}, u32[]{:S(2)}) copy-start(f32[96,8,132]{2,1,0:T(8,128)} %copy.77) | copy-start | bytes 1216516
  50.7 1.1 %copy-start.2 = (f32[96,8,132]{2,1,0:T(8,128)S(1)}, f32[96,8,132]{2,1,0:T(8,128)}, u32[]{:S(2)}) copy-start(f32[96,8,132]{2,1,0:T(8,128)} %copy.76) | copy-start | bytes 1216516
  50.7 1.4 %copy-start.3 = (f32[96,8,132]{2,1,0:T(8,128)S(1)}, f32[96,8,132]{2,1,0:T(8,128)}, u32[]{:S(2)}) copy-start(f32[96,8,132]{2,1,0:T(8,128)} %copy.78) | copy-start | bytes 1216516

commit v5 on v4

--- a/solution.py
+++ b/solution.py
@@ -1,6 +1,7 @@
 import jax
 import jax.numpy as jnp
 from jax import lax
+from jax.experimental.layout import Layout, with_layout_constraint
 from jax.sharding import PartitionSpec as P
 
 NS_DEV = 1
@@ -93,6 +94,10 @@
     return jnp.concatenate([from_low, cells, from_high], axis=dim)
 
 
+def row_major(x):
+    return with_layout_constraint(x, Layout(major_to_minor=tuple(range(x.ndim))))
+
+
 def encode_weights(group_part, sign_part, rows):
     picked = group_part[None, :] == rows[:, None]
     return jnp.where(picked, sign_part[None, :], 0).astype(jnp.float32).astype(jnp.bfloat16)
@@ -130,8 +135,8 @@
     planes = jnp.concatenate(
         [shot.reshape(-1, width_x, width_y), sigma_all.reshape(-1, width_x, width_y)], axis=0
     )
-    planes = halo(planes, "xb", 1, SWEEPS)
-    planes = halo(planes, "yb", 2, SWEEPS)
+    planes = row_major(halo(row_major(planes), "xb", 1, SWEEPS))
+    planes = row_major(halo(planes, "yb", 2, SWEEPS))
     shot_ext = planes[:shot_planes].reshape(shot.shape[:2] + (depth, ext_x, ext_y))
     sigma_ext = planes[shot_planes:].reshape(-1, depth, ext_x, ext_y)
 

time: 57.5 us -> 52.1 us (0.906)
  local copies, waits for them, and re-layouts: 15.4 us -> 11 us
  waiting for transfers between devices: 14.4 us -> 12.6 us
  other arithmetic: 19.3 us -> 20.3 us
    mul x3 -> x0, local copies, waits for them, and re-layouts: 7.04 us -> none  [the longest x1 2.37 us: body(): kappa = K_FREQ * sigma_ext]
    select_n x1 -> x3, local copies, waits for them, and re-layouts: 1.07 us -> 6.7 us  [the longest x1 2.35 us: halo(): send = jnp.where(even == lower_is_even, tail, head)]
    concatenate x1 -> x2, other arithmetic: 0.64 us -> 5.36 us  [halo(): return jnp.concatenate([from_low, cells, from_high], axis=dim)]
    reshape x1 -> x0, local copies, waits for them, and re-layouts: 2 us -> none  [body(): shot.reshape(-1, width_x, width_y)]
    ppermute x3, waiting for transfers between devices: 13 us -> 11.1 us  [halo(): got = lax.ppermute(send, axis, pairs)]
    div x1, other arithmetic: 1.89 us -> 0.29 us  [jacobi(): (4.0 * resid[..., 1, :, :, :, :] - kappa * resid[..., 0, :, :, :, :]) / d...]
    mul x1, other arithmetic: 1.5 us -> 0.2 us  [source_term(): delta * shot[..., 1, :, :, :, :]]
    select_n x2, other arithmetic: 3.54 us -> 2.47 us  [halo(): send = jnp.where(even == lower_is_even, tail, head)]
  transfers between devices with their start and end apart: 5 -> 5, of which waited for: 4 -> 4; matrix products, arithmetic and copies ran while one was open for 4% -> 3% of each run, Pallas kernels for 0% -> 0%
where the time goes in v5:
time: 52.1 us; the launch traced here: 51.7 us
  other arithmetic  20.3 us (39%)
  waiting for transfers between devices  12.6 us (24%)
  local copies, waits for them, and re-layouts  11 us (21%)
  starting transfers between devices  5.67 us (11%)
  matrix products  1.93 us (4%)
    ppermute x3, waiting for transfers between devices, halo(): got = lax.ppermute(send, axis, pairs)  11.1 us
    concatenate x2, other arithmetic, halo(): return jnp.concatenate([from_low, cells, from_high], axis=dim)  5.36 us
    ppermute x3, starting transfers between devices, halo(): got = lax.ppermute(send, axis, pairs)  5.16 us
    select_n x2, other arithmetic, halo(): send = jnp.where(even == lower_is_even, tail, head)  2.47 us
    select_n x1, local copies, waits for them, and re-layouts, halo(): send = jnp.where(even == lower_is_even, tail, head)  2.35 us
    select_n x1, local copies, waits for them, and re-layouts, halo(): from_low = jnp.where(even == lower_is_even, from_low, got)  2.19 us
    select_n x1, local copies, waits for them, and re-layouts, halo(): from_high = jnp.where(even == lower_is_even, got, from_high)  2.16 us
    dot_general x1, matrix products, body(): lax.dot_general(weights, primaries, (((1,), (0,)), ((), ())), preferred_e...  1.93 us
  transfers between devices with their start and end apart: 5, of which 4 were waited for; matrix products, arithmetic and copies ran while one was open for 3% of the time, Pallas kernels for 0%

profile of v5, /device:TPU:16, one launch (start us, length us, event | category | flops | bytes accessed | tf_op | source)
XLA Modules:
  0.0 51.7 jit_solution(9007029469391366559)
XLA Ops:
  0.0 0.9 %reshape.140 = s32[2,16]{1,0:T(2,128)S(1)} reshape(s32[32]{0:T(128)} %param.6) | data formatting | bytes 256 | tf_op jit(solution)/shard_map/reshape | solution.py:115
  0.9 0.8 %reshape.141 = s32[2,16]{1,0:T(2,128)S(1)} reshape(s32[32]{0:T(128)} %param.7) | data formatting | bytes 256 | tf_op jit(solution)/shard_map/reshape | solution.py:116
  1.9 1.9 %fusion = f32[2,2,3,32,4,128]{5,0,4,3,2,1:T(2,128)S(1)} fusion(bf16[16,2,3,32,4,128]{5,4,3,2,1,0:T(4,128)(2,1)S(1)} %copy-done, s32[16]{0:T(128)S(1)} %get-tuple-element.6, s32[16]{0:T(128)S(1)} %get-tuple-element.5, s32[2]{0:T(128)S(1)} %pad_add_fusion), kind=kOutput, calls=%fused_computation | convolution fusion | flops 6291584 | bytes 3932296 | tf_op jit(solution)/shard_map/dot_general | solution.py:119
  3.8 1.4 %fusion.59 = (f32[1,2,3,32,4,128]{5,0,4,3,2,1:T(1,128)S(1)}, f32[1,2,3,32,4,128]{5,0,4,3,2,1:T(1,128)}) fusion(f32[2,2,3,32,4,128]{5,0,4,3,2,1:T(2,128)S(1)} %fusion), kind=kLoop, calls=%fused_computation.142 | loop fusion | bytes 1572864 | tf_op jit(solution)/shard_map/slice | solution.py:123
  5.8 1.5 %collective-permute-done.1 = f32[3,16,4,128]{3,2,1,0:T(4,128)} collective-permute-done((f32[3,16,4,128]{3,2,1,0:T(4,128)}, f32[3,16,4,128]{3,2,1,0:T(4,128)}, u32[]{:S(2)}, u32[]{:S(2)}) %collective-permute-start.1) | collective-permute-done | bytes 98336 | tf_op jit(solution)/shard_map/ppermute | solution.py:124
  7.3 1.1 %maximum_select_fusion = f32[3,32,4,128]{3,2,1,0:T(4,128)S(1)} fusion(f32[3,16,4,128]{3,2,1,0:T(4,128)} %collective-permute-done.1, f32[3,16,4,128]{3,2,1,0:T(4,128)} %param.5, pred[]{:T(512)S(6)} %eq.46), kind=kLoop, calls=%fused_computation.104 | loop fusion | flops 147456 | bytes 393217 | tf_op jit(solution)/shard_map/jit(_where)/select_n | solution.py:127
  8.4 1.3 %add.122 = f32[2,3,32,4,128]{4,3,2,1,0:T(4,128)S(1)} add(f32[2,3,32,4,128]{4,3,2,1,0:T(4,128)} %bitcast.158, f32[2,3,32,4,128]{4,3,2,1,0:T(4,128)} %collective-permute-done) | non-fusion elementwise | flops 98304 | bytes 1179648 | tf_op jit(solution)/shard_map/add | solution.py:125
  9.7 1.1 %broadcast_select_fusion = (f32[288,2,128]{2,1,0:T(2,128)}, f32[288,2,128]{2,1,0:T(2,128)}) fusion(pred[]{:T(512)S(6)} %eq.39, f32[96,4,128]{2,1,0:T(4,128)S(1)} %bitcast.155, f32[192,4,128]{2,1,0:T(4,128)S(1)} %bitcast.152, pred[]{:T(512)S(6)} %eq.40), kind=kLoop, calls=%fused_computation.90 | loop fusion | flops 368640 | bytes 1179650 | tf_op jit(solution)/shard_map/jit(_where)/select_n | solution.py:90
  10.8 1.6 %collective-permute-start.2 = (f32[288,2,128]{2,1,0:T(2,128)}, f32[288,2,128]{2,1,0:T(2,128)}, u32[]{:S(2)}, u32[]{:S(2)}) collective-permute-start(f32[288,2,128]{2,1,0:T(2,128)} %get-tuple-element.30), channel_id=1, source_target_pairs={{0,4},{4,0},{8,12},{12,8},{1,5},{5,1},{9,13},{13,9},{2,6},{6,2},{1... | collective-permute-start | bytes 884744 | tf_op jit(solution)/shard_map/ppermute | solution.py:91
  12.3 2.1 %collective-permute-start.3 = (f32[288,2,128]{2,1,0:T(2,128)}, f32[288,2,128]{2,1,0:T(2,128)}, u32[]{:S(2)}, u32[]{:S(2)}) collective-permute-start(f32[288,2,128]{2,1,0:T(2,128)} %get-tuple-element.31), channel_id=1, source_target_pairs={{4,8},{8,4},{5,9},{9,5},{6,10},{10,6},{7,11},{11,7},{20,24},{24,20... | collective-permute-start | bytes 884744 | tf_op jit(solution)/shard_map/ppermute | solution.py:91
  14.7 5.4 %collective-permute-done.2 = f32[288,2,128]{2,1,0:T(2,128)} collective-permute-done((f32[288,2,128]{2,1,0:T(2,128)}, f32[288,2,128]{2,1,0:T(2,128)}, u32[]{:S(2)}, u32[]{:S(2)}) %collective-permute-start.2) | collective-permute-done | bytes 294944 | tf_op jit(solution)/shard_map/ppermute | solution.py:91
  20.1 3.2 %collective-permute-done.3 = f32[288,2,128]{2,1,0:T(2,128)} collective-permute-done((f32[288,2,128]{2,1,0:T(2,128)}, f32[288,2,128]{2,1,0:T(2,128)}, u32[]{:S(2)}, u32[]{:S(2)}) %collective-permute-start.3) | collective-permute-done | bytes 294944 | tf_op jit(solution)/shard_map/ppermute | solution.py:91
  23.3 1.3 %select_select_fusion.1 = (f32[288,2,128]{2,1,0:T(2,128)S(1)}, f32[288,2,128]{2,1,0:T(2,128)S(1)}) fusion(f32[288,2,128]{2,1,0:T(2,128)} %collective-permute-done.3, f32[288,2,128]{2,1,0:T(2,128)} %collective-permute-done.2, pred[]{:T(512)S(6)} %eq.39, pred[]{:T(512)S(6)} %eq.40), kind=kLoop, calls=%fused_computation.89 | loop fusion | flops 294912 | bytes 1179650 | tf_op jit(solution)/shard_map/jit(_where)/select_n | solution.py:93
  25.4 1.3 %pad_maximum_fusion.3 = f32[288,8,128]{2,1,0:T(8,128)S(1)} fusion(f32[288,2,128]{2,1,0:T(2,128)S(1)} %get-tuple-element.29, f32[96,4,128]{2,1,0:T(4,128)} %bitcast.156, f32[192,4,128]{2,1,0:T(4,128)S(1)} %bitcast.153, f32[288,2,128]{2,1,0:T(2,128)S(1)} %get-tuple-element.28), kind=kLoop, calls=%fused_computation.19 | loop fusion | flops 884736 | bytes 2359296 | tf_op jit(solution)/shard_map/concatenate | solution.py:94
  26.7 1.4 %slice_select_fusion = f32[288,8,2]{2,1,0:T(8,128)} fusion(f32[288,8,128]{2,1,0:T(8,128)S(1)} %pad_maximum_fusion.3, pred[]{:T(512)S(6)} %eq.38), kind=kLoop, calls=%fused_computation.18 | loop fusion | flops 4608 | bytes 55297 | tf_op jit(solution)/shard_map/jit(_where)/select_n | solution.py:90
  28.2 2.3 %copy.30 = f32[288,8,2]{0,1,2:T(8,128)} copy(f32[288,8,2]{2,1,0:T(8,128)} %slice_select_fusion) | data formatting | bytes 36864 | tf_op jit(solution)/shard_map/jit(_where)/select_n | solution.py:90
  30.5 1.5 %collective-permute-start.4 = (f32[288,8,2]{0,1,2:T(8,128)}, f32[288,8,2]{0,1,2:T(8,128)S(1)}, u32[]{:S(2)}, u32[]{:S(2)}) collective-permute-start(f32[288,8,2]{0,1,2:T(8,128)} %copy.30), channel_id=1, source_target_pairs={{0,2},{2,0},{1,3},{3,1},{4,6},{6,4},{5,7},{7,5},{8,10},{10,8},{9,1... | collective-permute-start | bytes 55304 | tf_op jit(solution)/shard_map/ppermute | solution.py:91
  32.1 2.5 %collective-permute-done.4 = f32[288,8,2]{0,1,2:T(8,128)S(1)} collective-permute-done((f32[288,8,2]{0,1,2:T(8,128)}, f32[288,8,2]{0,1,2:T(8,128)S(1)}, u32[]{:S(2)}, u32[]{:S(2)}) %collective-permute-start.4) | collective-permute-done | bytes 18464 | tf_op jit(solution)/shard_map/ppermute | solution.py:91
  35.2 2.2 %copy.33 = f32[288,8,2]{2,1,0:T(8,128)} copy(f32[288,8,2]{0,1,2:T(8,128)} %get-tuple-element.44) | data formatting | bytes 36864 | tf_op jit(solution)/shard_map/jit(_where)/select_n | solution.py:93
  37.4 2.2 %copy.34 = f32[288,8,2]{2,1,0:T(8,128)} copy(f32[288,8,2]{0,1,2:T(8,128)} %get-tuple-element.45) | data formatting | bytes 36864 | tf_op jit(solution)/shard_map/jit(_where)/select_n | solution.py:92
  39.5 4.1 %pad_maximum_fusion = f32[288,8,132]{2,1,0:T(8,128)S(1)} fusion(f32[288,8,2]{2,1,0:T(8,128)} %copy.34, f32[288,2,128]{2,1,0:T(2,128)} %copy-done.3, f32[96,4,128]{2,1,0:T(4,128)} %bitcast.157, f32[192,4,128]{2,1,0:T(4,128)S(1)} %bitcast.154, f32[288,2,128]{2,1,0:T(2,128)} %copy-done.2, f32[288,8,2]{2,1,0:T(8,128)} %copy.33), kind=kLoop, calls=%fused_computation.2 | loop fusion | flops 1520640 | bytes 2433024 | tf_op jit(solution)/shard_map/concatenate | solution.py:94
  44.8 1.0 %fusion.29 = (f32[2,1,32,6,130]{4,3,2,0,1:T(8,128)S(1)}, f32[2,1,32,6,130]{4,3,2,0,1:T(8,128)S(1)}, f32[2,1,32,6,130]{4,3,2,0,1:T(8,128)S(1)}) fusion(f32[2,33,7,131]{3,2,1,0:T(8,128)S(1)} %get-tuple-element.37, f32[2,33,7,131]{3,2,1,0:T(8,128)S(1)} %get-tuple-element.35, f32[2,33,7,131]{3,2,1,0:T(8,128)S(1)} %get-tuple-element.36), kind=kLoop, calls=%fused_computation.78 | loop fusion | flops 449280 | bytes 2396160 | tf_op jit(solution)/shard_map/stack | solution.py:53
  46.0 0.7 %fusion.10 = (f32[1,3,32,6,130]{4,3,2,1,0:T(8,128)S(1)}, f32[1,3,32,6,130]{4,3,2,1,0:T(8,128)S(1)}) fusion(f32[1,3,32,8,132]{4,3,2,1,0:T(8,128)S(1)} %get-tuple-element.13, f32[2,3,32,6,130]{4,3,2,0,1:T(8,128)S(1)} %pad_maximum_fusion.2, f32[3,32,8,132]{3,2,1,0:T(8,128)S(1)} %bitcast.142, f32[1,3,32,8,132]{4,3,2,1,0:T(8,128)S(1)} %get-tuple-element.14), kind=kLoop, calls=%fused_computation.30 | loop fusion | flops 299520 | bytes 2096640 | tf_op jit(solution)/shard_map/stack | solution.py:159
  50.6 1.0 %fusion.31 = f32[1,2,3,32,4,128]{5,4,3,2,1,0:T(4,128)} fusion(f32[2,3,32,6,130]{4,3,2,1,0:T(8,128)S(1)} %fusion.4, f32[1,3,32,4,128]{4,3,2,1,0:T(4,128)S(1)} %get-tuple-element.25, f32[1,3,32,4,128]{4,3,2,1,0:T(4,128)S(1)} %get-tuple-element.24), kind=kLoop, calls=%fused_computation.83 | loop fusion | flops 294912 | bytes 1179648 | tf_op jit(solution)/shard_map/broadcast_in_dim | solution.py:163
  (37 shorter events, 7.7 us)
Async XLA Ops:
  0.0 1.9 %copy-start = (bf16[16,2,3,32,4,128]{5,4,3,2,1,0:T(4,128)(2,1)S(1)}, bf16[16,2,3,32,4,128]{5,4,3,2,1,0:T(4,128)(2,1)}, u32[]{:S(2)}) copy-start(bf16[16,2,3,32,4,128]{5,4,3,2,1,0:T(4,128)(2,1)} %param.4) | copy-start | bytes 9437188
  5.3 3.1 %collective-permute-start = (f32[2,3,32,4,128]{4,3,2,1,0:T(4,128)S(1)}, f32[2,3,32,4,128]{4,3,2,1,0:T(4,128)}, u32[]{:S(2)}, u32[]{:S(2)}) collective-permute-start(f32[2,3,32,4,128]{4,3,2,1,0:T(4,128)S(1)} %bitcast.159), channel_id=1, source_target_pairs={{0,1},{1,0},{2,3},{3,2},{4,5},{5,4},{6,7},{7,6},{8,9},{9,8},{10,11... | collective-permute-start | bytes 1179656 | tf_op jit(solution)/shard_map/ppermute | solution.py:123
  5.3 2.0 %collective-permute-start.1 = (f32[3,16,4,128]{3,2,1,0:T(4,128)}, f32[3,16,4,128]{3,2,1,0:T(4,128)}, u32[]{:S(2)}, u32[]{:S(2)}) collective-permute-start(f32[3,16,4,128]{3,2,1,0:T(4,128)} %param.5), channel_id=1, source_target_pairs={{0,1},{1,0},{2,3},{3,2},{4,5},{5,4},{6,7},{7,6},{8,9},{9,8},{10,11... | collective-permute-start | bytes 294920 | tf_op jit(solution)/shard_map/ppermute | solution.py:124
  8.4 1.3 %copy-start.1 = (f32[3,32,4,128]{3,2,1,0:T(4,128)}, f32[3,32,4,128]{3,2,1,0:T(4,128)S(1)}, u32[]{:S(2)}) copy-start(f32[3,32,4,128]{3,2,1,0:T(4,128)S(1)} %maximum_select_fusion) | copy-start | bytes 589828
  10.8 9.4 %collective-permute-start.2 = (f32[288,2,128]{2,1,0:T(2,128)}, f32[288,2,128]{2,1,0:T(2,128)}, u32[]{:S(2)}, u32[]{:S(2)}) collective-permute-start(f32[288,2,128]{2,1,0:T(2,128)} %get-tuple-element.30), channel_id=1, source_target_pairs={{0,4},{4,0},{8,12},{12,8},{1,5},{5,1},{9,13},{13,9},{2,6},{6,2},{1... | collective-permute-start | bytes 884744 | tf_op jit(solution)/shard_map/ppermute | solution.py:91
  12.3 11.0 %collective-permute-start.3 = (f32[288,2,128]{2,1,0:T(2,128)}, f32[288,2,128]{2,1,0:T(2,128)}, u32[]{:S(2)}, u32[]{:S(2)}) collective-permute-start(f32[288,2,128]{2,1,0:T(2,128)} %get-tuple-element.31), channel_id=1, source_target_pairs={{4,8},{8,4},{5,9},{9,5},{6,10},{10,6},{7,11},{11,7},{20,24},{24,20... | collective-permute-start | bytes 884744 | tf_op jit(solution)/shard_map/ppermute | solution.py:91
  24.6 0.7 %copy-start.2 = (f32[288,2,128]{2,1,0:T(2,128)}, f32[288,2,128]{2,1,0:T(2,128)S(1)}, u32[]{:S(2)}) copy-start(f32[288,2,128]{2,1,0:T(2,128)S(1)} %get-tuple-element.28) | copy-start | bytes 884740
  24.6 0.8 %copy-start.3 = (f32[288,2,128]{2,1,0:T(2,128)}, f32[288,2,128]{2,1,0:T(2,128)S(1)}, u32[]{:S(2)}) copy-start(f32[288,2,128]{2,1,0:T(2,128)S(1)} %get-tuple-element.29) | copy-start | bytes 884740
  30.5 4.0 %collective-permute-start.4 = (f32[288,8,2]{0,1,2:T(8,128)}, f32[288,8,2]{0,1,2:T(8,128)S(1)}, u32[]{:S(2)}, u32[]{:S(2)}) collective-permute-start(f32[288,8,2]{0,1,2:T(8,128)} %copy.30), channel_id=1, source_target_pairs={{0,2},{2,0},{1,3},{3,1},{4,6},{6,4},{5,7},{7,5},{8,10},{10,8},{9,1... | collective-permute-start | bytes 55304 | tf_op jit(solution)/shard_map/ppermute | solution.py:91

commit v6 on v5

--- a/solution.py
+++ b/solution.py
@@ -72,26 +72,24 @@
     return jnp.pad(f, [(0, 0)] * (f.ndim - 3) + [(1, 1), (0, 0), (0, 0)])
 
 
-def halo(cells, axis, dim, width):
+def swap_rounds(axis):
     count = lax.axis_size(axis)
-    size = cells.shape[dim]
-    head = lax.slice_in_dim(cells, 0, width, axis=dim)
-    tail = lax.slice_in_dim(cells, size - width, size, axis=dim)
     even = lax.axis_index(axis) % 2 == 0
-    from_low = jnp.zeros_like(tail)
-    from_high = jnp.zeros_like(head)
     for first in (0, 1):
         pairs = []
         for i in range(first, count - 1, 2):
             pairs += [(i, i + 1), (i + 1, i)]
-        if not pairs:
-            continue
-        lower_is_even = first == 0
-        send = jnp.where(even == lower_is_even, tail, head)
-        got = lax.ppermute(send, axis, pairs)
-        from_high = jnp.where(even == lower_is_even, got, from_high)
-        from_low = jnp.where(even == lower_is_even, from_low, got)
-    return jnp.concatenate([from_low, cells, from_high], axis=dim)
+        if pairs:
+            yield pairs, even == (first == 0)
+
+
+def halo_into(ext, head, tail, axis, corner, dim, low_at, high_at):
+    for pairs, lower in swap_rounds(axis):
+        got = lax.ppermute(row_major(jnp.where(lower, tail, head)), axis, pairs)
+        start = list(corner)
+        start[dim] = jnp.where(lower, high_at, low_at)
+        ext = lax.dynamic_update_slice(ext, got, start)
+    return ext
 
 
 def row_major(x):
@@ -111,9 +109,11 @@
     n_tx = lax.axis_size("tx")
     tx_index = lax.axis_index("tx")
     other = (tx_index + 1) % n_tx
-    mine = lax.broadcasted_iota(jnp.int32, (n_tx, nt_local), 0) == tx_index
-    own_groups = jnp.sum(jnp.where(mine, group_of.reshape(n_tx, nt_local), 0), axis=0)
-    own_signs = jnp.sum(jnp.where(mine, sign_of.reshape(n_tx, nt_local), 0), axis=0)
+    own_groups = jnp.zeros((nt_local,), jnp.int32)
+    own_signs = jnp.zeros((nt_local,), jnp.int32)
+    for k in range(n_tx):
+        own_groups = jnp.where(tx_index == k, group_of[k * nt_local:(k + 1) * nt_local], own_groups)
+        own_signs = jnp.where(tx_index == k, sign_of[k * nt_local:(k + 1) * nt_local], own_signs)
     rows = jnp.stack([other, tx_index]).astype(jnp.int32)
     weights = encode_weights(own_groups, own_signs, rows)
     partial = lax.dot_general(
@@ -135,8 +135,15 @@
     planes = jnp.concatenate(
         [shot.reshape(-1, width_x, width_y), sigma_all.reshape(-1, width_x, width_y)], axis=0
     )
-    planes = row_major(halo(row_major(planes), "xb", 1, SWEEPS))
-    planes = row_major(halo(planes, "yb", 2, SWEEPS))
+    w = SWEEPS
+    ext = row_major(jnp.pad(planes, [(0, 0), (w, w), (w, w)]))
+    ext = halo_into(
+        ext, planes[:, :w], planes[:, width_x - w:], "xb", (0, 0, w), 1, 0, w + width_x
+    )
+    ext = halo_into(
+        ext, ext[:, :, w:2 * w], ext[:, :, width_y:width_y + w], "yb", (0, 0, 0), 2, 0, w + width_y
+    )
+    planes = row_major(ext)
     shot_ext = planes[:shot_planes].reshape(shot.shape[:2] + (depth, ext_x, ext_y))
     sigma_ext = planes[shot_planes:].reshape(-1, depth, ext_x, ext_y)
 

time: 52.1 us -> 291 us (5.59)
  local copies, waits for them, and re-layouts: 11 us -> 254 us
  waiting for transfers between devices: 12.6 us -> 8.89 us
    dynamic_update_slice x0 -> x3, local copies, waits for them, and re-layouts: none -> 246 us  [halo_into(): ext = lax.dynamic_update_slice(ext, got, start)]
    select_n x3 -> x0, local copies, waits for them, and re-layouts: 6.7 us -> none  [the longest x1 2.35 us: halo(): send = jnp.where(even == lower_is_even, tail, head)]
    concatenate x2 -> x1, other arithmetic: 5.36 us -> 1.05 us  [body(): jnp.concatenate([shot.reshape(-1, width_x, width_y), sigma_all.reshape(-1...]
    ppermute x3, waiting for transfers between devices: 11.1 us -> 7.41 us  [halo_into(): got = lax.ppermute(row_major(jnp.where(lower, tail, head)), axis, pairs)]
  transfers between devices with their start and end apart: 5 -> 5, of which waited for: 4 -> 3; matrix products, arithmetic and copies ran while one was open for 3% -> 36% of each run, Pallas kernels for 0% -> 0%
where the time goes in v6:
time: 291 us; the launch traced here: 288 us
  local copies, waits for them, and re-layouts  254 us (87%)
  other arithmetic  18.1 us (6%)
  waiting for transfers between devices  8.89 us (3%)
  starting transfers between devices  5 us (2%)
    dynamic_update_slice x3, local copies, waits for them, and re-layouts, halo_into(): ext = lax.dynamic_update_slice(ext, got, start)  246 us
    ppermute x3, waiting for transfers between devices, halo_into(): got = lax.ppermute(row_major(jnp.where(lower, tail, head)), axis, pairs)  7.41 us
  transfers between devices with their start and end apart: 5, of which 3 were waited for; matrix products, arithmetic and copies ran while one was open for 36% of the time, Pallas kernels for 0%

profile of v6, /device:TPU:16, one launch (start us, length us, event | category | flops | bytes accessed | tf_op | source)
XLA Modules:
  0.0 288.0 jit_solution(9565067891382186887)
XLA Ops:
  0.1 0.9 broadcast_select_fusion.4
  1.0 0.9 copy-done
  2.0 1.9 fusion
  3.9 1.4 fusion.60
  5.8 1.5 collective-permute-done.1
  7.3 1.1 maximum_select_fusion
  8.4 1.3 add.125
  9.7 1.1 broadcast_select_fusion
  10.8 2.3 collective-permute-start.3
  14.0 1.1 pad_maximum_fusion.2
  15.1 2.1 pad.12
  17.2 5.1 %collective-permute-done.2 = f32[288,2,128]{2,1,0:T(2,128)} collective-permute-done((f32[288,2,128]{2,1,0:T(2,128)}, f32[288,2,128]{2,1,0:T(2,128)}, u32[]{:S(2)}, u32[]{:S(2)}) %collective-permute-start.2) | collective-permute-done | bytes 294944 | tf_op jit(solution)/shard_map/ppermute | solution.py:88
  22.3 99.1 %dynamic_update_slice.9 = f32[288,8,132]{2,1,0:T(8,128)} dynamic-update-slice(f32[288,8,132]{2,1,0:T(8,128)} %pad.12, f32[288,2,128]{2,1,0:T(2,128)} %collective-permute-done.2, s32[]{:T(128)} %constant.61.clone.1, s32[]{:T(128)S(6)} %select_n.106, s32[]{:T(128)} %constant.67.clone.1) | dynamic-update-slice | bytes 589828 | tf_op jit(solution)/shard_map/dynamic_update_slice | solution.py:91
  121.4 99.1 %dynamic_update_slice.10 = f32[288,8,132]{2,1,0:T(8,128)} dynamic-update-slice(f32[288,8,132]{2,1,0:T(8,128)} %dynamic_update_slice.9, f32[288,2,128]{2,1,0:T(2,128)} %collective-permute-done.3, s32[]{:T(128)} %constant.61.clone.1, s32[]{:T(128)S(6)} %select_n.109, s32[]{:T(128)} %constant.67.clone.1) | dynamic-update-slice | bytes 589828 | tf_op jit(solution)/shard_map/dynamic_update_slice | solution.py:91
  220.5 3.0 %slice_select_fusion = f32[288,8,2]{2,1,0:T(8,128)} fusion(f32[288,8,132]{2,1,0:T(8,128)} %dynamic_update_slice.10, pred[]{:T(512)S(6)} %eq.42), kind=kLoop, calls=%fused_computation.17 | loop fusion | flops 4608 | bytes 55297 | tf_op jit(solution)/shard_map/jit(_where)/select_n | solution.py:88
  223.5 1.7 copy.15
  225.3 1.5 collective-permute-start.4
  226.9 2.3 collective-permute-done.4
  229.1 1.5 copy.16
  230.6 47.8 %dynamic_update_slice.11 = f32[288,8,132]{2,1,0:T(8,128)} dynamic-update-slice(f32[288,8,132]{2,1,0:T(8,128)} %dynamic_update_slice.10, f32[288,8,2]{2,1,0:T(8,128)} %copy.16, s32[]{:T(128)} %constant.61.clone.1, s32[]{:T(128)} %constant.61.clone.1, s32[]{:T(128)S(6)} %select_n.113) | dynamic-update-slice | bytes 36868 | tf_op jit(solution)/shard_map/dynamic_update_slice | solution.py:91
  278.4 1.8 slice_multiply_fusion.1
  281.2 1.0 fusion.29
  282.4 0.7 fusion.10
  287.0 1.0 fusion.31
  (30 shorter events, 6.5 us)
Async XLA Ops:
  0.0 2.0 copy-start
  5.3 3.1 %collective-permute-start = (f32[2,3,32,4,128]{4,3,2,1,0:T(4,128)S(1)}, f32[2,3,32,4,128]{4,3,2,1,0:T(4,128)}, u32[]{:S(2)}, u32[]{:S(2)}) collective-permute-start(f32[2,3,32,4,128]{4,3,2,1,0:T(4,128)S(1)} %bitcast.157), channel_id=1, source_target_pairs={{0,1},{1,0},{2,3},{3,2},{4,5},{5,4},{6,7},{7,6},{8,9},{9,8},{10,11... | collective-permute-start | bytes 1179656 | tf_op jit(solution)/shard_map/ppermute | solution.py:123
  5.3 2.0 collective-permute-start.1
  8.4 1.3 copy-start.1
  10.8 110.6 %collective-permute-start.3 = (f32[288,2,128]{2,1,0:T(2,128)}, f32[288,2,128]{2,1,0:T(2,128)}, u32[]{:S(2)}, u32[]{:S(2)}) collective-permute-start(f32[288,2,128]{2,1,0:T(2,128)} %get-tuple-element.26), channel_id=1, source_target_pairs={{4,8},{8,4},{5,9},{9,5},{6,10},{10,6},{7,11},{11,7},{20,24},{24,20... | collective-permute-start | bytes 884744 | tf_op jit(solution)/shard_map/ppermute | solution.py:88
  13.2 9.2 %collective-permute-start.2 = (f32[288,2,128]{2,1,0:T(2,128)}, f32[288,2,128]{2,1,0:T(2,128)}, u32[]{:S(2)}, u32[]{:S(2)}) collective-permute-start(f32[288,2,128]{2,1,0:T(2,128)} %get-tuple-element.27), channel_id=1, source_target_pairs={{0,4},{4,0},{8,12},{12,8},{1,5},{5,1},{9,13},{13,9},{2,6},{6,2},{1... | collective-permute-start | bytes 884744 | tf_op jit(solution)/shard_map/ppermute | solution.py:88
  225.3 3.9 %collective-permute-start.4 = (f32[288,8,2]{0,1,2:T(8,128)S(1)}, f32[288,8,2]{0,1,2:T(8,128)S(1)}, u32[]{:S(2)}, u32[]{:S(2)}) collective-permute-start(f32[288,8,2]{0,1,2:T(8,128)S(1)} %copy.15), channel_id=1, source_target_pairs={{0,2},{2,0},{1,3},{3,1},{4,6},{6,4},{5,7},{7,5},{8,10},{10,8},{9,1... | collective-permute-start | bytes 55304 | tf_op jit(solution)/shard_map/ppermute | solution.py:88

commit v7 on v5

--- a/solution.py
+++ b/solution.py
@@ -87,8 +87,8 @@
         if not pairs:
             continue
         lower_is_even = first == 0
-        send = jnp.where(even == lower_is_even, tail, head)
-        got = lax.ppermute(send, axis, pairs)
+        send = row_major(jnp.where(even == lower_is_even, tail, head))
+        got = row_major(lax.ppermute(send, axis, pairs))
         from_high = jnp.where(even == lower_is_even, got, from_high)
         from_low = jnp.where(even == lower_is_even, from_low, got)
     return jnp.concatenate([from_low, cells, from_high], axis=dim)

time: 52.1 us -> 49 us (0.940)
  local copies, waits for them, and re-layouts: 11 us -> 8.87 us
  other arithmetic: 20.3 us -> 19.2 us
    select_n x3 -> x0, local copies, waits for them, and re-layouts: 6.7 us -> none  [the longest x1 2.35 us: halo(): send = jnp.where(even == lower_is_even, tail, head)]
    another operation x0 -> x1, local copies, waits for them, and re-layouts: none -> 2.35 us  [row_major(): with_layout_constraint(x, Layout(major_to_minor=tuple(range(x.ndim))))]
    ppermute x0 -> x1, local copies, waits for them, and re-layouts: none -> 2.18 us  [halo(): got = row_major(lax.ppermute(send, axis, pairs))]
    concatenate x2, other arithmetic: 5.36 us -> 3.5 us  [halo(): return jnp.concatenate([from_low, cells, from_high], axis=dim)]
    select_n x2, other arithmetic: 1.93 us -> 2.8 us  [halo(): from_low = jnp.where(even == lower_is_even, from_low, got)]
where the time goes in v7:
time: 49 us; the launch traced here: 48.6 us
  other arithmetic  19.2 us (39%)
  waiting for transfers between devices  12.7 us (26%)
  local copies, waits for them, and re-layouts  8.87 us (18%)
  starting transfers between devices  5.67 us (12%)
  matrix products  1.93 us (4%)
    ppermute x3, waiting for transfers between devices, halo(): got = row_major(lax.ppermute(send, axis, pairs))  11.2 us
    ppermute x3, starting transfers between devices, halo(): got = row_major(lax.ppermute(send, axis, pairs))  5.16 us
    concatenate x2, other arithmetic, halo(): return jnp.concatenate([from_low, cells, from_high], axis=dim)  3.5 us
    select_n x2, other arithmetic, halo(): from_low = jnp.where(even == lower_is_even, from_low, got)  2.8 us
    select_n x2, other arithmetic, halo(): send = row_major(jnp.where(even == lower_is_even, tail, head))  2.45 us
    another operation x1, local copies, waits for them, and re-layouts, row_major(): with_layout_constraint(x, Layout(major_to_minor=tuple(range(x.ndim))))  2.35 us
    ppermute x1, local copies, waits for them, and re-layouts, halo(): got = row_major(lax.ppermute(send, axis, pairs))  2.18 us
    dot_general x1, matrix products, body(): lax.dot_general(weights, primaries, (((1,), (0,)), ((), ())), preferred_e...  1.93 us
  transfers between devices with their start and end apart: 5, of which 4 were waited for; matrix products, arithmetic and copies ran while one was open for 3% of the time, Pallas kernels for 0%

profile of v7, /device:TPU:16, one launch (start us, length us, event | category | flops | bytes accessed | tf_op | source)
XLA Modules:
  0.0 48.6 jit_solution(7189286324789355877)
XLA Ops:
  0.0 0.9 %reshape.140 = s32[2,16]{1,0:T(2,128)S(1)} reshape(s32[32]{0:T(128)} %param.6) | data formatting | bytes 256 | tf_op jit(solution)/shard_map/reshape | solution.py:115
  0.9 0.8 %reshape.141 = s32[2,16]{1,0:T(2,128)S(1)} reshape(s32[32]{0:T(128)} %param.7) | data formatting | bytes 256 | tf_op jit(solution)/shard_map/reshape | solution.py:116
  1.9 1.9 %fusion = f32[2,2,3,32,4,128]{5,0,4,3,2,1:T(2,128)S(1)} fusion(bf16[16,2,3,32,4,128]{5,4,3,2,1,0:T(4,128)(2,1)S(1)} %copy-done, s32[16]{0:T(128)S(1)} %get-tuple-element.6, s32[16]{0:T(128)S(1)} %get-tuple-element.5, s32[2]{0:T(128)S(1)} %pad_add_fusion), kind=kOutput, calls=%fused_computation | convolution fusion | flops 6291584 | bytes 3932296 | tf_op jit(solution)/shard_map/dot_general | solution.py:119
  3.8 1.4 %fusion.59 = (f32[1,2,3,32,4,128]{5,0,4,3,2,1:T(1,128)S(1)}, f32[1,2,3,32,4,128]{5,0,4,3,2,1:T(1,128)}) fusion(f32[2,2,3,32,4,128]{5,0,4,3,2,1:T(2,128)S(1)} %fusion), kind=kLoop, calls=%fused_computation.142 | loop fusion | bytes 1572864 | tf_op jit(solution)/shard_map/slice | solution.py:123
  5.8 1.5 %collective-permute-done.1 = f32[3,16,4,128]{3,2,1,0:T(4,128)} collective-permute-done((f32[3,16,4,128]{3,2,1,0:T(4,128)}, f32[3,16,4,128]{3,2,1,0:T(4,128)}, u32[]{:S(2)}, u32[]{:S(2)}) %collective-permute-start.1) | collective-permute-done | bytes 98336 | tf_op jit(solution)/shard_map/ppermute | solution.py:124
  7.3 1.1 %maximum_select_fusion = f32[3,32,4,128]{3,2,1,0:T(4,128)S(1)} fusion(f32[3,16,4,128]{3,2,1,0:T(4,128)} %collective-permute-done.1, f32[3,16,4,128]{3,2,1,0:T(4,128)} %param.5, pred[]{:T(512)S(6)} %eq.46), kind=kLoop, calls=%fused_computation.106 | loop fusion | flops 147456 | bytes 393217 | tf_op jit(solution)/shard_map/jit(_where)/select_n | solution.py:127
  8.4 1.3 %add.122 = f32[2,3,32,4,128]{4,3,2,1,0:T(4,128)S(1)} add(f32[2,3,32,4,128]{4,3,2,1,0:T(4,128)} %bitcast.158, f32[2,3,32,4,128]{4,3,2,1,0:T(4,128)} %collective-permute-done) | non-fusion elementwise | flops 98304 | bytes 1179648 | tf_op jit(solution)/shard_map/add | solution.py:125
  9.7 1.1 %broadcast_select_fusion.2 = (f32[288,2,128]{2,1,0:T(2,128)}, f32[288,2,128]{2,1,0:T(2,128)}) fusion(pred[]{:T(512)S(6)} %eq.39, f32[96,4,128]{2,1,0:T(4,128)S(1)} %bitcast.155, f32[192,4,128]{2,1,0:T(4,128)S(1)} %bitcast.152, pred[]{:T(512)S(6)} %eq.40), kind=kLoop, calls=%fused_computation.92 | loop fusion | flops 368640 | bytes 1179650 | tf_op jit(solution)/shard_map/jit(_where)/select_n | solution.py:90
  10.8 1.6 %collective-permute-start.2 = (f32[288,2,128]{2,1,0:T(2,128)}, f32[288,2,128]{2,1,0:T(2,128)}, u32[]{:S(2)}, u32[]{:S(2)}) collective-permute-start(f32[288,2,128]{2,1,0:T(2,128)} %get-tuple-element.32), channel_id=1, source_target_pairs={{0,4},{4,0},{8,12},{12,8},{1,5},{5,1},{9,13},{13,9},{2,6},{6,2},{1... | collective-permute-start | bytes 884744 | tf_op jit(solution)/shard_map/ppermute | solution.py:91
  12.3 2.1 %collective-permute-start.3 = (f32[288,2,128]{2,1,0:T(2,128)}, f32[288,2,128]{2,1,0:T(2,128)}, u32[]{:S(2)}, u32[]{:S(2)}) collective-permute-start(f32[288,2,128]{2,1,0:T(2,128)} %get-tuple-element.33), channel_id=1, source_target_pairs={{4,8},{8,4},{5,9},{9,5},{6,10},{10,6},{7,11},{11,7},{20,24},{24,20... | collective-permute-start | bytes 884744 | tf_op jit(solution)/shard_map/ppermute | solution.py:91
  14.7 5.4 %collective-permute-done.2 = f32[288,2,128]{2,1,0:T(2,128)} collective-permute-done((f32[288,2,128]{2,1,0:T(2,128)}, f32[288,2,128]{2,1,0:T(2,128)}, u32[]{:S(2)}, u32[]{:S(2)}) %collective-permute-start.2) | collective-permute-done | bytes 294944 | tf_op jit(solution)/shard_map/ppermute | solution.py:91
  20.1 3.2 %collective-permute-done.3 = f32[288,2,128]{2,1,0:T(2,128)} collective-permute-done((f32[288,2,128]{2,1,0:T(2,128)}, f32[288,2,128]{2,1,0:T(2,128)}, u32[]{:S(2)}, u32[]{:S(2)}) %collective-permute-start.3) | collective-permute-done | bytes 294944 | tf_op jit(solution)/shard_map/ppermute | solution.py:91
  23.3 1.3 %select_select_fusion.1 = (f32[288,2,128]{2,1,0:T(2,128)S(1)}, f32[288,2,128]{2,1,0:T(2,128)S(1)}) fusion(f32[288,2,128]{2,1,0:T(2,128)} %collective-permute-done.3, f32[288,2,128]{2,1,0:T(2,128)} %collective-permute-done.2, pred[]{:T(512)S(6)} %eq.39, pred[]{:T(512)S(6)} %eq.40), kind=kLoop, calls=%fused_computation.91 | loop fusion | flops 294912 | bytes 1179650 | tf_op jit(solution)/shard_map/jit(_where)/select_n | solution.py:93
  25.4 1.3 %pad_maximum_fusion.3 = f32[288,8,128]{2,1,0:T(8,128)S(1)} fusion(f32[288,2,128]{2,1,0:T(2,128)S(1)} %get-tuple-element.31, f32[96,4,128]{2,1,0:T(4,128)} %bitcast.156, f32[192,4,128]{2,1,0:T(4,128)S(1)} %bitcast.153, f32[288,2,128]{2,1,0:T(2,128)S(1)} %get-tuple-element.30), kind=kLoop, calls=%fused_computation.19 | loop fusion | flops 884736 | bytes 2359296 | tf_op jit(solution)/shard_map/concatenate | solution.py:94
  26.7 1.4 %slice_select_fusion = f32[288,8,2]{2,1,0:T(8,128)} fusion(f32[288,8,128]{2,1,0:T(8,128)S(1)} %pad_maximum_fusion.3, pred[]{:T(512)S(6)} %eq.38), kind=kLoop, calls=%fused_computation.18 | loop fusion | flops 4608 | bytes 55297 | tf_op jit(solution)/shard_map/jit(_where)/select_n | solution.py:90
  28.1 2.3 %copy.15 = f32[288,8,2]{0,1,2:T(8,128)} copy(f32[288,8,2]{2,1,0:T(8,128)} %slice_select_fusion) | data formatting | bytes 36864 | tf_op jit(solution)/shard_map/layout_constraint | solution.py:98
  30.5 1.5 %collective-permute-start.4 = (f32[288,8,2]{0,1,2:T(8,128)}, f32[288,8,2]{0,1,2:T(8,128)}, u32[]{:S(2)}, u32[]{:S(2)}) collective-permute-start(f32[288,8,2]{0,1,2:T(8,128)} %copy.15), channel_id=1, source_target_pairs={{0,2},{2,0},{1,3},{3,1},{4,6},{6,4},{5,7},{7,5},{8,10},{10,8},{9,1... | collective-permute-start | bytes 55304 | tf_op jit(solution)/shard_map/ppermute | solution.py:91
  32.1 2.6 %collective-permute-done.4 = f32[288,8,2]{0,1,2:T(8,128)} collective-permute-done((f32[288,8,2]{0,1,2:T(8,128)}, f32[288,8,2]{0,1,2:T(8,128)}, u32[]{:S(2)}, u32[]{:S(2)}) %collective-permute-start.4) | collective-permute-done | bytes 18464 | tf_op jit(solution)/shard_map/ppermute | solution.py:91
  34.6 2.2 %copy.16 = f32[288,8,2]{2,1,0:T(8,128)} copy(f32[288,8,2]{0,1,2:T(8,128)} %collective-permute-done.4) | data formatting | bytes 36864 | tf_op jit(solution)/shard_map/ppermute | solution.py:91
  36.8 1.5 %broadcast_select_fusion.1 = (f32[288,8,2]{2,1,0:T(8,128)S(1)}, f32[288,8,2]{2,1,0:T(8,128)S(1)}) fusion(f32[288,8,2]{2,1,0:T(8,128)} %copy.16, pred[]{:T(512)S(6)} %eq.38), kind=kLoop, calls=%fused_computation.45 | loop fusion | flops 9216 | bytes 55297 | tf_op jit(solution)/shard_map/jit(_where)/select_n | solution.py:93
  38.4 2.2 %pad_maximum_fusion = f32[288,8,132]{2,1,0:T(8,128)S(1)} fusion(f32[288,8,2]{2,1,0:T(8,128)S(1)} %get-tuple-element.27, f32[288,2,128]{2,1,0:T(2,128)S(1)} %copy-done.6, f32[96,4,128]{2,1,0:T(4,128)S(1)} %bitcast.157, f32[192,4,128]{2,1,0:T(4,128)S(1)} %bitcast.154, f32[288,2,128]{2,1,0:T(2,128)S(1)} %copy-done.4, f32[288,8,2]{2,1,0:T(8,128)S(1)} %get-tuple-element.26), kind=kLoop, calls=%fused_computation.2 | loop fusion | flops 1520640 | bytes 2433024 | tf_op jit(solution)/shard_map/concatenate | solution.py:94
  41.8 1.0 %fusion.29 = (f32[2,1,32,6,130]{4,3,2,0,1:T(8,128)S(1)}, f32[2,1,32,6,130]{4,3,2,0,1:T(8,128)S(1)}, f32[2,1,32,6,130]{4,3,2,0,1:T(8,128)S(1)}) fusion(f32[2,33,7,131]{3,2,1,0:T(8,128)S(1)} %get-tuple-element.39, f32[2,33,7,131]{3,2,1,0:T(8,128)S(1)} %get-tuple-element.37, f32[2,33,7,131]{3,2,1,0:T(8,128)S(1)} %get-tuple-element.38), kind=kLoop, calls=%fused_computation.80 | loop fusion | flops 449280 | bytes 2396160 | tf_op jit(solution)/shard_map/stack | solution.py:53
  43.0 0.7 %fusion.10 = (f32[1,3,32,6,130]{4,3,2,1,0:T(8,128)S(1)}, f32[1,3,32,6,130]{4,3,2,1,0:T(8,128)S(1)}) fusion(f32[1,3,32,8,132]{4,3,2,1,0:T(8,128)S(1)} %get-tuple-element.13, f32[2,3,32,6,130]{4,3,2,0,1:T(8,128)S(1)} %pad_maximum_fusion.2, f32[3,32,8,132]{3,2,1,0:T(8,128)S(1)} %bitcast.142, f32[1,3,32,8,132]{4,3,2,1,0:T(8,128)S(1)} %get-tuple-element.14), kind=kLoop, calls=%fused_computation.30 | loop fusion | flops 299520 | bytes 2096640 | tf_op jit(solution)/shard_map/stack | solution.py:159
  47.6 1.0 %fusion.31 = f32[1,2,3,32,4,128]{5,4,3,2,1,0:T(4,128)} fusion(f32[2,3,32,6,130]{4,3,2,1,0:T(8,128)S(1)} %fusion.4, f32[1,3,32,4,128]{4,3,2,1,0:T(4,128)S(1)} %get-tuple-element.25, f32[1,3,32,4,128]{4,3,2,1,0:T(4,128)S(1)} %get-tuple-element.24), kind=kLoop, calls=%fused_computation.85 | loop fusion | flops 294912 | bytes 1179648 | tf_op jit(solution)/shard_map/broadcast_in_dim | solution.py:163
  (42 shorter events, 7.0 us)
Async XLA Ops:
  0.0 1.9 %copy-start = (bf16[16,2,3,32,4,128]{5,4,3,2,1,0:T(4,128)(2,1)S(1)}, bf16[16,2,3,32,4,128]{5,4,3,2,1,0:T(4,128)(2,1)}, u32[]{:S(2)}) copy-start(bf16[16,2,3,32,4,128]{5,4,3,2,1,0:T(4,128)(2,1)} %param.4) | copy-start | bytes 9437188
  5.3 3.1 %collective-permute-start = (f32[2,3,32,4,128]{4,3,2,1,0:T(4,128)S(1)}, f32[2,3,32,4,128]{4,3,2,1,0:T(4,128)}, u32[]{:S(2)}, u32[]{:S(2)}) collective-permute-start(f32[2,3,32,4,128]{4,3,2,1,0:T(4,128)S(1)} %bitcast.159), channel_id=1, source_target_pairs={{0,1},{1,0},{2,3},{3,2},{4,5},{5,4},{6,7},{7,6},{8,9},{9,8},{10,11... | collective-permute-start | bytes 1179656 | tf_op jit(solution)/shard_map/ppermute | solution.py:123
  5.3 2.0 %collective-permute-start.1 = (f32[3,16,4,128]{3,2,1,0:T(4,128)}, f32[3,16,4,128]{3,2,1,0:T(4,128)}, u32[]{:S(2)}, u32[]{:S(2)}) collective-permute-start(f32[3,16,4,128]{3,2,1,0:T(4,128)} %param.5), channel_id=1, source_target_pairs={{0,1},{1,0},{2,3},{3,2},{4,5},{5,4},{6,7},{7,6},{8,9},{9,8},{10,11... | collective-permute-start | bytes 294920 | tf_op jit(solution)/shard_map/ppermute | solution.py:124
  8.4 1.3 %copy-start.1 = (f32[3,32,4,128]{3,2,1,0:T(4,128)}, f32[3,32,4,128]{3,2,1,0:T(4,128)S(1)}, u32[]{:S(2)}) copy-start(f32[3,32,4,128]{3,2,1,0:T(4,128)S(1)} %maximum_select_fusion) | copy-start | bytes 589828
  10.8 9.4 %collective-permute-start.2 = (f32[288,2,128]{2,1,0:T(2,128)}, f32[288,2,128]{2,1,0:T(2,128)}, u32[]{:S(2)}, u32[]{:S(2)}) collective-permute-start(f32[288,2,128]{2,1,0:T(2,128)} %get-tuple-element.32), channel_id=1, source_target_pairs={{0,4},{4,0},{8,12},{12,8},{1,5},{5,1},{9,13},{13,9},{2,6},{6,2},{1... | collective-permute-start | bytes 884744 | tf_op jit(solution)/shard_map/ppermute | solution.py:91
  12.3 11.0 %collective-permute-start.3 = (f32[288,2,128]{2,1,0:T(2,128)}, f32[288,2,128]{2,1,0:T(2,128)}, u32[]{:S(2)}, u32[]{:S(2)}) collective-permute-start(f32[288,2,128]{2,1,0:T(2,128)} %get-tuple-element.33), channel_id=1, source_target_pairs={{4,8},{8,4},{5,9},{9,5},{6,10},{10,6},{7,11},{11,7},{20,24},{24,20... | collective-permute-start | bytes 884744 | tf_op jit(solution)/shard_map/ppermute | solution.py:91
  24.6 0.7 %copy-start.3 = (f32[288,2,128]{2,1,0:T(2,128)}, f32[288,2,128]{2,1,0:T(2,128)S(1)}, u32[]{:S(2)}) copy-start(f32[288,2,128]{2,1,0:T(2,128)S(1)} %get-tuple-element.30) | copy-start | bytes 884740
  24.6 0.8 %copy-start.5 = (f32[288,2,128]{2,1,0:T(2,128)}, f32[288,2,128]{2,1,0:T(2,128)S(1)}, u32[]{:S(2)}) copy-start(f32[288,2,128]{2,1,0:T(2,128)S(1)} %get-tuple-element.31) | copy-start | bytes 884740
  30.5 4.1 %collective-permute-start.4 = (f32[288,8,2]{0,1,2:T(8,128)}, f32[288,8,2]{0,1,2:T(8,128)}, u32[]{:S(2)}, u32[]{:S(2)}) collective-permute-start(f32[288,8,2]{0,1,2:T(8,128)} %copy.15), channel_id=1, source_target_pairs={{0,2},{2,0},{1,3},{3,1},{4,6},{6,4},{5,7},{7,5},{8,10},{10,8},{9,1... | collective-permute-start | bytes 55304 | tf_op jit(solution)/shard_map/ppermute | solution.py:91
  36.8 1.5 %copy-start.2 = (f32[3,32,4,128]{3,2,1,0:T(4,128)S(1)}, f32[3,32,4,128]{3,2,1,0:T(4,128)}, u32[]{:S(2)}) copy-start(f32[3,32,4,128]{3,2,1,0:T(4,128)} %copy-done.1) | copy-start | bytes 589828
  36.8 1.5 %copy-start.4 = (f32[288,2,128]{2,1,0:T(2,128)S(1)}, f32[288,2,128]{2,1,0:T(2,128)}, u32[]{:S(2)}) copy-start(f32[288,2,128]{2,1,0:T(2,128)} %copy-done.3) | copy-start | bytes 884740
  36.8 1.5 %copy-start.6 = (f32[288,2,128]{2,1,0:T(2,128)S(1)}, f32[288,2,128]{2,1,0:T(2,128)}, u32[]{:S(2)}) copy-start(f32[288,2,128]{2,1,0:T(2,128)} %copy-done.5) | copy-start | bytes 884740

commit v8 on v7

--- a/solution.py
+++ b/solution.py
@@ -77,15 +77,19 @@
     size = cells.shape[dim]
     head = lax.slice_in_dim(cells, 0, width, axis=dim)
     tail = lax.slice_in_dim(cells, size - width, size, axis=dim)
+    if count == 2:
+        send = row_major(jnp.concatenate([tail, head], axis=dim))
+        got = row_major(lax.ppermute(send, axis, [(0, 1), (1, 0)]))
+        return jnp.concatenate(
+            [lax.slice_in_dim(got, 0, width, axis=dim), cells,
+             lax.slice_in_dim(got, width, 2 * width, axis=dim)], axis=dim)
     even = lax.axis_index(axis) % 2 == 0
-    from_low = jnp.zeros_like(tail)
-    from_high = jnp.zeros_like(head)
+    from_low = tail
+    from_high = head
     for first in (0, 1):
         pairs = []
         for i in range(first, count - 1, 2):
             pairs += [(i, i + 1), (i + 1, i)]
-        if not pairs:
-            continue
         lower_is_even = first == 0
         send = row_major(jnp.where(even == lower_is_even, tail, head))
         got = row_major(lax.ppermute(send, axis, pairs))
@@ -147,7 +151,7 @@
     kappa = K_FREQ * sigma_ext
     delta = K_FREQ * (sigma_ext - 1.0)
     rhs = source_term(shot_ext, delta)
-    field = jacobi(rhs, kappa)
+    field = jnp.where(inside, jacobi(rhs, kappa), 0.0)
     for sweep in range(SWEEPS):
         curled = curl_curl(pad_z(field))
         field = shrink(field, 1)

time: 49 us -> 52 us (1.061)
  local copies, waits for them, and re-layouts: 8.87 us -> 11.7 us
    concatenate x0 -> x2, other arithmetic: none -> 5.46 us  [the longest x1 4.06 us: halo(): jnp.concatenate([lax.slice_in_dim(got, 0, width, axis=dim), cells, lax.sl...]
    unnamed x14 -> x12, local copies, waits for them, and re-layouts: 0.86 us -> 5.2 us
    concatenate x2 -> x1, other arithmetic: 3.5 us -> 0.39 us  [halo(): return jnp.concatenate([from_low, cells, from_high], axis=dim)]
    ppermute x0 -> x1, waiting for transfers between devices: none -> 2.65 us  [halo(): got = row_major(lax.ppermute(send, axis, [(0, 1), (1, 0)]))]
    ppermute x3 -> x2, waiting for transfers between devices: 11.2 us -> 8.84 us  [halo(): got = row_major(lax.ppermute(send, axis, pairs))]
    ppermute x1 -> x0, local copies, waits for them, and re-layouts: 2.18 us -> none  [halo(): got = row_major(lax.ppermute(send, axis, pairs))]
    ppermute x0 -> x1, starting transfers between devices: none -> 1.49 us  [halo(): got = row_major(lax.ppermute(send, axis, [(0, 1), (1, 0)]))]
    ppermute x3 -> x2, starting transfers between devices: 5.16 us -> 3.67 us  [halo(): got = row_major(lax.ppermute(send, axis, pairs))]
  transfers between devices with their start and end apart: 5 -> 5, of which waited for: 4 -> 4; matrix products, arithmetic and copies ran while one was open for 3% -> 2% of each run, Pallas kernels for 0% -> 0%
where the time goes in v8:
time: 52 us; the launch traced here: 51.6 us
  other arithmetic  19.1 us (37%)
  waiting for transfers between devices  13 us (25%)
  local copies, waits for them, and re-layouts  11.7 us (22%)
  starting transfers between devices  5.67 us (11%)
  matrix products  1.93 us (4%)
    ppermute x2, waiting for transfers between devices, halo(): got = row_major(lax.ppermute(send, axis, pairs))  8.84 us
    unnamed x12, local copies, waits for them, and re-layouts  5.2 us
    concatenate x1, other arithmetic, halo(): jnp.concatenate([lax.slice_in_dim(got, 0, width, axis=dim), cells, lax.sl...  4.06 us
    ppermute x2, starting transfers between devices, halo(): got = row_major(lax.ppermute(send, axis, pairs))  3.67 us
    ppermute x1, waiting for transfers between devices, halo(): got = row_major(lax.ppermute(send, axis, [(0, 1), (1, 0)]))  2.65 us
    another operation x1, local copies, waits for them, and re-layouts, row_major(): with_layout_constraint(x, Layout(major_to_minor=tuple(range(x.ndim))))  2.36 us
    dot_general x1, matrix products, body(): lax.dot_general(weights, primaries, (((1,), (0,)), ((), ())), preferred_e...  1.93 us
    another operation x4, other arithmetic, curl_curl(): return jnp.stack([c_x, c_y, c_z], axis=-4)  1.85 us
  transfers between devices with their start and end apart: 5, of which 4 were waited for; matrix products, arithmetic and copies ran while one was open for 2% of the time, Pallas kernels for 0%

profile of v8, /device:TPU:16, one launch (start us, length us, event | category | flops | bytes accessed | tf_op | source)
XLA Modules:
  0.0 51.6 jit_solution(4413751631849407273)
XLA Ops:
  0.0 0.9 %reshape.140 = s32[2,16]{1,0:T(2,128)S(1)} reshape(s32[32]{0:T(128)} %param.6) | data formatting | bytes 256 | tf_op jit(solution)/shard_map/reshape | solution.py:119
  0.9 0.8 %reshape.141 = s32[2,16]{1,0:T(2,128)S(1)} reshape(s32[32]{0:T(128)} %param.7) | data formatting | bytes 256 | tf_op jit(solution)/shard_map/reshape | solution.py:120
  1.9 1.9 %fusion = f32[2,2,3,32,4,128]{5,0,4,3,2,1:T(2,128)S(1)} fusion(bf16[16,2,3,32,4,128]{5,4,3,2,1,0:T(4,128)(2,1)S(1)} %copy-done, s32[16]{0:T(128)S(1)} %get-tuple-element.6, s32[16]{0:T(128)S(1)} %get-tuple-element.5, s32[2]{0:T(128)S(1)} %pad_add_fusion), kind=kOutput, calls=%fused_computation | convolution fusion | flops 6291584 | bytes 3932296 | tf_op jit(solution)/shard_map/dot_general | solution.py:123
  3.8 1.4 %fusion.58 = (f32[1,2,3,32,4,128]{5,0,4,3,2,1:T(1,128)S(1)}, f32[1,2,3,32,4,128]{5,0,4,3,2,1:T(1,128)}) fusion(f32[2,2,3,32,4,128]{5,0,4,3,2,1:T(2,128)S(1)} %fusion), kind=kLoop, calls=%fused_computation.138 | loop fusion | bytes 1572864 | tf_op jit(solution)/shard_map/slice | solution.py:127
  5.8 1.5 %collective-permute-done.1 = f32[3,16,4,128]{3,2,1,0:T(4,128)} collective-permute-done((f32[3,16,4,128]{3,2,1,0:T(4,128)}, f32[3,16,4,128]{3,2,1,0:T(4,128)}, u32[]{:S(2)}, u32[]{:S(2)}) %collective-permute-start.1) | collective-permute-done | bytes 98336 | tf_op jit(solution)/shard_map/ppermute | solution.py:128
  7.3 1.1 %maximum_select_fusion.1 = f32[3,32,4,128]{3,2,1,0:T(4,128)S(1)} fusion(f32[3,16,4,128]{3,2,1,0:T(4,128)} %collective-permute-done.1, f32[3,16,4,128]{3,2,1,0:T(4,128)} %param.5, pred[]{:T(512)S(6)} %eq.41), kind=kLoop, calls=%fused_computation.101 | loop fusion | flops 147456 | bytes 393217 | tf_op jit(solution)/shard_map/jit(_where)/select_n | solution.py:131
  8.4 1.3 %add.118 = f32[2,3,32,4,128]{4,3,2,1,0:T(4,128)S(1)} add(f32[2,3,32,4,128]{4,3,2,1,0:T(4,128)} %bitcast.158, f32[2,3,32,4,128]{4,3,2,1,0:T(4,128)} %collective-permute-done) | non-fusion elementwise | flops 98304 | bytes 1179648 | tf_op jit(solution)/shard_map/add | solution.py:129
  9.7 1.1 %broadcast_select_fusion = (f32[288,2,128]{2,1,0:T(2,128)}, f32[288,2,128]{2,1,0:T(2,128)}) fusion(pred[]{:T(512)S(6)} %eq.34, f32[96,4,128]{2,1,0:T(4,128)S(1)} %bitcast.154, f32[192,4,128]{2,1,0:T(4,128)S(1)} %bitcast.150, pred[]{:T(512)S(6)} %eq.35), kind=kLoop, calls=%fused_computation.87 | loop fusion | flops 368640 | bytes 1179650 | tf_op jit(solution)/shard_map/jit(_where)/select_n | solution.py:94
  10.8 1.6 %collective-permute-start.2 = (f32[288,2,128]{2,1,0:T(2,128)}, f32[288,2,128]{2,1,0:T(2,128)}, u32[]{:S(2)}, u32[]{:S(2)}) collective-permute-start(f32[288,2,128]{2,1,0:T(2,128)} %get-tuple-element.32), channel_id=1, source_target_pairs={{0,4},{4,0},{8,12},{12,8},{1,5},{5,1},{9,13},{13,9},{2,6},{6,2},{1... | collective-permute-start | bytes 884744 | tf_op jit(solution)/shard_map/ppermute | solution.py:95
  12.3 2.1 %collective-permute-start.3 = (f32[288,2,128]{2,1,0:T(2,128)}, f32[288,2,128]{2,1,0:T(2,128)}, u32[]{:S(2)}, u32[]{:S(2)}) collective-permute-start(f32[288,2,128]{2,1,0:T(2,128)} %get-tuple-element.33), channel_id=1, source_target_pairs={{4,8},{8,4},{5,9},{9,5},{6,10},{10,6},{7,11},{11,7},{20,24},{24,20... | collective-permute-start | bytes 884744 | tf_op jit(solution)/shard_map/ppermute | solution.py:95
  14.5 5.7 %collective-permute-done.2 = f32[288,2,128]{2,1,0:T(2,128)} collective-permute-done((f32[288,2,128]{2,1,0:T(2,128)}, f32[288,2,128]{2,1,0:T(2,128)}, u32[]{:S(2)}, u32[]{:S(2)}) %collective-permute-start.2) | collective-permute-done | bytes 294944 | tf_op jit(solution)/shard_map/ppermute | solution.py:95
  20.1 3.2 %collective-permute-done.3 = f32[288,2,128]{2,1,0:T(2,128)} collective-permute-done((f32[288,2,128]{2,1,0:T(2,128)}, f32[288,2,128]{2,1,0:T(2,128)}, u32[]{:S(2)}, u32[]{:S(2)}) %collective-permute-start.3) | collective-permute-done | bytes 294944 | tf_op jit(solution)/shard_map/ppermute | solution.py:95
  23.3 1.5 %select_select_fusion.1 = (f32[288,2,128]{2,1,0:T(2,128)S(1)}, f32[288,2,128]{2,1,0:T(2,128)S(1)}) fusion(f32[288,2,128]{2,1,0:T(2,128)} %collective-permute-done.3, f32[288,2,128]{2,1,0:T(2,128)} %collective-permute-done.2, pred[]{:T(512)S(6)} %eq.34, pred[]{:T(512)S(6)} %eq.35, f32[96,4,128]{2,1,0:T(4,128)} %bitcast.155, f32[192,4,128]{2,1,0:T(4,128)S(1)} %bitcast.151), kind=kLoop, calls=%fused_computation.86 | loop fusion | flops 442368 | bytes 1769474 | tf_op jit(solution)/shard_map/jit(_where)/select_n | solution.py:97
  24.9 0.7 %copy-done.3 = f32[288,2,128]{2,1,0:T(2,128)} copy-done((f32[288,2,128]{2,1,0:T(2,128)}, f32[288,2,128]{2,1,0:T(2,128)S(1)}, u32[]{:S(2)}) %copy-start.3) | copy-done | bytes 294936
  26.4 1.4 %pad_maximum_fusion.3 = f32[288,8,4]{2,1,0:T(8,128)} fusion(f32[288,8,2]{2,1,0:T(8,128)S(1)} %get-tuple-element.27, f32[288,8,2]{2,1,0:T(8,128)S(1)} %get-tuple-element.26), kind=kLoop, calls=%fused_computation.16 | loop fusion | flops 9216 | bytes 73728 | tf_op jit(solution)/shard_map/concatenate | solution.py:81
  27.8 2.4 %copy.28 = f32[288,8,4]{0,1,2:T(8,128)} copy(f32[288,8,4]{2,1,0:T(8,128)} %pad_maximum_fusion.3) | data formatting | bytes 73728 | tf_op jit(solution)/shard_map/layout_constraint | solution.py:102
  30.2 1.5 %collective-permute-start.4 = (f32[288,8,4]{0,1,2:T(8,128)}, f32[288,8,4]{0,1,2:T(8,128)S(1)}, u32[]{:S(2)}, u32[]{:S(2)}) collective-permute-start(f32[288,8,4]{0,1,2:T(8,128)} %copy.28), channel_id=1, source_target_pairs={{0,2},{2,0},{1,3},{3,1},{4,6},{6,4},{5,7},{7,5},{8,10},{10,8},{9,1... | collective-permute-start | bytes 110600 | tf_op jit(solution)/shard_map/ppermute | solution.py:82
  31.9 2.7 %collective-permute-done.4 = f32[288,8,4]{0,1,2:T(8,128)S(1)} collective-permute-done((f32[288,8,4]{0,1,2:T(8,128)}, f32[288,8,4]{0,1,2:T(8,128)S(1)}, u32[]{:S(2)}, u32[]{:S(2)}) %collective-permute-start.4) | collective-permute-done | bytes 36896 | tf_op jit(solution)/shard_map/ppermute | solution.py:82
  35.1 2.2 %copy.38 = f32[288,8,2]{2,1,0:T(8,128)} copy(f32[288,8,2]{0,1,2:T(8,128)} %get-tuple-element.46) | data formatting | bytes 36864
  37.3 2.2 %copy.39 = f32[288,8,2]{2,1,0:T(8,128)} copy(f32[288,8,2]{0,1,2:T(8,128)} %get-tuple-element.47) | data formatting | bytes 36864
  39.5 4.1 %pad_maximum_fusion = f32[288,8,132]{2,1,0:T(8,128)S(1)} fusion(f32[288,8,2]{2,1,0:T(8,128)} %copy.39, f32[288,2,128]{2,1,0:T(2,128)} %copy-done.4, f32[96,4,128]{2,1,0:T(4,128)} %bitcast.156, f32[192,4,128]{2,1,0:T(4,128)S(1)} %bitcast.153, f32[288,2,128]{2,1,0:T(2,128)} %copy-done.3, f32[288,8,2]{2,1,0:T(8,128)} %copy.38), kind=kLoop, calls=%fused_computation.2 | loop fusion | flops 1520640 | bytes 2433024 | tf_op jit(solution)/shard_map/concatenate | solution.py:83
  44.8 1.0 %fusion.27 = (f32[2,1,32,6,130]{4,3,2,1,0:T(8,128)S(1)}, f32[2,1,32,6,130]{4,3,2,1,0:T(8,128)S(1)}, f32[2,1,32,6,130]{4,3,2,1,0:T(8,128)S(1)}) fusion(f32[2,33,7,131]{3,2,1,0:T(8,128)S(1)} %get-tuple-element.39, f32[2,33,7,131]{3,2,1,0:T(8,128)S(1)} %get-tuple-element.37, f32[2,33,7,131]{3,2,1,0:T(8,128)S(1)} %get-tuple-element.38), kind=kLoop, calls=%fused_computation.75 | loop fusion | flops 449280 | bytes 2396160 | tf_op jit(solution)/shard_map/stack | solution.py:53
  46.0 0.7 %fusion.8 = (f32[1,3,32,6,130]{4,3,2,1,0:T(8,128)S(1)}, f32[1,3,32,6,130]{4,3,2,1,0:T(8,128)S(1)}) fusion(f32[2,3,32,8,132]{4,3,2,1,0:T(8,128)S(1)} %maximum_select_fusion, f32[2,3,32,6,130]{4,3,2,1,0:T(8,128)S(1)} %pad_maximum_fusion.1, f32[3,32,8,132]{3,2,1,0:T(8,128)S(1)} %bitcast.140), kind=kLoop, calls=%fused_computation.27 | loop fusion | flops 299520 | bytes 2096640 | tf_op jit(solution)/shard_map/stack | solution.py:163
  50.6 1.0 %fusion.29 = f32[1,2,3,32,4,128]{5,4,3,2,1,0:T(4,128)} fusion(f32[2,3,32,6,130]{4,3,2,1,0:T(8,128)S(1)} %fusion.2, f32[1,3,32,4,128]{4,3,2,1,0:T(4,128)S(1)} %get-tuple-element.25, f32[1,3,32,4,128]{4,3,2,1,0:T(4,128)S(1)} %get-tuple-element.24), kind=kLoop, calls=%fused_computation.80 | loop fusion | flops 294912 | bytes 1179648 | tf_op jit(solution)/shard_map/broadcast_in_dim | solution.py:167
  (38 shorter events, 7.5 us)
Async XLA Ops:
  0.0 1.9 %copy-start = (bf16[16,2,3,32,4,128]{5,4,3,2,1,0:T(4,128)(2,1)S(1)}, bf16[16,2,3,32,4,128]{5,4,3,2,1,0:T(4,128)(2,1)}, u32[]{:S(2)}) copy-start(bf16[16,2,3,32,4,128]{5,4,3,2,1,0:T(4,128)(2,1)} %param.4) | copy-start | bytes 9437188
  5.3 3.1 %collective-permute-start = (f32[2,3,32,4,128]{4,3,2,1,0:T(4,128)S(1)}, f32[2,3,32,4,128]{4,3,2,1,0:T(4,128)}, u32[]{:S(2)}, u32[]{:S(2)}) collective-permute-start(f32[2,3,32,4,128]{4,3,2,1,0:T(4,128)S(1)} %bitcast.159), channel_id=1, source_target_pairs={{0,1},{1,0},{2,3},{3,2},{4,5},{5,4},{6,7},{7,6},{8,9},{9,8},{10,11... | collective-permute-start | bytes 1179656 | tf_op jit(solution)/shard_map/ppermute | solution.py:127
  5.3 2.0 %collective-permute-start.1 = (f32[3,16,4,128]{3,2,1,0:T(4,128)}, f32[3,16,4,128]{3,2,1,0:T(4,128)}, u32[]{:S(2)}, u32[]{:S(2)}) collective-permute-start(f32[3,16,4,128]{3,2,1,0:T(4,128)} %param.5), channel_id=1, source_target_pairs={{0,1},{1,0},{2,3},{3,2},{4,5},{5,4},{6,7},{7,6},{8,9},{9,8},{10,11... | collective-permute-start | bytes 294920 | tf_op jit(solution)/shard_map/ppermute | solution.py:128
  8.4 1.3 %copy-start.1 = (f32[3,32,4,128]{3,2,1,0:T(4,128)}, f32[3,32,4,128]{3,2,1,0:T(4,128)S(1)}, u32[]{:S(2)}) copy-start(f32[3,32,4,128]{3,2,1,0:T(4,128)S(1)} %maximum_select_fusion.1) | copy-start | bytes 589828
  10.8 9.4 %collective-permute-start.2 = (f32[288,2,128]{2,1,0:T(2,128)}, f32[288,2,128]{2,1,0:T(2,128)}, u32[]{:S(2)}, u32[]{:S(2)}) collective-permute-start(f32[288,2,128]{2,1,0:T(2,128)} %get-tuple-element.32), channel_id=1, source_target_pairs={{0,4},{4,0},{8,12},{12,8},{1,5},{5,1},{9,13},{13,9},{2,6},{6,2},{1... | collective-permute-start | bytes 884744 | tf_op jit(solution)/shard_map/ppermute | solution.py:95
  12.3 11.0 %collective-permute-start.3 = (f32[288,2,128]{2,1,0:T(2,128)}, f32[288,2,128]{2,1,0:T(2,128)}, u32[]{:S(2)}, u32[]{:S(2)}) collective-permute-start(f32[288,2,128]{2,1,0:T(2,128)} %get-tuple-element.33), channel_id=1, source_target_pairs={{4,8},{8,4},{5,9},{9,5},{6,10},{10,6},{7,11},{11,7},{20,24},{24,20... | collective-permute-start | bytes 884744 | tf_op jit(solution)/shard_map/ppermute | solution.py:95
  14.4 11.2 %copy-start.2 = (f32[3,32,4,128]{3,2,1,0:T(4,128)S(1)}, f32[3,32,4,128]{3,2,1,0:T(4,128)}, u32[]{:S(2)}) copy-start(f32[3,32,4,128]{3,2,1,0:T(4,128)} %copy-done.1) | copy-start | bytes 589828
  24.9 0.7 %copy-start.3 = (f32[288,2,128]{2,1,0:T(2,128)}, f32[288,2,128]{2,1,0:T(2,128)S(1)}, u32[]{:S(2)}) copy-start(f32[288,2,128]{2,1,0:T(2,128)S(1)} %get-tuple-element.28) | copy-start | bytes 884740
  24.9 0.8 %copy-start.4 = (f32[288,2,128]{2,1,0:T(2,128)}, f32[288,2,128]{2,1,0:T(2,128)S(1)}, u32[]{:S(2)}) copy-start(f32[288,2,128]{2,1,0:T(2,128)S(1)} %get-tuple-element.29) | copy-start | bytes 884740
  30.2 4.3 %collective-permute-start.4 = (f32[288,8,4]{0,1,2:T(8,128)}, f32[288,8,4]{0,1,2:T(8,128)S(1)}, u32[]{:S(2)}, u32[]{:S(2)}) collective-permute-start(f32[288,8,4]{0,1,2:T(8,128)} %copy.28), channel_id=1, source_target_pairs={{0,2},{2,0},{1,3},{3,1},{4,6},{6,4},{5,7},{7,5},{8,10},{10,8},{9,1... | collective-permute-start | bytes 110600 | tf_op jit(solution)/shard_map/ppermute | solution.py:82

commit v9 on v7

--- a/solution.py
+++ b/solution.py
@@ -1,6 +1,8 @@
 import jax
 import jax.numpy as jnp
 from jax import lax
+from jax.experimental import pallas as pl
+from jax.experimental.pallas import tpu as pltpu
 from jax.experimental.layout import Layout, with_layout_constraint
 from jax.sharding import PartitionSpec as P
 
@@ -98,6 +100,26 @@
     return with_layout_constraint(x, Layout(major_to_minor=tuple(range(x.ndim))))
 
 
+def sweep_all(shot_ext, sigma_ext, inside):
+    kappa = K_FREQ * sigma_ext
+    delta = K_FREQ * (sigma_ext - 1.0)
+    rhs = source_term(shot_ext, delta)
+    field = jacobi(rhs, kappa)
+    for sweep in range(SWEEPS):
+        curled = curl_curl(pad_z(field))
+        field = shrink(field, 1)
+        kappa = shrink(kappa, 1)
+        rhs = shrink(rhs, 1)
+        inside = shrink(inside, 1)
+        real_part = curled[..., 0, :, :, :, :] - kappa * field[..., 1, :, :, :, :]
+        imag_part = curled[..., 1, :, :, :, :] + kappa * field[..., 0, :, :, :, :]
+        applied = jnp.stack([real_part, imag_part], axis=-5)
+        field = field + RELAX * jacobi(rhs - applied, kappa)
+        if sweep < SWEEPS - 1:
+            field = jnp.where(inside, field, 0.0)
+    return field
+
+
 def encode_weights(group_part, sign_part, rows):
     picked = group_part[None, :] == rows[:, None]
     return jnp.where(picked, sign_part[None, :], 0).astype(jnp.float32).astype(jnp.bfloat16)
@@ -137,29 +159,25 @@
     )
     planes = row_major(halo(row_major(planes), "xb", 1, SWEEPS))
     planes = row_major(halo(planes, "yb", 2, SWEEPS))
-    shot_ext = planes[:shot_planes].reshape(shot.shape[:2] + (depth, ext_x, ext_y))
-    sigma_ext = planes[shot_planes:].reshape(-1, depth, ext_x, ext_y)
-
     gx = lax.axis_index("xb") * width_x - SWEEPS + lax.broadcasted_iota(jnp.int32, (ext_x, ext_y), 0)
     gy = lax.axis_index("yb") * width_y - SWEEPS + lax.broadcasted_iota(jnp.int32, (ext_x, ext_y), 1)
     inside = (gx >= 0) & (gx < width_x * lax.axis_size("xb")) & (gy >= 0) & (gy < width_y * lax.axis_size("yb"))
+    shot_shape = primaries.shape[1:3]
+    out_shape = shot_shape + (depth, width_x, width_y)
 
-    kappa = K_FREQ * sigma_ext
-    delta = K_FREQ * (sigma_ext - 1.0)
-    rhs = source_term(shot_ext, delta)
-    field = jacobi(rhs, kappa)
-    for sweep in range(SWEEPS):
-        curled = curl_curl(pad_z(field))
-        field = shrink(field, 1)
-        kappa = shrink(kappa, 1)
-        rhs = shrink(rhs, 1)
-        inside = shrink(inside, 1)
-        real_part = curled[..., 0, :, :, :, :] - kappa * field[..., 1, :, :, :, :]
-        imag_part = curled[..., 1, :, :, :, :] + kappa * field[..., 0, :, :, :, :]
-        applied = jnp.stack([real_part, imag_part], axis=-5)
-        field = field + RELAX * jacobi(rhs - applied, kappa)
-        if sweep < SWEEPS - 1:
-            field = jnp.where(inside, field, 0.0)
+    def sweeps_kernel(planes_ref, inside_ref, out_ref):
+        ext = planes_ref[...]
+        shot_ext = ext[:shot_planes].reshape(shot_shape + (depth, ext_x, ext_y))
+        sigma_ext = ext[shot_planes:].reshape(-1, depth, ext_x, ext_y)
+        keep = inside_ref[...] > 0.5
+        out_ref[...] = sweep_all(shot_ext, sigma_ext, keep)
+
+    field = pl.pallas_call(
+        sweeps_kernel,
+        out_shape=jax.ShapeDtypeStruct(out_shape, jnp.float32),
+        in_specs=[pl.BlockSpec(memory_space=pltpu.VMEM)] * 2,
+        out_specs=pl.BlockSpec(memory_space=pltpu.VMEM),
+    )(planes, inside.astype(jnp.float32))
     return field[None]
 
 

time: 49 us -> 48.6 us (level)
  Pallas kernels: 0 us -> 7.19 us
  other arithmetic: 19.2 us -> 12.5 us
    pallas_call x0 -> x1, Pallas kernels: none -> 7.19 us  [body(): pl.pallas_call(sweeps_kernel, out_shape=jax.ShapeDtypeStruct(out_shape, j...]
    another operation x9 -> x0, other arithmetic: 3.71 us -> none  [the longest x4 1.84 us: curl_curl(): return jnp.stack([c_x, c_y, c_z], axis=-4)]
    sub x4 -> x0, other arithmetic: 1.48 us -> none  [the longest x2 0.78 us: body(): field = field + RELAX * jacobi(rhs - applied, kappa)]
    broadcast_in_dim x1 -> x0, other arithmetic: 1.05 us -> none  [body(): return field[None]]
    convert_element_type x0 -> x1, other arithmetic: none -> 0.67 us  [body(): inside.astype(jnp.float32)]
    squeeze x1 -> x0, other arithmetic: 0.56 us -> none  [curl_curl(): e_x = padded[..., 0, :, :, :]]
    select_n x1 -> x0, other arithmetic: 0.53 us -> none  [body(): field = jnp.where(inside, field, 0.0)]
    concatenate x2, other arithmetic: 3.5 us -> 4 us  [halo(): return jnp.concatenate([from_low, cells, from_high], axis=dim)]
  transfers between devices with their start and end apart: 5 -> 5, of which waited for: 4 -> 4; matrix products, arithmetic and copies ran while one was open for 3% -> 4% of each run, Pallas kernels for 0% -> 0%
where the time goes in v9:
time: 48.6 us; the launch traced here: 48.2 us
  other arithmetic  12.5 us (26%)
  waiting for transfers between devices  12.3 us (25%)
  local copies, waits for them, and re-layouts  8.49 us (17%)
  Pallas kernels  7.19 us (15%)
  starting transfers between devices  5.67 us (12%)
  matrix products  1.93 us (4%)
    ppermute x3, waiting for transfers between devices, halo(): got = row_major(lax.ppermute(send, axis, pairs))  10.8 us
    pallas_call x1, Pallas kernels, body(): pl.pallas_call(sweeps_kernel, out_shape=jax.ShapeDtypeStruct(out_shape, j...  7.19 us
    ppermute x3, starting transfers between devices, halo(): got = row_major(lax.ppermute(send, axis, pairs))  5.16 us
    concatenate x2, other arithmetic, halo(): return jnp.concatenate([from_low, cells, from_high], axis=dim)  4 us
    select_n x2, other arithmetic, halo(): from_low = jnp.where(even == lower_is_even, from_low, got)  2.8 us
    select_n x2, other arithmetic, halo(): send = row_major(jnp.where(even == lower_is_even, tail, head))  2.45 us
    another operation x1, local copies, waits for them, and re-layouts, row_major(): with_layout_constraint(x, Layout(major_to_minor=tuple(range(x.ndim))))  2.34 us
    ppermute x1, local copies, waits for them, and re-layouts, halo(): got = row_major(lax.ppermute(send, axis, pairs))  2.18 us
  transfers between devices with their start and end apart: 5, of which 4 were waited for; matrix products, arithmetic and copies ran while one was open for 4% of the time, Pallas kernels for 0%

profile of v9, /device:TPU:16, one launch (start us, length us, event | category | flops | bytes accessed | tf_op | source)
XLA Modules:
  0.0 48.2 jit_solution(4107998488056320259)
XLA Ops:
  0.0 0.9 %reshape.17 = s32[2,16]{1,0:T(2,128)S(1)} reshape(s32[32]{0:T(128)} %param.6) | data formatting | bytes 256 | tf_op jit(solution)/shard_map/reshape | solution.py:137
  0.9 0.8 %reshape.18 = s32[2,16]{1,0:T(2,128)S(1)} reshape(s32[32]{0:T(128)} %param.7) | data formatting | bytes 256 | tf_op jit(solution)/shard_map/reshape | solution.py:138
  1.9 1.9 %fusion = f32[2,2,3,32,4,128]{5,0,4,3,2,1:T(2,128)S(1)} fusion(bf16[16,2,3,32,4,128]{5,4,3,2,1,0:T(4,128)(2,1)S(1)} %copy-done, s32[16]{0:T(128)S(1)} %get-tuple-element.6, s32[16]{0:T(128)S(1)} %get-tuple-element.5, s32[2]{0:T(128)S(1)} %pad_add_fusion), kind=kOutput, calls=%fused_computation | convolution fusion | flops 6291584 | bytes 3932296 | tf_op jit(solution)/shard_map/dot_general | solution.py:141
  3.8 1.4 %fusion.14 = (f32[1,2,3,32,4,128]{5,0,4,3,2,1:T(1,128)S(1)}, f32[1,2,3,32,4,128]{5,0,4,3,2,1:T(1,128)}) fusion(f32[2,2,3,32,4,128]{5,0,4,3,2,1:T(2,128)S(1)} %fusion), kind=kLoop, calls=%fused_computation.34 | loop fusion | bytes 1572864 | tf_op jit(solution)/shard_map/slice | solution.py:145
  5.3 0.5 %collective-permute-start.1 = (f32[3,16,4,128]{3,2,1,0:T(4,128)}, f32[3,16,4,128]{3,2,1,0:T(4,128)}, u32[]{:S(2)}, u32[]{:S(2)}) collective-permute-start(f32[3,16,4,128]{3,2,1,0:T(4,128)} %param.5), channel_id=1, source_target_pairs={{0,1},{1,0},{2,3},{3,2},{4,5},{5,4},{6,7},{7,6},{8,9},{9,8},{10,11... | collective-permute-start | bytes 294920 | tf_op jit(solution)/shard_map/ppermute | solution.py:146
  5.8 1.5 %collective-permute-done.1 = f32[3,16,4,128]{3,2,1,0:T(4,128)} collective-permute-done((f32[3,16,4,128]{3,2,1,0:T(4,128)}, f32[3,16,4,128]{3,2,1,0:T(4,128)}, u32[]{:S(2)}, u32[]{:S(2)}) %collective-permute-start.1) | collective-permute-done | bytes 98336 | tf_op jit(solution)/shard_map/ppermute | solution.py:146
  7.3 1.1 %maximum_select_fusion = f32[3,32,4,128]{3,2,1,0:T(4,128)S(1)} fusion(f32[3,16,4,128]{3,2,1,0:T(4,128)} %collective-permute-done.1, f32[3,16,4,128]{3,2,1,0:T(4,128)} %param.5, pred[]{:T(512)S(6)} %eq.46), kind=kLoop, calls=%fused_computation.15 | loop fusion | flops 147456 | bytes 393217 | tf_op jit(solution)/shard_map/jit(_where)/select_n | solution.py:149
  8.4 1.3 %add.36 = f32[2,3,32,4,128]{4,3,2,1,0:T(4,128)S(1)} add(f32[2,3,32,4,128]{4,3,2,1,0:T(4,128)} %bitcast.20, f32[2,3,32,4,128]{4,3,2,1,0:T(4,128)} %collective-permute-done) | non-fusion elementwise | flops 98304 | bytes 1179648 | tf_op jit(solution)/shard_map/add | solution.py:147
  9.7 1.1 %broadcast_select_fusion.2 = (f32[288,2,128]{2,1,0:T(2,128)}, f32[288,2,128]{2,1,0:T(2,128)}) fusion(pred[]{:T(512)S(6)} %eq.39, f32[96,4,128]{2,1,0:T(4,128)S(1)} %bitcast.17, f32[192,4,128]{2,1,0:T(4,128)S(1)} %bitcast.14, pred[]{:T(512)S(6)} %eq.40), kind=kLoop, calls=%fused_computation.13 | loop fusion | flops 368640 | bytes 1179650 | tf_op jit(solution)/shard_map/jit(_where)/select_n | solution.py:92
  10.7 1.6 %collective-permute-start.2 = (f32[288,2,128]{2,1,0:T(2,128)}, f32[288,2,128]{2,1,0:T(2,128)}, u32[]{:S(2)}, u32[]{:S(2)}) collective-permute-start(f32[288,2,128]{2,1,0:T(2,128)} %get-tuple-element.13), channel_id=1, source_target_pairs={{0,4},{4,0},{8,12},{12,8},{1,5},{5,1},{9,13},{13,9},{2,6},{6,2},{1... | collective-permute-start | bytes 884744 | tf_op jit(solution)/shard_map/ppermute | solution.py:93
  12.3 2.1 %collective-permute-start.3 = (f32[288,2,128]{2,1,0:T(2,128)}, f32[288,2,128]{2,1,0:T(2,128)}, u32[]{:S(2)}, u32[]{:S(2)}) collective-permute-start(f32[288,2,128]{2,1,0:T(2,128)} %get-tuple-element.14), channel_id=1, source_target_pairs={{4,8},{8,4},{5,9},{9,5},{6,10},{10,6},{7,11},{11,7},{20,24},{24,20... | collective-permute-start | bytes 884744 | tf_op jit(solution)/shard_map/ppermute | solution.py:93
  14.5 5.7 %collective-permute-done.2 = f32[288,2,128]{2,1,0:T(2,128)} collective-permute-done((f32[288,2,128]{2,1,0:T(2,128)}, f32[288,2,128]{2,1,0:T(2,128)}, u32[]{:S(2)}, u32[]{:S(2)}) %collective-permute-start.2) | collective-permute-done | bytes 294944 | tf_op jit(solution)/shard_map/ppermute | solution.py:93
  20.1 3.2 %collective-permute-done.3 = f32[288,2,128]{2,1,0:T(2,128)} collective-permute-done((f32[288,2,128]{2,1,0:T(2,128)}, f32[288,2,128]{2,1,0:T(2,128)}, u32[]{:S(2)}, u32[]{:S(2)}) %collective-permute-start.3) | collective-permute-done | bytes 294944 | tf_op jit(solution)/shard_map/ppermute | solution.py:93
  23.3 1.3 %select_select_fusion.1 = (f32[288,2,128]{2,1,0:T(2,128)S(1)}, f32[288,2,128]{2,1,0:T(2,128)S(1)}) fusion(f32[288,2,128]{2,1,0:T(2,128)} %collective-permute-done.3, f32[288,2,128]{2,1,0:T(2,128)} %collective-permute-done.2, pred[]{:T(512)S(6)} %eq.39, pred[]{:T(512)S(6)} %eq.40), kind=kLoop, calls=%fused_computation.12 | loop fusion | flops 294912 | bytes 1179650 | tf_op jit(solution)/shard_map/jit(_where)/select_n | solution.py:95
  24.6 0.7 %copy-done.4 = f32[288,2,128]{2,1,0:T(2,128)} copy-done((f32[288,2,128]{2,1,0:T(2,128)}, f32[288,2,128]{2,1,0:T(2,128)S(1)}, u32[]{:S(2)}) %copy-start.4) | copy-done | bytes 294936
  25.8 1.4 %slice_select_fusion = f32[288,8,2]{2,1,0:T(8,128)} fusion(f32[288,8,128]{2,1,0:T(8,128)S(1)} %pad_maximum_fusion.1, pred[]{:T(512)S(6)} %eq.38), kind=kLoop, calls=%fused_computation.3 | loop fusion | flops 4608 | bytes 55297 | tf_op jit(solution)/shard_map/jit(_where)/select_n | solution.py:92
  27.2 2.3 %copy.9 = f32[288,8,2]{0,1,2:T(8,128)} copy(f32[288,8,2]{2,1,0:T(8,128)} %slice_select_fusion) | data formatting | bytes 36864 | tf_op jit(solution)/shard_map/layout_constraint | solution.py:100
  29.6 1.5 %collective-permute-start.4 = (f32[288,8,2]{0,1,2:T(8,128)}, f32[288,8,2]{0,1,2:T(8,128)}, u32[]{:S(2)}, u32[]{:S(2)}) collective-permute-start(f32[288,8,2]{0,1,2:T(8,128)} %copy.9), channel_id=1, source_target_pairs={{0,2},{2,0},{1,3},{3,1},{4,6},{6,4},{5,7},{7,5},{8,10},{10,8},{9,1... | collective-permute-start | bytes 55304 | tf_op jit(solution)/shard_map/ppermute | solution.py:93
  31.1 0.7 %and_convert_fusion.inside_ref = f32[8,132]{1,0:T(8,128)} fusion(pred[132]{0:T(512)(128)(4,1)S(1)} %get-tuple-element.15, pred[132]{0:T(512)(128)(4,1)S(1)} %get-tuple-element.16, pred[8]{0:T(512)(128)(4,1)S(1)} %compare_and_fusion), kind=kLoop, calls=%fused_computation.16 | loop fusion | flops 3168 | bytes 4496 | tf_op jit(solution)/shard_map/convert_element_type | solution.py:180
  31.7 2.0 %collective-permute-done.4 = f32[288,8,2]{0,1,2:T(8,128)} collective-permute-done((f32[288,8,2]{0,1,2:T(8,128)}, f32[288,8,2]{0,1,2:T(8,128)}, u32[]{:S(2)}, u32[]{:S(2)}) %collective-permute-start.4) | collective-permute-done | bytes 18464 | tf_op jit(solution)/shard_map/ppermute | solution.py:93
  33.7 2.2 %copy.10 = f32[288,8,2]{2,1,0:T(8,128)} copy(f32[288,8,2]{0,1,2:T(8,128)} %collective-permute-done.4) | data formatting | bytes 36864 | tf_op jit(solution)/shard_map/ppermute | solution.py:93
  35.9 1.5 %broadcast_select_fusion.1 = (f32[288,8,2]{2,1,0:T(8,128)S(1)}, f32[288,8,2]{2,1,0:T(8,128)S(1)}) fusion(f32[288,8,2]{2,1,0:T(8,128)} %copy.10, pred[]{:T(512)S(6)} %eq.38), kind=kLoop, calls=%fused_computation.8 | loop fusion | flops 9216 | bytes 55297 | tf_op jit(solution)/shard_map/jit(_where)/select_n | solution.py:95
  37.4 3.6 %pad_maximum_fusion.planes_ref = f32[288,8,132]{2,1,0:T(8,128)} fusion(f32[288,8,2]{2,1,0:T(8,128)S(1)} %get-tuple-element.8, f32[288,2,128]{2,1,0:T(2,128)S(1)} %copy-done.7, f32[96,4,128]{2,1,0:T(4,128)S(1)} %bitcast.19, f32[192,4,128]{2,1,0:T(4,128)S(1)} %bitcast.16, f32[288,2,128]{2,1,0:T(2,128)S(1)} %copy-done.5, f32[288,8,2]{2,1,0:T(8,128)S(1)} %get-tuple-element.7), kind=kLoop, calls=%fused_computation.2 | loop fusion | flops 1520640 | bytes 2433024 | tf_op jit(solution)/shard_map/concatenate | solution.py:96
  41.0 7.2 %shard_map.46 = f32[2,3,32,4,128]{4,3,2,1,0:T(4,128)} custom-call(f32[288,8,132]{2,1,0:T(8,128)} %pad_maximum_fusion.planes_ref, f32[8,132]{1,0:T(8,128)} %and_convert_fusion.inside_ref), custom_call_target="tpu_custom_call" | custom-call | tf_op jit(solution)/shard_map/pallas_call | solution.py:175
  (23 shorter events, 0.7 us)
Async XLA Ops:
  0.0 1.9 %copy-start = (bf16[16,2,3,32,4,128]{5,4,3,2,1,0:T(4,128)(2,1)S(1)}, bf16[16,2,3,32,4,128]{5,4,3,2,1,0:T(4,128)(2,1)}, u32[]{:S(2)}) copy-start(bf16[16,2,3,32,4,128]{5,4,3,2,1,0:T(4,128)(2,1)} %param.4) | copy-start | bytes 9437188
  5.3 3.1 %collective-permute-start = (f32[2,3,32,4,128]{4,3,2,1,0:T(4,128)S(1)}, f32[2,3,32,4,128]{4,3,2,1,0:T(4,128)}, u32[]{:S(2)}, u32[]{:S(2)}) collective-permute-start(f32[2,3,32,4,128]{4,3,2,1,0:T(4,128)S(1)} %bitcast.21), channel_id=1, source_target_pairs={{0,1},{1,0},{2,3},{3,2},{4,5},{5,4},{6,7},{7,6},{8,9},{9,8},{10,11... | collective-permute-start | bytes 1179656 | tf_op jit(solution)/shard_map/ppermute | solution.py:145
  5.3 2.0 %collective-permute-start.1 = (f32[3,16,4,128]{3,2,1,0:T(4,128)}, f32[3,16,4,128]{3,2,1,0:T(4,128)}, u32[]{:S(2)}, u32[]{:S(2)}) collective-permute-start(f32[3,16,4,128]{3,2,1,0:T(4,128)} %param.5), channel_id=1, source_target_pairs={{0,1},{1,0},{2,3},{3,2},{4,5},{5,4},{6,7},{7,6},{8,9},{9,8},{10,11... | collective-permute-start | bytes 294920 | tf_op jit(solution)/shard_map/ppermute | solution.py:146
  8.4 2.4 %copy-start.1 = (f32[3,32,4,128]{3,2,1,0:T(4,128)}, f32[3,32,4,128]{3,2,1,0:T(4,128)S(1)}, u32[]{:S(2)}) copy-start(f32[3,32,4,128]{3,2,1,0:T(4,128)S(1)} %maximum_select_fusion) | copy-start | bytes 589828
  10.7 9.4 %collective-permute-start.2 = (f32[288,2,128]{2,1,0:T(2,128)}, f32[288,2,128]{2,1,0:T(2,128)}, u32[]{:S(2)}, u32[]{:S(2)}) collective-permute-start(f32[288,2,128]{2,1,0:T(2,128)} %get-tuple-element.13), channel_id=1, source_target_pairs={{0,4},{4,0},{8,12},{12,8},{1,5},{5,1},{9,13},{13,9},{2,6},{6,2},{1... | collective-permute-start | bytes 884744 | tf_op jit(solution)/shard_map/ppermute | solution.py:93
  12.3 11.0 %collective-permute-start.3 = (f32[288,2,128]{2,1,0:T(2,128)}, f32[288,2,128]{2,1,0:T(2,128)}, u32[]{:S(2)}, u32[]{:S(2)}) collective-permute-start(f32[288,2,128]{2,1,0:T(2,128)} %get-tuple-element.14), channel_id=1, source_target_pairs={{4,8},{8,4},{5,9},{9,5},{6,10},{10,6},{7,11},{11,7},{20,24},{24,20... | collective-permute-start | bytes 884744 | tf_op jit(solution)/shard_map/ppermute | solution.py:93
  14.4 11.0 %copy-start.2 = (f32[3,32,4,128]{3,2,1,0:T(4,128)S(1)}, f32[3,32,4,128]{3,2,1,0:T(4,128)}, u32[]{:S(2)}) copy-start(f32[3,32,4,128]{3,2,1,0:T(4,128)} %copy-done.1) | copy-start | bytes 589828
  24.6 0.7 %copy-start.4 = (f32[288,2,128]{2,1,0:T(2,128)}, f32[288,2,128]{2,1,0:T(2,128)S(1)}, u32[]{:S(2)}) copy-start(f32[288,2,128]{2,1,0:T(2,128)S(1)} %get-tuple-element.11) | copy-start | bytes 884740
  24.6 0.8 %copy-start.6 = (f32[288,2,128]{2,1,0:T(2,128)}, f32[288,2,128]{2,1,0:T(2,128)S(1)}, u32[]{:S(2)}) copy-start(f32[288,2,128]{2,1,0:T(2,128)S(1)} %get-tuple-element.12) | copy-start | bytes 884740
  29.6 4.1 %collective-permute-start.4 = (f32[288,8,2]{0,1,2:T(8,128)}, f32[288,8,2]{0,1,2:T(8,128)}, u32[]{:S(2)}, u32[]{:S(2)}) collective-permute-start(f32[288,8,2]{0,1,2:T(8,128)} %copy.9), channel_id=1, source_target_pairs={{0,2},{2,0},{1,3},{3,1},{4,6},{6,4},{5,7},{7,5},{8,10},{10,8},{9,1... | collective-permute-start | bytes 55304 | tf_op jit(solution)/shard_map/ppermute | solution.py:93
  35.9 1.5 %copy-start.3 = (f32[3,32,4,128]{3,2,1,0:T(4,128)S(1)}, f32[3,32,4,128]{3,2,1,0:T(4,128)}, u32[]{:S(2)}) copy-start(f32[3,32,4,128]{3,2,1,0:T(4,128)} %copy-done.1) | copy-start | bytes 589828
  35.9 1.5 %copy-start.5 = (f32[288,2,128]{2,1,0:T(2,128)S(1)}, f32[288,2,128]{2,1,0:T(2,128)}, u32[]{:S(2)}) copy-start(f32[288,2,128]{2,1,0:T(2,128)} %copy-done.4) | copy-start | bytes 884740
  35.9 1.5 %copy-start.7 = (f32[288,2,128]{2,1,0:T(2,128)S(1)}, f32[288,2,128]{2,1,0:T(2,128)}, u32[]{:S(2)}) copy-start(f32[288,2,128]{2,1,0:T(2,128)} %copy-done.6) | copy-start | bytes 884740

commit v10 on v9

--- a/solution.py
+++ b/solution.py
@@ -72,6 +72,29 @@
 
 def pad_z(f):
     return jnp.pad(f, [(0, 0)] * (f.ndim - 3) + [(1, 1), (0, 0), (0, 0)])
+
+
+def halo_faces(cells, axis, dim, width):
+    count = lax.axis_size(axis)
+    size = cells.shape[dim]
+    head = lax.slice_in_dim(cells, 0, width, axis=dim)
+    tail = lax.slice_in_dim(cells, size - width, size, axis=dim)
+    if count == 2:
+        got = row_major(lax.ppermute(row_major(jnp.where(lax.axis_index(axis) == 0, tail, head)), axis, [(0, 1), (1, 0)]))
+        return got, got
+    even = lax.axis_index(axis) % 2 == 0
+    from_low = jnp.zeros_like(tail)
+    from_high = jnp.zeros_like(head)
+    for first in (0, 1):
+        pairs = []
+        for i in range(first, count - 1, 2):
+            pairs += [(i, i + 1), (i + 1, i)]
+        lower_is_even = first == 0
+        send = row_major(jnp.where(even == lower_is_even, tail, head))
+        got = row_major(lax.ppermute(send, axis, pairs))
+        from_high = jnp.where(even == lower_is_even, got, from_high)
+        from_low = jnp.where(even == lower_is_even, from_low, got)
+    return from_low, from_high
 
 
 def halo(cells, axis, dim, width):
@@ -104,7 +127,7 @@
     kappa = K_FREQ * sigma_ext
     delta = K_FREQ * (sigma_ext - 1.0)
     rhs = source_term(shot_ext, delta)
-    field = jacobi(rhs, kappa)
+    field = jnp.where(inside, jacobi(rhs, kappa), 0.0)
     for sweep in range(SWEEPS):
         curled = curl_curl(pad_z(field))
         field = shrink(field, 1)
@@ -158,15 +181,15 @@
         [shot.reshape(-1, width_x, width_y), sigma_all.reshape(-1, width_x, width_y)], axis=0
     )
     planes = row_major(halo(row_major(planes), "xb", 1, SWEEPS))
-    planes = row_major(halo(planes, "yb", 2, SWEEPS))
+    y_low, y_high = halo_faces(planes, "yb", 2, SWEEPS)
     gx = lax.axis_index("xb") * width_x - SWEEPS + lax.broadcasted_iota(jnp.int32, (ext_x, ext_y), 0)
     gy = lax.axis_index("yb") * width_y - SWEEPS + lax.broadcasted_iota(jnp.int32, (ext_x, ext_y), 1)
     inside = (gx >= 0) & (gx < width_x * lax.axis_size("xb")) & (gy >= 0) & (gy < width_y * lax.axis_size("yb"))
     shot_shape = primaries.shape[1:3]
     out_shape = shot_shape + (depth, width_x, width_y)
 
-    def sweeps_kernel(planes_ref, inside_ref, out_ref):
-        ext = planes_ref[...]
+    def sweeps_kernel(planes_ref, low_ref, high_ref, inside_ref, out_ref):
+        ext = jnp.concatenate([low_ref[...], planes_ref[...], high_ref[...]], axis=2)
         shot_ext = ext[:shot_planes].reshape(shot_shape + (depth, ext_x, ext_y))
         sigma_ext = ext[shot_planes:].reshape(-1, depth, ext_x, ext_y)
         keep = inside_ref[...] > 0.5
@@ -175,9 +198,9 @@
     field = pl.pallas_call(
         sweeps_kernel,
         out_shape=jax.ShapeDtypeStruct(out_shape, jnp.float32),
-        in_specs=[pl.BlockSpec(memory_space=pltpu.VMEM)] * 2,
+        in_specs=[pl.BlockSpec(memory_space=pltpu.VMEM)] * 4,
         out_specs=pl.BlockSpec(memory_space=pltpu.VMEM),
-    )(planes, inside.astype(jnp.float32))
+    )(planes, y_low, y_high, inside.astype(jnp.float32))
     return field[None]
 
 

time: 48.6 us -> 43 us (0.88)
  other arithmetic: 12.5 us -> 7.41 us
  local copies, waits for them, and re-layouts: 8.49 us -> 7.38 us
  Pallas kernels: 7.19 us -> 8.18 us
    concatenate x2 -> x1, other arithmetic: 4 us -> 0.39 us  [halo(): return jnp.concatenate([from_low, cells, from_high], axis=dim)]
    ppermute x3 -> x2, waiting for transfers between devices: 10.8 us -> 9.02 us  [halo(): got = row_major(lax.ppermute(send, axis, pairs))]
    ppermute x3 -> x2, starting transfers between devices: 5.16 us -> 3.49 us  [halo(): got = row_major(lax.ppermute(send, axis, pairs))]
    ppermute x0 -> x1, waiting for transfers between devices: none -> 1.67 us  [halo_faces(): lax.ppermute(row_major(jnp.where(lax.axis_index(axis) == 0, tail, head)),...]
    ppermute x0 -> x1, starting transfers between devices: none -> 1.55 us  [halo_faces(): lax.ppermute(row_major(jnp.where(lax.axis_index(axis) == 0, tail, head)),...]
    select_n x2 -> x1, other arithmetic: 2.8 us -> 1.31 us  [halo(): from_low = jnp.where(even == lower_is_even, from_low, got)]
    select_n x0 -> x1, other arithmetic: none -> 1.42 us  [halo_faces(): jnp.where(lax.axis_index(axis) == 0, tail, head)]
    select_n x2 -> x1, other arithmetic: 2.45 us -> 1.06 us  [halo(): send = row_major(jnp.where(even == lower_is_even, tail, head))]
where the time goes in v10:
time: 43 us; the launch traced here: 42.7 us
  waiting for transfers between devices  12.2 us (28%)
  Pallas kernels  8.18 us (19%)
  other arithmetic  7.41 us (17%)
  local copies, waits for them, and re-layouts  7.38 us (17%)
  starting transfers between devices  5.55 us (13%)
  matrix products  1.93 us (4%)
    ppermute x2, waiting for transfers between devices, halo(): got = row_major(lax.ppermute(send, axis, pairs))  9.02 us
    pallas_call x1, Pallas kernels, body(): pl.pallas_call(sweeps_kernel, out_shape=jax.ShapeDtypeStruct(out_shape, j...  8.18 us
    ppermute x2, starting transfers between devices, halo(): got = row_major(lax.ppermute(send, axis, pairs))  3.49 us
    dot_general x1, matrix products, body(): lax.dot_general(weights, primaries, (((1,), (0,)), ((), ())), preferred_e...  1.93 us
    another operation x1, local copies, waits for them, and re-layouts, row_major(): with_layout_constraint(x, Layout(major_to_minor=tuple(range(x.ndim))))  1.73 us
    ppermute x1, waiting for transfers between devices, halo_faces(): lax.ppermute(row_major(jnp.where(lax.axis_index(axis) == 0, tail, head)),...  1.67 us
    ppermute x1, starting transfers between devices, halo_faces(): lax.ppermute(row_major(jnp.where(lax.axis_index(axis) == 0, tail, head)),...  1.55 us
    ppermute x1, waiting for transfers between devices, body(): sigma_other = lax.ppermute(conductivity, 'tx', tx_ring)  1.48 us
  transfers between devices with their start and end apart: 5, of which 4 were waited for; matrix products, arithmetic and copies ran while one was open for 4% of the time, Pallas kernels for 0%

profile of v10, /device:TPU:16, one launch (start us, length us, event | category | flops | bytes accessed | tf_op | source)
XLA Modules:
  0.0 42.7 jit_solution(13663371862371907745)
XLA Ops:
  0.0 0.9 %reshape.17 = s32[2,16]{1,0:T(2,128)S(1)} reshape(s32[32]{0:T(128)} %param.6) | data formatting | bytes 256 | tf_op jit(solution)/shard_map/reshape | solution.py:160
  0.9 0.8 %reshape.18 = s32[2,16]{1,0:T(2,128)S(1)} reshape(s32[32]{0:T(128)} %param.7) | data formatting | bytes 256 | tf_op jit(solution)/shard_map/reshape | solution.py:161
  1.8 0.1 select_reduce_fusion.1
  1.9 1.9 %fusion = f32[2,2,3,32,4,128]{5,0,4,3,2,1:T(2,128)S(1)} fusion(bf16[16,2,3,32,4,128]{5,4,3,2,1,0:T(4,128)(2,1)S(1)} %copy-done, s32[16]{0:T(128)S(1)} %get-tuple-element.6, s32[16]{0:T(128)S(1)} %get-tuple-element.5, s32[2]{0:T(128)S(1)} %pad_add_fusion), kind=kOutput, calls=%fused_computation | convolution fusion | flops 6291584 | bytes 3932296 | tf_op jit(solution)/shard_map/dot_general | solution.py:164
  3.8 1.4 %fusion.14 = (f32[1,2,3,32,4,128]{5,0,4,3,2,1:T(1,128)S(1)}, f32[1,2,3,32,4,128]{5,0,4,3,2,1:T(1,128)}) fusion(f32[2,2,3,32,4,128]{5,0,4,3,2,1:T(2,128)S(1)} %fusion), kind=kLoop, calls=%fused_computation.31 | loop fusion | bytes 1572864 | tf_op jit(solution)/shard_map/slice | solution.py:168
  5.3 0.5 %collective-permute-start.1 = (f32[3,16,4,128]{3,2,1,0:T(4,128)}, f32[3,16,4,128]{3,2,1,0:T(4,128)}, u32[]{:S(2)}, u32[]{:S(2)}) collective-permute-start(f32[3,16,4,128]{3,2,1,0:T(4,128)} %param.5), channel_id=1, source_target_pairs={{0,1},{1,0},{2,3},{3,2},{4,5},{5,4},{6,7},{7,6},{8,9},{9,8},{10,11... | collective-permute-start | bytes 294920 | tf_op jit(solution)/shard_map/ppermute | solution.py:169
  5.8 1.5 %collective-permute-done.1 = f32[3,16,4,128]{3,2,1,0:T(4,128)} collective-permute-done((f32[3,16,4,128]{3,2,1,0:T(4,128)}, f32[3,16,4,128]{3,2,1,0:T(4,128)}, u32[]{:S(2)}, u32[]{:S(2)}) %collective-permute-start.1) | collective-permute-done | bytes 98336 | tf_op jit(solution)/shard_map/ppermute | solution.py:169
  7.3 1.1 %maximum_select_fusion = f32[3,32,4,128]{3,2,1,0:T(4,128)S(1)} fusion(f32[3,16,4,128]{3,2,1,0:T(4,128)} %collective-permute-done.1, f32[3,16,4,128]{3,2,1,0:T(4,128)} %param.5, pred[]{:T(512)S(6)} %eq.44), kind=kLoop, calls=%fused_computation.12 | loop fusion | flops 147456 | bytes 393217 | tf_op jit(solution)/shard_map/jit(_where)/select_n | solution.py:172
  8.4 1.3 %add.32 = f32[2,3,32,4,128]{4,3,2,1,0:T(4,128)S(1)} add(f32[2,3,32,4,128]{4,3,2,1,0:T(4,128)} %bitcast.18, f32[2,3,32,4,128]{4,3,2,1,0:T(4,128)} %collective-permute-done) | non-fusion elementwise | flops 98304 | bytes 1179648 | tf_op jit(solution)/shard_map/add | solution.py:170
  9.7 1.1 %broadcast_select_fusion = (f32[288,2,128]{2,1,0:T(2,128)}, f32[288,2,128]{2,1,0:T(2,128)}) fusion(pred[]{:T(512)S(6)} %eq.37, f32[96,4,128]{2,1,0:T(4,128)S(1)} %bitcast.16, f32[192,4,128]{2,1,0:T(4,128)S(1)} %bitcast.14, pred[]{:T(512)S(6)} %eq.38), kind=kLoop, calls=%fused_computation.10 | loop fusion | flops 368640 | bytes 1179650 | tf_op jit(solution)/shard_map/jit(_where)/select_n | solution.py:115
  10.8 1.6 %collective-permute-start.2 = (f32[288,2,128]{2,1,0:T(2,128)}, f32[288,2,128]{2,1,0:T(2,128)}, u32[]{:S(2)}, u32[]{:S(2)}) collective-permute-start(f32[288,2,128]{2,1,0:T(2,128)} %get-tuple-element.11), channel_id=1, source_target_pairs={{0,4},{4,0},{8,12},{12,8},{1,5},{5,1},{9,13},{13,9},{2,6},{6,2},{1... | collective-permute-start | bytes 884744 | tf_op jit(solution)/shard_map/ppermute | solution.py:116
  12.3 1.9 %collective-permute-start.3 = (f32[288,2,128]{2,1,0:T(2,128)}, f32[288,2,128]{2,1,0:T(2,128)}, u32[]{:S(2)}, u32[]{:S(2)}) collective-permute-start(f32[288,2,128]{2,1,0:T(2,128)} %get-tuple-element.12), channel_id=1, source_target_pairs={{4,8},{8,4},{5,9},{9,5},{6,10},{10,6},{7,11},{11,7},{20,24},{24,20... | collective-permute-start | bytes 884744 | tf_op jit(solution)/shard_map/ppermute | solution.py:116
  14.3 5.8 %collective-permute-done.2 = f32[288,2,128]{2,1,0:T(2,128)} collective-permute-done((f32[288,2,128]{2,1,0:T(2,128)}, f32[288,2,128]{2,1,0:T(2,128)}, u32[]{:S(2)}, u32[]{:S(2)}) %collective-permute-start.2) | collective-permute-done | bytes 294944 | tf_op jit(solution)/shard_map/ppermute | solution.py:116
  20.1 3.2 %collective-permute-done.3 = f32[288,2,128]{2,1,0:T(2,128)} collective-permute-done((f32[288,2,128]{2,1,0:T(2,128)}, f32[288,2,128]{2,1,0:T(2,128)}, u32[]{:S(2)}, u32[]{:S(2)}) %collective-permute-start.3) | collective-permute-done | bytes 294944 | tf_op jit(solution)/shard_map/ppermute | solution.py:116
  23.3 1.3 %select_select_fusion.1 = (f32[288,2,128]{2,1,0:T(2,128)S(1)}, f32[288,2,128]{2,1,0:T(2,128)S(1)}) fusion(f32[288,2,128]{2,1,0:T(2,128)} %collective-permute-done.3, f32[288,2,128]{2,1,0:T(2,128)} %collective-permute-done.2, pred[]{:T(512)S(6)} %eq.37, pred[]{:T(512)S(6)} %eq.38), kind=kLoop, calls=%fused_computation.9 | loop fusion | flops 294912 | bytes 1179650 | tf_op jit(solution)/shard_map/jit(_where)/select_n | solution.py:118
  24.6 0.4 pad_maximum_fusion.planes_ref
  25.0 1.0 %copy-done.1 = f32[288,8,128]{2,1,0:T(8,128)} copy-done((f32[288,8,128]{2,1,0:T(8,128)}, f32[288,8,128]{2,1,0:T(8,128)S(1)}, u32[]{:S(2)}) %copy-start.1) | copy-done | bytes 1179672
  26.1 1.4 %slice_select_fusion = f32[288,8,2]{2,1,0:T(8,128)} fusion(f32[288,8,128]{2,1,0:T(8,128)S(1)} %pad_maximum_fusion.planes_ref, pred[]{:T(512)S(6)} %eq.45), kind=kLoop, calls=%fused_computation.2 | loop fusion | flops 4608 | bytes 55297 | tf_op jit(solution)/shard_map/jit(_where)/select_n | solution.py:83
  27.5 1.7 %copy.9 = f32[288,8,2]{0,1,2:T(8,128)S(1)} copy(f32[288,8,2]{2,1,0:T(8,128)} %slice_select_fusion) | data formatting | bytes 36864 | tf_op jit(solution)/shard_map/layout_constraint | solution.py:123
  29.2 1.5 %collective-permute-start.4 = (f32[288,8,2]{0,1,2:T(8,128)S(1)}, f32[288,8,2]{0,1,2:T(8,128)S(1)}, u32[]{:S(2)}, u32[]{:S(2)}) collective-permute-start(f32[288,8,2]{0,1,2:T(8,128)S(1)} %copy.9), channel_id=1, source_target_pairs={{0,2},{2,0},{1,3},{3,1},{4,6},{6,4},{5,7},{7,5},{8,10},{10,8},{9,1... | collective-permute-start | bytes 55304 | tf_op jit(solution)/shard_map/ppermute | solution.py:83
  30.8 0.7 %and_convert_fusion.inside_ref = f32[8,132]{1,0:T(8,128)} fusion(pred[132]{0:T(512)(128)(4,1)S(1)} %get-tuple-element.13, pred[132]{0:T(512)(128)(4,1)S(1)} %get-tuple-element.14, pred[8]{0:T(512)(128)(4,1)S(1)} %compare_and_fusion), kind=kLoop, calls=%fused_computation.13 | loop fusion | flops 3168 | bytes 4496 | tf_op jit(solution)/shard_map/convert_element_type | solution.py:203
  31.4 1.7 %collective-permute-done.4 = f32[288,8,2]{0,1,2:T(8,128)S(1)} collective-permute-done((f32[288,8,2]{0,1,2:T(8,128)S(1)}, f32[288,8,2]{0,1,2:T(8,128)S(1)}, u32[]{:S(2)}, u32[]{:S(2)}) %collective-permute-start.4) | collective-permute-done | bytes 18464 | tf_op jit(solution)/shard_map/ppermute | solution.py:83
  33.1 1.5 %copy.10.low_ref.high_ref = f32[288,8,2]{2,1,0:T(8,128)} copy(f32[288,8,2]{0,1,2:T(8,128)S(1)} %collective-permute-done.4) | data formatting | bytes 36864 | tf_op jit(solution)/shard_map/ppermute | solution.py:83
  34.6 8.2 %shard_map.46 = f32[2,3,32,4,128]{4,3,2,1,0:T(4,128)} custom-call(f32[288,8,128]{2,1,0:T(8,128)} %copy-done.1, f32[288,8,2]{2,1,0:T(8,128)} %copy.10.low_ref.high_ref, f32[288,8,2]{2,1,0:T(8,128)} %copy.10.low_ref.high_ref, f32[8,132]{1,0:T(8,128)} %and_convert_fusion.inside_ref), custom_call_target="tpu_custom_call" | custom-call | tf_op jit(solution)/shard_map/pallas_call | solution.py:198
  (13 shorter events, 0.2 us)
Async XLA Ops:
  0.0 1.9 %copy-start = (bf16[16,2,3,32,4,128]{5,4,3,2,1,0:T(4,128)(2,1)S(1)}, bf16[16,2,3,32,4,128]{5,4,3,2,1,0:T(4,128)(2,1)}, u32[]{:S(2)}) copy-start(bf16[16,2,3,32,4,128]{5,4,3,2,1,0:T(4,128)(2,1)} %param.4) | copy-start | bytes 9437188
  5.3 3.1 %collective-permute-start = (f32[2,3,32,4,128]{4,3,2,1,0:T(4,128)S(1)}, f32[2,3,32,4,128]{4,3,2,1,0:T(4,128)}, u32[]{:S(2)}, u32[]{:S(2)}) collective-permute-start(f32[2,3,32,4,128]{4,3,2,1,0:T(4,128)S(1)} %bitcast.19), channel_id=1, source_target_pairs={{0,1},{1,0},{2,3},{3,2},{4,5},{5,4},{6,7},{7,6},{8,9},{9,8},{10,11... | collective-permute-start | bytes 1179656 | tf_op jit(solution)/shard_map/ppermute | solution.py:168
  5.3 2.0 %collective-permute-start.1 = (f32[3,16,4,128]{3,2,1,0:T(4,128)}, f32[3,16,4,128]{3,2,1,0:T(4,128)}, u32[]{:S(2)}, u32[]{:S(2)}) collective-permute-start(f32[3,16,4,128]{3,2,1,0:T(4,128)} %param.5), channel_id=1, source_target_pairs={{0,1},{1,0},{2,3},{3,2},{4,5},{5,4},{6,7},{7,6},{8,9},{9,8},{10,11... | collective-permute-start | bytes 294920 | tf_op jit(solution)/shard_map/ppermute | solution.py:169
  8.4 2.4 %copy-start.2 = (f32[3,32,4,128]{3,2,1,0:T(4,128)}, f32[3,32,4,128]{3,2,1,0:T(4,128)S(1)}, u32[]{:S(2)}) copy-start(f32[3,32,4,128]{3,2,1,0:T(4,128)S(1)} %maximum_select_fusion) | copy-start | bytes 589828
  10.8 9.4 %collective-permute-start.2 = (f32[288,2,128]{2,1,0:T(2,128)}, f32[288,2,128]{2,1,0:T(2,128)}, u32[]{:S(2)}, u32[]{:S(2)}) collective-permute-start(f32[288,2,128]{2,1,0:T(2,128)} %get-tuple-element.11), channel_id=1, source_target_pairs={{0,4},{4,0},{8,12},{12,8},{1,5},{5,1},{9,13},{13,9},{2,6},{6,2},{1... | collective-permute-start | bytes 884744 | tf_op jit(solution)/shard_map/ppermute | solution.py:116
  12.3 11.0 %collective-permute-start.3 = (f32[288,2,128]{2,1,0:T(2,128)}, f32[288,2,128]{2,1,0:T(2,128)}, u32[]{:S(2)}, u32[]{:S(2)}) collective-permute-start(f32[288,2,128]{2,1,0:T(2,128)} %get-tuple-element.12), channel_id=1, source_target_pairs={{4,8},{8,4},{5,9},{9,5},{6,10},{10,6},{7,11},{11,7},{20,24},{24,20... | collective-permute-start | bytes 884744 | tf_op jit(solution)/shard_map/ppermute | solution.py:116
  14.3 10.4 %copy-start.3 = (f32[3,32,4,128]{3,2,1,0:T(4,128)S(1)}, f32[3,32,4,128]{3,2,1,0:T(4,128)}, u32[]{:S(2)}) copy-start(f32[3,32,4,128]{3,2,1,0:T(4,128)} %copy-done.2) | copy-start | bytes 589828
  25.0 1.0 %copy-start.1 = (f32[288,8,128]{2,1,0:T(8,128)}, f32[288,8,128]{2,1,0:T(8,128)S(1)}, u32[]{:S(2)}) copy-start(f32[288,8,128]{2,1,0:T(8,128)S(1)} %pad_maximum_fusion.planes_ref) | copy-start | bytes 3538948
  29.2 3.9 %collective-permute-start.4 = (f32[288,8,2]{0,1,2:T(8,128)S(1)}, f32[288,8,2]{0,1,2:T(8,128)S(1)}, u32[]{:S(2)}, u32[]{:S(2)}) collective-permute-start(f32[288,8,2]{0,1,2:T(8,128)S(1)} %copy.9), channel_id=1, source_target_pairs={{0,2},{2,0},{1,3},{3,1},{4,6},{6,4},{5,7},{7,5},{8,10},{10,8},{9,1... | collective-permute-start | bytes 55304 | tf_op jit(solution)/shard_map/ppermute | solution.py:83

commit v11 on v10

--- a/solution.py
+++ b/solution.py
@@ -72,6 +72,17 @@
 
 def pad_z(f):
     return jnp.pad(f, [(0, 0)] * (f.ndim - 3) + [(1, 1), (0, 0), (0, 0)])
+
+
+def swap_rounds(axis):
+    count = lax.axis_size(axis)
+    even = lax.axis_index(axis) % 2 == 0
+    for first in (0, 1):
+        pairs = []
+        for i in range(first, count - 1, 2):
+            pairs += [(i, i + 1), (i + 1, i)]
+        if pairs:
+            yield pairs, even == (first == 0)
 
 
 def halo_faces(cells, axis, dim, width):
@@ -174,14 +185,64 @@
         jnp.concatenate([conductivity, sigma_other], axis=1),
         jnp.concatenate([sigma_other, conductivity], axis=1),
     )
+    shot_planes = shot.shape[0] * shot.shape[1] * depth
     ext_x = width_x + 2 * SWEEPS
     ext_y = width_y + 2 * SWEEPS
-    shot_planes = shot.shape[0] * shot.shape[1] * depth
     planes = jnp.concatenate(
         [shot.reshape(-1, width_x, width_y), sigma_all.reshape(-1, width_x, width_y)], axis=0
     )
-    planes = row_major(halo(row_major(planes), "xb", 1, SWEEPS))
-    y_low, y_high = halo_faces(planes, "yb", 2, SWEEPS)
+    planes = row_major(planes)
+    w = SWEEPS
+    x_rounds = list(swap_rounds("xb"))
+    y_rounds = list(swap_rounds("yb"))
+    x_gots = []
+    for pairs, lower in x_rounds:
+        send = row_major(jnp.where(lower, planes[:, width_x - w:], planes[:, :w]))
+        x_gots.append(row_major(lax.ppermute(send, "xb", pairs)))
+    flags = jnp.stack(
+        [(lax.axis_index("xb") % 2 == 0).astype(jnp.int32)]
+        + [lower.astype(jnp.int32) for _, lower in y_rounds]
+    )
+    n_x = len(x_gots)
+    n_y = len(y_rounds)
+    face_shape = (planes.shape[0], ext_x, w)
+
+    def x_kernel(flags_ref, planes_ref, *refs):
+        got_refs = refs[:n_x]
+        planes_x_ref = refs[n_x]
+        send_refs = refs[n_x + 1:]
+        if n_x == 1:
+            low = high = got_refs[0][...]
+        else:
+            even = flags_ref[0] == 1
+            high = jnp.where(even, got_refs[0][...], got_refs[1][...])
+            low = jnp.where(even, got_refs[1][...], got_refs[0][...])
+        cells = jnp.concatenate([low, planes_ref[...], high], axis=1)
+        planes_x_ref[...] = cells
+        head = cells[:, :, :w]
+        tail = cells[:, :, width_y - w:]
+        for k in range(n_y):
+            send_refs[k][...] = jnp.where(flags_ref[1 + k] == 1, tail, head)
+
+    outs = pl.pallas_call(
+        x_kernel,
+        out_shape=[jax.ShapeDtypeStruct((planes.shape[0], ext_x, width_y), jnp.float32)]
+        + [jax.ShapeDtypeStruct(face_shape, jnp.float32)] * n_y,
+        in_specs=[pl.BlockSpec(memory_space=pltpu.SMEM)]
+        + [pl.BlockSpec(memory_space=pltpu.VMEM)] * (1 + n_x),
+        out_specs=[pl.BlockSpec(memory_space=pltpu.VMEM)] * (1 + n_y),
+    )(flags, planes, *x_gots)
+    planes = outs[0]
+    y_gots = [
+        row_major(lax.ppermute(row_major(send), "yb", pairs))
+        for send, (pairs, _) in zip(outs[1:], y_rounds)
+    ]
+    if n_y == 1:
+        y_low = y_high = y_gots[0]
+    else:
+        even_y = lax.axis_index("yb") % 2 == 0
+        y_high = jnp.where(even_y, y_gots[0], y_gots[1])
+        y_low = jnp.where(even_y, y_gots[1], y_gots[0])
     gx = lax.axis_index("xb") * width_x - SWEEPS + lax.broadcasted_iota(jnp.int32, (ext_x, ext_y), 0)
     gy = lax.axis_index("yb") * width_y - SWEEPS + lax.broadcasted_iota(jnp.int32, (ext_x, ext_y), 1)
     inside = (gx >= 0) & (gx < width_x * lax.axis_size("xb")) & (gy >= 0) & (gy < width_y * lax.axis_size("yb"))

time: 43 us -> 41.8 us (0.972)
  Pallas kernels: 8.18 us -> 11.1 us
  waiting for transfers between devices: 12.2 us -> 9.66 us
  local copies, waits for them, and re-layouts: 7.38 us -> 6.33 us
  other arithmetic: 7.41 us -> 6.84 us
    pallas_call x0 -> x1, Pallas kernels: none -> 2.95 us  [body(): pl.pallas_call(x_kernel, out_shape=[jax.ShapeDtypeStruct((planes.shape[0]...]
    select_n x3 -> x1, other arithmetic: 3.78 us -> 1.05 us  [body(): send = row_major(jnp.where(lower, planes[:, width_x - w:], planes[:, :w]))]
    ppermute x3, waiting for transfers between devices: 10.7 us -> 8.18 us  [the longest x2 6.52 us: body(): x_gots.append(row_major(lax.ppermute(send, 'xb', pairs)))]
    concatenate x1, other arithmetic: 0.39 us -> 1.88 us  [body(): jnp.concatenate([shot.reshape(-1, width_x, width_y), sigma_all.reshape(-1...]
    unnamed x8 -> x4, local copies, waits for them, and re-layouts: 1.08 us -> 0.05 us
    another operation x0 -> x1, other arithmetic: none -> 0.67 us  [body(): jnp.stack([(lax.axis_index('xb') % 2 == 0).astype(jnp.int32)] + [lower.as...]
  transfers between devices with their start and end apart: 5 -> 5, of which waited for: 4 -> 4; matrix products, arithmetic and copies ran while one was open for 4% -> 10% of each run, Pallas kernels for 0% -> 0%
where the time goes in v11:
time: 41.8 us; the launch traced here: 41.5 us
  Pallas kernels  11.1 us (27%)
  waiting for transfers between devices  9.66 us (23%)
  other arithmetic  6.84 us (16%)
  local copies, waits for them, and re-layouts  6.33 us (15%)
  starting transfers between devices  5.55 us (13%)
  matrix products  1.93 us (5%)
    pallas_call x1, Pallas kernels, body(): pl.pallas_call(sweeps_kernel, out_shape=jax.ShapeDtypeStruct(out_shape, j...  8.19 us
    ppermute x2, waiting for transfers between devices, body(): x_gots.append(row_major(lax.ppermute(send, 'xb', pairs)))  6.52 us
    ppermute x2, starting transfers between devices, body(): x_gots.append(row_major(lax.ppermute(send, 'xb', pairs)))  3.49 us
    pallas_call x1, Pallas kernels, body(): pl.pallas_call(x_kernel, out_shape=[jax.ShapeDtypeStruct((planes.shape[0]...  2.95 us
    dot_general x1, matrix products, body(): lax.dot_general(weights, primaries, (((1,), (0,)), ((), ())), preferred_e...  1.93 us
    concatenate x1, other arithmetic, body(): jnp.concatenate([shot.reshape(-1, width_x, width_y), sigma_all.reshape(-1...  1.88 us
    another operation x1, local copies, waits for them, and re-layouts, row_major(): with_layout_constraint(x, Layout(major_to_minor=tuple(range(x.ndim))))  1.73 us
    ppermute x1, waiting for transfers between devices, body(): lax.ppermute(row_major(send), 'yb', pairs)  1.66 us
  transfers between devices with their start and end apart: 5, of which 4 were waited for; matrix products, arithmetic and copies ran while one was open for 10% of the time, Pallas kernels for 0%

profile of v11, /device:TPU:16, one launch (start us, length us, event | category | flops | bytes accessed | tf_op | source)
XLA Modules:
  0.0 41.5 jit_solution(17538403577594653571)
XLA Ops:
  0.0 0.9 %reshape.17 = s32[2,16]{1,0:T(2,128)S(1)} reshape(s32[32]{0:T(128)} %param.6) | data formatting | bytes 256 | tf_op jit(solution)/shard_map/reshape | solution.py:171
  0.9 0.8 %reshape.18 = s32[2,16]{1,0:T(2,128)S(1)} reshape(s32[32]{0:T(128)} %param.7) | data formatting | bytes 256 | tf_op jit(solution)/shard_map/reshape | solution.py:172
  1.7 0.1 pad_add_fusion
  1.8 0.1 select_reduce_fusion.1
  1.9 1.9 %fusion = f32[2,2,3,32,4,128]{5,0,4,3,2,1:T(2,128)S(1)} fusion(bf16[16,2,3,32,4,128]{5,4,3,2,1,0:T(4,128)(2,1)S(1)} %copy-done, s32[16]{0:T(128)S(1)} %get-tuple-element.10, s32[16]{0:T(128)S(1)} %get-tuple-element.9, s32[2]{0:T(128)S(1)} %pad_add_fusion), kind=kOutput, calls=%fused_computation | convolution fusion | flops 6291584 | bytes 3932296 | tf_op jit(solution)/shard_map/dot_general | solution.py:175
  3.8 1.4 %fusion.15 = (f32[1,2,3,32,4,128]{5,0,4,3,2,1:T(1,128)S(1)}, f32[1,2,3,32,4,128]{5,0,4,3,2,1:T(1,128)}) fusion(f32[2,2,3,32,4,128]{5,0,4,3,2,1:T(2,128)S(1)} %fusion), kind=kLoop, calls=%fused_computation.31 | loop fusion | bytes 1572864 | tf_op jit(solution)/shard_map/slice | solution.py:179
  5.3 0.5 %collective-permute-start.1 = (f32[3,16,4,128]{3,2,1,0:T(4,128)}, f32[3,16,4,128]{3,2,1,0:T(4,128)}, u32[]{:S(2)}, u32[]{:S(2)}) collective-permute-start(f32[3,16,4,128]{3,2,1,0:T(4,128)} %param.5), channel_id=1, source_target_pairs={{0,1},{1,0},{2,3},{3,2},{4,5},{5,4},{6,7},{7,6},{8,9},{9,8},{10,11... | collective-permute-start | bytes 294920 | tf_op jit(solution)/shard_map/ppermute | solution.py:180
  5.8 1.5 %collective-permute-done.1 = f32[3,16,4,128]{3,2,1,0:T(4,128)} collective-permute-done((f32[3,16,4,128]{3,2,1,0:T(4,128)}, f32[3,16,4,128]{3,2,1,0:T(4,128)}, u32[]{:S(2)}, u32[]{:S(2)}) %collective-permute-start.1) | collective-permute-done | bytes 98336 | tf_op jit(solution)/shard_map/ppermute | solution.py:180
  7.3 1.1 %maximum_select_fusion = f32[3,32,4,128]{3,2,1,0:T(4,128)S(1)} fusion(f32[3,16,4,128]{3,2,1,0:T(4,128)} %collective-permute-done.1, f32[3,16,4,128]{3,2,1,0:T(4,128)} %param.5, pred[]{:T(512)S(6)} %eq.45), kind=kLoop, calls=%fused_computation.11 | loop fusion | flops 147456 | bytes 393217 | tf_op jit(solution)/shard_map/jit(_where)/select_n | solution.py:183
  8.4 1.3 %add.37 = f32[2,3,32,4,128]{4,3,2,1,0:T(4,128)S(1)} add(f32[2,3,32,4,128]{4,3,2,1,0:T(4,128)} %bitcast.20, f32[2,3,32,4,128]{4,3,2,1,0:T(4,128)} %collective-permute-done) | non-fusion elementwise | flops 98304 | bytes 1179648 | tf_op jit(solution)/shard_map/add | solution.py:181
  9.7 1.0 %broadcast_select_fusion = (f32[288,2,128]{2,1,0:T(2,128)}, f32[288,2,128]{2,1,0:T(2,128)}) fusion(pred[]{:T(512)S(6)} %eq.46, f32[96,4,128]{2,1,0:T(4,128)S(1)} %bitcast.18, f32[192,4,128]{2,1,0:T(4,128)S(1)} %bitcast.16, pred[]{:T(512)} %eq.38), kind=kLoop, calls=%fused_computation.9 | loop fusion | flops 442368 | bytes 1179650 | tf_op jit(solution)/shard_map/jit(_where)/select_n | solution.py:200
  10.7 1.6 %collective-permute-start.2 = (f32[288,2,128]{2,1,0:T(2,128)}, f32[288,2,128]{2,1,0:T(2,128)}, u32[]{:S(2)}, u32[]{:S(2)}) collective-permute-start(f32[288,2,128]{2,1,0:T(2,128)} %get-tuple-element.14), channel_id=1, source_target_pairs={{0,4},{4,0},{8,12},{12,8},{1,5},{5,1},{9,13},{13,9},{2,6},{6,2},{1... | collective-permute-start | bytes 884744 | tf_op jit(solution)/shard_map/ppermute | solution.py:201
  12.3 1.9 %collective-permute-start.3 = (f32[288,2,128]{2,1,0:T(2,128)}, f32[288,2,128]{2,1,0:T(2,128)}, u32[]{:S(2)}, u32[]{:S(2)}) collective-permute-start(f32[288,2,128]{2,1,0:T(2,128)} %get-tuple-element.13), channel_id=1, source_target_pairs={{4,8},{8,4},{5,9},{9,5},{6,10},{10,6},{7,11},{11,7},{20,24},{24,20... | collective-permute-start | bytes 884744 | tf_op jit(solution)/shard_map/ppermute | solution.py:201
  14.2 0.7 %add_convert_fusion.flags_ref = s32[2]{0:T(128)} fusion(pred[1]{0:T(512)(128)(4,1)} %bitcast.1, pred[1]{0:T(512)(128)(4,1)} %bitcast), kind=kLoop, calls=%fused_computation.13 | loop fusion | flops 4 | bytes 10 | tf_op jit(solution)/shard_map/stack | solution.py:202
  14.9 1.9 %pad_maximum_fusion.planes_ref = f32[288,4,128]{2,1,0:T(4,128)} fusion(f32[96,4,128]{2,1,0:T(4,128)} %bitcast.19, f32[192,4,128]{2,1,0:T(4,128)S(1)} %bitcast.17), kind=kLoop, calls=%fused_computation.4 | loop fusion | flops 147456 | bytes 1179648 | tf_op jit(solution)/shard_map/concatenate | solution.py:191
  16.8 3.3 %collective-permute-done.2.refs_0_ = f32[288,2,128]{2,1,0:T(2,128)} collective-permute-done((f32[288,2,128]{2,1,0:T(2,128)}, f32[288,2,128]{2,1,0:T(2,128)}, u32[]{:S(2)}, u32[]{:S(2)}) %collective-permute-start.2) | collective-permute-done | bytes 294944 | tf_op jit(solution)/shard_map/ppermute | solution.py:201
  20.1 3.2 %collective-permute-done.3.refs_1_ = f32[288,2,128]{2,1,0:T(2,128)} collective-permute-done((f32[288,2,128]{2,1,0:T(2,128)}, f32[288,2,128]{2,1,0:T(2,128)}, u32[]{:S(2)}, u32[]{:S(2)}) %collective-permute-start.3) | collective-permute-done | bytes 294944 | tf_op jit(solution)/shard_map/ppermute | solution.py:201
  23.3 2.9 %shard_map.46 = (f32[288,8,128]{2,1,0:T(8,128)}, f32[288,8,2]{2,1,0:T(8,128)}) custom-call(s32[2]{0:T(128)} %add_convert_fusion.flags_ref, f32[288,4,128]{2,1,0:T(4,128)} %pad_maximum_fusion.planes_ref, f32[288,2,128]{2,1,0:T(2,128)} %collective-permute-done.2.refs_0_, f32[288,2,128]{2,1,0:T(2,128)} %collective-permute-done.3.refs_1_), custom_call_target="tpu_custom_call" | custom-call | tf_op jit(solution)/shard_map/pallas_call | solution.py:227
  26.3 1.7 %copy.9 = f32[288,8,2]{0,1,2:T(8,128)S(1)} copy(f32[288,8,2]{2,1,0:T(8,128)} %get-tuple-element.8) | data formatting | bytes 36864 | tf_op jit(solution)/shard_map/layout_constraint | solution.py:134
  28.0 1.5 %collective-permute-start.4 = (f32[288,8,2]{0,1,2:T(8,128)S(1)}, f32[288,8,2]{0,1,2:T(8,128)S(1)}, u32[]{:S(2)}, u32[]{:S(2)}) collective-permute-start(f32[288,8,2]{0,1,2:T(8,128)S(1)} %copy.9), channel_id=1, source_target_pairs={{0,2},{2,0},{1,3},{3,1},{4,6},{6,4},{5,7},{7,5},{8,10},{10,8},{9,1... | collective-permute-start | bytes 55304 | tf_op jit(solution)/shard_map/ppermute | solution.py:237
  29.5 0.7 %and_convert_fusion.inside_ref = f32[8,132]{1,0:T(8,128)} fusion(pred[132]{0:T(512)(128)(4,1)S(1)} %get-tuple-element.15, pred[132]{0:T(512)(128)(4,1)S(1)} %get-tuple-element.16, pred[8]{0:T(512)(128)(4,1)S(1)} %compare_and_fusion), kind=kLoop, calls=%fused_computation.12 | loop fusion | flops 3168 | bytes 4496 | tf_op jit(solution)/shard_map/convert_element_type | solution.py:264
  30.2 1.7 %collective-permute-done.4 = f32[288,8,2]{0,1,2:T(8,128)S(1)} collective-permute-done((f32[288,8,2]{0,1,2:T(8,128)S(1)}, f32[288,8,2]{0,1,2:T(8,128)S(1)}, u32[]{:S(2)}, u32[]{:S(2)}) %collective-permute-start.4) | collective-permute-done | bytes 18464 | tf_op jit(solution)/shard_map/ppermute | solution.py:237
  31.9 1.4 %copy.10.low_ref.high_ref = f32[288,8,2]{2,1,0:T(8,128)} copy(f32[288,8,2]{0,1,2:T(8,128)S(1)} %collective-permute-done.4) | data formatting | bytes 36864 | tf_op jit(solution)/shard_map/ppermute | solution.py:237
  33.3 8.2 %shard_map.47 = f32[2,3,32,4,128]{4,3,2,1,0:T(4,128)} custom-call(f32[288,8,128]{2,1,0:T(8,128)} %get-tuple-element.7.planes_ref, f32[288,8,2]{2,1,0:T(8,128)} %copy.10.low_ref.high_ref, f32[288,8,2]{2,1,0:T(8,128)} %copy.10.low_ref.high_ref, f32[8,132]{1,0:T(8,128)} %and_convert_fusion.inside_ref), custom_call_target="tpu_custom_call" | custom-call | tf_op jit(solution)/shard_map/pallas_call | solution.py:259
  (9 shorter events, 0.1 us)
Async XLA Ops:
  0.0 1.9 %copy-start = (bf16[16,2,3,32,4,128]{5,4,3,2,1,0:T(4,128)(2,1)S(1)}, bf16[16,2,3,32,4,128]{5,4,3,2,1,0:T(4,128)(2,1)}, u32[]{:S(2)}) copy-start(bf16[16,2,3,32,4,128]{5,4,3,2,1,0:T(4,128)(2,1)} %param.4) | copy-start | bytes 9437188
  5.3 3.1 %collective-permute-start = (f32[2,3,32,4,128]{4,3,2,1,0:T(4,128)S(1)}, f32[2,3,32,4,128]{4,3,2,1,0:T(4,128)}, u32[]{:S(2)}, u32[]{:S(2)}) collective-permute-start(f32[2,3,32,4,128]{4,3,2,1,0:T(4,128)S(1)} %bitcast.21), channel_id=1, source_target_pairs={{0,1},{1,0},{2,3},{3,2},{4,5},{5,4},{6,7},{7,6},{8,9},{9,8},{10,11... | collective-permute-start | bytes 1179656 | tf_op jit(solution)/shard_map/ppermute | solution.py:179
  5.3 2.0 %collective-permute-start.1 = (f32[3,16,4,128]{3,2,1,0:T(4,128)}, f32[3,16,4,128]{3,2,1,0:T(4,128)}, u32[]{:S(2)}, u32[]{:S(2)}) collective-permute-start(f32[3,16,4,128]{3,2,1,0:T(4,128)} %param.5), channel_id=1, source_target_pairs={{0,1},{1,0},{2,3},{3,2},{4,5},{5,4},{6,7},{7,6},{8,9},{9,8},{10,11... | collective-permute-start | bytes 294920 | tf_op jit(solution)/shard_map/ppermute | solution.py:180
  8.4 1.3 %copy-start.1 = (f32[3,32,4,128]{3,2,1,0:T(4,128)}, f32[3,32,4,128]{3,2,1,0:T(4,128)S(1)}, u32[]{:S(2)}) copy-start(f32[3,32,4,128]{3,2,1,0:T(4,128)S(1)} %maximum_select_fusion) | copy-start | bytes 589828
  10.7 9.4 %collective-permute-start.2 = (f32[288,2,128]{2,1,0:T(2,128)}, f32[288,2,128]{2,1,0:T(2,128)}, u32[]{:S(2)}, u32[]{:S(2)}) collective-permute-start(f32[288,2,128]{2,1,0:T(2,128)} %get-tuple-element.14), channel_id=1, source_target_pairs={{0,4},{4,0},{8,12},{12,8},{1,5},{5,1},{9,13},{13,9},{2,6},{6,2},{1... | collective-permute-start | bytes 884744 | tf_op jit(solution)/shard_map/ppermute | solution.py:201
  12.3 11.0 %collective-permute-start.3 = (f32[288,2,128]{2,1,0:T(2,128)}, f32[288,2,128]{2,1,0:T(2,128)}, u32[]{:S(2)}, u32[]{:S(2)}) collective-permute-start(f32[288,2,128]{2,1,0:T(2,128)} %get-tuple-element.13), channel_id=1, source_target_pairs={{4,8},{8,4},{5,9},{9,5},{6,10},{10,6},{7,11},{11,7},{20,24},{24,20... | collective-permute-start | bytes 884744 | tf_op jit(solution)/shard_map/ppermute | solution.py:201
  28.0 3.9 %collective-permute-start.4 = (f32[288,8,2]{0,1,2:T(8,128)S(1)}, f32[288,8,2]{0,1,2:T(8,128)S(1)}, u32[]{:S(2)}, u32[]{:S(2)}) collective-permute-start(f32[288,8,2]{0,1,2:T(8,128)S(1)} %copy.9), channel_id=1, source_target_pairs={{0,2},{2,0},{1,3},{3,1},{4,6},{6,4},{5,7},{7,5},{8,10},{10,8},{9,1... | collective-permute-start | bytes 55304 | tf_op jit(solution)/shard_map/ppermute | solution.py:237

commit v12 on v11

--- a/solution.py
+++ b/solution.py
@@ -196,8 +196,22 @@
     x_rounds = list(swap_rounds("xb"))
     y_rounds = list(swap_rounds("yb"))
     x_gots = []
+
+    def rows(lo, hi):
+        shot_rows = partial[1][..., lo:hi, :] + got[..., lo:hi, :]
+        sigma_rows = jnp.where(
+            low_first,
+            jnp.concatenate([conductivity[..., lo:hi, :], sigma_other[..., lo:hi, :]], axis=1),
+            jnp.concatenate([sigma_other[..., lo:hi, :], conductivity[..., lo:hi, :]], axis=1),
+        )
+        return jnp.concatenate(
+            [shot_rows.reshape(-1, hi - lo, width_y), sigma_rows.reshape(-1, hi - lo, width_y)], axis=0
+        )
+
+    head_x = rows(0, w)
+    tail_x = rows(width_x - w, width_x)
     for pairs, lower in x_rounds:
-        send = row_major(jnp.where(lower, planes[:, width_x - w:], planes[:, :w]))
+        send = row_major(jnp.where(lower, tail_x, head_x))
         x_gots.append(row_major(lax.ppermute(send, "xb", pairs)))
     flags = jnp.stack(
         [(lax.axis_index("xb") % 2 == 0).astype(jnp.int32)]

time: 41.8 us -> 42.2 us (level)
  waiting for transfers between devices: 9.66 us -> 6.77 us
  local copies, waits for them, and re-layouts: 6.33 us -> 8.99 us
    slice x0 -> x2, local copies, waits for them, and re-layouts: none -> 2.65 us  [the longest x1 1.64 us: rows(): conductivity[..., lo:hi, :]]
    ppermute x1, waiting for transfers between devices: 1.48 us -> 0.01 us  [body(): sigma_other = lax.ppermute(conductivity, 'tx', tx_ring)]
    ppermute x2, waiting for transfers between devices: 6.52 us -> 5.07 us  [body(): x_gots.append(row_major(lax.ppermute(send, 'xb', pairs)))]
    add x0 -> x1, other arithmetic: none -> 1.36 us  [rows(): shot_rows = partial[1][..., lo:hi, :] + got[..., lo:hi, :]]
    concatenate x1, other arithmetic: 1.88 us -> 0.96 us  [body(): jnp.concatenate([shot.reshape(-1, width_x, width_y), sigma_all.reshape(-1...]
    select_n x1 -> x2, other arithmetic: 1.05 us -> 1.31 us  [the longest x1 1.05 us: rows(): jnp.where(low_first, jnp.concatenate([conductivity[..., lo:hi, :], sigma_...]
  transfers between devices with their start and end apart: 5 -> 5, of which waited for: 4 -> 3; matrix products, arithmetic and copies ran while one was open for 10% -> 19% of each run, Pallas kernels for 0% -> 0%
where the time goes in v12:
time: 42.2 us; the launch traced here: 41.8 us
  Pallas kernels  11.2 us (27%)
  local copies, waits for them, and re-layouts  8.99 us (21%)
  other arithmetic  7.26 us (17%)
  waiting for transfers between devices  6.77 us (16%)
  starting transfers between devices  5.61 us (13%)
  matrix products  1.93 us (5%)
    pallas_call x1, Pallas kernels, body(): pl.pallas_call(sweeps_kernel, out_shape=jax.ShapeDtypeStruct(out_shape, j...  8.18 us
    ppermute x2, waiting for transfers between devices, body(): x_gots.append(row_major(lax.ppermute(send, 'xb', pairs)))  5.07 us
    ppermute x2, starting transfers between devices, body(): x_gots.append(row_major(lax.ppermute(send, 'xb', pairs)))  3.55 us
    pallas_call x1, Pallas kernels, body(): pl.pallas_call(x_kernel, out_shape=[jax.ShapeDtypeStruct((planes.shape[0]...  2.97 us
    dot_general x1, matrix products, body(): lax.dot_general(weights, primaries, (((1,), (0,)), ((), ())), preferred_e...  1.93 us
    another operation x1, local copies, waits for them, and re-layouts, row_major(): with_layout_constraint(x, Layout(major_to_minor=tuple(range(x.ndim))))  1.73 us
    ppermute x1, waiting for transfers between devices, body(): lax.ppermute(row_major(send), 'yb', pairs)  1.68 us
    slice x1, local copies, waits for them, and re-layouts, rows(): conductivity[..., lo:hi, :]  1.64 us
  transfers between devices with their start and end apart: 5, of which 3 were waited for; matrix products, arithmetic and copies ran while one was open for 19% of the time, Pallas kernels for 0%

profile of v12, /device:TPU:16, one launch (start us, length us, event | category | flops | bytes accessed | tf_op | source)
XLA Modules:
  0.0 41.8 jit_solution(17282708823934005253)
XLA Ops:
  0.0 0.9 %reshape.33 = s32[2,16]{1,0:T(2,128)S(1)} reshape(s32[32]{0:T(128)} %param.6) | data formatting | bytes 256 | tf_op jit(solution)/shard_map/reshape | solution.py:171
  0.9 0.8 %reshape.34 = s32[2,16]{1,0:T(2,128)S(1)} reshape(s32[32]{0:T(128)} %param.7) | data formatting | bytes 256 | tf_op jit(solution)/shard_map/reshape | solution.py:172
  1.9 1.9 %fusion = f32[2,2,3,32,4,128]{5,0,4,3,2,1:T(2,128)S(1)} fusion(bf16[16,2,3,32,4,128]{5,4,3,2,1,0:T(4,128)(2,1)S(1)} %copy-done, s32[16]{0:T(128)S(1)} %get-tuple-element.10, s32[16]{0:T(128)S(1)} %get-tuple-element.9, s32[2]{0:T(128)S(1)} %pad_add_fusion), kind=kOutput, calls=%fused_computation | convolution fusion | flops 6291584 | bytes 3932296 | tf_op jit(solution)/shard_map/dot_general | solution.py:175
  3.8 1.4 %fusion.13 = (f32[1,2,3,32,4,128]{5,0,4,3,2,1:T(1,128)}, f32[1,2,3,32,4,128]{5,0,4,3,2,1:T(1,128)S(1)}) fusion(f32[2,2,3,32,4,128]{5,0,4,3,2,1:T(2,128)S(1)} %fusion), kind=kLoop, calls=%fused_computation.31 | loop fusion | bytes 1572864 | tf_op jit(solution)/shard_map/slice | solution.py:179
  5.3 0.5 %collective-permute-start.1 = (f32[3,16,4,128]{3,2,1,0:T(4,128)}, f32[3,16,4,128]{3,2,1,0:T(4,128)}, u32[]{:S(2)}, u32[]{:S(2)}) collective-permute-start(f32[3,16,4,128]{3,2,1,0:T(4,128)} %param.5), channel_id=1, source_target_pairs={{0,1},{1,0},{2,3},{3,2},{4,5},{5,4},{6,7},{7,6},{8,9},{9,8},{10,11... | collective-permute-start | bytes 294920 | tf_op jit(solution)/shard_map/ppermute | solution.py:180
  5.8 1.6 %fusion.14 = (f32[3,16,2,128]{3,2,1,0:T(2,128)}, f32[3,16,2,128]{3,2,1,0:T(2,128)}) fusion(f32[3,16,4,128]{3,2,1,0:T(4,128)} %param.5), kind=kLoop, calls=%fused_computation.32 | loop fusion | bytes 196608 | tf_op jit(solution)/shard_map/slice | solution.py:204
  7.5 1.0 %fusion.15 = (f32[3,16,2,128]{3,2,1,0:T(2,128)S(1)}, f32[3,16,2,128]{3,2,1,0:T(2,128)S(1)}) fusion(f32[3,16,4,128]{3,2,1,0:T(4,128)} %collective-permute-done.1), kind=kLoop, calls=%fused_computation.33 | loop fusion | bytes 196608 | tf_op jit(solution)/shard_map/slice | solution.py:204
  8.5 1.0 %maximum_select_fusion.1 = (f32[3,32,2,128]{3,2,1,0:T(2,128)S(1)}, f32[3,32,2,128]{3,2,1,0:T(2,128)S(1)}) fusion(f32[3,16,2,128]{3,2,1,0:T(2,128)S(1)} %get-tuple-element.19, f32[3,16,2,128]{3,2,1,0:T(2,128)} %get-tuple-element.17, pred[]{:T(512)S(6)} %eq.45, f32[3,16,2,128]{3,2,1,0:T(2,128)} %get-tuple-element.18, f32[3,16,2,128]{3,2,1,0:T(2,128)S(1)} %get-tuple-element.20), kind=kLoop, calls=%fused_computation.10 | loop fusion | flops 147456 | bytes 393217 | tf_op jit(solution)/shard_map/jit(_where)/select_n | solution.py:202
  9.5 1.4 %slice_add_fusion.1 = (f32[2,3,32,2,128]{4,3,2,1,0:T(2,128)S(1)}, f32[2,3,32,2,128]{4,3,2,1,0:T(2,128)S(1)}) fusion(f32[2,3,32,4,128]{4,3,2,1,0:T(4,128)} %collective-permute-done, f32[2,3,32,4,128]{4,3,2,1,0:T(4,128)S(1)} %bitcast.20), kind=kLoop, calls=%fused_computation.8 | loop fusion | flops 98304 | bytes 1179648 | tf_op jit(solution)/shard_map/add | solution.py:201
  11.2 1.6 %collective-permute-start.2 = (f32[288,2,128]{2,1,0:T(2,128)S(1)}, f32[288,2,128]{2,1,0:T(2,128)}, u32[]{:S(2)}, u32[]{:S(2)}) collective-permute-start(f32[288,2,128]{2,1,0:T(2,128)S(1)} %get-tuple-element.16), channel_id=1, source_target_pairs={{0,4},{4,0},{8,12},{12,8},{1,5},{5,1},{9,13},{13,9},{2,6},{6,2},{1... | collective-permute-start | bytes 884744 | tf_op jit(solution)/shard_map/ppermute | solution.py:215
  12.8 1.9 %collective-permute-start.3 = (f32[288,2,128]{2,1,0:T(2,128)S(1)}, f32[288,2,128]{2,1,0:T(2,128)}, u32[]{:S(2)}, u32[]{:S(2)}) collective-permute-start(f32[288,2,128]{2,1,0:T(2,128)S(1)} %get-tuple-element.15), channel_id=1, source_target_pairs={{4,8},{8,4},{5,9},{9,5},{6,10},{10,6},{7,11},{11,7},{20,24},{24,20... | collective-permute-start | bytes 884744 | tf_op jit(solution)/shard_map/ppermute | solution.py:215
  14.7 0.6 %add_convert_fusion.flags_ref = s32[2]{0:T(128)} fusion(pred[1]{0:T(512)(128)(4,1)} %bitcast.1, pred[1]{0:T(512)(128)(4,1)} %bitcast), kind=kLoop, calls=%fused_computation.13 | loop fusion | flops 4 | bytes 10 | tf_op jit(solution)/shard_map/stack | solution.py:216
  15.3 1.1 %maximum_select_fusion = f32[3,32,4,128]{3,2,1,0:T(4,128)S(1)} fusion(f32[3,16,4,128]{3,2,1,0:T(4,128)} %collective-permute-done.1, f32[3,16,4,128]{3,2,1,0:T(4,128)} %param.5, pred[]{:T(512)S(6)} %eq.45), kind=kLoop, calls=%fused_computation.9 | loop fusion | flops 147456 | bytes 393217 | tf_op jit(solution)/shard_map/jit(_where)/select_n | solution.py:183
  16.4 1.1 %add.43 = f32[2,3,32,4,128]{4,3,2,1,0:T(4,128)S(1)} add(f32[2,3,32,4,128]{4,3,2,1,0:T(4,128)S(1)} %bitcast.21, f32[2,3,32,4,128]{4,3,2,1,0:T(4,128)} %collective-permute-done) | non-fusion elementwise | flops 98304 | bytes 1179648 | tf_op jit(solution)/shard_map/add | solution.py:181
  17.5 1.0 %pad_maximum_fusion.planes_ref = f32[288,4,128]{2,1,0:T(4,128)} fusion(f32[96,4,128]{2,1,0:T(4,128)S(1)} %bitcast.23, f32[192,4,128]{2,1,0:T(4,128)S(1)} %bitcast.22), kind=kLoop, calls=%fused_computation.2 | loop fusion | flops 147456 | bytes 1179648 | tf_op jit(solution)/shard_map/concatenate | solution.py:191
  18.5 1.9 %collective-permute-done.2.refs_0_ = f32[288,2,128]{2,1,0:T(2,128)} collective-permute-done((f32[288,2,128]{2,1,0:T(2,128)S(1)}, f32[288,2,128]{2,1,0:T(2,128)}, u32[]{:S(2)}, u32[]{:S(2)}) %collective-permute-start.2) | collective-permute-done | bytes 294944 | tf_op jit(solution)/shard_map/ppermute | solution.py:215
  20.4 3.2 %collective-permute-done.3.refs_1_ = f32[288,2,128]{2,1,0:T(2,128)} collective-permute-done((f32[288,2,128]{2,1,0:T(2,128)S(1)}, f32[288,2,128]{2,1,0:T(2,128)}, u32[]{:S(2)}, u32[]{:S(2)}) %collective-permute-start.3) | collective-permute-done | bytes 294944 | tf_op jit(solution)/shard_map/ppermute | solution.py:215
  23.6 3.0 %shard_map.46 = (f32[288,8,128]{2,1,0:T(8,128)}, f32[288,8,2]{2,1,0:T(8,128)}) custom-call(s32[2]{0:T(128)} %add_convert_fusion.flags_ref, f32[288,4,128]{2,1,0:T(4,128)} %pad_maximum_fusion.planes_ref, f32[288,2,128]{2,1,0:T(2,128)} %collective-permute-done.2.refs_0_, f32[288,2,128]{2,1,0:T(2,128)} %collective-permute-done.3.refs_1_), custom_call_target="tpu_custom_call" | custom-call | tf_op jit(solution)/shard_map/pallas_call | solution.py:241
  26.6 1.7 %copy.9 = f32[288,8,2]{0,1,2:T(8,128)S(1)} copy(f32[288,8,2]{2,1,0:T(8,128)} %get-tuple-element.8) | data formatting | bytes 36864 | tf_op jit(solution)/shard_map/layout_constraint | solution.py:134
  28.3 1.5 %collective-permute-start.4 = (f32[288,8,2]{0,1,2:T(8,128)S(1)}, f32[288,8,2]{0,1,2:T(8,128)S(1)}, u32[]{:S(2)}, u32[]{:S(2)}) collective-permute-start(f32[288,8,2]{0,1,2:T(8,128)S(1)} %copy.9), channel_id=1, source_target_pairs={{0,2},{2,0},{1,3},{3,1},{4,6},{6,4},{5,7},{7,5},{8,10},{10,8},{9,1... | collective-permute-start | bytes 55304 | tf_op jit(solution)/shard_map/ppermute | solution.py:251
  29.8 0.7 %and_convert_fusion.inside_ref = f32[8,132]{1,0:T(8,128)} fusion(pred[132]{0:T(512)(128)(4,1)S(1)} %get-tuple-element.23, pred[132]{0:T(512)(128)(4,1)S(1)} %get-tuple-element.24, pred[8]{0:T(512)(128)(4,1)S(1)} %compare_and_fusion), kind=kLoop, calls=%fused_computation.12 | loop fusion | flops 3168 | bytes 4496 | tf_op jit(solution)/shard_map/convert_element_type | solution.py:278
  30.5 1.7 %collective-permute-done.4 = f32[288,8,2]{0,1,2:T(8,128)S(1)} collective-permute-done((f32[288,8,2]{0,1,2:T(8,128)S(1)}, f32[288,8,2]{0,1,2:T(8,128)S(1)}, u32[]{:S(2)}, u32[]{:S(2)}) %collective-permute-start.4) | collective-permute-done | bytes 18464 | tf_op jit(solution)/shard_map/ppermute | solution.py:251
  32.2 1.5 %copy.10.low_ref.high_ref = f32[288,8,2]{2,1,0:T(8,128)} copy(f32[288,8,2]{0,1,2:T(8,128)S(1)} %collective-permute-done.4) | data formatting | bytes 36864 | tf_op jit(solution)/shard_map/ppermute | solution.py:251
  33.6 8.2 %shard_map.47 = f32[2,3,32,4,128]{4,3,2,1,0:T(4,128)} custom-call(f32[288,8,128]{2,1,0:T(8,128)} %get-tuple-element.7.planes_ref, f32[288,8,2]{2,1,0:T(8,128)} %copy.10.low_ref.high_ref, f32[288,8,2]{2,1,0:T(8,128)} %copy.10.low_ref.high_ref, f32[8,132]{1,0:T(8,128)} %and_convert_fusion.inside_ref), custom_call_target="tpu_custom_call" | custom-call | tf_op jit(solution)/shard_map/pallas_call | solution.py:273
  (11 shorter events, 0.5 us)
Async XLA Ops:
  0.0 1.9 %copy-start = (bf16[16,2,3,32,4,128]{5,4,3,2,1,0:T(4,128)(2,1)S(1)}, bf16[16,2,3,32,4,128]{5,4,3,2,1,0:T(4,128)(2,1)}, u32[]{:S(2)}) copy-start(bf16[16,2,3,32,4,128]{5,4,3,2,1,0:T(4,128)(2,1)} %param.4) | copy-start | bytes 9437188
  5.3 4.3 %collective-permute-start = (f32[2,3,32,4,128]{4,3,2,1,0:T(4,128)}, f32[2,3,32,4,128]{4,3,2,1,0:T(4,128)}, u32[]{:S(2)}, u32[]{:S(2)}) collective-permute-start(f32[2,3,32,4,128]{4,3,2,1,0:T(4,128)} %bitcast.7), channel_id=1, source_target_pairs={{0,1},{1,0},{2,3},{3,2},{4,5},{5,4},{6,7},{7,6},{8,9},{9,8},{10,11... | collective-permute-start | bytes 1179656 | tf_op jit(solution)/shard_map/ppermute | solution.py:179
  5.3 2.2 %collective-permute-start.1 = (f32[3,16,4,128]{3,2,1,0:T(4,128)}, f32[3,16,4,128]{3,2,1,0:T(4,128)}, u32[]{:S(2)}, u32[]{:S(2)}) collective-permute-start(f32[3,16,4,128]{3,2,1,0:T(4,128)} %param.5), channel_id=1, source_target_pairs={{0,1},{1,0},{2,3},{3,2},{4,5},{5,4},{6,7},{7,6},{8,9},{9,8},{10,11... | collective-permute-start | bytes 294920 | tf_op jit(solution)/shard_map/ppermute | solution.py:180
  11.2 9.2 %collective-permute-start.2 = (f32[288,2,128]{2,1,0:T(2,128)S(1)}, f32[288,2,128]{2,1,0:T(2,128)}, u32[]{:S(2)}, u32[]{:S(2)}) collective-permute-start(f32[288,2,128]{2,1,0:T(2,128)S(1)} %get-tuple-element.16), channel_id=1, source_target_pairs={{0,4},{4,0},{8,12},{12,8},{1,5},{5,1},{9,13},{13,9},{2,6},{6,2},{1... | collective-permute-start | bytes 884744 | tf_op jit(solution)/shard_map/ppermute | solution.py:215
  12.8 10.8 %collective-permute-start.3 = (f32[288,2,128]{2,1,0:T(2,128)S(1)}, f32[288,2,128]{2,1,0:T(2,128)}, u32[]{:S(2)}, u32[]{:S(2)}) collective-permute-start(f32[288,2,128]{2,1,0:T(2,128)S(1)} %get-tuple-element.15), channel_id=1, source_target_pairs={{4,8},{8,4},{5,9},{9,5},{6,10},{10,6},{7,11},{11,7},{20,24},{24,20... | collective-permute-start | bytes 884744 | tf_op jit(solution)/shard_map/ppermute | solution.py:215
  28.3 3.9 %collective-permute-start.4 = (f32[288,8,2]{0,1,2:T(8,128)S(1)}, f32[288,8,2]{0,1,2:T(8,128)S(1)}, u32[]{:S(2)}, u32[]{:S(2)}) collective-permute-start(f32[288,8,2]{0,1,2:T(8,128)S(1)} %copy.9), channel_id=1, source_target_pairs={{0,2},{2,0},{1,3},{3,1},{4,6},{6,4},{5,7},{7,5},{8,10},{10,8},{9,1... | collective-permute-start | bytes 55304 | tf_op jit(solution)/shard_map/ppermute | solution.py:251

commit v13 on v11

--- a/solution.py
+++ b/solution.py
@@ -178,60 +178,79 @@
     tx_ring = [(i, (i + 1) % n_tx) for i in range(n_tx)]
     got = lax.ppermute(partial[0], "tx", tx_ring)
     sigma_other = lax.ppermute(conductivity, "tx", tx_ring)
-    shot = partial[1] + got
-    low_first = tx_index == 0
-    sigma_all = jnp.where(
-        low_first,
-        jnp.concatenate([conductivity, sigma_other], axis=1),
-        jnp.concatenate([sigma_other, conductivity], axis=1),
-    )
-    shot_planes = shot.shape[0] * shot.shape[1] * depth
+    shot_planes = partial.shape[1] * partial.shape[2] * depth
     ext_x = width_x + 2 * SWEEPS
     ext_y = width_y + 2 * SWEEPS
-    planes = jnp.concatenate(
-        [shot.reshape(-1, width_x, width_y), sigma_all.reshape(-1, width_x, width_y)], axis=0
-    )
-    planes = row_major(planes)
     w = SWEEPS
     x_rounds = list(swap_rounds("xb"))
     y_rounds = list(swap_rounds("yb"))
-    x_gots = []
-    for pairs, lower in x_rounds:
-        send = row_major(jnp.where(lower, planes[:, width_x - w:], planes[:, :w]))
-        x_gots.append(row_major(lax.ppermute(send, "xb", pairs)))
+    n_x = len(x_rounds)
+    n_y = len(y_rounds)
     flags = jnp.stack(
-        [(lax.axis_index("xb") % 2 == 0).astype(jnp.int32)]
+        [(tx_index == 0).astype(jnp.int32), (lax.axis_index("xb") % 2 == 0).astype(jnp.int32)]
+        + [lower.astype(jnp.int32) for _, lower in x_rounds]
         + [lower.astype(jnp.int32) for _, lower in y_rounds]
     )
-    n_x = len(x_gots)
-    n_y = len(y_rounds)
-    face_shape = (planes.shape[0], ext_x, w)
-
-    def x_kernel(flags_ref, planes_ref, *refs):
+    pieces = (partial[1], got, conductivity, sigma_other)
+    n_planes = shot_planes + 2 * conductivity.shape[0] * conductivity.shape[1]
+    vmem = pl.BlockSpec(memory_space=pltpu.VMEM)
+    smem = pl.BlockSpec(memory_space=pltpu.SMEM)
+
+    def planes_of(flags_ref, own_ref, got_ref, sigma_ref, other_ref):
+        shot = (own_ref[...] + got_ref[...]).reshape(shot_planes, width_x, width_y)
+        mine = sigma_ref[...]
+        theirs = other_ref[...]
+        sigma = jnp.where(
+            flags_ref[0] == 1,
+            jnp.concatenate([mine, theirs], axis=1),
+            jnp.concatenate([theirs, mine], axis=1),
+        ).reshape(-1, width_x, width_y)
+        return jnp.concatenate([shot, sigma], axis=0)
+
+    def send_kernel(flags_ref, own_ref, got_ref, sigma_ref, other_ref, *send_refs):
+        cells = planes_of(flags_ref, own_ref, got_ref, sigma_ref, other_ref)
+        head = cells[:, :w]
+        tail = cells[:, width_x - w:]
+        for k in range(n_x):
+            send_refs[k][...] = jnp.where(flags_ref[2 + k] == 1, tail, head)
+
+    x_sends = pl.pallas_call(
+        send_kernel,
+        out_shape=[jax.ShapeDtypeStruct((n_planes, w, width_y), jnp.float32)] * n_x,
+        in_specs=[smem] + [vmem] * 4,
+        out_specs=[vmem] * n_x,
+    )(flags, *pieces)
+    x_gots = [
+        row_major(lax.ppermute(row_major(send), "xb", pairs))
+        for send, (pairs, _) in zip(x_sends, x_rounds)
+    ]
+    face_shape = (n_planes, ext_x, w)
+
+    def x_kernel(flags_ref, own_ref, got_ref, sigma_ref, other_ref, *refs):
         got_refs = refs[:n_x]
         planes_x_ref = refs[n_x]
         send_refs = refs[n_x + 1:]
         if n_x == 1:
             low = high = got_refs[0][...]
         else:
-            even = flags_ref[0] == 1
+            even = flags_ref[1] == 1
             high = jnp.where(even, got_refs[0][...], got_refs[1][...])
             low = jnp.where(even, got_refs[1][...], got_refs[0][...])
-        cells = jnp.concatenate([low, planes_ref[...], high], axis=1)
+        middle = planes_of(flags_ref, own_ref, got_ref, sigma_ref, other_ref)
+        cells = jnp.concatenate([low, middle, high], axis=1)
         planes_x_ref[...] = cells
         head = cells[:, :, :w]
         tail = cells[:, :, width_y - w:]
         for k in range(n_y):
-            send_refs[k][...] = jnp.where(flags_ref[1 + k] == 1, tail, head)
+            send_refs[k][...] = jnp.where(flags_ref[2 + n_x + k] == 1, tail, head)
 
     outs = pl.pallas_call(
         x_kernel,
-        out_shape=[jax.ShapeDtypeStruct((planes.shape[0], ext_x, width_y), jnp.float32)]
+        out_shape=[jax.ShapeDtypeStruct((n_planes, ext_x, width_y), jnp.float32)]
         + [jax.ShapeDtypeStruct(face_shape, jnp.float32)] * n_y,
-        in_specs=[pl.BlockSpec(memory_space=pltpu.SMEM)]
-        + [pl.BlockSpec(memory_space=pltpu.VMEM)] * (1 + n_x),
-        out_specs=[pl.BlockSpec(memory_space=pltpu.VMEM)] * (1 + n_y),
-    )(flags, planes, *x_gots)
+        in_specs=[smem] + [vmem] * (4 + n_x),
+        out_specs=[vmem] * (1 + n_y),
+    )(flags, *pieces, *x_gots)
     planes = outs[0]
     y_gots = [
         row_major(lax.ppermute(row_major(send), "yb", pairs))

time: 41.8 us -> 41.6 us (level)
  other arithmetic: 6.84 us -> 1.33 us
  Pallas kernels: 11.1 us -> 13.5 us
  waiting for transfers between devices: 9.66 us -> 11.8 us
  local copies, waits for them, and re-layouts: 6.33 us -> 7.32 us
    ppermute x2, waiting for transfers between devices: 6.52 us -> 9.01 us  [body(): lax.ppermute(row_major(send), 'xb', pairs)]
    pallas_call x1 -> x2, Pallas kernels: 2.95 us -> 5.28 us  [the longest x1 3.11 us: body(): pl.pallas_call(x_kernel, out_shape=[jax.ShapeDtypeStruct((n_planes, ext_x...]
    select_n x2 -> x0, other arithmetic: 2.16 us -> none  [the longest x1 1.12 us: body(): jnp.where(low_first, jnp.concatenate([conductivity, sigma_other], axis=1)...]
    concatenate x1 -> x0, other arithmetic: 1.88 us -> none  [body(): jnp.concatenate([shot.reshape(-1, width_x, width_y), sigma_all.reshape(-1...]
    add x1 -> x0, other arithmetic: 1.29 us -> none  [body(): shot = partial[1] + got]
    unnamed x4 -> x6, local copies, waits for them, and re-layouts: 0.05 us -> 0.8 us
  transfers between devices with their start and end apart: 5 -> 5, of which waited for: 4 -> 4; matrix products, arithmetic and copies ran while one was open for 10% -> 3% of each run, Pallas kernels for 0% -> 0%
where the time goes in v13:
time: 41.6 us; the launch traced here: 41.4 us
  Pallas kernels  13.5 us (32%)
  waiting for transfers between devices  11.8 us (28%)
  local copies, waits for them, and re-layouts  7.32 us (18%)
  starting transfers between devices  5.55 us (13%)
  matrix products  1.93 us (5%)
  other arithmetic  1.33 us (3%)
    ppermute x2, waiting for transfers between devices, body(): lax.ppermute(row_major(send), 'xb', pairs)  9.01 us
    pallas_call x1, Pallas kernels, body(): pl.pallas_call(sweeps_kernel, out_shape=jax.ShapeDtypeStruct(out_shape, j...  8.18 us
    ppermute x2, starting transfers between devices, body(): lax.ppermute(row_major(send), 'xb', pairs)  3.49 us
    pallas_call x1, Pallas kernels, body(): pl.pallas_call(x_kernel, out_shape=[jax.ShapeDtypeStruct((n_planes, ext_x...  3.11 us
    pallas_call x1, Pallas kernels, body(): pl.pallas_call(send_kernel, out_shape=[jax.ShapeDtypeStruct((n_planes, w,...  2.17 us
    dot_general x1, matrix products, body(): lax.dot_general(weights, primaries, (((1,), (0,)), ((), ())), preferred_e...  1.93 us
    another operation x1, local copies, waits for them, and re-layouts, row_major(): with_layout_constraint(x, Layout(major_to_minor=tuple(range(x.ndim))))  1.73 us
    ppermute x1, waiting for transfers between devices, body(): lax.ppermute(row_major(send), 'yb', pairs)  1.67 us
  transfers between devices with their start and end apart: 5, of which 4 were waited for; matrix products, arithmetic and copies ran while one was open for 3% of the time, Pallas kernels for 0%

profile of v13, /device:TPU:16, one launch (start us, length us, event | category | flops | bytes accessed | tf_op | source)
XLA Modules:
  0.0 41.4 jit_solution(2337734110211130906)
XLA Ops:
  0.0 0.9 %reshape.10 = s32[2,16]{1,0:T(2,128)S(1)} reshape(s32[32]{0:T(128)} %param.7) | data formatting | bytes 256 | tf_op jit(solution)/shard_map/reshape | solution.py:172
  0.9 0.8 %reshape.9 = s32[2,16]{1,0:T(2,128)S(1)} reshape(s32[32]{0:T(128)} %param.6) | data formatting | bytes 256 | tf_op jit(solution)/shard_map/reshape | solution.py:171
  1.7 0.1 pad_add_fusion
  1.8 0.1 select_reduce_fusion.1
  1.9 0.0 copy-done
  1.9 1.9 %fusion = f32[2,2,3,32,4,128]{5,0,4,3,2,1:T(2,128)S(1)} fusion(bf16[16,2,3,32,4,128]{5,4,3,2,1,0:T(4,128)(2,1)S(1)} %copy-done, s32[16]{0:T(128)S(1)} %get-tuple-element.14, s32[16]{0:T(128)S(1)} %get-tuple-element.13, s32[2]{0:T(128)S(1)} %pad_add_fusion), kind=kOutput, calls=%fused_computation | convolution fusion | flops 6291584 | bytes 3932296 | tf_op jit(solution)/shard_map/dot_general | solution.py:175
  3.8 1.5 %fusion.13 = (f32[1,2,3,32,4,128]{5,0,4,3,2,1:T(1,128)}, f32[1,2,3,32,4,128]{5,0,4,3,2,1:T(1,128)}) fusion(f32[2,2,3,32,4,128]{5,0,4,3,2,1:T(2,128)S(1)} %fusion), kind=kLoop, calls=%fused_computation.20 | loop fusion | bytes 1572864 | tf_op jit(solution)/shard_map/slice | solution.py:179
  5.4 0.5 %collective-permute-start.1 = (f32[3,16,4,128]{3,2,1,0:T(4,128)}, f32[3,16,4,128]{3,2,1,0:T(4,128)}, u32[]{:S(2)}, u32[]{:S(2)}) collective-permute-start(f32[3,16,4,128]{3,2,1,0:T(4,128)} %sigma_ref.3), channel_id=1, source_target_pairs={{0,1},{1,0},{2,3},{3,2},{4,5},{5,4},{6,7},{7,6},{8,9},{9,8},{10,11... | collective-permute-start | bytes 294920 | tf_op jit(solution)/shard_map/ppermute | solution.py:180
  5.9 0.1 stack.35
  6.0 0.5 %stack.36.flags_ref = s32[5]{0:T(128)} convert(pred[5]{0:T(512)(128)(4,1)S(1)} %stack.35) | non-fusion elementwise | flops 5 | bytes 25 | tf_op jit(solution)/shard_map/stack | solution.py:189
  6.5 1.1 %collective-permute-done.1.other_ref = f32[3,16,4,128]{3,2,1,0:T(4,128)} collective-permute-done((f32[3,16,4,128]{3,2,1,0:T(4,128)}, f32[3,16,4,128]{3,2,1,0:T(4,128)}, u32[]{:S(2)}, u32[]{:S(2)}) %collective-permute-start.1) | collective-permute-done | bytes 98336 | tf_op jit(solution)/shard_map/ppermute | solution.py:180
  7.6 0.7 %copy-done.1 = f32[2,3,32,4,128]{4,3,2,1,0:T(4,128)} copy-done((f32[2,3,32,4,128]{4,3,2,1,0:T(4,128)}, f32[2,3,32,4,128]{4,3,2,1,0:T(4,128)S(1)}, u32[]{:S(2)}) %copy-start.1) | copy-done | bytes 393240
  8.3 2.2 %shard_map.46 = (f32[288,2,128]{2,1,0:T(2,128)}, f32[288,2,128]{2,1,0:T(2,128)}) custom-call(s32[5]{0:T(128)} %stack.36.flags_ref, f32[2,3,32,4,128]{4,3,2,1,0:T(4,128)} %bitcast.18, f32[2,3,32,4,128]{4,3,2,1,0:T(4,128)} %copy-done.1, f32[3,16,4,128]{3,2,1,0:T(4,128)} %sigma_ref.3, f32[3,16,4,128]{3,2,1,0:T(4,128)} %collective-permute-done.1.other_ref), custom_call_target="tpu_custom_call" | custom-call | tf_op jit(solution)/shard_map/pallas_call | solution.py:217
  10.5 1.6 %collective-permute-start.2 = (f32[288,2,128]{2,1,0:T(2,128)}, f32[288,2,128]{2,1,0:T(2,128)S(1)}, u32[]{:S(2)}, u32[]{:S(2)}) collective-permute-start(f32[288,2,128]{2,1,0:T(2,128)} %get-tuple-element.9), channel_id=1, source_target_pairs={{0,4},{4,0},{8,12},{12,8},{1,5},{5,1},{9,13},{13,9},{2,6},{6,2},{1... | collective-permute-start | bytes 884744 | tf_op jit(solution)/shard_map/ppermute | solution.py:224
  12.1 1.9 %collective-permute-start.3 = (f32[288,2,128]{2,1,0:T(2,128)}, f32[288,2,128]{2,1,0:T(2,128)}, u32[]{:S(2)}, u32[]{:S(2)}) collective-permute-start(f32[288,2,128]{2,1,0:T(2,128)} %get-tuple-element.10), channel_id=1, source_target_pairs={{4,8},{8,4},{5,9},{9,5},{6,10},{10,6},{7,11},{11,7},{20,24},{24,20... | collective-permute-start | bytes 884744 | tf_op jit(solution)/shard_map/ppermute | solution.py:224
  14.0 5.7 %collective-permute-done.2.refs_0_ = f32[288,2,128]{2,1,0:T(2,128)S(1)} collective-permute-done((f32[288,2,128]{2,1,0:T(2,128)}, f32[288,2,128]{2,1,0:T(2,128)S(1)}, u32[]{:S(2)}, u32[]{:S(2)}) %collective-permute-start.2) | collective-permute-done | bytes 294944 | tf_op jit(solution)/shard_map/ppermute | solution.py:224
  19.8 3.3 %collective-permute-done.3.refs_1_ = f32[288,2,128]{2,1,0:T(2,128)} collective-permute-done((f32[288,2,128]{2,1,0:T(2,128)}, f32[288,2,128]{2,1,0:T(2,128)}, u32[]{:S(2)}, u32[]{:S(2)}) %collective-permute-start.3) | collective-permute-done | bytes 294944 | tf_op jit(solution)/shard_map/ppermute | solution.py:224
  23.1 3.1 %shard_map.47 = (f32[288,8,128]{2,1,0:T(8,128)}, f32[288,8,2]{2,1,0:T(8,128)}) custom-call(s32[5]{0:T(128)} %stack.36.flags_ref, f32[2,3,32,4,128]{4,3,2,1,0:T(4,128)} %bitcast.19, f32[2,3,32,4,128]{4,3,2,1,0:T(4,128)} %copy-done.1, f32[3,16,4,128]{3,2,1,0:T(4,128)} %sigma_ref.3, f32[3,16,4,128]{3,2,1,0:T(4,128)} %collective-permute-done.1.other_ref, ...), custom_call_target="tpu_custom_call" | custom-call | tf_op jit(solution)/shard_map/pallas_call | solution.py:247
  26.2 1.7 %copy.11 = f32[288,8,2]{0,1,2:T(8,128)S(1)} copy(f32[288,8,2]{2,1,0:T(8,128)} %get-tuple-element.12) | data formatting | bytes 36864 | tf_op jit(solution)/shard_map/layout_constraint | solution.py:134
  27.9 1.5 %collective-permute-start.4 = (f32[288,8,2]{0,1,2:T(8,128)S(1)}, f32[288,8,2]{0,1,2:T(8,128)S(1)}, u32[]{:S(2)}, u32[]{:S(2)}) collective-permute-start(f32[288,8,2]{0,1,2:T(8,128)S(1)} %copy.11), channel_id=1, source_target_pairs={{0,2},{2,0},{1,3},{3,1},{4,6},{6,4},{5,7},{7,5},{8,10},{10,8},{9,1... | collective-permute-start | bytes 55304 | tf_op jit(solution)/shard_map/ppermute | solution.py:256
  29.5 0.7 %and_convert_fusion.inside_ref = f32[8,132]{1,0:T(8,128)} fusion(pred[132]{0:T(512)(128)(4,1)S(1)} %get-tuple-element.17, pred[132]{0:T(512)(128)(4,1)S(1)} %get-tuple-element.18, pred[8]{0:T(512)(128)(4,1)S(1)} %compare_and_fusion), kind=kLoop, calls=%fused_computation.2 | loop fusion | flops 3168 | bytes 4496 | tf_op jit(solution)/shard_map/convert_element_type | solution.py:283
  30.1 1.7 %collective-permute-done.4 = f32[288,8,2]{0,1,2:T(8,128)S(1)} collective-permute-done((f32[288,8,2]{0,1,2:T(8,128)S(1)}, f32[288,8,2]{0,1,2:T(8,128)S(1)}, u32[]{:S(2)}, u32[]{:S(2)}) %collective-permute-start.4) | collective-permute-done | bytes 18464 | tf_op jit(solution)/shard_map/ppermute | solution.py:256
  31.8 1.4 %copy.12.low_ref.high_ref = f32[288,8,2]{2,1,0:T(8,128)} copy(f32[288,8,2]{0,1,2:T(8,128)S(1)} %collective-permute-done.4) | data formatting | bytes 36864 | tf_op jit(solution)/shard_map/ppermute | solution.py:256
  33.2 8.2 %shard_map.48 = f32[2,3,32,4,128]{4,3,2,1,0:T(4,128)} custom-call(f32[288,8,128]{2,1,0:T(8,128)} %get-tuple-element.11.planes_ref, f32[288,8,2]{2,1,0:T(8,128)} %copy.12.low_ref.high_ref, f32[288,8,2]{2,1,0:T(8,128)} %copy.12.low_ref.high_ref, f32[8,132]{1,0:T(8,128)} %and_convert_fusion.inside_ref), custom_call_target="tpu_custom_call" | custom-call | tf_op jit(solution)/shard_map/pallas_call | solution.py:278
  (9 shorter events, 0.0 us)
Async XLA Ops:
  0.0 1.9 %copy-start = (bf16[16,2,3,32,4,128]{5,4,3,2,1,0:T(4,128)(2,1)S(1)}, bf16[16,2,3,32,4,128]{5,4,3,2,1,0:T(4,128)(2,1)}, u32[]{:S(2)}) copy-start(bf16[16,2,3,32,4,128]{5,4,3,2,1,0:T(4,128)(2,1)} %param.4) | copy-start | bytes 9437188
  5.4 2.2 %collective-permute-start = (f32[2,3,32,4,128]{4,3,2,1,0:T(4,128)}, f32[2,3,32,4,128]{4,3,2,1,0:T(4,128)S(1)}, u32[]{:S(2)}, u32[]{:S(2)}) collective-permute-start(f32[2,3,32,4,128]{4,3,2,1,0:T(4,128)} %bitcast.9), channel_id=1, source_target_pairs={{0,1},{1,0},{2,3},{3,2},{4,5},{5,4},{6,7},{7,6},{8,9},{9,8},{10,11... | collective-permute-start | bytes 1179656 | tf_op jit(solution)/shard_map/ppermute | solution.py:179
  5.4 2.2 %collective-permute-start.1 = (f32[3,16,4,128]{3,2,1,0:T(4,128)}, f32[3,16,4,128]{3,2,1,0:T(4,128)}, u32[]{:S(2)}, u32[]{:S(2)}) collective-permute-start(f32[3,16,4,128]{3,2,1,0:T(4,128)} %sigma_ref.3), channel_id=1, source_target_pairs={{0,1},{1,0},{2,3},{3,2},{4,5},{5,4},{6,7},{7,6},{8,9},{9,8},{10,11... | collective-permute-start | bytes 294920 | tf_op jit(solution)/shard_map/ppermute | solution.py:180
  7.6 0.7 %copy-start.1 = (f32[2,3,32,4,128]{4,3,2,1,0:T(4,128)}, f32[2,3,32,4,128]{4,3,2,1,0:T(4,128)S(1)}, u32[]{:S(2)}) copy-start(f32[2,3,32,4,128]{4,3,2,1,0:T(4,128)S(1)} %collective-permute-done.got_ref) | copy-start | bytes 1179652
  10.5 9.3 %collective-permute-start.2 = (f32[288,2,128]{2,1,0:T(2,128)}, f32[288,2,128]{2,1,0:T(2,128)S(1)}, u32[]{:S(2)}, u32[]{:S(2)}) collective-permute-start(f32[288,2,128]{2,1,0:T(2,128)} %get-tuple-element.9), channel_id=1, source_target_pairs={{0,4},{4,0},{8,12},{12,8},{1,5},{5,1},{9,13},{13,9},{2,6},{6,2},{1... | collective-permute-start | bytes 884744 | tf_op jit(solution)/shard_map/ppermute | solution.py:224
  12.1 11.0 %collective-permute-start.3 = (f32[288,2,128]{2,1,0:T(2,128)}, f32[288,2,128]{2,1,0:T(2,128)}, u32[]{:S(2)}, u32[]{:S(2)}) collective-permute-start(f32[288,2,128]{2,1,0:T(2,128)} %get-tuple-element.10), channel_id=1, source_target_pairs={{4,8},{8,4},{5,9},{9,5},{6,10},{10,6},{7,11},{11,7},{20,24},{24,20... | collective-permute-start | bytes 884744 | tf_op jit(solution)/shard_map/ppermute | solution.py:224
  19.8 3.3 %copy-start.2 = (f32[288,2,128]{2,1,0:T(2,128)}, f32[288,2,128]{2,1,0:T(2,128)S(1)}, u32[]{:S(2)}) copy-start(f32[288,2,128]{2,1,0:T(2,128)S(1)} %collective-permute-done.2.refs_0_) | copy-start | bytes 884740
  27.9 3.9 %collective-permute-start.4 = (f32[288,8,2]{0,1,2:T(8,128)S(1)}, f32[288,8,2]{0,1,2:T(8,128)S(1)}, u32[]{:S(2)}, u32[]{:S(2)}) collective-permute-start(f32[288,8,2]{0,1,2:T(8,128)S(1)} %copy.11), channel_id=1, source_target_pairs={{0,2},{2,0},{1,3},{3,1},{4,6},{6,4},{5,7},{7,5},{8,10},{10,8},{9,1... | collective-permute-start | bytes 55304 | tf_op jit(solution)/shard_map/ppermute | solution.py:256

commit v14 on v13

--- a/solution.py
+++ b/solution.py
@@ -208,9 +208,19 @@
         return jnp.concatenate([shot, sigma], axis=0)
 
     def send_kernel(flags_ref, own_ref, got_ref, sigma_ref, other_ref, *send_refs):
-        cells = planes_of(flags_ref, own_ref, got_ref, sigma_ref, other_ref)
-        head = cells[:, :w]
-        tail = cells[:, width_x - w:]
+        def rows(lo, hi):
+            shot = (own_ref[:, :, :, lo:hi, :] + got_ref[:, :, :, lo:hi, :]).reshape(-1, hi - lo, width_y)
+            mine = sigma_ref[:, :, lo:hi, :]
+            theirs = other_ref[:, :, lo:hi, :]
+            sigma = jnp.where(
+                flags_ref[0] == 1,
+                jnp.concatenate([mine, theirs], axis=1),
+                jnp.concatenate([theirs, mine], axis=1),
+            ).reshape(-1, hi - lo, width_y)
+            return jnp.concatenate([shot, sigma], axis=0)
+
+        head = rows(0, w)
+        tail = rows(width_x - w, width_x)
         for k in range(n_x):
             send_refs[k][...] = jnp.where(flags_ref[2 + k] == 1, tail, head)
 

time: 41.6 us -> 41.8 us (level)
  no operation moved by 1% of the time
where the time goes in v14:
time: 41.8 us; the launch traced here: 41.5 us
  Pallas kernels  13.6 us (33%)
  waiting for transfers between devices  11.8 us (28%)
  local copies, waits for them, and re-layouts  7.32 us (18%)
  starting transfers between devices  5.55 us (13%)
  matrix products  1.93 us (5%)
  other arithmetic  1.33 us (3%)
    ppermute x2, waiting for transfers between devices, body(): lax.ppermute(row_major(send), 'xb', pairs)  9.01 us
    pallas_call x1, Pallas kernels, body(): pl.pallas_call(sweeps_kernel, out_shape=jax.ShapeDtypeStruct(out_shape, j...  8.18 us
    ppermute x2, starting transfers between devices, body(): lax.ppermute(row_major(send), 'xb', pairs)  3.49 us
    pallas_call x1, Pallas kernels, body(): pl.pallas_call(x_kernel, out_shape=[jax.ShapeDtypeStruct((n_planes, ext_x...  3.11 us
    pallas_call x1, Pallas kernels, body(): pl.pallas_call(send_kernel, out_shape=[jax.ShapeDtypeStruct((n_planes, w,...  2.3 us
    dot_general x1, matrix products, body(): lax.dot_general(weights, primaries, (((1,), (0,)), ((), ())), preferred_e...  1.93 us
    another operation x1, local copies, waits for them, and re-layouts, row_major(): with_layout_constraint(x, Layout(major_to_minor=tuple(range(x.ndim))))  1.73 us
    ppermute x1, waiting for transfers between devices, body(): lax.ppermute(row_major(send), 'yb', pairs)  1.67 us
  transfers between devices with their start and end apart: 5, of which 4 were waited for; matrix products, arithmetic and copies ran while one was open for 3% of the time, Pallas kernels for 0%

profile of v14, /device:TPU:16, one launch (start us, length us, event | category | flops | bytes accessed | tf_op | source)
XLA Modules:
  0.0 41.5 jit_solution(8910742061211846354)
XLA Ops:
  0.0 0.9 %reshape.10 = s32[2,16]{1,0:T(2,128)S(1)} reshape(s32[32]{0:T(128)} %param.7) | data formatting | bytes 256 | tf_op jit(solution)/shard_map/reshape | solution.py:172
  0.9 0.8 %reshape.9 = s32[2,16]{1,0:T(2,128)S(1)} reshape(s32[32]{0:T(128)} %param.6) | data formatting | bytes 256 | tf_op jit(solution)/shard_map/reshape | solution.py:171
  1.7 0.1 pad_add_fusion
  1.8 0.1 select_reduce_fusion.1
  1.9 0.0 copy-done
  1.9 1.9 %fusion = f32[2,2,3,32,4,128]{5,0,4,3,2,1:T(2,128)S(1)} fusion(bf16[16,2,3,32,4,128]{5,4,3,2,1,0:T(4,128)(2,1)S(1)} %copy-done, s32[16]{0:T(128)S(1)} %get-tuple-element.14, s32[16]{0:T(128)S(1)} %get-tuple-element.13, s32[2]{0:T(128)S(1)} %pad_add_fusion), kind=kOutput, calls=%fused_computation | convolution fusion | flops 6291584 | bytes 3932296 | tf_op jit(solution)/shard_map/dot_general | solution.py:175
  3.8 1.5 %fusion.13 = (f32[1,2,3,32,4,128]{5,0,4,3,2,1:T(1,128)}, f32[1,2,3,32,4,128]{5,0,4,3,2,1:T(1,128)}) fusion(f32[2,2,3,32,4,128]{5,0,4,3,2,1:T(2,128)S(1)} %fusion), kind=kLoop, calls=%fused_computation.20 | loop fusion | bytes 1572864 | tf_op jit(solution)/shard_map/slice | solution.py:179
  5.4 0.5 %collective-permute-start.1 = (f32[3,16,4,128]{3,2,1,0:T(4,128)}, f32[3,16,4,128]{3,2,1,0:T(4,128)}, u32[]{:S(2)}, u32[]{:S(2)}) collective-permute-start(f32[3,16,4,128]{3,2,1,0:T(4,128)} %sigma_ref.3), channel_id=1, source_target_pairs={{0,1},{1,0},{2,3},{3,2},{4,5},{5,4},{6,7},{7,6},{8,9},{9,8},{10,11... | collective-permute-start | bytes 294920 | tf_op jit(solution)/shard_map/ppermute | solution.py:180
  5.9 0.1 stack.35
  6.0 0.5 %stack.36.flags_ref = s32[5]{0:T(128)} convert(pred[5]{0:T(512)(128)(4,1)S(1)} %stack.35) | non-fusion elementwise | flops 5 | bytes 25 | tf_op jit(solution)/shard_map/stack | solution.py:189
  6.5 1.1 %collective-permute-done.1.other_ref = f32[3,16,4,128]{3,2,1,0:T(4,128)} collective-permute-done((f32[3,16,4,128]{3,2,1,0:T(4,128)}, f32[3,16,4,128]{3,2,1,0:T(4,128)}, u32[]{:S(2)}, u32[]{:S(2)}) %collective-permute-start.1) | collective-permute-done | bytes 98336 | tf_op jit(solution)/shard_map/ppermute | solution.py:180
  7.6 0.7 %copy-done.1 = f32[2,3,32,4,128]{4,3,2,1,0:T(4,128)} copy-done((f32[2,3,32,4,128]{4,3,2,1,0:T(4,128)}, f32[2,3,32,4,128]{4,3,2,1,0:T(4,128)S(1)}, u32[]{:S(2)}) %copy-start.1) | copy-done | bytes 393240
  8.3 2.3 %shard_map.46 = (f32[288,2,128]{2,1,0:T(2,128)}, f32[288,2,128]{2,1,0:T(2,128)}) custom-call(s32[5]{0:T(128)} %stack.36.flags_ref, f32[2,3,32,4,128]{4,3,2,1,0:T(4,128)} %bitcast.18, f32[2,3,32,4,128]{4,3,2,1,0:T(4,128)} %copy-done.1, f32[3,16,4,128]{3,2,1,0:T(4,128)} %sigma_ref.3, f32[3,16,4,128]{3,2,1,0:T(4,128)} %collective-permute-done.1.other_ref), custom_call_target="tpu_custom_call" | custom-call | tf_op jit(solution)/shard_map/pallas_call | solution.py:227
  10.6 1.6 %collective-permute-start.2 = (f32[288,2,128]{2,1,0:T(2,128)}, f32[288,2,128]{2,1,0:T(2,128)S(1)}, u32[]{:S(2)}, u32[]{:S(2)}) collective-permute-start(f32[288,2,128]{2,1,0:T(2,128)} %get-tuple-element.9), channel_id=1, source_target_pairs={{0,4},{4,0},{8,12},{12,8},{1,5},{5,1},{9,13},{13,9},{2,6},{6,2},{1... | collective-permute-start | bytes 884744 | tf_op jit(solution)/shard_map/ppermute | solution.py:234
  12.2 1.9 %collective-permute-start.3 = (f32[288,2,128]{2,1,0:T(2,128)}, f32[288,2,128]{2,1,0:T(2,128)}, u32[]{:S(2)}, u32[]{:S(2)}) collective-permute-start(f32[288,2,128]{2,1,0:T(2,128)} %get-tuple-element.10), channel_id=1, source_target_pairs={{4,8},{8,4},{5,9},{9,5},{6,10},{10,6},{7,11},{11,7},{20,24},{24,20... | collective-permute-start | bytes 884744 | tf_op jit(solution)/shard_map/ppermute | solution.py:234
  14.2 5.7 %collective-permute-done.2.refs_0_ = f32[288,2,128]{2,1,0:T(2,128)S(1)} collective-permute-done((f32[288,2,128]{2,1,0:T(2,128)}, f32[288,2,128]{2,1,0:T(2,128)S(1)}, u32[]{:S(2)}, u32[]{:S(2)}) %collective-permute-start.2) | collective-permute-done | bytes 294944 | tf_op jit(solution)/shard_map/ppermute | solution.py:234
  19.9 3.3 %collective-permute-done.3.refs_1_ = f32[288,2,128]{2,1,0:T(2,128)} collective-permute-done((f32[288,2,128]{2,1,0:T(2,128)}, f32[288,2,128]{2,1,0:T(2,128)}, u32[]{:S(2)}, u32[]{:S(2)}) %collective-permute-start.3) | collective-permute-done | bytes 294944 | tf_op jit(solution)/shard_map/ppermute | solution.py:234
  23.2 3.1 %shard_map.47 = (f32[288,8,128]{2,1,0:T(8,128)}, f32[288,8,2]{2,1,0:T(8,128)}) custom-call(s32[5]{0:T(128)} %stack.36.flags_ref, f32[2,3,32,4,128]{4,3,2,1,0:T(4,128)} %bitcast.19, f32[2,3,32,4,128]{4,3,2,1,0:T(4,128)} %copy-done.1, f32[3,16,4,128]{3,2,1,0:T(4,128)} %sigma_ref.3, f32[3,16,4,128]{3,2,1,0:T(4,128)} %collective-permute-done.1.other_ref, ...), custom_call_target="tpu_custom_call" | custom-call | tf_op jit(solution)/shard_map/pallas_call | solution.py:257
  26.3 1.7 %copy.11 = f32[288,8,2]{0,1,2:T(8,128)S(1)} copy(f32[288,8,2]{2,1,0:T(8,128)} %get-tuple-element.12) | data formatting | bytes 36864 | tf_op jit(solution)/shard_map/layout_constraint | solution.py:134
  28.0 1.5 %collective-permute-start.4 = (f32[288,8,2]{0,1,2:T(8,128)S(1)}, f32[288,8,2]{0,1,2:T(8,128)S(1)}, u32[]{:S(2)}, u32[]{:S(2)}) collective-permute-start(f32[288,8,2]{0,1,2:T(8,128)S(1)} %copy.11), channel_id=1, source_target_pairs={{0,2},{2,0},{1,3},{3,1},{4,6},{6,4},{5,7},{7,5},{8,10},{10,8},{9,1... | collective-permute-start | bytes 55304 | tf_op jit(solution)/shard_map/ppermute | solution.py:266
  29.6 0.7 %and_convert_fusion.inside_ref = f32[8,132]{1,0:T(8,128)} fusion(pred[132]{0:T(512)(128)(4,1)S(1)} %get-tuple-element.17, pred[132]{0:T(512)(128)(4,1)S(1)} %get-tuple-element.18, pred[8]{0:T(512)(128)(4,1)S(1)} %compare_and_fusion), kind=kLoop, calls=%fused_computation.2 | loop fusion | flops 3168 | bytes 4496 | tf_op jit(solution)/shard_map/convert_element_type | solution.py:293
  30.3 1.7 %collective-permute-done.4 = f32[288,8,2]{0,1,2:T(8,128)S(1)} collective-permute-done((f32[288,8,2]{0,1,2:T(8,128)S(1)}, f32[288,8,2]{0,1,2:T(8,128)S(1)}, u32[]{:S(2)}, u32[]{:S(2)}) %collective-permute-start.4) | collective-permute-done | bytes 18464 | tf_op jit(solution)/shard_map/ppermute | solution.py:266
  31.9 1.4 %copy.12.low_ref.high_ref = f32[288,8,2]{2,1,0:T(8,128)} copy(f32[288,8,2]{0,1,2:T(8,128)S(1)} %collective-permute-done.4) | data formatting | bytes 36864 | tf_op jit(solution)/shard_map/ppermute | solution.py:266
  33.4 8.2 %shard_map.48 = f32[2,3,32,4,128]{4,3,2,1,0:T(4,128)} custom-call(f32[288,8,128]{2,1,0:T(8,128)} %get-tuple-element.11.planes_ref, f32[288,8,2]{2,1,0:T(8,128)} %copy.12.low_ref.high_ref, f32[288,8,2]{2,1,0:T(8,128)} %copy.12.low_ref.high_ref, f32[8,132]{1,0:T(8,128)} %and_convert_fusion.inside_ref), custom_call_target="tpu_custom_call" | custom-call | tf_op jit(solution)/shard_map/pallas_call | solution.py:288
  (9 shorter events, 0.0 us)
Async XLA Ops:
  0.0 1.9 %copy-start = (bf16[16,2,3,32,4,128]{5,4,3,2,1,0:T(4,128)(2,1)S(1)}, bf16[16,2,3,32,4,128]{5,4,3,2,1,0:T(4,128)(2,1)}, u32[]{:S(2)}) copy-start(bf16[16,2,3,32,4,128]{5,4,3,2,1,0:T(4,128)(2,1)} %param.4) | copy-start | bytes 9437188
  5.4 2.2 %collective-permute-start = (f32[2,3,32,4,128]{4,3,2,1,0:T(4,128)}, f32[2,3,32,4,128]{4,3,2,1,0:T(4,128)S(1)}, u32[]{:S(2)}, u32[]{:S(2)}) collective-permute-start(f32[2,3,32,4,128]{4,3,2,1,0:T(4,128)} %bitcast.9), channel_id=1, source_target_pairs={{0,1},{1,0},{2,3},{3,2},{4,5},{5,4},{6,7},{7,6},{8,9},{9,8},{10,11... | collective-permute-start | bytes 1179656 | tf_op jit(solution)/shard_map/ppermute | solution.py:179
  5.4 2.2 %collective-permute-start.1 = (f32[3,16,4,128]{3,2,1,0:T(4,128)}, f32[3,16,4,128]{3,2,1,0:T(4,128)}, u32[]{:S(2)}, u32[]{:S(2)}) collective-permute-start(f32[3,16,4,128]{3,2,1,0:T(4,128)} %sigma_ref.3), channel_id=1, source_target_pairs={{0,1},{1,0},{2,3},{3,2},{4,5},{5,4},{6,7},{7,6},{8,9},{9,8},{10,11... | collective-permute-start | bytes 294920 | tf_op jit(solution)/shard_map/ppermute | solution.py:180
  7.6 0.7 %copy-start.1 = (f32[2,3,32,4,128]{4,3,2,1,0:T(4,128)}, f32[2,3,32,4,128]{4,3,2,1,0:T(4,128)S(1)}, u32[]{:S(2)}) copy-start(f32[2,3,32,4,128]{4,3,2,1,0:T(4,128)S(1)} %collective-permute-done.got_ref) | copy-start | bytes 1179652
  10.6 9.3 %collective-permute-start.2 = (f32[288,2,128]{2,1,0:T(2,128)}, f32[288,2,128]{2,1,0:T(2,128)S(1)}, u32[]{:S(2)}, u32[]{:S(2)}) collective-permute-start(f32[288,2,128]{2,1,0:T(2,128)} %get-tuple-element.9), channel_id=1, source_target_pairs={{0,4},{4,0},{8,12},{12,8},{1,5},{5,1},{9,13},{13,9},{2,6},{6,2},{1... | collective-permute-start | bytes 884744 | tf_op jit(solution)/shard_map/ppermute | solution.py:234
  12.2 11.0 %collective-permute-start.3 = (f32[288,2,128]{2,1,0:T(2,128)}, f32[288,2,128]{2,1,0:T(2,128)}, u32[]{:S(2)}, u32[]{:S(2)}) collective-permute-start(f32[288,2,128]{2,1,0:T(2,128)} %get-tuple-element.10), channel_id=1, source_target_pairs={{4,8},{8,4},{5,9},{9,5},{6,10},{10,6},{7,11},{11,7},{20,24},{24,20... | collective-permute-start | bytes 884744 | tf_op jit(solution)/shard_map/ppermute | solution.py:234
  19.9 3.3 %copy-start.2 = (f32[288,2,128]{2,1,0:T(2,128)}, f32[288,2,128]{2,1,0:T(2,128)S(1)}, u32[]{:S(2)}) copy-start(f32[288,2,128]{2,1,0:T(2,128)S(1)} %collective-permute-done.2.refs_0_) | copy-start | bytes 884740
  28.0 3.9 %collective-permute-start.4 = (f32[288,8,2]{0,1,2:T(8,128)S(1)}, f32[288,8,2]{0,1,2:T(8,128)S(1)}, u32[]{:S(2)}, u32[]{:S(2)}) collective-permute-start(f32[288,8,2]{0,1,2:T(8,128)S(1)} %copy.11), channel_id=1, source_target_pairs={{0,2},{2,0},{1,3},{3,1},{4,6},{6,4},{5,7},{7,5},{8,10},{10,8},{9,1... | collective-permute-start | bytes 55304 | tf_op jit(solution)/shard_map/ppermute | solution.py:266

commit v15 on v13

--- a/solution.py
+++ b/solution.py
@@ -224,7 +224,7 @@
         row_major(lax.ppermute(row_major(send), "xb", pairs))
         for send, (pairs, _) in zip(x_sends, x_rounds)
     ]
-    face_shape = (n_planes, ext_x, w)
+    face_shape = (w, n_planes * ext_x)
 
     def x_kernel(flags_ref, own_ref, got_ref, sigma_ref, other_ref, *refs):
         got_refs = refs[:n_x]
@@ -239,8 +239,9 @@
         middle = planes_of(flags_ref, own_ref, got_ref, sigma_ref, other_ref)
         cells = jnp.concatenate([low, middle, high], axis=1)
         planes_x_ref[...] = cells
-        head = cells[:, :, :w]
-        tail = cells[:, :, width_y - w:]
+        columns = cells.reshape(n_planes * ext_x, width_y).T
+        head = columns[:w]
+        tail = columns[width_y - w:]
         for k in range(n_y):
             send_refs[k][...] = jnp.where(flags_ref[2 + n_x + k] == 1, tail, head)
 
@@ -268,8 +269,15 @@
     shot_shape = primaries.shape[1:3]
     out_shape = shot_shape + (depth, width_x, width_y)
 
+    def unflip(face):
+        filler = jnp.zeros((width_y - w, face.shape[1]), face.dtype)
+        back = jnp.concatenate([face, filler], axis=0).T.reshape(n_planes, ext_x, width_y)
+        return back[:, :, :w]
+
     def sweeps_kernel(planes_ref, low_ref, high_ref, inside_ref, out_ref):
-        ext = jnp.concatenate([low_ref[...], planes_ref[...], high_ref[...]], axis=2)
+        low = unflip(low_ref[...])
+        high = low if n_y == 1 else unflip(high_ref[...])
+        ext = jnp.concatenate([low, planes_ref[...], high], axis=2)
         shot_ext = ext[:shot_planes].reshape(shot_shape + (depth, ext_x, ext_y))
         sigma_ext = ext[shot_planes:].reshape(-1, depth, ext_x, ext_y)
         keep = inside_ref[...] > 0.5

time: 41.6 us -> 38.4 us (0.923)
  local copies, waits for them, and re-layouts: 7.32 us -> 4.76 us
  Pallas kernels: 13.5 us -> 12.7 us
    another operation x1 -> x0, local copies, waits for them, and re-layouts: 1.73 us -> none  [row_major(): with_layout_constraint(x, Layout(major_to_minor=tuple(range(x.ndim))))]
    ppermute x1 -> x0, local copies, waits for them, and re-layouts: 1.45 us -> none  [body(): lax.ppermute(row_major(send), 'yb', pairs)]
    unnamed x6 -> x8, local copies, waits for them, and re-layouts: 0.8 us -> 1.4 us
where the time goes in v15:
time: 38.4 us; the launch traced here: 38.2 us
  Pallas kernels  12.7 us (33%)
  waiting for transfers between devices  11.9 us (31%)
  starting transfers between devices  5.49 us (14%)
  local copies, waits for them, and re-layouts  4.76 us (12%)
  matrix products  1.93 us (5%)
  other arithmetic  1.35 us (4%)
    ppermute x2, waiting for transfers between devices, body(): lax.ppermute(row_major(send), 'xb', pairs)  9.01 us
    pallas_call x1, Pallas kernels, body(): pl.pallas_call(sweeps_kernel, out_shape=jax.ShapeDtypeStruct(out_shape, j...  7.83 us
    ppermute x2, starting transfers between devices, body(): lax.ppermute(row_major(send), 'xb', pairs)  3.49 us
    pallas_call x1, Pallas kernels, body(): pl.pallas_call(x_kernel, out_shape=[jax.ShapeDtypeStruct((n_planes, ext_x...  2.7 us
    pallas_call x1, Pallas kernels, body(): pl.pallas_call(send_kernel, out_shape=[jax.ShapeDtypeStruct((n_planes, w,...  2.19 us
    dot_general x1, matrix products, body(): lax.dot_general(weights, primaries, (((1,), (0,)), ((), ())), preferred_e...  1.93 us
    ppermute x1, waiting for transfers between devices, body(): lax.ppermute(row_major(send), 'yb', pairs)  1.81 us
    slice x1, local copies, waits for them, and re-layouts, body(): got = lax.ppermute(partial[0], 'tx', tx_ring)  1.57 us
  transfers between devices with their start and end apart: 5, of which 4 were waited for; matrix products, arithmetic and copies ran while one was open for 3% of the time, Pallas kernels for 0%

profile of v15, /device:TPU:16, one launch (start us, length us, event | category | flops | bytes accessed | tf_op | source)
XLA Modules:
  0.0 38.2 jit_solution(12254778978788824074)
XLA Ops:
  0.0 0.9 %reshape.10 = s32[2,16]{1,0:T(2,128)S(1)} reshape(s32[32]{0:T(128)} %param.7) | data formatting | bytes 256 | tf_op jit(solution)/shard_map/reshape | solution.py:172
  0.9 0.8 %reshape.9 = s32[2,16]{1,0:T(2,128)S(1)} reshape(s32[32]{0:T(128)} %param.6) | data formatting | bytes 256 | tf_op jit(solution)/shard_map/reshape | solution.py:171
  1.7 0.1 pad_add_fusion
  1.8 0.1 select_reduce_fusion.1
  1.9 0.0 copy-done
  1.9 1.9 %fusion = f32[2,2,3,32,4,128]{5,0,4,3,2,1:T(2,128)S(1)} fusion(bf16[16,2,3,32,4,128]{5,4,3,2,1,0:T(4,128)(2,1)S(1)} %copy-done, s32[16]{0:T(128)S(1)} %get-tuple-element.14, s32[16]{0:T(128)S(1)} %get-tuple-element.13, s32[2]{0:T(128)S(1)} %pad_add_fusion), kind=kOutput, calls=%fused_computation | convolution fusion | flops 6291584 | bytes 3932296 | tf_op jit(solution)/shard_map/dot_general | solution.py:175
  3.8 1.6 %fusion.13 = (f32[1,2,3,32,4,128]{5,0,4,3,2,1:T(1,128)}, f32[1,2,3,32,4,128]{5,0,4,3,2,1:T(1,128)}) fusion(f32[2,2,3,32,4,128]{5,0,4,3,2,1:T(2,128)S(1)} %fusion), kind=kLoop, calls=%fused_computation.20 | loop fusion | bytes 1572864 | tf_op jit(solution)/shard_map/slice | solution.py:179
  5.4 0.0 collective-permute-start
  5.4 0.5 %collective-permute-start.1 = (f32[3,16,4,128]{3,2,1,0:T(4,128)}, f32[3,16,4,128]{3,2,1,0:T(4,128)}, u32[]{:S(2)}, u32[]{:S(2)}) collective-permute-start(f32[3,16,4,128]{3,2,1,0:T(4,128)} %sigma_ref.3), channel_id=1, source_target_pairs={{0,1},{1,0},{2,3},{3,2},{4,5},{5,4},{6,7},{7,6},{8,9},{9,8},{10,11... | collective-permute-start | bytes 294920 | tf_op jit(solution)/shard_map/ppermute | solution.py:180
  5.9 0.1 stack.35
  6.0 0.5 %stack.36.flags_ref = s32[5]{0:T(128)} convert(pred[5]{0:T(512)(128)(4,1)S(1)} %stack.35) | non-fusion elementwise | flops 5 | bytes 25 | tf_op jit(solution)/shard_map/stack | solution.py:189
  6.5 1.1 %collective-permute-done.1.other_ref = f32[3,16,4,128]{3,2,1,0:T(4,128)} collective-permute-done((f32[3,16,4,128]{3,2,1,0:T(4,128)}, f32[3,16,4,128]{3,2,1,0:T(4,128)}, u32[]{:S(2)}, u32[]{:S(2)}) %collective-permute-start.1) | collective-permute-done | bytes 98336 | tf_op jit(solution)/shard_map/ppermute | solution.py:180
  7.6 0.7 %copy-done.1 = f32[2,3,32,4,128]{4,3,2,1,0:T(4,128)} copy-done((f32[2,3,32,4,128]{4,3,2,1,0:T(4,128)}, f32[2,3,32,4,128]{4,3,2,1,0:T(4,128)S(1)}, u32[]{:S(2)}) %copy-start.1) | copy-done | bytes 393240
  8.4 2.2 %shard_map.46 = (f32[288,2,128]{2,1,0:T(2,128)}, f32[288,2,128]{2,1,0:T(2,128)}) custom-call(s32[5]{0:T(128)} %stack.36.flags_ref, f32[2,3,32,4,128]{4,3,2,1,0:T(4,128)} %bitcast.18, f32[2,3,32,4,128]{4,3,2,1,0:T(4,128)} %copy-done.1, f32[3,16,4,128]{3,2,1,0:T(4,128)} %sigma_ref.3, f32[3,16,4,128]{3,2,1,0:T(4,128)} %collective-permute-done.1.other_ref), custom_call_target="tpu_custom_call" | custom-call | tf_op jit(solution)/shard_map/pallas_call | solution.py:217
  10.6 1.6 %collective-permute-start.2 = (f32[288,2,128]{2,1,0:T(2,128)}, f32[288,2,128]{2,1,0:T(2,128)S(1)}, u32[]{:S(2)}, u32[]{:S(2)}) collective-permute-start(f32[288,2,128]{2,1,0:T(2,128)} %get-tuple-element.9), channel_id=1, source_target_pairs={{0,4},{4,0},{8,12},{12,8},{1,5},{5,1},{9,13},{13,9},{2,6},{6,2},{1... | collective-permute-start | bytes 884744 | tf_op jit(solution)/shard_map/ppermute | solution.py:224
  12.1 1.9 %collective-permute-start.3 = (f32[288,2,128]{2,1,0:T(2,128)}, f32[288,2,128]{2,1,0:T(2,128)}, u32[]{:S(2)}, u32[]{:S(2)}) collective-permute-start(f32[288,2,128]{2,1,0:T(2,128)} %get-tuple-element.10), channel_id=1, source_target_pairs={{4,8},{8,4},{5,9},{9,5},{6,10},{10,6},{7,11},{11,7},{20,24},{24,20... | collective-permute-start | bytes 884744 | tf_op jit(solution)/shard_map/ppermute | solution.py:224
  14.1 5.7 %collective-permute-done.2.refs_0_ = f32[288,2,128]{2,1,0:T(2,128)S(1)} collective-permute-done((f32[288,2,128]{2,1,0:T(2,128)}, f32[288,2,128]{2,1,0:T(2,128)S(1)}, u32[]{:S(2)}, u32[]{:S(2)}) %collective-permute-start.2) | collective-permute-done | bytes 294944 | tf_op jit(solution)/shard_map/ppermute | solution.py:224
  19.8 3.3 %collective-permute-done.3.refs_1_ = f32[288,2,128]{2,1,0:T(2,128)} collective-permute-done((f32[288,2,128]{2,1,0:T(2,128)}, f32[288,2,128]{2,1,0:T(2,128)}, u32[]{:S(2)}, u32[]{:S(2)}) %collective-permute-start.3) | collective-permute-done | bytes 294944 | tf_op jit(solution)/shard_map/ppermute | solution.py:224
  23.1 2.7 %shard_map.47 = (f32[288,8,128]{2,1,0:T(8,128)}, f32[2,2304]{1,0:T(2,128)}) custom-call(s32[5]{0:T(128)} %stack.36.flags_ref, f32[2,3,32,4,128]{4,3,2,1,0:T(4,128)} %bitcast.19, f32[2,3,32,4,128]{4,3,2,1,0:T(4,128)} %copy-done.1, f32[3,16,4,128]{3,2,1,0:T(4,128)} %sigma_ref.3, f32[3,16,4,128]{3,2,1,0:T(4,128)} %collective-permute-done.1.other_ref, ...), custom_call_target="tpu_custom_call" | custom-call | tf_op jit(solution)/shard_map/pallas_call | solution.py:248
  25.8 1.5 %collective-permute-start.4 = (f32[2,2304]{1,0:T(2,128)}, f32[2,2304]{1,0:T(2,128)S(1)}, u32[]{:S(2)}, u32[]{:S(2)}) collective-permute-start(f32[2,2304]{1,0:T(2,128)} %get-tuple-element.12), channel_id=1, source_target_pairs={{0,2},{2,0},{1,3},{3,1},{4,6},{6,4},{5,7},{7,5},{8,10},{10,8},{9,1... | collective-permute-start | bytes 55304 | tf_op jit(solution)/shard_map/ppermute | solution.py:257
  27.3 0.7 %and_convert_fusion.inside_ref = f32[8,132]{1,0:T(8,128)} fusion(pred[132]{0:T(512)(128)(4,1)S(1)} %get-tuple-element.17, pred[132]{0:T(512)(128)(4,1)S(1)} %get-tuple-element.18, pred[8]{0:T(512)(128)(4,1)S(1)} %compare_and_fusion), kind=kLoop, calls=%fused_computation.2 | loop fusion | flops 3168 | bytes 4496 | tf_op jit(solution)/shard_map/convert_element_type | solution.py:291
  28.0 1.8 %collective-permute-done.4.low_ref.high_ref = f32[2,2304]{1,0:T(2,128)S(1)} collective-permute-done((f32[2,2304]{1,0:T(2,128)}, f32[2,2304]{1,0:T(2,128)S(1)}, u32[]{:S(2)}, u32[]{:S(2)}) %collective-permute-start.4) | collective-permute-done | bytes 18464 | tf_op jit(solution)/shard_map/ppermute | solution.py:257
  29.8 0.6 %copy-done.3 = f32[2,2304]{1,0:T(2,128)} copy-done((f32[2,2304]{1,0:T(2,128)}, f32[2,2304]{1,0:T(2,128)S(1)}, u32[]{:S(2)}) %copy-start.3) | copy-done | bytes 18456
  30.4 7.8 %shard_map.48 = f32[2,3,32,4,128]{4,3,2,1,0:T(4,128)} custom-call(f32[288,8,128]{2,1,0:T(8,128)} %get-tuple-element.11.planes_ref, f32[2,2304]{1,0:T(2,128)} %copy-done.3, f32[2,2304]{1,0:T(2,128)} %copy-done.3, f32[8,132]{1,0:T(8,128)} %and_convert_fusion.inside_ref), custom_call_target="tpu_custom_call" | custom-call | tf_op jit(solution)/shard_map/pallas_call | solution.py:286
  (9 shorter events, 0.0 us)
Async XLA Ops:
  0.0 1.9 %copy-start = (bf16[16,2,3,32,4,128]{5,4,3,2,1,0:T(4,128)(2,1)S(1)}, bf16[16,2,3,32,4,128]{5,4,3,2,1,0:T(4,128)(2,1)}, u32[]{:S(2)}) copy-start(bf16[16,2,3,32,4,128]{5,4,3,2,1,0:T(4,128)(2,1)} %param.4) | copy-start | bytes 9437188
  5.4 2.2 %collective-permute-start = (f32[2,3,32,4,128]{4,3,2,1,0:T(4,128)}, f32[2,3,32,4,128]{4,3,2,1,0:T(4,128)S(1)}, u32[]{:S(2)}, u32[]{:S(2)}) collective-permute-start(f32[2,3,32,4,128]{4,3,2,1,0:T(4,128)} %bitcast.9), channel_id=1, source_target_pairs={{0,1},{1,0},{2,3},{3,2},{4,5},{5,4},{6,7},{7,6},{8,9},{9,8},{10,11... | collective-permute-start | bytes 1179656 | tf_op jit(solution)/shard_map/ppermute | solution.py:179
  5.4 2.2 %collective-permute-start.1 = (f32[3,16,4,128]{3,2,1,0:T(4,128)}, f32[3,16,4,128]{3,2,1,0:T(4,128)}, u32[]{:S(2)}, u32[]{:S(2)}) collective-permute-start(f32[3,16,4,128]{3,2,1,0:T(4,128)} %sigma_ref.3), channel_id=1, source_target_pairs={{0,1},{1,0},{2,3},{3,2},{4,5},{5,4},{6,7},{7,6},{8,9},{9,8},{10,11... | collective-permute-start | bytes 294920 | tf_op jit(solution)/shard_map/ppermute | solution.py:180
  7.6 0.7 %copy-start.1 = (f32[2,3,32,4,128]{4,3,2,1,0:T(4,128)}, f32[2,3,32,4,128]{4,3,2,1,0:T(4,128)S(1)}, u32[]{:S(2)}) copy-start(f32[2,3,32,4,128]{4,3,2,1,0:T(4,128)S(1)} %collective-permute-done.got_ref) | copy-start | bytes 1179652
  10.6 9.3 %collective-permute-start.2 = (f32[288,2,128]{2,1,0:T(2,128)}, f32[288,2,128]{2,1,0:T(2,128)S(1)}, u32[]{:S(2)}, u32[]{:S(2)}) collective-permute-start(f32[288,2,128]{2,1,0:T(2,128)} %get-tuple-element.9), channel_id=1, source_target_pairs={{0,4},{4,0},{8,12},{12,8},{1,5},{5,1},{9,13},{13,9},{2,6},{6,2},{1... | collective-permute-start | bytes 884744 | tf_op jit(solution)/shard_map/ppermute | solution.py:224
  12.1 11.0 %collective-permute-start.3 = (f32[288,2,128]{2,1,0:T(2,128)}, f32[288,2,128]{2,1,0:T(2,128)}, u32[]{:S(2)}, u32[]{:S(2)}) collective-permute-start(f32[288,2,128]{2,1,0:T(2,128)} %get-tuple-element.10), channel_id=1, source_target_pairs={{4,8},{8,4},{5,9},{9,5},{6,10},{10,6},{7,11},{11,7},{20,24},{24,20... | collective-permute-start | bytes 884744 | tf_op jit(solution)/shard_map/ppermute | solution.py:224
  19.8 3.3 %copy-start.2 = (f32[288,2,128]{2,1,0:T(2,128)}, f32[288,2,128]{2,1,0:T(2,128)S(1)}, u32[]{:S(2)}) copy-start(f32[288,2,128]{2,1,0:T(2,128)S(1)} %collective-permute-done.2.refs_0_) | copy-start | bytes 884740
  25.8 4.0 %collective-permute-start.4 = (f32[2,2304]{1,0:T(2,128)}, f32[2,2304]{1,0:T(2,128)S(1)}, u32[]{:S(2)}, u32[]{:S(2)}) collective-permute-start(f32[2,2304]{1,0:T(2,128)} %get-tuple-element.12), channel_id=1, source_target_pairs={{0,2},{2,0},{1,3},{3,1},{4,6},{6,4},{5,7},{7,5},{8,10},{10,8},{9,1... | collective-permute-start | bytes 55304 | tf_op jit(solution)/shard_map/ppermute | solution.py:257
  29.8 0.6 %copy-start.3 = (f32[2,2304]{1,0:T(2,128)}, f32[2,2304]{1,0:T(2,128)S(1)}, u32[]{:S(2)}) copy-start(f32[2,2304]{1,0:T(2,128)S(1)} %collective-permute-done.4.low_ref.high_ref) | copy-start | bytes 55300

commit v16 on v15

--- a/solution.py
+++ b/solution.py
@@ -226,10 +226,7 @@
     ]
     face_shape = (w, n_planes * ext_x)
 
-    def x_kernel(flags_ref, own_ref, got_ref, sigma_ref, other_ref, *refs):
-        got_refs = refs[:n_x]
-        planes_x_ref = refs[n_x]
-        send_refs = refs[n_x + 1:]
+    def x_cells(flags_ref, own_ref, got_ref, sigma_ref, other_ref, got_refs):
         if n_x == 1:
             low = high = got_refs[0][...]
         else:
@@ -237,25 +234,27 @@
             high = jnp.where(even, got_refs[0][...], got_refs[1][...])
             low = jnp.where(even, got_refs[1][...], got_refs[0][...])
         middle = planes_of(flags_ref, own_ref, got_ref, sigma_ref, other_ref)
-        cells = jnp.concatenate([low, middle, high], axis=1)
-        planes_x_ref[...] = cells
+        return jnp.concatenate([low, middle, high], axis=1)
+
+    def x_kernel(flags_ref, own_ref, got_ref, sigma_ref, other_ref, *refs):
+        got_refs = refs[:n_x]
+        send_refs = refs[n_x:]
+        cells = x_cells(flags_ref, own_ref, got_ref, sigma_ref, other_ref, got_refs)
         columns = cells.reshape(n_planes * ext_x, width_y).T
         head = columns[:w]
         tail = columns[width_y - w:]
         for k in range(n_y):
             send_refs[k][...] = jnp.where(flags_ref[2 + n_x + k] == 1, tail, head)
 
-    outs = pl.pallas_call(
+    y_sends = pl.pallas_call(
         x_kernel,
-        out_shape=[jax.ShapeDtypeStruct((n_planes, ext_x, width_y), jnp.float32)]
-        + [jax.ShapeDtypeStruct(face_shape, jnp.float32)] * n_y,
+        out_shape=[jax.ShapeDtypeStruct(face_shape, jnp.float32)] * n_y,
         in_specs=[smem] + [vmem] * (4 + n_x),
-        out_specs=[vmem] * (1 + n_y),
+        out_specs=[vmem] * n_y,
     )(flags, *pieces, *x_gots)
-    planes = outs[0]
     y_gots = [
         row_major(lax.ppermute(row_major(send), "yb", pairs))
-        for send, (pairs, _) in zip(outs[1:], y_rounds)
+        for send, (pairs, _) in zip(y_sends, y_rounds)
     ]
     if n_y == 1:
         y_low = y_high = y_gots[0]
@@ -274,10 +273,13 @@
         back = jnp.concatenate([face, filler], axis=0).T.reshape(n_planes, ext_x, width_y)
         return back[:, :, :w]
 
-    def sweeps_kernel(planes_ref, low_ref, high_ref, inside_ref, out_ref):
+    def sweeps_kernel(flags_ref, own_ref, got_ref, sigma_ref, other_ref, *refs):
+        got_refs = refs[:n_x]
+        low_ref, high_ref, inside_ref, out_ref = refs[n_x:]
+        cells = x_cells(flags_ref, own_ref, got_ref, sigma_ref, other_ref, got_refs)
         low = unflip(low_ref[...])
         high = low if n_y == 1 else unflip(high_ref[...])
-        ext = jnp.concatenate([low, planes_ref[...], high], axis=2)
+        ext = jnp.concatenate([low, cells, high], axis=2)
         shot_ext = ext[:shot_planes].reshape(shot_shape + (depth, ext_x, ext_y))
         sigma_ext = ext[shot_planes:].reshape(-1, depth, ext_x, ext_y)
         keep = inside_ref[...] > 0.5
@@ -286,9 +288,9 @@
     field = pl.pallas_call(
         sweeps_kernel,
         out_shape=jax.ShapeDtypeStruct(out_shape, jnp.float32),
-        in_specs=[pl.BlockSpec(memory_space=pltpu.VMEM)] * 4,
-        out_specs=pl.BlockSpec(memory_space=pltpu.VMEM),
-    )(planes, y_low, y_high, inside.astype(jnp.float32))
+        in_specs=[smem] + [vmem] * (4 + n_x + 3),
+        out_specs=vmem,
+    )(flags, *pieces, *x_gots, y_low, y_high, inside.astype(jnp.float32))
     return field[None]
 
 

time: 38.4 us -> 38.1 us (level)
  transfers between devices with their start and end apart: 5 -> 5, of which waited for: 4 -> 4; matrix products, arithmetic and copies ran while one was open for 3% -> 4% of each run, Pallas kernels for 0% -> 0%
where the time goes in v16:
time: 38.1 us; the launch traced here: 37.9 us
  Pallas kernels  12.4 us (33%)
  waiting for transfers between devices  11.8 us (31%)
  starting transfers between devices  5.49 us (14%)
  local copies, waits for them, and re-layouts  4.75 us (12%)
  matrix products  1.93 us (5%)
  other arithmetic  1.43 us (4%)
    ppermute x2, waiting for transfers between devices, body(): lax.ppermute(row_major(send), 'xb', pairs)  9.01 us
    pallas_call x1, Pallas kernels, body(): pl.pallas_call(sweeps_kernel, out_shape=jax.ShapeDtypeStruct(out_shape, j...  7.91 us
    ppermute x2, starting transfers between devices, body(): lax.ppermute(row_major(send), 'xb', pairs)  3.49 us
    pallas_call x1, Pallas kernels, body(): pl.pallas_call(x_kernel, out_shape=[jax.ShapeDtypeStruct(face_shape, jnp....  2.36 us
    pallas_call x1, Pallas kernels, body(): pl.pallas_call(send_kernel, out_shape=[jax.ShapeDtypeStruct((n_planes, w,...  2.17 us
    dot_general x1, matrix products, body(): lax.dot_general(weights, primaries, (((1,), (0,)), ((), ())), preferred_e...  1.93 us
    ppermute x1, waiting for transfers between devices, body(): lax.ppermute(row_major(send), 'yb', pairs)  1.82 us
    slice x1, local copies, waits for them, and re-layouts, body(): got = lax.ppermute(partial[0], 'tx', tx_ring)  1.55 us
  transfers between devices with their start and end apart: 5, of which 4 were waited for; matrix products, arithmetic and copies ran while one was open for 4% of the time, Pallas kernels for 0%

profile of v16, /device:TPU:16, one launch (start us, length us, event | category | flops | bytes accessed | tf_op | source)
XLA Modules:
  0.0 37.9 jit_solution(16181272818514828967)
XLA Ops:
  0.0 0.9 %reshape.9 = s32[2,16]{1,0:T(2,128)S(1)} reshape(s32[32]{0:T(128)} %param.6) | data formatting | bytes 256 | tf_op jit(solution)/shard_map/reshape | solution.py:171
  0.9 0.8 %reshape.10 = s32[2,16]{1,0:T(2,128)S(1)} reshape(s32[32]{0:T(128)} %param.7) | data formatting | bytes 256 | tf_op jit(solution)/shard_map/reshape | solution.py:172
  1.7 0.1 pad_add_fusion
  1.8 0.1 select_reduce_fusion.1
  1.9 0.0 copy-done
  1.9 1.9 %fusion = f32[2,2,3,32,4,128]{5,0,4,3,2,1:T(2,128)S(1)} fusion(bf16[16,2,3,32,4,128]{5,4,3,2,1,0:T(4,128)(2,1)S(1)} %copy-done, s32[16]{0:T(128)S(1)} %get-tuple-element.10, s32[16]{0:T(128)S(1)} %get-tuple-element.9, s32[2]{0:T(128)S(1)} %pad_add_fusion), kind=kOutput, calls=%fused_computation | convolution fusion | flops 6291584 | bytes 3932296 | tf_op jit(solution)/shard_map/dot_general | solution.py:175
  3.8 1.6 %fusion.13 = (f32[1,2,3,32,4,128]{5,0,4,3,2,1:T(1,128)}, f32[1,2,3,32,4,128]{5,0,4,3,2,1:T(1,128)}) fusion(f32[2,2,3,32,4,128]{5,0,4,3,2,1:T(2,128)S(1)} %fusion), kind=kLoop, calls=%fused_computation.20 | loop fusion | bytes 1572864 | tf_op jit(solution)/shard_map/slice | solution.py:179
  5.4 0.0 collective-permute-start
  5.4 0.5 %collective-permute-start.1 = (f32[3,16,4,128]{3,2,1,0:T(4,128)}, f32[3,16,4,128]{3,2,1,0:T(4,128)}, u32[]{:S(2)}, u32[]{:S(2)}) collective-permute-start(f32[3,16,4,128]{3,2,1,0:T(4,128)} %sigma_ref.5), channel_id=1, source_target_pairs={{0,1},{1,0},{2,3},{3,2},{4,5},{5,4},{6,7},{7,6},{8,9},{9,8},{10,11... | collective-permute-start | bytes 294920 | tf_op jit(solution)/shard_map/ppermute | solution.py:180
  5.9 0.1 stack.35
  6.0 0.6 %stack.36.flags_ref = s32[5]{0:T(128)} convert(pred[5]{0:T(512)(128)(4,1)S(1)} %stack.35) | non-fusion elementwise | flops 5 | bytes 25 | tf_op jit(solution)/shard_map/stack | solution.py:189
  6.6 1.0 %collective-permute-done.1.other_ref = f32[3,16,4,128]{3,2,1,0:T(4,128)} collective-permute-done((f32[3,16,4,128]{3,2,1,0:T(4,128)}, f32[3,16,4,128]{3,2,1,0:T(4,128)}, u32[]{:S(2)}, u32[]{:S(2)}) %collective-permute-start.1) | collective-permute-done | bytes 98336 | tf_op jit(solution)/shard_map/ppermute | solution.py:180
  7.6 0.8 %copy-done.1 = f32[2,3,32,4,128]{4,3,2,1,0:T(4,128)} copy-done((f32[2,3,32,4,128]{4,3,2,1,0:T(4,128)}, f32[2,3,32,4,128]{4,3,2,1,0:T(4,128)S(1)}, u32[]{:S(2)}) %copy-start.1) | copy-done | bytes 393240
  8.4 2.2 %shard_map.46 = (f32[288,2,128]{2,1,0:T(2,128)}, f32[288,2,128]{2,1,0:T(2,128)}) custom-call(s32[5]{0:T(128)} %stack.36.flags_ref, f32[2,3,32,4,128]{4,3,2,1,0:T(4,128)} %bitcast.18, f32[2,3,32,4,128]{4,3,2,1,0:T(4,128)} %copy-done.1, f32[3,16,4,128]{3,2,1,0:T(4,128)} %sigma_ref.5, f32[3,16,4,128]{3,2,1,0:T(4,128)} %collective-permute-done.1.other_ref), custom_call_target="tpu_custom_call" | custom-call | tf_op jit(solution)/shard_map/pallas_call | solution.py:217
  10.5 1.6 %collective-permute-start.2 = (f32[288,2,128]{2,1,0:T(2,128)}, f32[288,2,128]{2,1,0:T(2,128)S(1)}, u32[]{:S(2)}, u32[]{:S(2)}) collective-permute-start(f32[288,2,128]{2,1,0:T(2,128)} %get-tuple-element.7), channel_id=1, source_target_pairs={{0,4},{4,0},{8,12},{12,8},{1,5},{5,1},{9,13},{13,9},{2,6},{6,2},{1... | collective-permute-start | bytes 884744 | tf_op jit(solution)/shard_map/ppermute | solution.py:224
  12.1 1.9 %collective-permute-start.3 = (f32[288,2,128]{2,1,0:T(2,128)}, f32[288,2,128]{2,1,0:T(2,128)}, u32[]{:S(2)}, u32[]{:S(2)}) collective-permute-start(f32[288,2,128]{2,1,0:T(2,128)} %get-tuple-element.8), channel_id=1, source_target_pairs={{4,8},{8,4},{5,9},{9,5},{6,10},{10,6},{7,11},{11,7},{20,24},{24,20... | collective-permute-start | bytes 884744 | tf_op jit(solution)/shard_map/ppermute | solution.py:224
  14.1 5.7 %collective-permute-done.2.refs_0_ = f32[288,2,128]{2,1,0:T(2,128)S(1)} collective-permute-done((f32[288,2,128]{2,1,0:T(2,128)}, f32[288,2,128]{2,1,0:T(2,128)S(1)}, u32[]{:S(2)}, u32[]{:S(2)}) %collective-permute-start.2) | collective-permute-done | bytes 294944 | tf_op jit(solution)/shard_map/ppermute | solution.py:224
  19.8 3.3 %collective-permute-done.3.refs_1_ = f32[288,2,128]{2,1,0:T(2,128)} collective-permute-done((f32[288,2,128]{2,1,0:T(2,128)}, f32[288,2,128]{2,1,0:T(2,128)}, u32[]{:S(2)}, u32[]{:S(2)}) %collective-permute-start.3) | collective-permute-done | bytes 294944 | tf_op jit(solution)/shard_map/ppermute | solution.py:224
  23.1 2.4 %shard_map.47 = f32[2,2304]{1,0:T(2,128)} custom-call(s32[5]{0:T(128)} %stack.36.flags_ref, f32[2,3,32,4,128]{4,3,2,1,0:T(4,128)} %bitcast.19, f32[2,3,32,4,128]{4,3,2,1,0:T(4,128)} %copy-done.1, f32[3,16,4,128]{3,2,1,0:T(4,128)} %sigma_ref.5, f32[3,16,4,128]{3,2,1,0:T(4,128)} %collective-permute-done.1.other_ref, f32[288,2,128]{2,1,0:T(2,128)} %copy-done.2, ...), custom_call_target="tpu_custom_call" | custom-call | tf_op jit(solution)/shard_map/pallas_call | solution.py:249
  25.4 1.5 %collective-permute-start.4 = (f32[2,2304]{1,0:T(2,128)}, f32[2,2304]{1,0:T(2,128)S(1)}, u32[]{:S(2)}, u32[]{:S(2)}) collective-permute-start(f32[2,2304]{1,0:T(2,128)} %shard_map.47), channel_id=1, source_target_pairs={{0,2},{2,0},{1,3},{3,1},{4,6},{6,4},{5,7},{7,5},{8,10},{10,8},{9,1... | collective-permute-start | bytes 55304 | tf_op jit(solution)/shard_map/ppermute | solution.py:256
  26.9 0.7 %and_convert_fusion.refs_4_ = f32[8,132]{1,0:T(8,128)} fusion(pred[132]{0:T(512)(128)(4,1)S(1)} %get-tuple-element.13, pred[132]{0:T(512)(128)(4,1)S(1)} %get-tuple-element.14, pred[8]{0:T(512)(128)(4,1)S(1)} %compare_and_fusion), kind=kLoop, calls=%fused_computation.2 | loop fusion | flops 3168 | bytes 4496 | tf_op jit(solution)/shard_map/convert_element_type | solution.py:293
  27.6 1.8 %collective-permute-done.4.refs_2_.refs_3_ = f32[2,2304]{1,0:T(2,128)S(1)} collective-permute-done((f32[2,2304]{1,0:T(2,128)}, f32[2,2304]{1,0:T(2,128)S(1)}, u32[]{:S(2)}, u32[]{:S(2)}) %collective-permute-start.4) | collective-permute-done | bytes 18464 | tf_op jit(solution)/shard_map/ppermute | solution.py:256
  29.4 0.6 %copy-done.3 = f32[2,2304]{1,0:T(2,128)} copy-done((f32[2,2304]{1,0:T(2,128)}, f32[2,2304]{1,0:T(2,128)S(1)}, u32[]{:S(2)}) %copy-start.3) | copy-done | bytes 18456
  30.0 7.9 %shard_map.48 = f32[2,3,32,4,128]{4,3,2,1,0:T(4,128)} custom-call(s32[5]{0:T(128)} %stack.36.flags_ref, f32[2,3,32,4,128]{4,3,2,1,0:T(4,128)} %bitcast.20, f32[2,3,32,4,128]{4,3,2,1,0:T(4,128)} %copy-done.1, f32[3,16,4,128]{3,2,1,0:T(4,128)} %sigma_ref.5, f32[3,16,4,128]{3,2,1,0:T(4,128)} %collective-permute-done.1.other_ref, f32[288,2,128]{2,1,0:T(2,128)} %copy-done.2, ...), custom_call_target="tpu_custom_call" | custom-call | tf_op jit(solution)/shard_map/pallas_call | solution.py:288
  (9 shorter events, 0.0 us)
Async XLA Ops:
  0.0 1.9 %copy-start = (bf16[16,2,3,32,4,128]{5,4,3,2,1,0:T(4,128)(2,1)S(1)}, bf16[16,2,3,32,4,128]{5,4,3,2,1,0:T(4,128)(2,1)}, u32[]{:S(2)}) copy-start(bf16[16,2,3,32,4,128]{5,4,3,2,1,0:T(4,128)(2,1)} %param.4) | copy-start | bytes 9437188
  5.4 2.2 %collective-permute-start = (f32[2,3,32,4,128]{4,3,2,1,0:T(4,128)}, f32[2,3,32,4,128]{4,3,2,1,0:T(4,128)S(1)}, u32[]{:S(2)}, u32[]{:S(2)}) collective-permute-start(f32[2,3,32,4,128]{4,3,2,1,0:T(4,128)} %bitcast.9), channel_id=1, source_target_pairs={{0,1},{1,0},{2,3},{3,2},{4,5},{5,4},{6,7},{7,6},{8,9},{9,8},{10,11... | collective-permute-start | bytes 1179656 | tf_op jit(solution)/shard_map/ppermute | solution.py:179
  5.4 2.2 %collective-permute-start.1 = (f32[3,16,4,128]{3,2,1,0:T(4,128)}, f32[3,16,4,128]{3,2,1,0:T(4,128)}, u32[]{:S(2)}, u32[]{:S(2)}) collective-permute-start(f32[3,16,4,128]{3,2,1,0:T(4,128)} %sigma_ref.5), channel_id=1, source_target_pairs={{0,1},{1,0},{2,3},{3,2},{4,5},{5,4},{6,7},{7,6},{8,9},{9,8},{10,11... | collective-permute-start | bytes 294920 | tf_op jit(solution)/shard_map/ppermute | solution.py:180
  7.6 0.8 %copy-start.1 = (f32[2,3,32,4,128]{4,3,2,1,0:T(4,128)}, f32[2,3,32,4,128]{4,3,2,1,0:T(4,128)S(1)}, u32[]{:S(2)}) copy-start(f32[2,3,32,4,128]{4,3,2,1,0:T(4,128)S(1)} %collective-permute-done.got_ref) | copy-start | bytes 1179652
  10.5 9.3 %collective-permute-start.2 = (f32[288,2,128]{2,1,0:T(2,128)}, f32[288,2,128]{2,1,0:T(2,128)S(1)}, u32[]{:S(2)}, u32[]{:S(2)}) collective-permute-start(f32[288,2,128]{2,1,0:T(2,128)} %get-tuple-element.7), channel_id=1, source_target_pairs={{0,4},{4,0},{8,12},{12,8},{1,5},{5,1},{9,13},{13,9},{2,6},{6,2},{1... | collective-permute-start | bytes 884744 | tf_op jit(solution)/shard_map/ppermute | solution.py:224
  12.1 11.0 %collective-permute-start.3 = (f32[288,2,128]{2,1,0:T(2,128)}, f32[288,2,128]{2,1,0:T(2,128)}, u32[]{:S(2)}, u32[]{:S(2)}) collective-permute-start(f32[288,2,128]{2,1,0:T(2,128)} %get-tuple-element.8), channel_id=1, source_target_pairs={{4,8},{8,4},{5,9},{9,5},{6,10},{10,6},{7,11},{11,7},{20,24},{24,20... | collective-permute-start | bytes 884744 | tf_op jit(solution)/shard_map/ppermute | solution.py:224
  19.8 3.3 %copy-start.2 = (f32[288,2,128]{2,1,0:T(2,128)}, f32[288,2,128]{2,1,0:T(2,128)S(1)}, u32[]{:S(2)}) copy-start(f32[288,2,128]{2,1,0:T(2,128)S(1)} %collective-permute-done.2.refs_0_) | copy-start | bytes 884740
  25.4 4.0 %collective-permute-start.4 = (f32[2,2304]{1,0:T(2,128)}, f32[2,2304]{1,0:T(2,128)S(1)}, u32[]{:S(2)}, u32[]{:S(2)}) collective-permute-start(f32[2,2304]{1,0:T(2,128)} %shard_map.47), channel_id=1, source_target_pairs={{0,2},{2,0},{1,3},{3,1},{4,6},{6,4},{5,7},{7,5},{8,10},{10,8},{9,1... | collective-permute-start | bytes 55304 | tf_op jit(solution)/shard_map/ppermute | solution.py:256
  29.4 0.6 %copy-start.3 = (f32[2,2304]{1,0:T(2,128)}, f32[2,2304]{1,0:T(2,128)S(1)}, u32[]{:S(2)}) copy-start(f32[2,2304]{1,0:T(2,128)S(1)} %collective-permute-done.4.refs_2_.refs_3_) | copy-start | bytes 55300

commit v17 on v16

--- a/solution.py
+++ b/solution.py
@@ -134,11 +134,11 @@
     return with_layout_constraint(x, Layout(major_to_minor=tuple(range(x.ndim))))
 
 
-def sweep_all(shot_ext, sigma_ext, inside):
+def sweep_all(shot_ext, sigma_ext, inside, outer):
     kappa = K_FREQ * sigma_ext
     delta = K_FREQ * (sigma_ext - 1.0)
     rhs = source_term(shot_ext, delta)
-    field = jnp.where(inside, jacobi(rhs, kappa), 0.0)
+    field = jnp.where(inside, jnp.where(outer, shot_ext, jacobi(rhs, kappa)), 0.0)
     for sweep in range(SWEEPS):
         curled = curl_curl(pad_z(field))
         field = shrink(field, 1)
@@ -207,16 +207,31 @@
         ).reshape(-1, width_x, width_y)
         return jnp.concatenate([shot, sigma], axis=0)
 
+    row_shot = primaries.shape[1:3] + (depth, 1, width_y)
+    payload_planes = n_planes * (w - 1) + shot_planes
+
+    def field0_row(row):
+        shot = row[:shot_planes].reshape(row_shot)
+        sigma = row[shot_planes:].reshape(-1, depth, 1, width_y)
+        rhs = source_term(shot, K_FREQ * (sigma - 1.0))
+        return jacobi(rhs, K_FREQ * sigma).reshape(shot_planes, 1, width_y)
+
     def send_kernel(flags_ref, own_ref, got_ref, sigma_ref, other_ref, *send_refs):
         cells = planes_of(flags_ref, own_ref, got_ref, sigma_ref, other_ref)
-        head = cells[:, :w]
-        tail = cells[:, width_x - w:]
+
+        def payload(inner_rows, outer_row):
+            parts = [cells[:, r:r + 1] for r in inner_rows]
+            parts.append(field0_row(cells[:, outer_row:outer_row + 1]))
+            return jnp.concatenate(parts, axis=0)
+
+        head = payload(range(0, w - 1), w - 1)
+        tail = payload(range(width_x - w + 1, width_x), width_x - w)
         for k in range(n_x):
             send_refs[k][...] = jnp.where(flags_ref[2 + k] == 1, tail, head)
 
     x_sends = pl.pallas_call(
         send_kernel,
-        out_shape=[jax.ShapeDtypeStruct((n_planes, w, width_y), jnp.float32)] * n_x,
+        out_shape=[jax.ShapeDtypeStruct((payload_planes, 1, width_y), jnp.float32)] * n_x,
         in_specs=[smem] + [vmem] * 4,
         out_specs=[vmem] * n_x,
     )(flags, *pieces)
@@ -226,6 +241,13 @@
     ]
     face_shape = (w, n_planes * ext_x)
 
+    def decode(payload, outer_first):
+        inner = [payload[k * n_planes:(k + 1) * n_planes] for k in range(w - 1)]
+        field0 = payload[n_planes * (w - 1):]
+        filler = jnp.zeros((n_planes - shot_planes, 1, width_y), payload.dtype)
+        outer = jnp.concatenate([field0, filler], axis=0)
+        return jnp.concatenate([outer] + inner if outer_first else inner + [outer], axis=1)
+
     def x_cells(flags_ref, own_ref, got_ref, sigma_ref, other_ref, got_refs):
         if n_x == 1:
             low = high = got_refs[0][...]
@@ -233,6 +255,8 @@
             even = flags_ref[1] == 1
             high = jnp.where(even, got_refs[0][...], got_refs[1][...])
             low = jnp.where(even, got_refs[1][...], got_refs[0][...])
+        low = decode(low, True)
+        high = decode(high, False)
         middle = planes_of(flags_ref, own_ref, got_ref, sigma_ref, other_ref)
         return jnp.concatenate([low, middle, high], axis=1)
 
@@ -283,7 +307,9 @@
         shot_ext = ext[:shot_planes].reshape(shot_shape + (depth, ext_x, ext_y))
         sigma_ext = ext[shot_planes:].reshape(-1, depth, ext_x, ext_y)
         keep = inside_ref[...] > 0.5
-        out_ref[...] = sweep_all(shot_ext, sigma_ext, keep)
+        row = lax.broadcasted_iota(jnp.int32, (ext_x, ext_y), 0)
+        outer = (row == 0) | (row == ext_x - 1)
+        out_ref[...] = sweep_all(shot_ext, sigma_ext, keep, outer)
 
     field = pl.pallas_call(
         sweeps_kernel,

time: 38.1 us -> 37.8 us (level)
  waiting for transfers between devices: 11.8 us -> 10.9 us
  Pallas kernels: 12.4 us -> 13.2 us
    ppermute x2, waiting for transfers between devices: 9.01 us -> 7.96 us  [body(): lax.ppermute(row_major(send), 'xb', pairs)]
    pallas_call x1, Pallas kernels: 2.17 us -> 2.63 us  [body(): pl.pallas_call(send_kernel, out_shape=[jax.ShapeDtypeStruct((payload_plan...]
  transfers between devices with their start and end apart: 5 -> 5, of which waited for: 4 -> 4; matrix products, arithmetic and copies ran while one was open for 4% -> 3% of each run, Pallas kernels for 0% -> 0%
where the time goes in v17:
time: 37.8 us; the launch traced here: 37.6 us
  Pallas kernels  13.2 us (35%)
  waiting for transfers between devices  10.9 us (29%)
  starting transfers between devices  5.49 us (15%)
  local copies, waits for them, and re-layouts  4.75 us (13%)
  matrix products  1.93 us (5%)
  other arithmetic  1.33 us (4%)
    pallas_call x1, Pallas kernels, body(): pl.pallas_call(sweeps_kernel, out_shape=jax.ShapeDtypeStruct(out_shape, j...  8.09 us
    ppermute x2, waiting for transfers between devices, body(): lax.ppermute(row_major(send), 'xb', pairs)  7.96 us
    ppermute x2, starting transfers between devices, body(): lax.ppermute(row_major(send), 'xb', pairs)  3.49 us
    pallas_call x1, Pallas kernels, body(): pl.pallas_call(send_kernel, out_shape=[jax.ShapeDtypeStruct((payload_plan...  2.63 us
    pallas_call x1, Pallas kernels, body(): pl.pallas_call(x_kernel, out_shape=[jax.ShapeDtypeStruct(face_shape, jnp....  2.49 us
    dot_general x1, matrix products, body(): lax.dot_general(weights, primaries, (((1,), (0,)), ((), ())), preferred_e...  1.93 us
    ppermute x1, waiting for transfers between devices, body(): lax.ppermute(row_major(send), 'yb', pairs)  1.82 us
    slice x1, local copies, waits for them, and re-layouts, body(): got = lax.ppermute(partial[0], 'tx', tx_ring)  1.55 us
  transfers between devices with their start and end apart: 5, of which 4 were waited for; matrix products, arithmetic and copies ran while one was open for 3% of the time, Pallas kernels for 0%

profile of v17, /device:TPU:16, one launch (start us, length us, event | category | flops | bytes accessed | tf_op | source)
XLA Modules:
  0.0 37.6 jit_solution(2731410349115576099)
XLA Ops:
  0.0 0.9 %reshape.9 = s32[2,16]{1,0:T(2,128)S(1)} reshape(s32[32]{0:T(128)} %param.6) | data formatting | bytes 256 | tf_op jit(solution)/shard_map/reshape | solution.py:171
  0.9 0.8 %reshape.10 = s32[2,16]{1,0:T(2,128)S(1)} reshape(s32[32]{0:T(128)} %param.7) | data formatting | bytes 256 | tf_op jit(solution)/shard_map/reshape | solution.py:172
  1.7 0.1 pad_add_fusion
  1.8 0.1 select_reduce_fusion.1
  1.9 0.0 copy-done
  1.9 1.9 %fusion = f32[2,2,3,32,4,128]{5,0,4,3,2,1:T(2,128)S(1)} fusion(bf16[16,2,3,32,4,128]{5,4,3,2,1,0:T(4,128)(2,1)S(1)} %copy-done, s32[16]{0:T(128)S(1)} %get-tuple-element.10, s32[16]{0:T(128)S(1)} %get-tuple-element.9, s32[2]{0:T(128)S(1)} %pad_add_fusion), kind=kOutput, calls=%fused_computation | convolution fusion | flops 6291584 | bytes 3932296 | tf_op jit(solution)/shard_map/dot_general | solution.py:175
  3.8 1.6 %fusion.13 = (f32[1,2,3,32,4,128]{5,0,4,3,2,1:T(1,128)}, f32[1,2,3,32,4,128]{5,0,4,3,2,1:T(1,128)}) fusion(f32[2,2,3,32,4,128]{5,0,4,3,2,1:T(2,128)S(1)} %fusion), kind=kLoop, calls=%fused_computation.20 | loop fusion | bytes 1572864 | tf_op jit(solution)/shard_map/slice | solution.py:179
  5.4 0.0 collective-permute-start
  5.4 0.5 %collective-permute-start.1 = (f32[3,16,4,128]{3,2,1,0:T(4,128)}, f32[3,16,4,128]{3,2,1,0:T(4,128)}, u32[]{:S(2)}, u32[]{:S(2)}) collective-permute-start(f32[3,16,4,128]{3,2,1,0:T(4,128)} %sigma_ref.5), channel_id=1, source_target_pairs={{0,1},{1,0},{2,3},{3,2},{4,5},{5,4},{6,7},{7,6},{8,9},{9,8},{10,11... | collective-permute-start | bytes 294920 | tf_op jit(solution)/shard_map/ppermute | solution.py:180
  5.9 0.1 stack.35
  6.0 0.5 %stack.36.flags_ref = s32[5]{0:T(128)} convert(pred[5]{0:T(512)(128)(4,1)S(1)} %stack.35) | non-fusion elementwise | flops 5 | bytes 25 | tf_op jit(solution)/shard_map/stack | solution.py:189
  6.5 1.1 %collective-permute-done.1.other_ref = f32[3,16,4,128]{3,2,1,0:T(4,128)} collective-permute-done((f32[3,16,4,128]{3,2,1,0:T(4,128)}, f32[3,16,4,128]{3,2,1,0:T(4,128)}, u32[]{:S(2)}, u32[]{:S(2)}) %collective-permute-start.1) | collective-permute-done | bytes 98336 | tf_op jit(solution)/shard_map/ppermute | solution.py:180
  7.6 0.8 %copy-done.1 = f32[2,3,32,4,128]{4,3,2,1,0:T(4,128)} copy-done((f32[2,3,32,4,128]{4,3,2,1,0:T(4,128)}, f32[2,3,32,4,128]{4,3,2,1,0:T(4,128)S(1)}, u32[]{:S(2)}) %copy-start.1) | copy-done | bytes 393240
  8.4 2.6 %shard_map.46 = (f32[480,1,128]{2,1,0:T(1,128)}, f32[480,1,128]{2,1,0:T(1,128)}) custom-call(s32[5]{0:T(128)} %stack.36.flags_ref, f32[2,3,32,4,128]{4,3,2,1,0:T(4,128)} %bitcast.18, f32[2,3,32,4,128]{4,3,2,1,0:T(4,128)} %copy-done.1, f32[3,16,4,128]{3,2,1,0:T(4,128)} %sigma_ref.5, f32[3,16,4,128]{3,2,1,0:T(4,128)} %collective-permute-done.1.other_ref), custom_call_target="tpu_custom_call" | custom-call | tf_op jit(solution)/shard_map/pallas_call | solution.py:232
  11.0 1.6 %collective-permute-start.2 = (f32[480,1,128]{2,1,0:T(1,128)}, f32[480,1,128]{2,1,0:T(1,128)S(1)}, u32[]{:S(2)}, u32[]{:S(2)}) collective-permute-start(f32[480,1,128]{2,1,0:T(1,128)} %get-tuple-element.7), channel_id=1, source_target_pairs={{0,4},{4,0},{8,12},{12,8},{1,5},{5,1},{9,13},{13,9},{2,6},{6,2},{1... | collective-permute-start | bytes 737288 | tf_op jit(solution)/shard_map/ppermute | solution.py:239
  12.6 1.9 %collective-permute-start.3 = (f32[480,1,128]{2,1,0:T(1,128)}, f32[480,1,128]{2,1,0:T(1,128)}, u32[]{:S(2)}, u32[]{:S(2)}) collective-permute-start(f32[480,1,128]{2,1,0:T(1,128)} %get-tuple-element.8), channel_id=1, source_target_pairs={{4,8},{8,4},{5,9},{9,5},{6,10},{10,6},{7,11},{11,7},{20,24},{24,20... | collective-permute-start | bytes 737288 | tf_op jit(solution)/shard_map/ppermute | solution.py:239
  14.5 4.7 %collective-permute-done.2.refs_0_ = f32[480,1,128]{2,1,0:T(1,128)S(1)} collective-permute-done((f32[480,1,128]{2,1,0:T(1,128)}, f32[480,1,128]{2,1,0:T(1,128)S(1)}, u32[]{:S(2)}, u32[]{:S(2)}) %collective-permute-start.2) | collective-permute-done | bytes 245792 | tf_op jit(solution)/shard_map/ppermute | solution.py:239
  19.2 3.3 %collective-permute-done.3.refs_1_ = f32[480,1,128]{2,1,0:T(1,128)} collective-permute-done((f32[480,1,128]{2,1,0:T(1,128)}, f32[480,1,128]{2,1,0:T(1,128)}, u32[]{:S(2)}, u32[]{:S(2)}) %collective-permute-start.3) | collective-permute-done | bytes 245792 | tf_op jit(solution)/shard_map/ppermute | solution.py:239
  22.5 2.5 %shard_map.47 = f32[2,2304]{1,0:T(2,128)} custom-call(s32[5]{0:T(128)} %stack.36.flags_ref, f32[2,3,32,4,128]{4,3,2,1,0:T(4,128)} %bitcast.19, f32[2,3,32,4,128]{4,3,2,1,0:T(4,128)} %copy-done.1, f32[3,16,4,128]{3,2,1,0:T(4,128)} %sigma_ref.5, f32[3,16,4,128]{3,2,1,0:T(4,128)} %collective-permute-done.1.other_ref, f32[480,1,128]{2,1,0:T(1,128)} %copy-done.2, ...), custom_call_target="tpu_custom_call" | custom-call | tf_op jit(solution)/shard_map/pallas_call | solution.py:273
  25.0 1.5 %collective-permute-start.4 = (f32[2,2304]{1,0:T(2,128)}, f32[2,2304]{1,0:T(2,128)S(1)}, u32[]{:S(2)}, u32[]{:S(2)}) collective-permute-start(f32[2,2304]{1,0:T(2,128)} %shard_map.47), channel_id=1, source_target_pairs={{0,2},{2,0},{1,3},{3,1},{4,6},{6,4},{5,7},{7,5},{8,10},{10,8},{9,1... | collective-permute-start | bytes 55304 | tf_op jit(solution)/shard_map/ppermute | solution.py:280
  26.5 0.7 %and_convert_fusion.refs_4_ = f32[8,132]{1,0:T(8,128)} fusion(pred[132]{0:T(512)(128)(4,1)S(1)} %get-tuple-element.13, pred[132]{0:T(512)(128)(4,1)S(1)} %get-tuple-element.14, pred[8]{0:T(512)(128)(4,1)S(1)} %compare_and_fusion), kind=kLoop, calls=%fused_computation.2 | loop fusion | flops 3168 | bytes 4496 | tf_op jit(solution)/shard_map/convert_element_type | solution.py:319
  27.1 1.8 %collective-permute-done.4.refs_2_.refs_3_ = f32[2,2304]{1,0:T(2,128)S(1)} collective-permute-done((f32[2,2304]{1,0:T(2,128)}, f32[2,2304]{1,0:T(2,128)S(1)}, u32[]{:S(2)}, u32[]{:S(2)}) %collective-permute-start.4) | collective-permute-done | bytes 18464 | tf_op jit(solution)/shard_map/ppermute | solution.py:280
  28.9 0.6 %copy-done.3 = f32[2,2304]{1,0:T(2,128)} copy-done((f32[2,2304]{1,0:T(2,128)}, f32[2,2304]{1,0:T(2,128)S(1)}, u32[]{:S(2)}) %copy-start.3) | copy-done | bytes 18456
  29.5 8.1 %shard_map.48 = f32[2,3,32,4,128]{4,3,2,1,0:T(4,128)} custom-call(s32[5]{0:T(128)} %stack.36.flags_ref, f32[2,3,32,4,128]{4,3,2,1,0:T(4,128)} %bitcast.20, f32[2,3,32,4,128]{4,3,2,1,0:T(4,128)} %copy-done.1, f32[3,16,4,128]{3,2,1,0:T(4,128)} %sigma_ref.5, f32[3,16,4,128]{3,2,1,0:T(4,128)} %collective-permute-done.1.other_ref, f32[480,1,128]{2,1,0:T(1,128)} %copy-done.2, ...), custom_call_target="tpu_custom_call" | custom-call | tf_op jit(solution)/shard_map/pallas_call | solution.py:314
  (9 shorter events, 0.0 us)
Async XLA Ops:
  0.0 1.9 %copy-start = (bf16[16,2,3,32,4,128]{5,4,3,2,1,0:T(4,128)(2,1)S(1)}, bf16[16,2,3,32,4,128]{5,4,3,2,1,0:T(4,128)(2,1)}, u32[]{:S(2)}) copy-start(bf16[16,2,3,32,4,128]{5,4,3,2,1,0:T(4,128)(2,1)} %param.4) | copy-start | bytes 9437188
  5.4 2.2 %collective-permute-start = (f32[2,3,32,4,128]{4,3,2,1,0:T(4,128)}, f32[2,3,32,4,128]{4,3,2,1,0:T(4,128)S(1)}, u32[]{:S(2)}, u32[]{:S(2)}) collective-permute-start(f32[2,3,32,4,128]{4,3,2,1,0:T(4,128)} %bitcast.9), channel_id=1, source_target_pairs={{0,1},{1,0},{2,3},{3,2},{4,5},{5,4},{6,7},{7,6},{8,9},{9,8},{10,11... | collective-permute-start | bytes 1179656 | tf_op jit(solution)/shard_map/ppermute | solution.py:179
  5.4 2.2 %collective-permute-start.1 = (f32[3,16,4,128]{3,2,1,0:T(4,128)}, f32[3,16,4,128]{3,2,1,0:T(4,128)}, u32[]{:S(2)}, u32[]{:S(2)}) collective-permute-start(f32[3,16,4,128]{3,2,1,0:T(4,128)} %sigma_ref.5), channel_id=1, source_target_pairs={{0,1},{1,0},{2,3},{3,2},{4,5},{5,4},{6,7},{7,6},{8,9},{9,8},{10,11... | collective-permute-start | bytes 294920 | tf_op jit(solution)/shard_map/ppermute | solution.py:180
  7.6 0.8 %copy-start.1 = (f32[2,3,32,4,128]{4,3,2,1,0:T(4,128)}, f32[2,3,32,4,128]{4,3,2,1,0:T(4,128)S(1)}, u32[]{:S(2)}) copy-start(f32[2,3,32,4,128]{4,3,2,1,0:T(4,128)S(1)} %collective-permute-done.got_ref) | copy-start | bytes 1179652
  11.0 8.2 %collective-permute-start.2 = (f32[480,1,128]{2,1,0:T(1,128)}, f32[480,1,128]{2,1,0:T(1,128)S(1)}, u32[]{:S(2)}, u32[]{:S(2)}) collective-permute-start(f32[480,1,128]{2,1,0:T(1,128)} %get-tuple-element.7), channel_id=1, source_target_pairs={{0,4},{4,0},{8,12},{12,8},{1,5},{5,1},{9,13},{13,9},{2,6},{6,2},{1... | collective-permute-start | bytes 737288 | tf_op jit(solution)/shard_map/ppermute | solution.py:239
  12.6 9.9 %collective-permute-start.3 = (f32[480,1,128]{2,1,0:T(1,128)}, f32[480,1,128]{2,1,0:T(1,128)}, u32[]{:S(2)}, u32[]{:S(2)}) collective-permute-start(f32[480,1,128]{2,1,0:T(1,128)} %get-tuple-element.8), channel_id=1, source_target_pairs={{4,8},{8,4},{5,9},{9,5},{6,10},{10,6},{7,11},{11,7},{20,24},{24,20... | collective-permute-start | bytes 737288 | tf_op jit(solution)/shard_map/ppermute | solution.py:239
  19.2 3.3 %copy-start.2 = (f32[480,1,128]{2,1,0:T(1,128)}, f32[480,1,128]{2,1,0:T(1,128)S(1)}, u32[]{:S(2)}) copy-start(f32[480,1,128]{2,1,0:T(1,128)S(1)} %collective-permute-done.2.refs_0_) | copy-start | bytes 737284
  25.0 4.0 %collective-permute-start.4 = (f32[2,2304]{1,0:T(2,128)}, f32[2,2304]{1,0:T(2,128)S(1)}, u32[]{:S(2)}, u32[]{:S(2)}) collective-permute-start(f32[2,2304]{1,0:T(2,128)} %shard_map.47), channel_id=1, source_target_pairs={{0,2},{2,0},{1,3},{3,1},{4,6},{6,4},{5,7},{7,5},{8,10},{10,8},{9,1... | collective-permute-start | bytes 55304 | tf_op jit(solution)/shard_map/ppermute | solution.py:280
  28.9 0.6 %copy-start.3 = (f32[2,2304]{1,0:T(2,128)}, f32[2,2304]{1,0:T(2,128)S(1)}, u32[]{:S(2)}) copy-start(f32[2,2304]{1,0:T(2,128)S(1)} %collective-permute-done.4.refs_2_.refs_3_) | copy-start | bytes 55300

commit v18 on v17

--- a/solution.py
+++ b/solution.py
@@ -145,6 +145,60 @@
         kappa = shrink(kappa, 1)
         rhs = shrink(rhs, 1)
         inside = shrink(inside, 1)
+        real_part = curled[..., 0, :, :, :, :] - kappa * field[..., 1, :, :, :, :]
+        imag_part = curled[..., 1, :, :, :, :] + kappa * field[..., 0, :, :, :, :]
+        applied = jnp.stack([real_part, imag_part], axis=-5)
+        field = field + RELAX * jacobi(rhs - applied, kappa)
+        if sweep < SWEEPS - 1:
+            field = jnp.where(inside, field, 0.0)
+    return field
+
+
+def rolled_sweeps(shot_ext, sigma_ext, inside, outer, rows, lanes):
+    def nxt(f, axis):
+        return pltpu.roll(f, (lanes if axis == -1 else rows) - 1, axis=f.ndim + axis)
+
+    def prv(f, axis):
+        return pltpu.roll(f, 1, axis=f.ndim + axis)
+
+    def curl(field):
+        padded = pad_z(field)
+        above = padded[..., 1:, :, :]
+        here = padded[..., :-1, :, :]
+
+        def dz(c):
+            return above[..., c, :, :, :] - here[..., c, :, :, :]
+
+        def dx(c):
+            return nxt(here[..., c, :, :, :], -2) - here[..., c, :, :, :]
+
+        def dy(c):
+            return nxt(here[..., c, :, :, :], -1) - here[..., c, :, :, :]
+
+        h_x = dy(2) - dz(1)
+        h_y = dz(0) - dx(2)
+        h_z = dx(1) - dy(0)
+
+        def bz(g):
+            return g[..., 1:, :, :] - g[..., :-1, :, :]
+
+        def bx(g):
+            return g[..., 1:, :, :] - prv(g[..., 1:, :, :], -2)
+
+        def by(g):
+            return g[..., 1:, :, :] - prv(g[..., 1:, :, :], -1)
+
+        c_x = by(h_z) - bz(h_y)
+        c_y = bz(h_x) - bx(h_z)
+        c_z = bx(h_y) - by(h_x)
+        return jnp.stack([c_x, c_y, c_z], axis=-4)
+
+    kappa = K_FREQ * sigma_ext
+    delta = K_FREQ * (sigma_ext - 1.0)
+    rhs = source_term(shot_ext, delta)
+    field = jnp.where(inside, jnp.where(outer, shot_ext, jacobi(rhs, kappa)), 0.0)
+    for sweep in range(SWEEPS):
+        curled = curl(field)
         real_part = curled[..., 0, :, :, :, :] - kappa * field[..., 1, :, :, :, :]
         imag_part = curled[..., 1, :, :, :, :] + kappa * field[..., 0, :, :, :, :]
         applied = jnp.stack([real_part, imag_part], axis=-5)
@@ -286,9 +340,13 @@
         even_y = lax.axis_index("yb") % 2 == 0
         y_high = jnp.where(even_y, y_gots[0], y_gots[1])
         y_low = jnp.where(even_y, y_gots[1], y_gots[0])
-    gx = lax.axis_index("xb") * width_x - SWEEPS + lax.broadcasted_iota(jnp.int32, (ext_x, ext_y), 0)
-    gy = lax.axis_index("yb") * width_y - SWEEPS + lax.broadcasted_iota(jnp.int32, (ext_x, ext_y), 1)
+    lanes = 2 * width_y
+    gx = lax.axis_index("xb") * width_x - SWEEPS + lax.broadcasted_iota(jnp.int32, (ext_x, lanes), 0)
+    lane = lax.broadcasted_iota(jnp.int32, (ext_x, lanes), 1)
+    local_y = jnp.where(lane >= lanes - SWEEPS, lane - lanes, lane)
+    gy = lax.axis_index("yb") * width_y + local_y
     inside = (gx >= 0) & (gx < width_x * lax.axis_size("xb")) & (gy >= 0) & (gy < width_y * lax.axis_size("yb"))
+    inside = inside & (local_y < width_y + SWEEPS)
     shot_shape = primaries.shape[1:3]
     out_shape = shot_shape + (depth, width_x, width_y)
 
@@ -303,13 +361,15 @@
         cells = x_cells(flags_ref, own_ref, got_ref, sigma_ref, other_ref, got_refs)
         low = unflip(low_ref[...])
         high = low if n_y == 1 else unflip(high_ref[...])
-        ext = jnp.concatenate([low, cells, high], axis=2)
-        shot_ext = ext[:shot_planes].reshape(shot_shape + (depth, ext_x, ext_y))
-        sigma_ext = ext[shot_planes:].reshape(-1, depth, ext_x, ext_y)
+        gap = jnp.zeros((n_planes, ext_x, lanes - width_y - 2 * w), jnp.float32)
+        ext = jnp.concatenate([cells, high, gap, low], axis=2)
+        shot_ext = ext[:shot_planes].reshape(shot_shape + (depth, ext_x, lanes))
+        sigma_ext = ext[shot_planes:].reshape(-1, depth, ext_x, lanes)
         keep = inside_ref[...] > 0.5
-        row = lax.broadcasted_iota(jnp.int32, (ext_x, ext_y), 0)
+        row = lax.broadcasted_iota(jnp.int32, (ext_x, lanes), 0)
         outer = (row == 0) | (row == ext_x - 1)
-        out_ref[...] = sweep_all(shot_ext, sigma_ext, keep, outer)
+        field = rolled_sweeps(shot_ext, sigma_ext, keep, outer, ext_x, lanes)
+        out_ref[...] = field[..., w:w + width_x, :width_y]
 
     field = pl.pallas_call(
         sweeps_kernel,

time: 37.8 us -> 35.6 us (0.942)
  Pallas kernels: 13.2 us -> 11 us
    pallas_call x1, Pallas kernels: 8.09 us -> 5.81 us  [body(): pl.pallas_call(sweeps_kernel, out_shape=jax.ShapeDtypeStruct(out_shape, j...]
  transfers between devices with their start and end apart: 5 -> 5, of which waited for: 4 -> 4; matrix products, arithmetic and copies ran while one was open for 3% -> 4% of each run, Pallas kernels for 0% -> 0%
where the time goes in v18:
time: 35.6 us; the launch traced here: 35.4 us
  Pallas kernels  11 us (31%)
  waiting for transfers between devices  10.8 us (30%)
  starting transfers between devices  5.49 us (15%)
  local copies, waits for them, and re-layouts  4.78 us (13%)
  matrix products  1.93 us (5%)
  other arithmetic  1.42 us (4%)
    ppermute x2, waiting for transfers between devices, body(): lax.ppermute(row_major(send), 'xb', pairs)  7.95 us
    pallas_call x1, Pallas kernels, body(): pl.pallas_call(sweeps_kernel, out_shape=jax.ShapeDtypeStruct(out_shape, j...  5.81 us
    ppermute x2, starting transfers between devices, body(): lax.ppermute(row_major(send), 'xb', pairs)  3.49 us
    pallas_call x1, Pallas kernels, body(): pl.pallas_call(send_kernel, out_shape=[jax.ShapeDtypeStruct((payload_plan...  2.65 us
    pallas_call x1, Pallas kernels, body(): pl.pallas_call(x_kernel, out_shape=[jax.ShapeDtypeStruct(face_shape, jnp....  2.49 us
    dot_general x1, matrix products, body(): lax.dot_general(weights, primaries, (((1,), (0,)), ((), ())), preferred_e...  1.93 us
    ppermute x1, waiting for transfers between devices, body(): lax.ppermute(row_major(send), 'yb', pairs)  1.82 us
    slice x1, local copies, waits for them, and re-layouts, body(): got = lax.ppermute(partial[0], 'tx', tx_ring)  1.56 us
  transfers between devices with their start and end apart: 5, of which 4 were waited for; matrix products, arithmetic and copies ran while one was open for 4% of the time, Pallas kernels for 0%

profile of v18, /device:TPU:16, one launch (start us, length us, event | category | flops | bytes accessed | tf_op | source)
XLA Modules:
  0.0 35.4 jit_solution(11464145064392221716)
XLA Ops:
  0.0 0.9 %reshape.9 = s32[2,16]{1,0:T(2,128)S(1)} reshape(s32[32]{0:T(128)} %param.6) | data formatting | bytes 256 | tf_op jit(solution)/shard_map/reshape | solution.py:225
  0.9 0.8 %reshape.10 = s32[2,16]{1,0:T(2,128)S(1)} reshape(s32[32]{0:T(128)} %param.7) | data formatting | bytes 256 | tf_op jit(solution)/shard_map/reshape | solution.py:226
  1.7 0.1 pad_add_fusion
  1.8 0.1 select_reduce_fusion.1
  1.9 0.0 copy-done
  1.9 1.9 %fusion = f32[2,2,3,32,4,128]{5,0,4,3,2,1:T(2,128)S(1)} fusion(bf16[16,2,3,32,4,128]{5,4,3,2,1,0:T(4,128)(2,1)S(1)} %copy-done, s32[16]{0:T(128)S(1)} %get-tuple-element.10, s32[16]{0:T(128)S(1)} %get-tuple-element.9, s32[2]{0:T(128)S(1)} %pad_add_fusion), kind=kOutput, calls=%fused_computation | convolution fusion | flops 6291584 | bytes 3932296 | tf_op jit(solution)/shard_map/dot_general | solution.py:229
  3.8 1.6 %fusion.19 = (f32[1,2,3,32,4,128]{5,0,4,3,2,1:T(1,128)}, f32[1,2,3,32,4,128]{5,0,4,3,2,1:T(1,128)}) fusion(f32[2,2,3,32,4,128]{5,0,4,3,2,1:T(2,128)S(1)} %fusion), kind=kLoop, calls=%fused_computation.27 | loop fusion | bytes 1572864 | tf_op jit(solution)/shard_map/slice | solution.py:233
  5.4 0.0 collective-permute-start
  5.4 0.5 %collective-permute-start.1 = (f32[3,16,4,128]{3,2,1,0:T(4,128)}, f32[3,16,4,128]{3,2,1,0:T(4,128)}, u32[]{:S(2)}, u32[]{:S(2)}) collective-permute-start(f32[3,16,4,128]{3,2,1,0:T(4,128)} %sigma_ref.5), channel_id=1, source_target_pairs={{0,1},{1,0},{2,3},{3,2},{4,5},{5,4},{6,7},{7,6},{8,9},{9,8},{10,11... | collective-permute-start | bytes 294920 | tf_op jit(solution)/shard_map/ppermute | solution.py:234
  5.9 0.1 stack.35
  6.0 0.6 %stack.36.flags_ref = s32[5]{0:T(128)} convert(pred[5]{0:T(512)(128)(4,1)S(1)} %stack.35) | non-fusion elementwise | flops 5 | bytes 25 | tf_op jit(solution)/shard_map/stack | solution.py:243
  6.6 1.0 %collective-permute-done.1.other_ref = f32[3,16,4,128]{3,2,1,0:T(4,128)} collective-permute-done((f32[3,16,4,128]{3,2,1,0:T(4,128)}, f32[3,16,4,128]{3,2,1,0:T(4,128)}, u32[]{:S(2)}, u32[]{:S(2)}) %collective-permute-start.1) | collective-permute-done | bytes 98336 | tf_op jit(solution)/shard_map/ppermute | solution.py:234
  7.6 0.8 %copy-done.1 = f32[2,3,32,4,128]{4,3,2,1,0:T(4,128)} copy-done((f32[2,3,32,4,128]{4,3,2,1,0:T(4,128)}, f32[2,3,32,4,128]{4,3,2,1,0:T(4,128)S(1)}, u32[]{:S(2)}) %copy-start.1) | copy-done | bytes 393240
  8.4 2.7 %shard_map.46 = (f32[480,1,128]{2,1,0:T(1,128)}, f32[480,1,128]{2,1,0:T(1,128)}) custom-call(s32[5]{0:T(128)} %stack.36.flags_ref, f32[2,3,32,4,128]{4,3,2,1,0:T(4,128)} %bitcast.18, f32[2,3,32,4,128]{4,3,2,1,0:T(4,128)} %copy-done.1, f32[3,16,4,128]{3,2,1,0:T(4,128)} %sigma_ref.5, f32[3,16,4,128]{3,2,1,0:T(4,128)} %collective-permute-done.1.other_ref), custom_call_target="tpu_custom_call" | custom-call | tf_op jit(solution)/shard_map/pallas_call | solution.py:286
  11.0 1.6 %collective-permute-start.2 = (f32[480,1,128]{2,1,0:T(1,128)}, f32[480,1,128]{2,1,0:T(1,128)S(1)}, u32[]{:S(2)}, u32[]{:S(2)}) collective-permute-start(f32[480,1,128]{2,1,0:T(1,128)} %get-tuple-element.7), channel_id=1, source_target_pairs={{0,4},{4,0},{8,12},{12,8},{1,5},{5,1},{9,13},{13,9},{2,6},{6,2},{1... | collective-permute-start | bytes 737288 | tf_op jit(solution)/shard_map/ppermute | solution.py:293
  12.6 1.9 %collective-permute-start.3 = (f32[480,1,128]{2,1,0:T(1,128)}, f32[480,1,128]{2,1,0:T(1,128)}, u32[]{:S(2)}, u32[]{:S(2)}) collective-permute-start(f32[480,1,128]{2,1,0:T(1,128)} %get-tuple-element.8), channel_id=1, source_target_pairs={{4,8},{8,4},{5,9},{9,5},{6,10},{10,6},{7,11},{11,7},{20,24},{24,20... | collective-permute-start | bytes 737288 | tf_op jit(solution)/shard_map/ppermute | solution.py:293
  14.6 4.7 %collective-permute-done.2.refs_0_ = f32[480,1,128]{2,1,0:T(1,128)S(1)} collective-permute-done((f32[480,1,128]{2,1,0:T(1,128)}, f32[480,1,128]{2,1,0:T(1,128)S(1)}, u32[]{:S(2)}, u32[]{:S(2)}) %collective-permute-start.2) | collective-permute-done | bytes 245792 | tf_op jit(solution)/shard_map/ppermute | solution.py:293
  19.2 3.3 %collective-permute-done.3.refs_1_ = f32[480,1,128]{2,1,0:T(1,128)} collective-permute-done((f32[480,1,128]{2,1,0:T(1,128)}, f32[480,1,128]{2,1,0:T(1,128)}, u32[]{:S(2)}, u32[]{:S(2)}) %collective-permute-start.3) | collective-permute-done | bytes 245792 | tf_op jit(solution)/shard_map/ppermute | solution.py:293
  22.5 2.5 %shard_map.47 = f32[2,2304]{1,0:T(2,128)} custom-call(s32[5]{0:T(128)} %stack.36.flags_ref, f32[2,3,32,4,128]{4,3,2,1,0:T(4,128)} %bitcast.19, f32[2,3,32,4,128]{4,3,2,1,0:T(4,128)} %copy-done.1, f32[3,16,4,128]{3,2,1,0:T(4,128)} %sigma_ref.5, f32[3,16,4,128]{3,2,1,0:T(4,128)} %collective-permute-done.1.other_ref, f32[480,1,128]{2,1,0:T(1,128)} %copy-done.2, ...), custom_call_target="tpu_custom_call" | custom-call | tf_op jit(solution)/shard_map/pallas_call | solution.py:327
  25.0 1.5 %collective-permute-start.4 = (f32[2,2304]{1,0:T(2,128)}, f32[2,2304]{1,0:T(2,128)S(1)}, u32[]{:S(2)}, u32[]{:S(2)}) collective-permute-start(f32[2,2304]{1,0:T(2,128)} %shard_map.47), channel_id=1, source_target_pairs={{0,2},{2,0},{1,3},{3,1},{4,6},{6,4},{5,7},{7,5},{8,10},{10,8},{9,1... | collective-permute-start | bytes 55304 | tf_op jit(solution)/shard_map/ppermute | solution.py:334
  26.5 0.7 %fusion.9.refs_4_ = f32[8,256]{1,0:T(8,128)} fusion(s32[256]{0:T(256)S(1)} %iota_add_fusion, s32[]{:T(128)S(6)} %mul.7, pred[8]{0:T(512)(128)(4,1)S(1)} %compare_and_fusion, pred[256]{0:T(512)(128)(4,1)S(1)} %iota_compare_fusion), kind=kLoop, calls=%fused_computation.10 | loop fusion | flops 18432 | bytes 9484 | tf_op jit(solution)/shard_map/convert_element_type | solution.py:379
  27.2 1.8 %collective-permute-done.4.refs_2_.refs_3_ = f32[2,2304]{1,0:T(2,128)S(1)} collective-permute-done((f32[2,2304]{1,0:T(2,128)}, f32[2,2304]{1,0:T(2,128)S(1)}, u32[]{:S(2)}, u32[]{:S(2)}) %collective-permute-start.4) | collective-permute-done | bytes 18464 | tf_op jit(solution)/shard_map/ppermute | solution.py:334
  29.0 0.6 %copy-done.3 = f32[2,2304]{1,0:T(2,128)} copy-done((f32[2,2304]{1,0:T(2,128)}, f32[2,2304]{1,0:T(2,128)S(1)}, u32[]{:S(2)}) %copy-start.3) | copy-done | bytes 18456
  29.6 5.8 %shard_map.48 = f32[2,3,32,4,128]{4,3,2,1,0:T(4,128)} custom-call(s32[5]{0:T(128)} %stack.36.flags_ref, f32[2,3,32,4,128]{4,3,2,1,0:T(4,128)} %bitcast.20, f32[2,3,32,4,128]{4,3,2,1,0:T(4,128)} %copy-done.1, f32[3,16,4,128]{3,2,1,0:T(4,128)} %sigma_ref.5, f32[3,16,4,128]{3,2,1,0:T(4,128)} %collective-permute-done.1.other_ref, f32[480,1,128]{2,1,0:T(1,128)} %copy-done.2, ...), custom_call_target="tpu_custom_call" | custom-call | tf_op jit(solution)/shard_map/pallas_call | solution.py:374
  (10 shorter events, 0.0 us)
Async XLA Ops:
  0.0 1.9 %copy-start = (bf16[16,2,3,32,4,128]{5,4,3,2,1,0:T(4,128)(2,1)S(1)}, bf16[16,2,3,32,4,128]{5,4,3,2,1,0:T(4,128)(2,1)}, u32[]{:S(2)}) copy-start(bf16[16,2,3,32,4,128]{5,4,3,2,1,0:T(4,128)(2,1)} %param.4) | copy-start | bytes 9437188
  5.4 2.2 %collective-permute-start = (f32[2,3,32,4,128]{4,3,2,1,0:T(4,128)}, f32[2,3,32,4,128]{4,3,2,1,0:T(4,128)S(1)}, u32[]{:S(2)}, u32[]{:S(2)}) collective-permute-start(f32[2,3,32,4,128]{4,3,2,1,0:T(4,128)} %bitcast.9), channel_id=1, source_target_pairs={{0,1},{1,0},{2,3},{3,2},{4,5},{5,4},{6,7},{7,6},{8,9},{9,8},{10,11... | collective-permute-start | bytes 1179656 | tf_op jit(solution)/shard_map/ppermute | solution.py:233
  5.4 2.2 %collective-permute-start.1 = (f32[3,16,4,128]{3,2,1,0:T(4,128)}, f32[3,16,4,128]{3,2,1,0:T(4,128)}, u32[]{:S(2)}, u32[]{:S(2)}) collective-permute-start(f32[3,16,4,128]{3,2,1,0:T(4,128)} %sigma_ref.5), channel_id=1, source_target_pairs={{0,1},{1,0},{2,3},{3,2},{4,5},{5,4},{6,7},{7,6},{8,9},{9,8},{10,11... | collective-permute-start | bytes 294920 | tf_op jit(solution)/shard_map/ppermute | solution.py:234
  7.6 0.8 %copy-start.1 = (f32[2,3,32,4,128]{4,3,2,1,0:T(4,128)}, f32[2,3,32,4,128]{4,3,2,1,0:T(4,128)S(1)}, u32[]{:S(2)}) copy-start(f32[2,3,32,4,128]{4,3,2,1,0:T(4,128)S(1)} %collective-permute-done.got_ref) | copy-start | bytes 1179652
  11.0 8.2 %collective-permute-start.2 = (f32[480,1,128]{2,1,0:T(1,128)}, f32[480,1,128]{2,1,0:T(1,128)S(1)}, u32[]{:S(2)}, u32[]{:S(2)}) collective-permute-start(f32[480,1,128]{2,1,0:T(1,128)} %get-tuple-element.7), channel_id=1, source_target_pairs={{0,4},{4,0},{8,12},{12,8},{1,5},{5,1},{9,13},{13,9},{2,6},{6,2},{1... | collective-permute-start | bytes 737288 | tf_op jit(solution)/shard_map/ppermute | solution.py:293
  12.6 9.9 %collective-permute-start.3 = (f32[480,1,128]{2,1,0:T(1,128)}, f32[480,1,128]{2,1,0:T(1,128)}, u32[]{:S(2)}, u32[]{:S(2)}) collective-permute-start(f32[480,1,128]{2,1,0:T(1,128)} %get-tuple-element.8), channel_id=1, source_target_pairs={{4,8},{8,4},{5,9},{9,5},{6,10},{10,6},{7,11},{11,7},{20,24},{24,20... | collective-permute-start | bytes 737288 | tf_op jit(solution)/shard_map/ppermute | solution.py:293
  19.2 3.3 %copy-start.2 = (f32[480,1,128]{2,1,0:T(1,128)}, f32[480,1,128]{2,1,0:T(1,128)S(1)}, u32[]{:S(2)}) copy-start(f32[480,1,128]{2,1,0:T(1,128)S(1)} %collective-permute-done.2.refs_0_) | copy-start | bytes 737284
  25.0 4.0 %collective-permute-start.4 = (f32[2,2304]{1,0:T(2,128)}, f32[2,2304]{1,0:T(2,128)S(1)}, u32[]{:S(2)}, u32[]{:S(2)}) collective-permute-start(f32[2,2304]{1,0:T(2,128)} %shard_map.47), channel_id=1, source_target_pairs={{0,2},{2,0},{1,3},{3,1},{4,6},{6,4},{5,7},{7,5},{8,10},{10,8},{9,1... | collective-permute-start | bytes 55304 | tf_op jit(solution)/shard_map/ppermute | solution.py:334
  29.0 0.6 %copy-start.3 = (f32[2,2304]{1,0:T(2,128)}, f32[2,2304]{1,0:T(2,128)S(1)}, u32[]{:S(2)}) copy-start(f32[2,2304]{1,0:T(2,128)S(1)} %collective-permute-done.4.refs_2_.refs_3_) | copy-start | bytes 55300

commit v19 on v18

--- a/solution.py
+++ b/solution.py
@@ -359,10 +359,10 @@
         got_refs = refs[:n_x]
         low_ref, high_ref, inside_ref, out_ref = refs[n_x:]
         cells = x_cells(flags_ref, own_ref, got_ref, sigma_ref, other_ref, got_refs)
-        low = unflip(low_ref[...])
-        high = low if n_y == 1 else unflip(high_ref[...])
-        gap = jnp.zeros((n_planes, ext_x, lanes - width_y - 2 * w), jnp.float32)
-        ext = jnp.concatenate([cells, high, gap, low], axis=2)
+        gap = jnp.zeros((lanes - width_y - 2 * w, n_planes * ext_x), jnp.float32)
+        upper = jnp.concatenate([high_ref[...], gap, low_ref[...]], axis=0)
+        upper = upper.T.reshape(n_planes, ext_x, lanes - width_y)
+        ext = jnp.concatenate([cells, upper], axis=2)
         shot_ext = ext[:shot_planes].reshape(shot_shape + (depth, ext_x, lanes))
         sigma_ext = ext[shot_planes:].reshape(-1, depth, ext_x, lanes)
         keep = inside_ref[...] > 0.5

time: 35.6 us -> 35.2 us (0.989)
  Pallas kernels: 11 us -> 10.5 us
    pallas_call x1, Pallas kernels: 5.81 us -> 5.37 us  [body(): pl.pallas_call(sweeps_kernel, out_shape=jax.ShapeDtypeStruct(out_shape, j...]
where the time goes in v19:
time: 35.2 us; the launch traced here: 35 us
  waiting for transfers between devices  10.8 us (31%)
  Pallas kernels  10.5 us (30%)
  starting transfers between devices  5.49 us (16%)
  local copies, waits for them, and re-layouts  4.78 us (14%)
  matrix products  1.93 us (5%)
  other arithmetic  1.42 us (4%)
    ppermute x2, waiting for transfers between devices, body(): lax.ppermute(row_major(send), 'xb', pairs)  7.95 us
    pallas_call x1, Pallas kernels, body(): pl.pallas_call(sweeps_kernel, out_shape=jax.ShapeDtypeStruct(out_shape, j...  5.37 us
    ppermute x2, starting transfers between devices, body(): lax.ppermute(row_major(send), 'xb', pairs)  3.49 us
    pallas_call x1, Pallas kernels, body(): pl.pallas_call(send_kernel, out_shape=[jax.ShapeDtypeStruct((payload_plan...  2.65 us
    pallas_call x1, Pallas kernels, body(): pl.pallas_call(x_kernel, out_shape=[jax.ShapeDtypeStruct(face_shape, jnp....  2.49 us
    dot_general x1, matrix products, body(): lax.dot_general(weights, primaries, (((1,), (0,)), ((), ())), preferred_e...  1.93 us
    ppermute x1, waiting for transfers between devices, body(): lax.ppermute(row_major(send), 'yb', pairs)  1.82 us
    slice x1, local copies, waits for them, and re-layouts, body(): got = lax.ppermute(partial[0], 'tx', tx_ring)  1.56 us
  transfers between devices with their start and end apart: 5, of which 4 were waited for; matrix products, arithmetic and copies ran while one was open for 4% of the time, Pallas kernels for 0%

profile of v19, /device:TPU:16, one launch (start us, length us, event | category | flops | bytes accessed | tf_op | source)
XLA Modules:
  0.0 35.0 jit_solution(9916950894147108084)
XLA Ops:
  0.0 0.9 %reshape.9 = s32[2,16]{1,0:T(2,128)S(1)} reshape(s32[32]{0:T(128)} %param.6) | data formatting | bytes 256 | tf_op jit(solution)/shard_map/reshape | solution.py:225
  0.9 0.8 %reshape.10 = s32[2,16]{1,0:T(2,128)S(1)} reshape(s32[32]{0:T(128)} %param.7) | data formatting | bytes 256 | tf_op jit(solution)/shard_map/reshape | solution.py:226
  1.7 0.1 pad_add_fusion
  1.8 0.1 select_reduce_fusion.1
  1.9 0.0 copy-done
  1.9 1.9 %fusion = f32[2,2,3,32,4,128]{5,0,4,3,2,1:T(2,128)S(1)} fusion(bf16[16,2,3,32,4,128]{5,4,3,2,1,0:T(4,128)(2,1)S(1)} %copy-done, s32[16]{0:T(128)S(1)} %get-tuple-element.10, s32[16]{0:T(128)S(1)} %get-tuple-element.9, s32[2]{0:T(128)S(1)} %pad_add_fusion), kind=kOutput, calls=%fused_computation | convolution fusion | flops 6291584 | bytes 3932296 | tf_op jit(solution)/shard_map/dot_general | solution.py:229
  3.8 1.6 %fusion.19 = (f32[1,2,3,32,4,128]{5,0,4,3,2,1:T(1,128)}, f32[1,2,3,32,4,128]{5,0,4,3,2,1:T(1,128)}) fusion(f32[2,2,3,32,4,128]{5,0,4,3,2,1:T(2,128)S(1)} %fusion), kind=kLoop, calls=%fused_computation.27 | loop fusion | bytes 1572864 | tf_op jit(solution)/shard_map/slice | solution.py:233
  5.4 0.0 collective-permute-start
  5.4 0.5 %collective-permute-start.1 = (f32[3,16,4,128]{3,2,1,0:T(4,128)}, f32[3,16,4,128]{3,2,1,0:T(4,128)}, u32[]{:S(2)}, u32[]{:S(2)}) collective-permute-start(f32[3,16,4,128]{3,2,1,0:T(4,128)} %sigma_ref.5), channel_id=1, source_target_pairs={{0,1},{1,0},{2,3},{3,2},{4,5},{5,4},{6,7},{7,6},{8,9},{9,8},{10,11... | collective-permute-start | bytes 294920 | tf_op jit(solution)/shard_map/ppermute | solution.py:234
  5.9 0.1 stack.35
  6.0 0.6 %stack.36.flags_ref = s32[5]{0:T(128)} convert(pred[5]{0:T(512)(128)(4,1)S(1)} %stack.35) | non-fusion elementwise | flops 5 | bytes 25 | tf_op jit(solution)/shard_map/stack | solution.py:243
  6.6 1.0 %collective-permute-done.1.other_ref = f32[3,16,4,128]{3,2,1,0:T(4,128)} collective-permute-done((f32[3,16,4,128]{3,2,1,0:T(4,128)}, f32[3,16,4,128]{3,2,1,0:T(4,128)}, u32[]{:S(2)}, u32[]{:S(2)}) %collective-permute-start.1) | collective-permute-done | bytes 98336 | tf_op jit(solution)/shard_map/ppermute | solution.py:234
  7.6 0.8 %copy-done.1 = f32[2,3,32,4,128]{4,3,2,1,0:T(4,128)} copy-done((f32[2,3,32,4,128]{4,3,2,1,0:T(4,128)}, f32[2,3,32,4,128]{4,3,2,1,0:T(4,128)S(1)}, u32[]{:S(2)}) %copy-start.1) | copy-done | bytes 393240
  8.4 2.7 %shard_map.46 = (f32[480,1,128]{2,1,0:T(1,128)}, f32[480,1,128]{2,1,0:T(1,128)}) custom-call(s32[5]{0:T(128)} %stack.36.flags_ref, f32[2,3,32,4,128]{4,3,2,1,0:T(4,128)} %bitcast.18, f32[2,3,32,4,128]{4,3,2,1,0:T(4,128)} %copy-done.1, f32[3,16,4,128]{3,2,1,0:T(4,128)} %sigma_ref.5, f32[3,16,4,128]{3,2,1,0:T(4,128)} %collective-permute-done.1.other_ref), custom_call_target="tpu_custom_call" | custom-call | tf_op jit(solution)/shard_map/pallas_call | solution.py:286
  11.0 1.6 %collective-permute-start.2 = (f32[480,1,128]{2,1,0:T(1,128)}, f32[480,1,128]{2,1,0:T(1,128)S(1)}, u32[]{:S(2)}, u32[]{:S(2)}) collective-permute-start(f32[480,1,128]{2,1,0:T(1,128)} %get-tuple-element.7), channel_id=1, source_target_pairs={{0,4},{4,0},{8,12},{12,8},{1,5},{5,1},{9,13},{13,9},{2,6},{6,2},{1... | collective-permute-start | bytes 737288 | tf_op jit(solution)/shard_map/ppermute | solution.py:293
  12.6 1.9 %collective-permute-start.3 = (f32[480,1,128]{2,1,0:T(1,128)}, f32[480,1,128]{2,1,0:T(1,128)}, u32[]{:S(2)}, u32[]{:S(2)}) collective-permute-start(f32[480,1,128]{2,1,0:T(1,128)} %get-tuple-element.8), channel_id=1, source_target_pairs={{4,8},{8,4},{5,9},{9,5},{6,10},{10,6},{7,11},{11,7},{20,24},{24,20... | collective-permute-start | bytes 737288 | tf_op jit(solution)/shard_map/ppermute | solution.py:293
  14.6 4.7 %collective-permute-done.2.refs_0_ = f32[480,1,128]{2,1,0:T(1,128)S(1)} collective-permute-done((f32[480,1,128]{2,1,0:T(1,128)}, f32[480,1,128]{2,1,0:T(1,128)S(1)}, u32[]{:S(2)}, u32[]{:S(2)}) %collective-permute-start.2) | collective-permute-done | bytes 245792 | tf_op jit(solution)/shard_map/ppermute | solution.py:293
  19.2 3.3 %collective-permute-done.3.refs_1_ = f32[480,1,128]{2,1,0:T(1,128)} collective-permute-done((f32[480,1,128]{2,1,0:T(1,128)}, f32[480,1,128]{2,1,0:T(1,128)}, u32[]{:S(2)}, u32[]{:S(2)}) %collective-permute-start.3) | collective-permute-done | bytes 245792 | tf_op jit(solution)/shard_map/ppermute | solution.py:293
  22.5 2.5 %shard_map.47 = f32[2,2304]{1,0:T(2,128)} custom-call(s32[5]{0:T(128)} %stack.36.flags_ref, f32[2,3,32,4,128]{4,3,2,1,0:T(4,128)} %bitcast.19, f32[2,3,32,4,128]{4,3,2,1,0:T(4,128)} %copy-done.1, f32[3,16,4,128]{3,2,1,0:T(4,128)} %sigma_ref.5, f32[3,16,4,128]{3,2,1,0:T(4,128)} %collective-permute-done.1.other_ref, f32[480,1,128]{2,1,0:T(1,128)} %copy-done.2, ...), custom_call_target="tpu_custom_call" | custom-call | tf_op jit(solution)/shard_map/pallas_call | solution.py:327
  25.0 1.5 %collective-permute-start.4 = (f32[2,2304]{1,0:T(2,128)}, f32[2,2304]{1,0:T(2,128)S(1)}, u32[]{:S(2)}, u32[]{:S(2)}) collective-permute-start(f32[2,2304]{1,0:T(2,128)} %shard_map.47), channel_id=1, source_target_pairs={{0,2},{2,0},{1,3},{3,1},{4,6},{6,4},{5,7},{7,5},{8,10},{10,8},{9,1... | collective-permute-start | bytes 55304 | tf_op jit(solution)/shard_map/ppermute | solution.py:334
  26.5 0.7 %fusion.9.refs_4_ = f32[8,256]{1,0:T(8,128)} fusion(s32[256]{0:T(256)S(1)} %iota_add_fusion, s32[]{:T(128)S(6)} %mul.7, pred[8]{0:T(512)(128)(4,1)S(1)} %compare_and_fusion, pred[256]{0:T(512)(128)(4,1)S(1)} %iota_compare_fusion), kind=kLoop, calls=%fused_computation.10 | loop fusion | flops 18432 | bytes 9484 | tf_op jit(solution)/shard_map/convert_element_type | solution.py:379
  27.2 1.8 %collective-permute-done.4.refs_2_.refs_3_ = f32[2,2304]{1,0:T(2,128)S(1)} collective-permute-done((f32[2,2304]{1,0:T(2,128)}, f32[2,2304]{1,0:T(2,128)S(1)}, u32[]{:S(2)}, u32[]{:S(2)}) %collective-permute-start.4) | collective-permute-done | bytes 18464 | tf_op jit(solution)/shard_map/ppermute | solution.py:334
  29.0 0.6 %copy-done.3 = f32[2,2304]{1,0:T(2,128)} copy-done((f32[2,2304]{1,0:T(2,128)}, f32[2,2304]{1,0:T(2,128)S(1)}, u32[]{:S(2)}) %copy-start.3) | copy-done | bytes 18456
  29.6 5.4 %shard_map.48 = f32[2,3,32,4,128]{4,3,2,1,0:T(4,128)} custom-call(s32[5]{0:T(128)} %stack.36.flags_ref, f32[2,3,32,4,128]{4,3,2,1,0:T(4,128)} %bitcast.20, f32[2,3,32,4,128]{4,3,2,1,0:T(4,128)} %copy-done.1, f32[3,16,4,128]{3,2,1,0:T(4,128)} %sigma_ref.5, f32[3,16,4,128]{3,2,1,0:T(4,128)} %collective-permute-done.1.other_ref, f32[480,1,128]{2,1,0:T(1,128)} %copy-done.2, ...), custom_call_target="tpu_custom_call" | custom-call | tf_op jit(solution)/shard_map/pallas_call | solution.py:374
  (10 shorter events, 0.0 us)
Async XLA Ops:
  0.0 1.9 %copy-start = (bf16[16,2,3,32,4,128]{5,4,3,2,1,0:T(4,128)(2,1)S(1)}, bf16[16,2,3,32,4,128]{5,4,3,2,1,0:T(4,128)(2,1)}, u32[]{:S(2)}) copy-start(bf16[16,2,3,32,4,128]{5,4,3,2,1,0:T(4,128)(2,1)} %param.4) | copy-start | bytes 9437188
  5.4 2.2 %collective-permute-start = (f32[2,3,32,4,128]{4,3,2,1,0:T(4,128)}, f32[2,3,32,4,128]{4,3,2,1,0:T(4,128)S(1)}, u32[]{:S(2)}, u32[]{:S(2)}) collective-permute-start(f32[2,3,32,4,128]{4,3,2,1,0:T(4,128)} %bitcast.9), channel_id=1, source_target_pairs={{0,1},{1,0},{2,3},{3,2},{4,5},{5,4},{6,7},{7,6},{8,9},{9,8},{10,11... | collective-permute-start | bytes 1179656 | tf_op jit(solution)/shard_map/ppermute | solution.py:233
  5.4 2.2 %collective-permute-start.1 = (f32[3,16,4,128]{3,2,1,0:T(4,128)}, f32[3,16,4,128]{3,2,1,0:T(4,128)}, u32[]{:S(2)}, u32[]{:S(2)}) collective-permute-start(f32[3,16,4,128]{3,2,1,0:T(4,128)} %sigma_ref.5), channel_id=1, source_target_pairs={{0,1},{1,0},{2,3},{3,2},{4,5},{5,4},{6,7},{7,6},{8,9},{9,8},{10,11... | collective-permute-start | bytes 294920 | tf_op jit(solution)/shard_map/ppermute | solution.py:234
  7.6 0.8 %copy-start.1 = (f32[2,3,32,4,128]{4,3,2,1,0:T(4,128)}, f32[2,3,32,4,128]{4,3,2,1,0:T(4,128)S(1)}, u32[]{:S(2)}) copy-start(f32[2,3,32,4,128]{4,3,2,1,0:T(4,128)S(1)} %collective-permute-done.got_ref) | copy-start | bytes 1179652
  11.0 8.2 %collective-permute-start.2 = (f32[480,1,128]{2,1,0:T(1,128)}, f32[480,1,128]{2,1,0:T(1,128)S(1)}, u32[]{:S(2)}, u32[]{:S(2)}) collective-permute-start(f32[480,1,128]{2,1,0:T(1,128)} %get-tuple-element.7), channel_id=1, source_target_pairs={{0,4},{4,0},{8,12},{12,8},{1,5},{5,1},{9,13},{13,9},{2,6},{6,2},{1... | collective-permute-start | bytes 737288 | tf_op jit(solution)/shard_map/ppermute | solution.py:293
  12.6 9.9 %collective-permute-start.3 = (f32[480,1,128]{2,1,0:T(1,128)}, f32[480,1,128]{2,1,0:T(1,128)}, u32[]{:S(2)}, u32[]{:S(2)}) collective-permute-start(f32[480,1,128]{2,1,0:T(1,128)} %get-tuple-element.8), channel_id=1, source_target_pairs={{4,8},{8,4},{5,9},{9,5},{6,10},{10,6},{7,11},{11,7},{20,24},{24,20... | collective-permute-start | bytes 737288 | tf_op jit(solution)/shard_map/ppermute | solution.py:293
  19.2 3.3 %copy-start.2 = (f32[480,1,128]{2,1,0:T(1,128)}, f32[480,1,128]{2,1,0:T(1,128)S(1)}, u32[]{:S(2)}) copy-start(f32[480,1,128]{2,1,0:T(1,128)S(1)} %collective-permute-done.2.refs_0_) | copy-start | bytes 737284
  25.0 4.0 %collective-permute-start.4 = (f32[2,2304]{1,0:T(2,128)}, f32[2,2304]{1,0:T(2,128)S(1)}, u32[]{:S(2)}, u32[]{:S(2)}) collective-permute-start(f32[2,2304]{1,0:T(2,128)} %shard_map.47), channel_id=1, source_target_pairs={{0,2},{2,0},{1,3},{3,1},{4,6},{6,4},{5,7},{7,5},{8,10},{10,8},{9,1... | collective-permute-start | bytes 55304 | tf_op jit(solution)/shard_map/ppermute | solution.py:334
  29.0 0.6 %copy-start.3 = (f32[2,2304]{1,0:T(2,128)}, f32[2,2304]{1,0:T(2,128)S(1)}, u32[]{:S(2)}) copy-start(f32[2,2304]{1,0:T(2,128)S(1)} %collective-permute-done.4.refs_2_.refs_3_) | copy-start | bytes 55300

commit v20 on v19

--- a/solution.py
+++ b/solution.py
@@ -162,34 +162,36 @@
         return pltpu.roll(f, 1, axis=f.ndim + axis)
 
     def curl(field):
-        padded = pad_z(field)
-        above = padded[..., 1:, :, :]
-        here = padded[..., :-1, :, :]
+        def comp(c):
+            return field[..., c, :, :, :]
 
         def dz(c):
-            return above[..., c, :, :, :] - here[..., c, :, :, :]
+            e = comp(c)
+            return jnp.concatenate([e[..., 1:, :, :] - e[..., :-1, :, :], 0.0 - e[..., -1:, :, :]], axis=-3)
 
         def dx(c):
-            return nxt(here[..., c, :, :, :], -2) - here[..., c, :, :, :]
+            return nxt(comp(c), -2) - comp(c)
 
         def dy(c):
-            return nxt(here[..., c, :, :, :], -1) - here[..., c, :, :, :]
+            return nxt(comp(c), -1) - comp(c)
 
         h_x = dy(2) - dz(1)
         h_y = dz(0) - dx(2)
         h_z = dx(1) - dy(0)
-
-        def bz(g):
-            return g[..., 1:, :, :] - g[..., :-1, :, :]
+        below_x = 0.0 - comp(1)[..., :1, :, :]
+        below_y = comp(0)[..., :1, :, :] - 0.0
+
+        def bz(g, below):
+            return jnp.concatenate([g[..., :1, :, :] - below, g[..., 1:, :, :] - g[..., :-1, :, :]], axis=-3)
 
         def bx(g):
-            return g[..., 1:, :, :] - prv(g[..., 1:, :, :], -2)
+            return g - prv(g, -2)
 
         def by(g):
-            return g[..., 1:, :, :] - prv(g[..., 1:, :, :], -1)
-
-        c_x = by(h_z) - bz(h_y)
-        c_y = bz(h_x) - bx(h_z)
+            return g - prv(g, -1)
+
+        c_x = by(h_z) - bz(h_y, below_y)
+        c_y = bz(h_x, below_x) - bx(h_z)
         c_z = bx(h_y) - by(h_x)
         return jnp.stack([c_x, c_y, c_z], axis=-4)
 

time: 35.2 us -> 35.2 us (level)
  no operation moved by 1% of the time
where the time goes in v20:
time: 35.2 us; the launch traced here: 35 us
  waiting for transfers between devices  10.8 us (31%)
  Pallas kernels  10.5 us (30%)
  starting transfers between devices  5.49 us (16%)
  local copies, waits for them, and re-layouts  4.78 us (14%)
  matrix products  1.93 us (5%)
  other arithmetic  1.42 us (4%)
    ppermute x2, waiting for transfers between devices, body(): lax.ppermute(row_major(send), 'xb', pairs)  7.95 us
    pallas_call x1, Pallas kernels, body(): pl.pallas_call(sweeps_kernel, out_shape=jax.ShapeDtypeStruct(out_shape, j...  5.38 us
    ppermute x2, starting transfers between devices, body(): lax.ppermute(row_major(send), 'xb', pairs)  3.49 us
    pallas_call x1, Pallas kernels, body(): pl.pallas_call(send_kernel, out_shape=[jax.ShapeDtypeStruct((payload_plan...  2.65 us
    pallas_call x1, Pallas kernels, body(): pl.pallas_call(x_kernel, out_shape=[jax.ShapeDtypeStruct(face_shape, jnp....  2.49 us
    dot_general x1, matrix products, body(): lax.dot_general(weights, primaries, (((1,), (0,)), ((), ())), preferred_e...  1.93 us
    ppermute x1, waiting for transfers between devices, body(): lax.ppermute(row_major(send), 'yb', pairs)  1.82 us
    slice x1, local copies, waits for them, and re-layouts, body(): got = lax.ppermute(partial[0], 'tx', tx_ring)  1.56 us
  transfers between devices with their start and end apart: 5, of which 4 were waited for; matrix products, arithmetic and copies ran while one was open for 4% of the time, Pallas kernels for 0%

profile of v20, /device:TPU:16, one launch (start us, length us, event | category | flops | bytes accessed | tf_op | source)
XLA Modules:
  0.0 35.0 jit_solution(7483109014762237045)
XLA Ops:
  0.0 0.9 %reshape.9 = s32[2,16]{1,0:T(2,128)S(1)} reshape(s32[32]{0:T(128)} %param.6) | data formatting | bytes 256 | tf_op jit(solution)/shard_map/reshape | solution.py:227
  0.9 0.8 %reshape.10 = s32[2,16]{1,0:T(2,128)S(1)} reshape(s32[32]{0:T(128)} %param.7) | data formatting | bytes 256 | tf_op jit(solution)/shard_map/reshape | solution.py:228
  1.7 0.1 pad_add_fusion
  1.8 0.1 select_reduce_fusion.1
  1.9 0.0 copy-done
  1.9 1.9 %fusion = f32[2,2,3,32,4,128]{5,0,4,3,2,1:T(2,128)S(1)} fusion(bf16[16,2,3,32,4,128]{5,4,3,2,1,0:T(4,128)(2,1)S(1)} %copy-done, s32[16]{0:T(128)S(1)} %get-tuple-element.10, s32[16]{0:T(128)S(1)} %get-tuple-element.9, s32[2]{0:T(128)S(1)} %pad_add_fusion), kind=kOutput, calls=%fused_computation | convolution fusion | flops 6291584 | bytes 3932296 | tf_op jit(solution)/shard_map/dot_general | solution.py:231
  3.8 1.6 %fusion.19 = (f32[1,2,3,32,4,128]{5,0,4,3,2,1:T(1,128)}, f32[1,2,3,32,4,128]{5,0,4,3,2,1:T(1,128)}) fusion(f32[2,2,3,32,4,128]{5,0,4,3,2,1:T(2,128)S(1)} %fusion), kind=kLoop, calls=%fused_computation.27 | loop fusion | bytes 1572864 | tf_op jit(solution)/shard_map/slice | solution.py:235
  5.4 0.0 collective-permute-start
  5.4 0.5 %collective-permute-start.1 = (f32[3,16,4,128]{3,2,1,0:T(4,128)}, f32[3,16,4,128]{3,2,1,0:T(4,128)}, u32[]{:S(2)}, u32[]{:S(2)}) collective-permute-start(f32[3,16,4,128]{3,2,1,0:T(4,128)} %sigma_ref.5), channel_id=1, source_target_pairs={{0,1},{1,0},{2,3},{3,2},{4,5},{5,4},{6,7},{7,6},{8,9},{9,8},{10,11... | collective-permute-start | bytes 294920 | tf_op jit(solution)/shard_map/ppermute | solution.py:236
  5.9 0.1 stack.35
  6.0 0.6 %stack.36.flags_ref = s32[5]{0:T(128)} convert(pred[5]{0:T(512)(128)(4,1)S(1)} %stack.35) | non-fusion elementwise | flops 5 | bytes 25 | tf_op jit(solution)/shard_map/stack | solution.py:245
  6.6 1.0 %collective-permute-done.1.other_ref = f32[3,16,4,128]{3,2,1,0:T(4,128)} collective-permute-done((f32[3,16,4,128]{3,2,1,0:T(4,128)}, f32[3,16,4,128]{3,2,1,0:T(4,128)}, u32[]{:S(2)}, u32[]{:S(2)}) %collective-permute-start.1) | collective-permute-done | bytes 98336 | tf_op jit(solution)/shard_map/ppermute | solution.py:236
  7.6 0.8 %copy-done.1 = f32[2,3,32,4,128]{4,3,2,1,0:T(4,128)} copy-done((f32[2,3,32,4,128]{4,3,2,1,0:T(4,128)}, f32[2,3,32,4,128]{4,3,2,1,0:T(4,128)S(1)}, u32[]{:S(2)}) %copy-start.1) | copy-done | bytes 393240
  8.4 2.7 %shard_map.46 = (f32[480,1,128]{2,1,0:T(1,128)}, f32[480,1,128]{2,1,0:T(1,128)}) custom-call(s32[5]{0:T(128)} %stack.36.flags_ref, f32[2,3,32,4,128]{4,3,2,1,0:T(4,128)} %bitcast.18, f32[2,3,32,4,128]{4,3,2,1,0:T(4,128)} %copy-done.1, f32[3,16,4,128]{3,2,1,0:T(4,128)} %sigma_ref.5, f32[3,16,4,128]{3,2,1,0:T(4,128)} %collective-permute-done.1.other_ref), custom_call_target="tpu_custom_call" | custom-call | tf_op jit(solution)/shard_map/pallas_call | solution.py:288
  11.0 1.6 %collective-permute-start.2 = (f32[480,1,128]{2,1,0:T(1,128)}, f32[480,1,128]{2,1,0:T(1,128)S(1)}, u32[]{:S(2)}, u32[]{:S(2)}) collective-permute-start(f32[480,1,128]{2,1,0:T(1,128)} %get-tuple-element.7), channel_id=1, source_target_pairs={{0,4},{4,0},{8,12},{12,8},{1,5},{5,1},{9,13},{13,9},{2,6},{6,2},{1... | collective-permute-start | bytes 737288 | tf_op jit(solution)/shard_map/ppermute | solution.py:295
  12.6 1.9 %collective-permute-start.3 = (f32[480,1,128]{2,1,0:T(1,128)}, f32[480,1,128]{2,1,0:T(1,128)}, u32[]{:S(2)}, u32[]{:S(2)}) collective-permute-start(f32[480,1,128]{2,1,0:T(1,128)} %get-tuple-element.8), channel_id=1, source_target_pairs={{4,8},{8,4},{5,9},{9,5},{6,10},{10,6},{7,11},{11,7},{20,24},{24,20... | collective-permute-start | bytes 737288 | tf_op jit(solution)/shard_map/ppermute | solution.py:295
  14.6 4.7 %collective-permute-done.2.refs_0_ = f32[480,1,128]{2,1,0:T(1,128)S(1)} collective-permute-done((f32[480,1,128]{2,1,0:T(1,128)}, f32[480,1,128]{2,1,0:T(1,128)S(1)}, u32[]{:S(2)}, u32[]{:S(2)}) %collective-permute-start.2) | collective-permute-done | bytes 245792 | tf_op jit(solution)/shard_map/ppermute | solution.py:295
  19.2 3.3 %collective-permute-done.3.refs_1_ = f32[480,1,128]{2,1,0:T(1,128)} collective-permute-done((f32[480,1,128]{2,1,0:T(1,128)}, f32[480,1,128]{2,1,0:T(1,128)}, u32[]{:S(2)}, u32[]{:S(2)}) %collective-permute-start.3) | collective-permute-done | bytes 245792 | tf_op jit(solution)/shard_map/ppermute | solution.py:295
  22.5 2.5 %shard_map.47 = f32[2,2304]{1,0:T(2,128)} custom-call(s32[5]{0:T(128)} %stack.36.flags_ref, f32[2,3,32,4,128]{4,3,2,1,0:T(4,128)} %bitcast.19, f32[2,3,32,4,128]{4,3,2,1,0:T(4,128)} %copy-done.1, f32[3,16,4,128]{3,2,1,0:T(4,128)} %sigma_ref.5, f32[3,16,4,128]{3,2,1,0:T(4,128)} %collective-permute-done.1.other_ref, f32[480,1,128]{2,1,0:T(1,128)} %copy-done.2, ...), custom_call_target="tpu_custom_call" | custom-call | tf_op jit(solution)/shard_map/pallas_call | solution.py:329
  25.0 1.5 %collective-permute-start.4 = (f32[2,2304]{1,0:T(2,128)}, f32[2,2304]{1,0:T(2,128)S(1)}, u32[]{:S(2)}, u32[]{:S(2)}) collective-permute-start(f32[2,2304]{1,0:T(2,128)} %shard_map.47), channel_id=1, source_target_pairs={{0,2},{2,0},{1,3},{3,1},{4,6},{6,4},{5,7},{7,5},{8,10},{10,8},{9,1... | collective-permute-start | bytes 55304 | tf_op jit(solution)/shard_map/ppermute | solution.py:336
  26.5 0.7 %fusion.9.refs_4_ = f32[8,256]{1,0:T(8,128)} fusion(s32[256]{0:T(256)S(1)} %iota_add_fusion, s32[]{:T(128)S(6)} %mul.7, pred[8]{0:T(512)(128)(4,1)S(1)} %compare_and_fusion, pred[256]{0:T(512)(128)(4,1)S(1)} %iota_compare_fusion), kind=kLoop, calls=%fused_computation.10 | loop fusion | flops 18432 | bytes 9484 | tf_op jit(solution)/shard_map/convert_element_type | solution.py:381
  27.2 1.8 %collective-permute-done.4.refs_2_.refs_3_ = f32[2,2304]{1,0:T(2,128)S(1)} collective-permute-done((f32[2,2304]{1,0:T(2,128)}, f32[2,2304]{1,0:T(2,128)S(1)}, u32[]{:S(2)}, u32[]{:S(2)}) %collective-permute-start.4) | collective-permute-done | bytes 18464 | tf_op jit(solution)/shard_map/ppermute | solution.py:336
  29.0 0.6 %copy-done.3 = f32[2,2304]{1,0:T(2,128)} copy-done((f32[2,2304]{1,0:T(2,128)}, f32[2,2304]{1,0:T(2,128)S(1)}, u32[]{:S(2)}) %copy-start.3) | copy-done | bytes 18456
  29.6 5.4 %shard_map.48 = f32[2,3,32,4,128]{4,3,2,1,0:T(4,128)} custom-call(s32[5]{0:T(128)} %stack.36.flags_ref, f32[2,3,32,4,128]{4,3,2,1,0:T(4,128)} %bitcast.20, f32[2,3,32,4,128]{4,3,2,1,0:T(4,128)} %copy-done.1, f32[3,16,4,128]{3,2,1,0:T(4,128)} %sigma_ref.5, f32[3,16,4,128]{3,2,1,0:T(4,128)} %collective-permute-done.1.other_ref, f32[480,1,128]{2,1,0:T(1,128)} %copy-done.2, ...), custom_call_target="tpu_custom_call" | custom-call | tf_op jit(solution)/shard_map/pallas_call | solution.py:376
  (10 shorter events, 0.0 us)
Async XLA Ops:
  0.0 1.9 %copy-start = (bf16[16,2,3,32,4,128]{5,4,3,2,1,0:T(4,128)(2,1)S(1)}, bf16[16,2,3,32,4,128]{5,4,3,2,1,0:T(4,128)(2,1)}, u32[]{:S(2)}) copy-start(bf16[16,2,3,32,4,128]{5,4,3,2,1,0:T(4,128)(2,1)} %param.4) | copy-start | bytes 9437188
  5.4 2.2 %collective-permute-start = (f32[2,3,32,4,128]{4,3,2,1,0:T(4,128)}, f32[2,3,32,4,128]{4,3,2,1,0:T(4,128)S(1)}, u32[]{:S(2)}, u32[]{:S(2)}) collective-permute-start(f32[2,3,32,4,128]{4,3,2,1,0:T(4,128)} %bitcast.9), channel_id=1, source_target_pairs={{0,1},{1,0},{2,3},{3,2},{4,5},{5,4},{6,7},{7,6},{8,9},{9,8},{10,11... | collective-permute-start | bytes 1179656 | tf_op jit(solution)/shard_map/ppermute | solution.py:235
  5.4 2.2 %collective-permute-start.1 = (f32[3,16,4,128]{3,2,1,0:T(4,128)}, f32[3,16,4,128]{3,2,1,0:T(4,128)}, u32[]{:S(2)}, u32[]{:S(2)}) collective-permute-start(f32[3,16,4,128]{3,2,1,0:T(4,128)} %sigma_ref.5), channel_id=1, source_target_pairs={{0,1},{1,0},{2,3},{3,2},{4,5},{5,4},{6,7},{7,6},{8,9},{9,8},{10,11... | collective-permute-start | bytes 294920 | tf_op jit(solution)/shard_map/ppermute | solution.py:236
  7.6 0.8 %copy-start.1 = (f32[2,3,32,4,128]{4,3,2,1,0:T(4,128)}, f32[2,3,32,4,128]{4,3,2,1,0:T(4,128)S(1)}, u32[]{:S(2)}) copy-start(f32[2,3,32,4,128]{4,3,2,1,0:T(4,128)S(1)} %collective-permute-done.got_ref) | copy-start | bytes 1179652
  11.0 8.2 %collective-permute-start.2 = (f32[480,1,128]{2,1,0:T(1,128)}, f32[480,1,128]{2,1,0:T(1,128)S(1)}, u32[]{:S(2)}, u32[]{:S(2)}) collective-permute-start(f32[480,1,128]{2,1,0:T(1,128)} %get-tuple-element.7), channel_id=1, source_target_pairs={{0,4},{4,0},{8,12},{12,8},{1,5},{5,1},{9,13},{13,9},{2,6},{6,2},{1... | collective-permute-start | bytes 737288 | tf_op jit(solution)/shard_map/ppermute | solution.py:295
  12.6 9.9 %collective-permute-start.3 = (f32[480,1,128]{2,1,0:T(1,128)}, f32[480,1,128]{2,1,0:T(1,128)}, u32[]{:S(2)}, u32[]{:S(2)}) collective-permute-start(f32[480,1,128]{2,1,0:T(1,128)} %get-tuple-element.8), channel_id=1, source_target_pairs={{4,8},{8,4},{5,9},{9,5},{6,10},{10,6},{7,11},{11,7},{20,24},{24,20... | collective-permute-start | bytes 737288 | tf_op jit(solution)/shard_map/ppermute | solution.py:295
  19.2 3.3 %copy-start.2 = (f32[480,1,128]{2,1,0:T(1,128)}, f32[480,1,128]{2,1,0:T(1,128)S(1)}, u32[]{:S(2)}) copy-start(f32[480,1,128]{2,1,0:T(1,128)S(1)} %collective-permute-done.2.refs_0_) | copy-start | bytes 737284
  25.0 4.0 %collective-permute-start.4 = (f32[2,2304]{1,0:T(2,128)}, f32[2,2304]{1,0:T(2,128)S(1)}, u32[]{:S(2)}, u32[]{:S(2)}) collective-permute-start(f32[2,2304]{1,0:T(2,128)} %shard_map.47), channel_id=1, source_target_pairs={{0,2},{2,0},{1,3},{3,1},{4,6},{6,4},{5,7},{7,5},{8,10},{10,8},{9,1... | collective-permute-start | bytes 55304 | tf_op jit(solution)/shard_map/ppermute | solution.py:336
  29.0 0.6 %copy-start.3 = (f32[2,2304]{1,0:T(2,128)}, f32[2,2304]{1,0:T(2,128)S(1)}, u32[]{:S(2)}) copy-start(f32[2,2304]{1,0:T(2,128)S(1)} %collective-permute-done.4.refs_2_.refs_3_) | copy-start | bytes 55300

commit v21 on v19

--- a/solution.py
+++ b/solution.py
@@ -195,14 +195,21 @@
 
     kappa = K_FREQ * sigma_ext
     delta = K_FREQ * (sigma_ext - 1.0)
+    inverse = 1.0 / (16.0 + kappa * kappa)
+
+    def jac(resid):
+        real_part = (4.0 * resid[..., 0, :, :, :, :] + kappa * resid[..., 1, :, :, :, :]) * inverse
+        imag_part = (4.0 * resid[..., 1, :, :, :, :] - kappa * resid[..., 0, :, :, :, :]) * inverse
+        return jnp.stack([real_part, imag_part], axis=-5)
+
     rhs = source_term(shot_ext, delta)
-    field = jnp.where(inside, jnp.where(outer, shot_ext, jacobi(rhs, kappa)), 0.0)
+    field = jnp.where(inside, jnp.where(outer, shot_ext, jac(rhs)), 0.0)
     for sweep in range(SWEEPS):
         curled = curl(field)
         real_part = curled[..., 0, :, :, :, :] - kappa * field[..., 1, :, :, :, :]
         imag_part = curled[..., 1, :, :, :, :] + kappa * field[..., 0, :, :, :, :]
         applied = jnp.stack([real_part, imag_part], axis=-5)
-        field = field + RELAX * jacobi(rhs - applied, kappa)
+        field = field + RELAX * jac(rhs - applied)
         if sweep < SWEEPS - 1:
             field = jnp.where(inside, field, 0.0)
     return field

time: 35.2 us -> 35.2 us (level)
  no operation moved by 1% of the time
where the time goes in v21:
time: 35.2 us; the launch traced here: 35 us
  waiting for transfers between devices  10.8 us (31%)
  Pallas kernels  10.5 us (30%)
  starting transfers between devices  5.49 us (16%)
  local copies, waits for them, and re-layouts  4.78 us (14%)
  matrix products  1.93 us (5%)
  other arithmetic  1.42 us (4%)
    ppermute x2, waiting for transfers between devices, body(): lax.ppermute(row_major(send), 'xb', pairs)  7.95 us
    pallas_call x1, Pallas kernels, body(): pl.pallas_call(sweeps_kernel, out_shape=jax.ShapeDtypeStruct(out_shape, j...  5.38 us
    ppermute x2, starting transfers between devices, body(): lax.ppermute(row_major(send), 'xb', pairs)  3.49 us
    pallas_call x1, Pallas kernels, body(): pl.pallas_call(send_kernel, out_shape=[jax.ShapeDtypeStruct((payload_plan...  2.65 us
    pallas_call x1, Pallas kernels, body(): pl.pallas_call(x_kernel, out_shape=[jax.ShapeDtypeStruct(face_shape, jnp....  2.49 us
    dot_general x1, matrix products, body(): lax.dot_general(weights, primaries, (((1,), (0,)), ((), ())), preferred_e...  1.93 us
    ppermute x1, waiting for transfers between devices, body(): lax.ppermute(row_major(send), 'yb', pairs)  1.82 us
    slice x1, local copies, waits for them, and re-layouts, body(): got = lax.ppermute(partial[0], 'tx', tx_ring)  1.56 us
  transfers between devices with their start and end apart: 5, of which 4 were waited for; matrix products, arithmetic and copies ran while one was open for 4% of the time, Pallas kernels for 0%

profile of v21, /device:TPU:16, one launch (start us, length us, event | category | flops | bytes accessed | tf_op | source)
XLA Modules:
  0.0 35.0 jit_solution(13799916488037562220)
XLA Ops:
  0.0 0.9 %reshape.9 = s32[2,16]{1,0:T(2,128)S(1)} reshape(s32[32]{0:T(128)} %param.6) | data formatting | bytes 256 | tf_op jit(solution)/shard_map/reshape | solution.py:232
  0.9 0.8 %reshape.10 = s32[2,16]{1,0:T(2,128)S(1)} reshape(s32[32]{0:T(128)} %param.7) | data formatting | bytes 256 | tf_op jit(solution)/shard_map/reshape | solution.py:233
  1.7 0.1 pad_add_fusion
  1.8 0.1 select_reduce_fusion.1
  1.9 0.0 copy-done
  1.9 1.9 %fusion = f32[2,2,3,32,4,128]{5,0,4,3,2,1:T(2,128)S(1)} fusion(bf16[16,2,3,32,4,128]{5,4,3,2,1,0:T(4,128)(2,1)S(1)} %copy-done, s32[16]{0:T(128)S(1)} %get-tuple-element.10, s32[16]{0:T(128)S(1)} %get-tuple-element.9, s32[2]{0:T(128)S(1)} %pad_add_fusion), kind=kOutput, calls=%fused_computation | convolution fusion | flops 6291584 | bytes 3932296 | tf_op jit(solution)/shard_map/dot_general | solution.py:236
  3.8 1.6 %fusion.19 = (f32[1,2,3,32,4,128]{5,0,4,3,2,1:T(1,128)}, f32[1,2,3,32,4,128]{5,0,4,3,2,1:T(1,128)}) fusion(f32[2,2,3,32,4,128]{5,0,4,3,2,1:T(2,128)S(1)} %fusion), kind=kLoop, calls=%fused_computation.27 | loop fusion | bytes 1572864 | tf_op jit(solution)/shard_map/slice | solution.py:240
  5.4 0.0 collective-permute-start
  5.4 0.5 %collective-permute-start.1 = (f32[3,16,4,128]{3,2,1,0:T(4,128)}, f32[3,16,4,128]{3,2,1,0:T(4,128)}, u32[]{:S(2)}, u32[]{:S(2)}) collective-permute-start(f32[3,16,4,128]{3,2,1,0:T(4,128)} %sigma_ref.5), channel_id=1, source_target_pairs={{0,1},{1,0},{2,3},{3,2},{4,5},{5,4},{6,7},{7,6},{8,9},{9,8},{10,11... | collective-permute-start | bytes 294920 | tf_op jit(solution)/shard_map/ppermute | solution.py:241
  5.9 0.1 stack.35
  6.0 0.6 %stack.36.flags_ref = s32[5]{0:T(128)} convert(pred[5]{0:T(512)(128)(4,1)S(1)} %stack.35) | non-fusion elementwise | flops 5 | bytes 25 | tf_op jit(solution)/shard_map/stack | solution.py:250
  6.6 1.0 %collective-permute-done.1.other_ref = f32[3,16,4,128]{3,2,1,0:T(4,128)} collective-permute-done((f32[3,16,4,128]{3,2,1,0:T(4,128)}, f32[3,16,4,128]{3,2,1,0:T(4,128)}, u32[]{:S(2)}, u32[]{:S(2)}) %collective-permute-start.1) | collective-permute-done | bytes 98336 | tf_op jit(solution)/shard_map/ppermute | solution.py:241
  7.6 0.8 %copy-done.1 = f32[2,3,32,4,128]{4,3,2,1,0:T(4,128)} copy-done((f32[2,3,32,4,128]{4,3,2,1,0:T(4,128)}, f32[2,3,32,4,128]{4,3,2,1,0:T(4,128)S(1)}, u32[]{:S(2)}) %copy-start.1) | copy-done | bytes 393240
  8.4 2.7 %shard_map.46 = (f32[480,1,128]{2,1,0:T(1,128)}, f32[480,1,128]{2,1,0:T(1,128)}) custom-call(s32[5]{0:T(128)} %stack.36.flags_ref, f32[2,3,32,4,128]{4,3,2,1,0:T(4,128)} %bitcast.18, f32[2,3,32,4,128]{4,3,2,1,0:T(4,128)} %copy-done.1, f32[3,16,4,128]{3,2,1,0:T(4,128)} %sigma_ref.5, f32[3,16,4,128]{3,2,1,0:T(4,128)} %collective-permute-done.1.other_ref), custom_call_target="tpu_custom_call" | custom-call | tf_op jit(solution)/shard_map/pallas_call | solution.py:293
  11.0 1.6 %collective-permute-start.2 = (f32[480,1,128]{2,1,0:T(1,128)}, f32[480,1,128]{2,1,0:T(1,128)S(1)}, u32[]{:S(2)}, u32[]{:S(2)}) collective-permute-start(f32[480,1,128]{2,1,0:T(1,128)} %get-tuple-element.7), channel_id=1, source_target_pairs={{0,4},{4,0},{8,12},{12,8},{1,5},{5,1},{9,13},{13,9},{2,6},{6,2},{1... | collective-permute-start | bytes 737288 | tf_op jit(solution)/shard_map/ppermute | solution.py:300
  12.6 1.9 %collective-permute-start.3 = (f32[480,1,128]{2,1,0:T(1,128)}, f32[480,1,128]{2,1,0:T(1,128)}, u32[]{:S(2)}, u32[]{:S(2)}) collective-permute-start(f32[480,1,128]{2,1,0:T(1,128)} %get-tuple-element.8), channel_id=1, source_target_pairs={{4,8},{8,4},{5,9},{9,5},{6,10},{10,6},{7,11},{11,7},{20,24},{24,20... | collective-permute-start | bytes 737288 | tf_op jit(solution)/shard_map/ppermute | solution.py:300
  14.6 4.7 %collective-permute-done.2.refs_0_ = f32[480,1,128]{2,1,0:T(1,128)S(1)} collective-permute-done((f32[480,1,128]{2,1,0:T(1,128)}, f32[480,1,128]{2,1,0:T(1,128)S(1)}, u32[]{:S(2)}, u32[]{:S(2)}) %collective-permute-start.2) | collective-permute-done | bytes 245792 | tf_op jit(solution)/shard_map/ppermute | solution.py:300
  19.2 3.3 %collective-permute-done.3.refs_1_ = f32[480,1,128]{2,1,0:T(1,128)} collective-permute-done((f32[480,1,128]{2,1,0:T(1,128)}, f32[480,1,128]{2,1,0:T(1,128)}, u32[]{:S(2)}, u32[]{:S(2)}) %collective-permute-start.3) | collective-permute-done | bytes 245792 | tf_op jit(solution)/shard_map/ppermute | solution.py:300
  22.5 2.5 %shard_map.47 = f32[2,2304]{1,0:T(2,128)} custom-call(s32[5]{0:T(128)} %stack.36.flags_ref, f32[2,3,32,4,128]{4,3,2,1,0:T(4,128)} %bitcast.19, f32[2,3,32,4,128]{4,3,2,1,0:T(4,128)} %copy-done.1, f32[3,16,4,128]{3,2,1,0:T(4,128)} %sigma_ref.5, f32[3,16,4,128]{3,2,1,0:T(4,128)} %collective-permute-done.1.other_ref, f32[480,1,128]{2,1,0:T(1,128)} %copy-done.2, ...), custom_call_target="tpu_custom_call" | custom-call | tf_op jit(solution)/shard_map/pallas_call | solution.py:334
  25.0 1.5 %collective-permute-start.4 = (f32[2,2304]{1,0:T(2,128)}, f32[2,2304]{1,0:T(2,128)S(1)}, u32[]{:S(2)}, u32[]{:S(2)}) collective-permute-start(f32[2,2304]{1,0:T(2,128)} %shard_map.47), channel_id=1, source_target_pairs={{0,2},{2,0},{1,3},{3,1},{4,6},{6,4},{5,7},{7,5},{8,10},{10,8},{9,1... | collective-permute-start | bytes 55304 | tf_op jit(solution)/shard_map/ppermute | solution.py:341
  26.5 0.7 %fusion.9.refs_4_ = f32[8,256]{1,0:T(8,128)} fusion(s32[256]{0:T(256)S(1)} %iota_add_fusion, s32[]{:T(128)S(6)} %mul.7, pred[8]{0:T(512)(128)(4,1)S(1)} %compare_and_fusion, pred[256]{0:T(512)(128)(4,1)S(1)} %iota_compare_fusion), kind=kLoop, calls=%fused_computation.10 | loop fusion | flops 18432 | bytes 9484 | tf_op jit(solution)/shard_map/convert_element_type | solution.py:386
  27.2 1.8 %collective-permute-done.4.refs_2_.refs_3_ = f32[2,2304]{1,0:T(2,128)S(1)} collective-permute-done((f32[2,2304]{1,0:T(2,128)}, f32[2,2304]{1,0:T(2,128)S(1)}, u32[]{:S(2)}, u32[]{:S(2)}) %collective-permute-start.4) | collective-permute-done | bytes 18464 | tf_op jit(solution)/shard_map/ppermute | solution.py:341
  29.0 0.6 %copy-done.3 = f32[2,2304]{1,0:T(2,128)} copy-done((f32[2,2304]{1,0:T(2,128)}, f32[2,2304]{1,0:T(2,128)S(1)}, u32[]{:S(2)}) %copy-start.3) | copy-done | bytes 18456
  29.6 5.4 %shard_map.48 = f32[2,3,32,4,128]{4,3,2,1,0:T(4,128)} custom-call(s32[5]{0:T(128)} %stack.36.flags_ref, f32[2,3,32,4,128]{4,3,2,1,0:T(4,128)} %bitcast.20, f32[2,3,32,4,128]{4,3,2,1,0:T(4,128)} %copy-done.1, f32[3,16,4,128]{3,2,1,0:T(4,128)} %sigma_ref.5, f32[3,16,4,128]{3,2,1,0:T(4,128)} %collective-permute-done.1.other_ref, f32[480,1,128]{2,1,0:T(1,128)} %copy-done.2, ...), custom_call_target="tpu_custom_call" | custom-call | tf_op jit(solution)/shard_map/pallas_call | solution.py:381
  (10 shorter events, 0.0 us)
Async XLA Ops:
  0.0 1.9 %copy-start = (bf16[16,2,3,32,4,128]{5,4,3,2,1,0:T(4,128)(2,1)S(1)}, bf16[16,2,3,32,4,128]{5,4,3,2,1,0:T(4,128)(2,1)}, u32[]{:S(2)}) copy-start(bf16[16,2,3,32,4,128]{5,4,3,2,1,0:T(4,128)(2,1)} %param.4) | copy-start | bytes 9437188
  5.4 2.2 %collective-permute-start = (f32[2,3,32,4,128]{4,3,2,1,0:T(4,128)}, f32[2,3,32,4,128]{4,3,2,1,0:T(4,128)S(1)}, u32[]{:S(2)}, u32[]{:S(2)}) collective-permute-start(f32[2,3,32,4,128]{4,3,2,1,0:T(4,128)} %bitcast.9), channel_id=1, source_target_pairs={{0,1},{1,0},{2,3},{3,2},{4,5},{5,4},{6,7},{7,6},{8,9},{9,8},{10,11... | collective-permute-start | bytes 1179656 | tf_op jit(solution)/shard_map/ppermute | solution.py:240
  5.4 2.2 %collective-permute-start.1 = (f32[3,16,4,128]{3,2,1,0:T(4,128)}, f32[3,16,4,128]{3,2,1,0:T(4,128)}, u32[]{:S(2)}, u32[]{:S(2)}) collective-permute-start(f32[3,16,4,128]{3,2,1,0:T(4,128)} %sigma_ref.5), channel_id=1, source_target_pairs={{0,1},{1,0},{2,3},{3,2},{4,5},{5,4},{6,7},{7,6},{8,9},{9,8},{10,11... | collective-permute-start | bytes 294920 | tf_op jit(solution)/shard_map/ppermute | solution.py:241
  7.6 0.8 %copy-start.1 = (f32[2,3,32,4,128]{4,3,2,1,0:T(4,128)}, f32[2,3,32,4,128]{4,3,2,1,0:T(4,128)S(1)}, u32[]{:S(2)}) copy-start(f32[2,3,32,4,128]{4,3,2,1,0:T(4,128)S(1)} %collective-permute-done.got_ref) | copy-start | bytes 1179652
  11.0 8.2 %collective-permute-start.2 = (f32[480,1,128]{2,1,0:T(1,128)}, f32[480,1,128]{2,1,0:T(1,128)S(1)}, u32[]{:S(2)}, u32[]{:S(2)}) collective-permute-start(f32[480,1,128]{2,1,0:T(1,128)} %get-tuple-element.7), channel_id=1, source_target_pairs={{0,4},{4,0},{8,12},{12,8},{1,5},{5,1},{9,13},{13,9},{2,6},{6,2},{1... | collective-permute-start | bytes 737288 | tf_op jit(solution)/shard_map/ppermute | solution.py:300
  12.6 9.9 %collective-permute-start.3 = (f32[480,1,128]{2,1,0:T(1,128)}, f32[480,1,128]{2,1,0:T(1,128)}, u32[]{:S(2)}, u32[]{:S(2)}) collective-permute-start(f32[480,1,128]{2,1,0:T(1,128)} %get-tuple-element.8), channel_id=1, source_target_pairs={{4,8},{8,4},{5,9},{9,5},{6,10},{10,6},{7,11},{11,7},{20,24},{24,20... | collective-permute-start | bytes 737288 | tf_op jit(solution)/shard_map/ppermute | solution.py:300
  19.2 3.3 %copy-start.2 = (f32[480,1,128]{2,1,0:T(1,128)}, f32[480,1,128]{2,1,0:T(1,128)S(1)}, u32[]{:S(2)}) copy-start(f32[480,1,128]{2,1,0:T(1,128)S(1)} %collective-permute-done.2.refs_0_) | copy-start | bytes 737284
  25.0 4.0 %collective-permute-start.4 = (f32[2,2304]{1,0:T(2,128)}, f32[2,2304]{1,0:T(2,128)S(1)}, u32[]{:S(2)}, u32[]{:S(2)}) collective-permute-start(f32[2,2304]{1,0:T(2,128)} %shard_map.47), channel_id=1, source_target_pairs={{0,2},{2,0},{1,3},{3,1},{4,6},{6,4},{5,7},{7,5},{8,10},{10,8},{9,1... | collective-permute-start | bytes 55304 | tf_op jit(solution)/shard_map/ppermute | solution.py:341
  29.0 0.6 %copy-start.3 = (f32[2,2304]{1,0:T(2,128)}, f32[2,2304]{1,0:T(2,128)S(1)}, u32[]{:S(2)}) copy-start(f32[2,2304]{1,0:T(2,128)S(1)} %collective-permute-done.4.refs_2_.refs_3_) | copy-start | bytes 55300

commit v22 on v19

--- a/solution.py
+++ b/solution.py
@@ -274,8 +274,8 @@
         cells = planes_of(flags_ref, own_ref, got_ref, sigma_ref, other_ref)
 
         def payload(inner_rows, outer_row):
-            parts = [cells[:, r:r + 1] for r in inner_rows]
-            parts.append(field0_row(cells[:, outer_row:outer_row + 1]))
+            parts = [cells[:, r, :] for r in inner_rows]
+            parts.append(field0_row(cells[:, outer_row:outer_row + 1]).reshape(shot_planes, width_y))
             return jnp.concatenate(parts, axis=0)
 
         head = payload(range(0, w - 1), w - 1)
@@ -285,7 +285,7 @@
 
     x_sends = pl.pallas_call(
         send_kernel,
-        out_shape=[jax.ShapeDtypeStruct((payload_planes, 1, width_y), jnp.float32)] * n_x,
+        out_shape=[jax.ShapeDtypeStruct((payload_planes, width_y), jnp.float32)] * n_x,
         in_specs=[smem] + [vmem] * 4,
         out_specs=[vmem] * n_x,
     )(flags, *pieces)
@@ -296,8 +296,8 @@
     face_shape = (w, n_planes * ext_x)
 
     def decode(payload, outer_first):
-        inner = [payload[k * n_planes:(k + 1) * n_planes] for k in range(w - 1)]
-        field0 = payload[n_planes * (w - 1):]
+        inner = [payload[k * n_planes:(k + 1) * n_planes].reshape(n_planes, 1, width_y) for k in range(w - 1)]
+        field0 = payload[n_planes * (w - 1):].reshape(shot_planes, 1, width_y)
         filler = jnp.zeros((n_planes - shot_planes, 1, width_y), payload.dtype)
         outer = jnp.concatenate([field0, filler], axis=0)
         return jnp.concatenate([outer] + inner if outer_first else inner + [outer], axis=1)

time: 35.2 us -> 35.2 us (level)
  no operation moved by 1% of the time
where the time goes in v22:
time: 35.2 us; the launch traced here: 35 us
  waiting for transfers between devices  10.8 us (31%)
  Pallas kernels  10.6 us (30%)
  starting transfers between devices  5.49 us (16%)
  local copies, waits for them, and re-layouts  4.78 us (14%)
  matrix products  1.93 us (5%)
  other arithmetic  1.42 us (4%)
    ppermute x2, waiting for transfers between devices, body(): lax.ppermute(row_major(send), 'xb', pairs)  7.95 us
    pallas_call x1, Pallas kernels, body(): pl.pallas_call(sweeps_kernel, out_shape=jax.ShapeDtypeStruct(out_shape, j...  5.48 us
    ppermute x2, starting transfers between devices, body(): lax.ppermute(row_major(send), 'xb', pairs)  3.49 us
    pallas_call x1, Pallas kernels, body(): pl.pallas_call(x_kernel, out_shape=[jax.ShapeDtypeStruct(face_shape, jnp....  2.58 us
    pallas_call x1, Pallas kernels, body(): pl.pallas_call(send_kernel, out_shape=[jax.ShapeDtypeStruct((payload_plan...  2.5 us
    dot_general x1, matrix products, body(): lax.dot_general(weights, primaries, (((1,), (0,)), ((), ())), preferred_e...  1.93 us
    ppermute x1, waiting for transfers between devices, body(): lax.ppermute(row_major(send), 'yb', pairs)  1.82 us
    slice x1, local copies, waits for them, and re-layouts, body(): got = lax.ppermute(partial[0], 'tx', tx_ring)  1.56 us
  transfers between devices with their start and end apart: 5, of which 4 were waited for; matrix products, arithmetic and copies ran while one was open for 4% of the time, Pallas kernels for 0%

profile of v22, /device:TPU:16, one launch (start us, length us, event | category | flops | bytes accessed | tf_op | source)
XLA Modules:
  0.0 35.0 jit_solution(15487716784950527379)
XLA Ops:
  0.0 0.9 %reshape.9 = s32[2,16]{1,0:T(2,128)S(1)} reshape(s32[32]{0:T(128)} %param.6) | data formatting | bytes 256 | tf_op jit(solution)/shard_map/reshape | solution.py:225
  0.9 0.8 %reshape.10 = s32[2,16]{1,0:T(2,128)S(1)} reshape(s32[32]{0:T(128)} %param.7) | data formatting | bytes 256 | tf_op jit(solution)/shard_map/reshape | solution.py:226
  1.7 0.1 pad_add_fusion
  1.8 0.1 select_reduce_fusion.1
  1.9 0.0 copy-done
  1.9 1.9 %fusion = f32[2,2,3,32,4,128]{5,0,4,3,2,1:T(2,128)S(1)} fusion(bf16[16,2,3,32,4,128]{5,4,3,2,1,0:T(4,128)(2,1)S(1)} %copy-done, s32[16]{0:T(128)S(1)} %get-tuple-element.10, s32[16]{0:T(128)S(1)} %get-tuple-element.9, s32[2]{0:T(128)S(1)} %pad_add_fusion), kind=kOutput, calls=%fused_computation | convolution fusion | flops 6291584 | bytes 3932296 | tf_op jit(solution)/shard_map/dot_general | solution.py:229
  3.8 1.6 %fusion.19 = (f32[1,2,3,32,4,128]{5,0,4,3,2,1:T(1,128)}, f32[1,2,3,32,4,128]{5,0,4,3,2,1:T(1,128)}) fusion(f32[2,2,3,32,4,128]{5,0,4,3,2,1:T(2,128)S(1)} %fusion), kind=kLoop, calls=%fused_computation.27 | loop fusion | bytes 1572864 | tf_op jit(solution)/shard_map/slice | solution.py:233
  5.4 0.0 collective-permute-start
  5.4 0.5 %collective-permute-start.1 = (f32[3,16,4,128]{3,2,1,0:T(4,128)}, f32[3,16,4,128]{3,2,1,0:T(4,128)}, u32[]{:S(2)}, u32[]{:S(2)}) collective-permute-start(f32[3,16,4,128]{3,2,1,0:T(4,128)} %sigma_ref.5), channel_id=1, source_target_pairs={{0,1},{1,0},{2,3},{3,2},{4,5},{5,4},{6,7},{7,6},{8,9},{9,8},{10,11... | collective-permute-start | bytes 294920 | tf_op jit(solution)/shard_map/ppermute | solution.py:234
  5.9 0.1 stack.35
  6.0 0.6 %stack.36.flags_ref = s32[5]{0:T(128)} convert(pred[5]{0:T(512)(128)(4,1)S(1)} %stack.35) | non-fusion elementwise | flops 5 | bytes 25 | tf_op jit(solution)/shard_map/stack | solution.py:243
  6.6 1.0 %collective-permute-done.1.other_ref = f32[3,16,4,128]{3,2,1,0:T(4,128)} collective-permute-done((f32[3,16,4,128]{3,2,1,0:T(4,128)}, f32[3,16,4,128]{3,2,1,0:T(4,128)}, u32[]{:S(2)}, u32[]{:S(2)}) %collective-permute-start.1) | collective-permute-done | bytes 98336 | tf_op jit(solution)/shard_map/ppermute | solution.py:234
  7.6 0.8 %copy-done.1 = f32[2,3,32,4,128]{4,3,2,1,0:T(4,128)} copy-done((f32[2,3,32,4,128]{4,3,2,1,0:T(4,128)}, f32[2,3,32,4,128]{4,3,2,1,0:T(4,128)S(1)}, u32[]{:S(2)}) %copy-start.1) | copy-done | bytes 393240
  8.4 2.5 %shard_map.46 = (f32[480,128]{1,0:T(8,128)}, f32[480,128]{1,0:T(8,128)}) custom-call(s32[5]{0:T(128)} %stack.36.flags_ref, f32[2,3,32,4,128]{4,3,2,1,0:T(4,128)} %bitcast.18, f32[2,3,32,4,128]{4,3,2,1,0:T(4,128)} %copy-done.1, f32[3,16,4,128]{3,2,1,0:T(4,128)} %sigma_ref.5, f32[3,16,4,128]{3,2,1,0:T(4,128)} %collective-permute-done.1.other_ref), custom_call_target="tpu_custom_call" | custom-call | tf_op jit(solution)/shard_map/pallas_call | solution.py:286
  10.9 1.6 %collective-permute-start.2 = (f32[480,128]{1,0:T(8,128)}, f32[480,128]{1,0:T(8,128)S(1)}, u32[]{:S(2)}, u32[]{:S(2)}) collective-permute-start(f32[480,128]{1,0:T(8,128)} %get-tuple-element.7), channel_id=1, source_target_pairs={{0,4},{4,0},{8,12},{12,8},{1,5},{5,1},{9,13},{13,9},{2,6},{6,2},{1... | collective-permute-start | bytes 737288 | tf_op jit(solution)/shard_map/ppermute | solution.py:293
  12.4 1.9 %collective-permute-start.3 = (f32[480,128]{1,0:T(8,128)}, f32[480,128]{1,0:T(8,128)}, u32[]{:S(2)}, u32[]{:S(2)}) collective-permute-start(f32[480,128]{1,0:T(8,128)} %get-tuple-element.8), channel_id=1, source_target_pairs={{4,8},{8,4},{5,9},{9,5},{6,10},{10,6},{7,11},{11,7},{20,24},{24,20... | collective-permute-start | bytes 737288 | tf_op jit(solution)/shard_map/ppermute | solution.py:293
  14.4 4.7 %collective-permute-done.2.refs_0_ = f32[480,128]{1,0:T(8,128)S(1)} collective-permute-done((f32[480,128]{1,0:T(8,128)}, f32[480,128]{1,0:T(8,128)S(1)}, u32[]{:S(2)}, u32[]{:S(2)}) %collective-permute-start.2) | collective-permute-done | bytes 245792 | tf_op jit(solution)/shard_map/ppermute | solution.py:293
  19.1 3.3 %collective-permute-done.3.refs_1_ = f32[480,128]{1,0:T(8,128)} collective-permute-done((f32[480,128]{1,0:T(8,128)}, f32[480,128]{1,0:T(8,128)}, u32[]{:S(2)}, u32[]{:S(2)}) %collective-permute-start.3) | collective-permute-done | bytes 245792 | tf_op jit(solution)/shard_map/ppermute | solution.py:293
  22.4 2.6 %shard_map.47 = f32[2,2304]{1,0:T(2,128)} custom-call(s32[5]{0:T(128)} %stack.36.flags_ref, f32[2,3,32,4,128]{4,3,2,1,0:T(4,128)} %bitcast.19, f32[2,3,32,4,128]{4,3,2,1,0:T(4,128)} %copy-done.1, f32[3,16,4,128]{3,2,1,0:T(4,128)} %sigma_ref.5, f32[3,16,4,128]{3,2,1,0:T(4,128)} %collective-permute-done.1.other_ref, f32[480,128]{1,0:T(8,128)} %copy-done.2, ...), custom_call_target="tpu_custom_call" | custom-call | tf_op jit(solution)/shard_map/pallas_call | solution.py:327
  24.9 1.5 %collective-permute-start.4 = (f32[2,2304]{1,0:T(2,128)}, f32[2,2304]{1,0:T(2,128)S(1)}, u32[]{:S(2)}, u32[]{:S(2)}) collective-permute-start(f32[2,2304]{1,0:T(2,128)} %shard_map.47), channel_id=1, source_target_pairs={{0,2},{2,0},{1,3},{3,1},{4,6},{6,4},{5,7},{7,5},{8,10},{10,8},{9,1... | collective-permute-start | bytes 55304 | tf_op jit(solution)/shard_map/ppermute | solution.py:334
  26.4 0.7 %fusion.9.refs_4_ = f32[8,256]{1,0:T(8,128)} fusion(s32[256]{0:T(256)S(1)} %iota_add_fusion, s32[]{:T(128)S(6)} %mul.7, pred[8]{0:T(512)(128)(4,1)S(1)} %compare_and_fusion, pred[256]{0:T(512)(128)(4,1)S(1)} %iota_compare_fusion), kind=kLoop, calls=%fused_computation.10 | loop fusion | flops 18432 | bytes 9484 | tf_op jit(solution)/shard_map/convert_element_type | solution.py:379
  27.1 1.8 %collective-permute-done.4.refs_2_.refs_3_ = f32[2,2304]{1,0:T(2,128)S(1)} collective-permute-done((f32[2,2304]{1,0:T(2,128)}, f32[2,2304]{1,0:T(2,128)S(1)}, u32[]{:S(2)}, u32[]{:S(2)}) %collective-permute-start.4) | collective-permute-done | bytes 18464 | tf_op jit(solution)/shard_map/ppermute | solution.py:334
  28.9 0.6 %copy-done.3 = f32[2,2304]{1,0:T(2,128)} copy-done((f32[2,2304]{1,0:T(2,128)}, f32[2,2304]{1,0:T(2,128)S(1)}, u32[]{:S(2)}) %copy-start.3) | copy-done | bytes 18456
  29.5 5.5 %shard_map.48 = f32[2,3,32,4,128]{4,3,2,1,0:T(4,128)} custom-call(s32[5]{0:T(128)} %stack.36.flags_ref, f32[2,3,32,4,128]{4,3,2,1,0:T(4,128)} %bitcast.20, f32[2,3,32,4,128]{4,3,2,1,0:T(4,128)} %copy-done.1, f32[3,16,4,128]{3,2,1,0:T(4,128)} %sigma_ref.5, f32[3,16,4,128]{3,2,1,0:T(4,128)} %collective-permute-done.1.other_ref, f32[480,128]{1,0:T(8,128)} %copy-done.2, ...), custom_call_target="tpu_custom_call" | custom-call | tf_op jit(solution)/shard_map/pallas_call | solution.py:374
  (10 shorter events, 0.0 us)
Async XLA Ops:
  0.0 1.9 %copy-start = (bf16[16,2,3,32,4,128]{5,4,3,2,1,0:T(4,128)(2,1)S(1)}, bf16[16,2,3,32,4,128]{5,4,3,2,1,0:T(4,128)(2,1)}, u32[]{:S(2)}) copy-start(bf16[16,2,3,32,4,128]{5,4,3,2,1,0:T(4,128)(2,1)} %param.4) | copy-start | bytes 9437188
  5.4 2.2 %collective-permute-start = (f32[2,3,32,4,128]{4,3,2,1,0:T(4,128)}, f32[2,3,32,4,128]{4,3,2,1,0:T(4,128)S(1)}, u32[]{:S(2)}, u32[]{:S(2)}) collective-permute-start(f32[2,3,32,4,128]{4,3,2,1,0:T(4,128)} %bitcast.9), channel_id=1, source_target_pairs={{0,1},{1,0},{2,3},{3,2},{4,5},{5,4},{6,7},{7,6},{8,9},{9,8},{10,11... | collective-permute-start | bytes 1179656 | tf_op jit(solution)/shard_map/ppermute | solution.py:233
  5.4 2.2 %collective-permute-start.1 = (f32[3,16,4,128]{3,2,1,0:T(4,128)}, f32[3,16,4,128]{3,2,1,0:T(4,128)}, u32[]{:S(2)}, u32[]{:S(2)}) collective-permute-start(f32[3,16,4,128]{3,2,1,0:T(4,128)} %sigma_ref.5), channel_id=1, source_target_pairs={{0,1},{1,0},{2,3},{3,2},{4,5},{5,4},{6,7},{7,6},{8,9},{9,8},{10,11... | collective-permute-start | bytes 294920 | tf_op jit(solution)/shard_map/ppermute | solution.py:234
  7.6 0.8 %copy-start.1 = (f32[2,3,32,4,128]{4,3,2,1,0:T(4,128)}, f32[2,3,32,4,128]{4,3,2,1,0:T(4,128)S(1)}, u32[]{:S(2)}) copy-start(f32[2,3,32,4,128]{4,3,2,1,0:T(4,128)S(1)} %collective-permute-done.got_ref) | copy-start | bytes 1179652
  10.9 8.2 %collective-permute-start.2 = (f32[480,128]{1,0:T(8,128)}, f32[480,128]{1,0:T(8,128)S(1)}, u32[]{:S(2)}, u32[]{:S(2)}) collective-permute-start(f32[480,128]{1,0:T(8,128)} %get-tuple-element.7), channel_id=1, source_target_pairs={{0,4},{4,0},{8,12},{12,8},{1,5},{5,1},{9,13},{13,9},{2,6},{6,2},{1... | collective-permute-start | bytes 737288 | tf_op jit(solution)/shard_map/ppermute | solution.py:293
  12.4 9.9 %collective-permute-start.3 = (f32[480,128]{1,0:T(8,128)}, f32[480,128]{1,0:T(8,128)}, u32[]{:S(2)}, u32[]{:S(2)}) collective-permute-start(f32[480,128]{1,0:T(8,128)} %get-tuple-element.8), channel_id=1, source_target_pairs={{4,8},{8,4},{5,9},{9,5},{6,10},{10,6},{7,11},{11,7},{20,24},{24,20... | collective-permute-start | bytes 737288 | tf_op jit(solution)/shard_map/ppermute | solution.py:293
  19.1 3.3 %copy-start.2 = (f32[480,128]{1,0:T(8,128)}, f32[480,128]{1,0:T(8,128)S(1)}, u32[]{:S(2)}) copy-start(f32[480,128]{1,0:T(8,128)S(1)} %collective-permute-done.2.refs_0_) | copy-start | bytes 737284
  24.9 4.0 %collective-permute-start.4 = (f32[2,2304]{1,0:T(2,128)}, f32[2,2304]{1,0:T(2,128)S(1)}, u32[]{:S(2)}, u32[]{:S(2)}) collective-permute-start(f32[2,2304]{1,0:T(2,128)} %shard_map.47), channel_id=1, source_target_pairs={{0,2},{2,0},{1,3},{3,1},{4,6},{6,4},{5,7},{7,5},{8,10},{10,8},{9,1... | collective-permute-start | bytes 55304 | tf_op jit(solution)/shard_map/ppermute | solution.py:334
  28.9 0.6 %copy-start.3 = (f32[2,2304]{1,0:T(2,128)}, f32[2,2304]{1,0:T(2,128)S(1)}, u32[]{:S(2)}) copy-start(f32[2,2304]{1,0:T(2,128)S(1)} %collective-permute-done.4.refs_2_.refs_3_) | copy-start | bytes 55300
